TPU v7x, 512 devices: a whole 4x8x8 slice. The times are simulated.
512 devices in a mesh: gx: 16 (over x_hi, z), gy: 32 (over y, x_lo, core).
Axes of the slice: x: 4 (x_hi: 2, x_lo: 2; x = x_hi * 2 + x_lo), y: 8, z: 8, core: 2. Of those that a mesh axis runs over, the one named last changes fastest.
Arguments:
- features: bfloat16 [16, 32, 16, 256], P('gx', 'gy'), may hold values from -6 to 6
- atom_kinds: int32 [16, 32, 16], P('gx', 'gy'), may hold values from 0 to 1
- kind_table: float32 [2, 256], replicated, may hold values from -6 to 6
- band_vectors: bfloat16 [16, 32, 16, 13, 32], P('gx', 'gy'), may hold values from -6 to 6
- pair_offsets: float32 [16, 32, 3, 9, 128], P('gx', 'gy'), may hold values from -7 to 7, as said below
- pair_source: int32 [16, 32, 9, 128], P('gx', 'gy'), may hold values from 0 to 15
- pair_target: int32 [16, 32, 9, 128], P('gx', 'gy'), may hold values from 0 to 15
- pair_live_mask: int32 [16, 32, 9, 128], P('gx', 'gy'), may hold values from 0 to 1, as said below
- radial_weight: bfloat16 [16, 256], replicated, may hold values from -1.5 to 1.5
- w_source: bfloat16 [256, 256], replicated, may hold values from -0.375 to 0.375
- w_target: bfloat16 [256, 256], replicated, may hold values from -0.375 to 0.375
- mixing_weight: bfloat16 [256, 256], replicated, may hold values from -0.375 to 0.375
- gate_weight: bfloat16 [256, 256], replicated, may hold values from -0.375 to 0.375
- output_weight: bfloat16 [256, 169], replicated, may hold values from -0.375 to 0.375
- w_site: bfloat16 [256, 169], replicated, may hold values from -0.375 to 0.375
Outputs:
- filtered: float32 [16, 32, 16, 13, 32], P('gx', 'gy')
Inputs may be any that keep to these rules, and one draw needn't show every extreme that they name: `pair_offsets`: the length of every offset lies between 1.2 and 8. `pair_live_mask`: the share of live slots differs from block to block.
All inputs are finite; a program needn't handle non-finite values.
Results may differ from a plain program's by a relative error of at most 0.007.
Values may be sent and summed in bfloat16 or wider, within the bound.
No kernel may reach another device: no remote copies, remote signals or barrier semaphores. Data moves between devices by JAX's collectives and lax.ppermute only.
A program may use at most 64 MiB of HBM per device.

v0:
```python
import math

import jax
import jax.numpy as jnp
from jax import lax
from jax.sharding import PartitionSpec as P

NEIGHBOUR_SLOTS = 72
RBF = 16
ORBITAL_COUNT = 13
FILTER = 3


cutoff = 8.0
onsite_scale = 0.15


def padded(cells, sides, width):
    for axis, dim in sides:
        count = lax.axis_size(axis)
        head = lax.slice_in_dim(cells, 0, width, axis=dim)
        tail = lax.slice_in_dim(cells, cells.shape[dim] - width, cells.shape[dim], axis=dim)
        cells = jnp.concatenate(
            [
                lax.ppermute(tail, axis, [(i, (i + 1) % count) for i in range(count)]),
                cells,
                lax.ppermute(head, axis, [((i + 1) % count, i) for i in range(count)]),
            ],
            axis=dim,
        )
    return cells


def shifted(value, axis, steps):
    count = lax.axis_size(axis)
    pairs = [(source, (source + steps) % count) for source in range(count)]
    return lax.ppermute(value, axis, pairs)


def radial(block_offsets):
    distance = jnp.sqrt(
        block_offsets[0] * block_offsets[0]
        + block_offsets[1] * block_offsets[1]
        + block_offsets[2] * block_offsets[2]
    )
    centres = cutoff * jnp.arange(RBF, dtype=jnp.float32) / (RBF - 1)
    spacing = cutoff / (RBF - 1)
    basis = jnp.exp(-jnp.square((distance[:, None] - centres[None, :]) / spacing)).astype(
        jnp.bfloat16
    )
    cutoff_envelope = jnp.square(1.0 - jnp.square(distance / cutoff))
    return (basis, cutoff_envelope)


def pair_block_matrices(
    source_atom_rows,
    target_atom_rows,
    block_offsets,
    live_flags,
    radial_weight,
    mixing_weight,
    gate_weight,
    output_weight,
):
    basis, cutoff_envelope = radial(block_offsets)
    before = (
        source_atom_rows
        + target_atom_rows
        + jnp.dot(basis, radial_weight, preferred_element_type=jnp.float32)
    )
    edge = jax.nn.silu(before).astype(jnp.bfloat16)
    opened = jax.nn.silu(jnp.dot(edge, mixing_weight, preferred_element_type=jnp.float32))
    mixed = (opened * jnp.dot(edge, gate_weight, preferred_element_type=jnp.float32)).astype(
        jnp.bfloat16
    )
    raw_out = jnp.dot(mixed, output_weight, preferred_element_type=jnp.float32)
    scale_factor = 1.5 / math.sqrt(NEIGHBOUR_SLOTS * ORBITAL_COUNT) * cutoff_envelope * live_flags
    return (raw_out * scale_factor[:, None]).astype(jnp.bfloat16)


def onsite_blocks(atoms, w_site):
    square = jnp.dot(atoms, w_site, preferred_element_type=jnp.float32).reshape(
        -1, ORBITAL_COUNT, ORBITAL_COUNT
    )
    return (onsite_scale * 0.5 * (square + jnp.swapaxes(square, 1, 2))).astype(jnp.bfloat16)


def blocks_last(flat_blocks):
    return jnp.transpose(flat_blocks.reshape(-1, ORBITAL_COUNT * ORBITAL_COUNT)).reshape(
        ORBITAL_COUNT, ORBITAL_COUNT, -1
    )


def orbital_product(blocks, vectors, transposed):
    if transposed:
        return jnp.einsum("oqp,ovp->qvp", blocks, vectors, preferred_element_type=jnp.float32)
    return jnp.einsum("oqp,qvp->ovp", blocks, vectors, preferred_element_type=jnp.float32)


def one_hot_rows(indices, segments):
    return (indices[:, None] == jnp.arange(segments, dtype=jnp.int32)[None, :]).astype(jnp.float32)


def scatter_rows(values, hot_table):
    flat = values.reshape(-1, values.shape[2])
    summed = jnp.dot(flat, hot_table, precision=lax.Precision.HIGHEST)
    return summed.reshape(values.shape[0], values.shape[1], hot_table.shape[1])


def on_device(
    features,
    atom_kinds,
    kind_table,
    band_vectors,
    pair_offsets,
    pair_source,
    pair_target,
    pair_live_mask,
    radial_weight,
    w_source,
    w_target,
    mixing_weight,
    gate_weight,
    output_weight,
    w_site,
):
    atom_count = features.shape[2]
    kind_hot = (
        atom_kinds[0, 0][:, None] == jnp.arange(kind_table.shape[0], dtype=jnp.int32)[None, :]
    ).astype(jnp.float32)
    embedded = jnp.dot(kind_hot, kind_table, precision=lax.Precision.HIGHEST)
    atoms = (features[0, 0].astype(jnp.float32) + embedded).astype(jnp.bfloat16)
    beside_all = padded(atoms[None, None], (("gx", 0), ("gy", 1)), 1)
    beside_all = beside_all.reshape(9 * atom_count, atoms.shape[1])
    source_projection = jnp.dot(atoms, w_source, preferred_element_type=jnp.float32)
    target_projection = jnp.dot(beside_all, w_target, preferred_element_type=jnp.float32)
    source_indices = pair_source[0, 0].reshape(-1)
    block_base = jnp.arange(9, dtype=jnp.int32)[:, None] * atom_count
    target_indices = (block_base + pair_target[0, 0]).reshape(-1)
    live_flags = pair_live_mask[0, 0].reshape(-1).astype(jnp.float32)
    block_offsets = pair_offsets[0, 0].reshape(3, -1)
    hopping_block = pair_block_matrices(
        source_projection[source_indices],
        target_projection[target_indices],
        block_offsets,
        live_flags,
        radial_weight,
        mixing_weight,
        gate_weight,
        output_weight,
    )
    onsite_laid = blocks_last(onsite_blocks(atoms, w_site))
    matrices = blocks_last(hopping_block)
    source_hot = one_hot_rows(source_indices, atom_count)
    target_hot = one_hot_rows(target_indices, 9 * atom_count)

    def apply(vector_rows):
        rim = padded(vector_rows[None, None], (("gx", 0), ("gy", 1)), 1)
        rim = jnp.transpose(rim, (2, 3, 0, 1, 4)).reshape(
            ORBITAL_COUNT, vector_rows.shape[1], 9 * atom_count
        )
        summed = orbital_product(onsite_laid, vector_rows, False)
        forward = orbital_product(matrices, jnp.take(rim, target_indices, axis=2), False)
        summed = summed + scatter_rows(forward, source_hot)
        backward = orbital_product(matrices, jnp.take(vector_rows, source_indices, axis=2), True)
        spill = scatter_rows(backward, target_hot).reshape(ORBITAL_COUNT, -1, 3, 3, atom_count)
        from_low = shifted(spill[:, :, :, 2].astype(jnp.bfloat16), "gy", 1).astype(jnp.float32)
        from_high = shifted(spill[:, :, :, 0].astype(jnp.bfloat16), "gy", -1).astype(jnp.float32)
        column = spill[:, :, :, 1] + from_low + from_high
        from_west = shifted(column[:, :, 2], "gx", 1)
        from_east = shifted(column[:, :, 0], "gx", -1)
        summed = summed + column[:, :, 1] + from_west + from_east
        return summed

    first = jnp.transpose(band_vectors[0, 0], (1, 2, 0))
    previous = first.astype(jnp.float32)
    current = apply(first)
    for repeat in range(FILTER - 1):
        upcoming = 2.0 * apply(current.astype(jnp.bfloat16)) - previous
        previous, current = (current, upcoming)
    return jnp.transpose(current, (2, 0, 1))[None, None]


def solution(mesh):
    in_specs = (
        P("gx", "gy", None, None),
        P("gx", "gy", None),
        P(),
        P("gx", "gy", None, None, None),
        P("gx", "gy", None, None, None),
        P("gx", "gy", None, None),
        P("gx", "gy", None, None),
        P("gx", "gy", None, None),
        P(),
        P(),
        P(),
        P(),
        P(),
        P(),
        P(),
    )
    out_specs = P("gx", "gy", None, None, None)
    return jax.shard_map(
        on_device, mesh=mesh, in_specs=in_specs, out_specs=out_specs, check_vma=False
    )
```

profile of v0, /device:TPU:1, one launch (start us, length us, event | category | flops | bytes accessed | tf_op | source)
XLA Modules:
  0.0 257.1 jit_solution(9673416044247901132)
XLA Ops:
  0.0 1.0 fusion.77
  1.0 14.0 %collective-permute-start.5 = (bf16[1,1,16,256]{3,2,1,0:T(8,128)(2,1)S(1)}, bf16[1,1,16,256]{3,2,1,0:T(8,128)(2,1)S(1)}, u32[]{:S(2)}, u32[]{:S(2)}) collective-permute-start(bf16[1,1,16,256]{3,2,1,0:T(8,128)(2,1)S(1)} %bitcast.266), channel_id=1, source_target_pairs={{32,0},{64,32},{96,64},{128,96},{160,128},{192,160},{224,192},{256... | collective-permute-start | bytes 24584 | tf_op jit(solution)/shard_map/ppermute | solution.py:27
  14.9 1.9 collective-permute-start.4
  16.9 0.8 copy.101
  17.7 7.0 %collective-permute-start.1 = (bf16[1,1,13,32,16]{3,2,4,1,0:T(8,128)(2,1)S(1)}, bf16[1,1,13,32,16]{3,2,4,1,0:T(8,128)(2,1)S(1)}, u32[]{:S(2)}, u32[]{:S(2)}) collective-permute-start(bf16[1,1,13,32,16]{3,2,4,1,0:T(8,128)(2,1)S(1)} %bitcast.254), channel_id=1, source_target_pairs={{32,0},{64,32},{96,64},{128,96},{160,128},{192,160},{224,192},{256... | collective-permute-start | bytes 39944 | tf_op jit(solution)/shard_map/ppermute | solution.py:27
  24.7 1.9 collective-permute-start
  27.2 0.7 reduce.5
  28.0 0.7 fusion.118
  28.7 0.8 sqrt_reduce_fusion
  29.5 0.7 reduce
  30.2 0.7 fusion.119
  31.0 0.7 convert_reduce_fusion
  31.8 1.0 fusion.132
  32.8 1.0 fusion.131
  35.6 3.3 %gather_fusion = f32[1152,256]{1,0:T(8,128)S(1)} fusion(f32[16,256]{1,0:T(8,128)S(1)} %fusion.132, s32[2048]{0:T(1024)S(1)} %pad_clamp_fusion.2), kind=kCustom, calls=%fused_computation.6 | custom fusion | bytes 2363904 | tf_op jit(solution)/shard_map/gather | solution.py:143
  38.9 4.8 %gather_fusion.3 = bf16[1152,13,32]{2,1,0:T(8,128)(2,1)} fusion(bf16[13,32,16]{1,0,2:T(8,128)(2,1)S(1)} %bitcast.256, s32[2048]{0:T(1024)S(1)} %pad_clamp_fusion), kind=kCustom, calls=%fused_computation.1.clone | custom fusion | bytes 1921536 | tf_op jit(solution)/shard_map/jit(_take)/gather | solution.py:165
  43.8 3.4 %collective-permute-start.7 = (bf16[3,1,16,256]{3,2,1,0:T(8,128)(2,1)S(1)}, bf16[3,1,16,256]{3,2,1,0:T(8,128)(2,1)S(1)}, u32[]{:S(2)}, u32[]{:S(2)}) collective-permute-start(bf16[3,1,16,256]{3,2,1,0:T(8,128)(2,1)S(1)} %pad_maximum_fusion.7), channel_id=1, source_target_pairs={{1,0},{2,1},{3,2},{4,3},{5,4},{6,5},{7,6},{8,7},{9,8},{10,9},{11,1... | collective-permute-start | bytes 73736 | tf_op jit(solution)/shard_map/ppermute | solution.py:27
  47.2 2.1 collective-permute-start.6
  49.4 0.7 pad_maximum_fusion.3
  50.1 3.8 %collective-permute-start.3 = (bf16[3,1,13,32,16]{3,2,4,1,0:T(8,128)(2,1)}, bf16[3,1,13,32,16]{3,2,4,1,0:T(8,128)(2,1)}, u32[]{:S(2)}, u32[]{:S(2)}) collective-permute-start(bf16[3,1,13,32,16]{3,2,4,1,0:T(8,128)(2,1)} %pad_maximum_fusion.3), channel_id=1, source_target_pairs={{1,0},{2,1},{3,2},{4,3},{5,4},{6,5},{7,6},{8,7},{9,8},{10,9},{11,1... | collective-permute-start | bytes 119816 | tf_op jit(solution)/shard_map/ppermute | solution.py:27
  53.9 2.1 collective-permute-start.2
  56.2 3.3 %gather_fusion.1 = f32[1152,256]{1,0:T(8,128)S(1)} fusion(f32[144,256]{1,0:T(8,128)S(1)} %fusion.133, s32[2048]{0:T(1024)S(1)} %pad_clamp_fusion.1), kind=kCustom, calls=%fused_computation.7 | custom fusion | bytes 2363904 | tf_op jit(solution)/shard_map/gather | solution.py:144
  60.5 1.6 fusion.56
  62.3 4.9 %copy.45 = bf16[13,13,1152]{0,1,2:T(8,128)(2,1)} copy(bf16[13,13,1152]{2,1,0:T(8,128)(2,1)S(1)} %reshape.215) | data formatting | bytes 778752 | tf_op jit(solution)/shard_map/reshape | solution.py:89
  67.2 6.6 %fusion.39 = f32[13,32,1152,1,1]{1,0,2,4,3:T(8,128)S(1)} fusion(bf16[13,13,1152]{0,1,2:T(8,128)(2,1)} %copy.45, bf16[1152,13,32]{2,1,0:T(8,128)(2,1)} %gather_fusion.3, pred[1152]{0:T(1024)(128)(4,1)S(1)} %compare_and_fusion), kind=kOutput, calls=%fused_computation.45 | convolution fusion | flops 12939264 | bytes 3265920 | tf_op jit(solution)/shard_map/oqp,ovp->qvp/dot_general | solution.py:96
  73.8 5.2 %fusion.4 = f32[13,32,3,3,16]{1,4,3,2,0:T(8,128)S(1)} fusion(f32[13,32,1152,1,1]{1,0,2,4,3:T(8,128)S(1)} %fusion.39, s32[3,3,16]{2,1,0:T(4,128)S(1)} %copy-done.13, s32[1152]{0:T(1024)S(1)} %get-tuple-element.10), kind=kOutput, calls=%fused_computation.12 | convolution fusion | flops 828278784 | bytes 2161728 | tf_op jit(solution)/shard_map/dot_general | solution.py:106
  80.1 5.3 %copy.42 = bf16[13,13,1152]{1,0,2:T(8,128)(2,1)} copy(bf16[13,13,1152]{2,1,0:T(8,128)(2,1)S(1)} %reshape.215) | data formatting | bytes 778752 | tf_op jit(solution)/shard_map/reshape | solution.py:89
  85.8 2.6 %collective-permute-start.8 = (bf16[13,32,3,16]{1,0,3,2:T(8,128)(2,1)}, bf16[13,32,3,16]{1,0,3,2:T(8,128)(2,1)S(1)}, u32[]{:S(2)}, u32[]{:S(2)}) collective-permute-start(bf16[13,32,3,16]{1,0,3,2:T(8,128)(2,1)} %get-tuple-element.15), channel_id=1, source_target_pairs={{0,1},{1,2},{2,3},{3,4},{4,5},{5,6},{6,7},{7,8},{8,9},{9,10},{10,1... | collective-permute-start | bytes 119816 | tf_op jit(solution)/shard_map/ppermute | solution.py:37
  88.4 5.3 %collective-permute-start.9 = (bf16[13,32,3,16]{1,0,3,2:T(8,128)(2,1)S(1)}, bf16[13,32,3,16]{1,0,3,2:T(8,128)(2,1)S(1)}, u32[]{:S(2)}, u32[]{:S(2)}) collective-permute-start(bf16[13,32,3,16]{1,0,3,2:T(8,128)(2,1)S(1)} %get-tuple-element.16), channel_id=1, source_target_pairs={{0,31},{1,0},{2,1},{3,2},{4,3},{5,4},{6,5},{7,6},{8,7},{9,8},{10,9... | collective-permute-start | bytes 119816 | tf_op jit(solution)/shard_map/ppermute | solution.py:37
  93.7 1.2 pad_maximum_fusion
  94.9 4.8 %gather_fusion.2 = bf16[1152,13,32]{2,1,0:T(8,128)(2,1)} fusion(bf16[13,32,144]{1,0,2:T(8,128)(2,1)S(1)} %bitcast.259, s32[2048]{0:T(1024)S(1)} %pad_clamp_fusion.3), kind=kCustom, calls=%fused_computation.clone | custom fusion | bytes 1921536 | tf_op jit(solution)/shard_map/jit(_take)/gather | solution.py:163
  99.8 6.6 %fusion.36 = f32[13,32,1152]{1,0,2:T(8,128)S(1)} fusion(bf16[13,13,1152]{1,0,2:T(8,128)(2,1)} %copy.42, bf16[1152,13,32]{2,1,0:T(8,128)(2,1)} %gather_fusion.2, pred[1152]{0:T(1024)(128)(4,1)S(1)} %get-tuple-element.9), kind=kOutput, calls=%fused_computation.44 | convolution fusion | flops 12939264 | bytes 3265920 | tf_op jit(solution)/shard_map/oqp,qvp->ovp/dot_general | solution.py:97
  106.4 4.5 %fusion.10 = f32[13,32,16]{1,2,0:T(8,128)S(1)} fusion(f32[13,32,1152]{1,0,2:T(8,128)S(1)} %fusion.36, s32[1152]{0:T(1024)S(1)} %bitcast.263), kind=kOutput, calls=%fused_computation.18 | convolution fusion | flops 92030976 | bytes 1948160 | tf_op jit(solution)/shard_map/dot_general | solution.py:106
  111.1 1.9 collective-permute-start.10
  113.0 7.6 %collective-permute-start.11 = (f32[13,32,16]{1,0,2:T(8,128)S(1)}, f32[13,32,16]{1,0,2:T(8,128)S(1)}, u32[]{:S(2)}, u32[]{:S(2)}) collective-permute-start(f32[13,32,16]{1,0,2:T(8,128)S(1)} %get-tuple-element.22), channel_id=1, source_target_pairs={{0,480},{32,0},{64,32},{96,64},{128,96},{160,128},{192,160},{224,1... | collective-permute-start | bytes 79880 | tf_op jit(solution)/shard_map/ppermute | solution.py:37
  121.0 1.5 collective-permute-done.11
  122.6 7.4 %collective-permute-start.13 = (bf16[1,1,13,32,16]{3,2,4,1,0:T(8,128)(2,1)S(1)}, bf16[1,1,13,32,16]{3,2,4,1,0:T(8,128)(2,1)S(1)}, u32[]{:S(2)}, u32[]{:S(2)}) collective-permute-start(bf16[1,1,13,32,16]{3,2,4,1,0:T(8,128)(2,1)S(1)} %bitcast.250), channel_id=1, source_target_pairs={{32,0},{64,32},{96,64},{128,96},{160,128},{192,160},{224,192},{256... | collective-permute-start | bytes 39944 | tf_op jit(solution)/shard_map/ppermute | solution.py:27
  130.0 2.2 collective-permute-start.12
  132.2 4.8 %gather_fusion.5 = bf16[1152,13,32]{2,1,0:T(8,128)(2,1)} fusion(bf16[13,32,16]{1,0,2:T(8,128)(2,1)S(1)} %get-tuple-element.6, s32[2048]{0:T(1024)S(1)} %copy-done.6), kind=kCustom, calls=%fused_computation.4.clone | custom fusion | bytes 1921536 | tf_op jit(solution)/shard_map/jit(_take)/gather | solution.py:165
  137.0 6.6 %fusion.45 = f32[13,32,1152,1,1]{1,0,2,4,3:T(8,128)S(1)} fusion(bf16[13,13,1152]{0,1,2:T(8,128)(2,1)} %copy.45, bf16[1152,13,32]{2,1,0:T(8,128)(2,1)} %gather_fusion.5, pred[1152]{0:T(1024)(128)(4,1)S(1)} %copy-done.9), kind=kOutput, calls=%fused_computation.47 | convolution fusion | flops 12939264 | bytes 3265920 | tf_op jit(solution)/shard_map/oqp,ovp->qvp/dot_general | solution.py:96
  143.7 5.2 %fusion.2 = f32[13,32,3,3,16]{1,4,3,2,0:T(8,128)S(1)} fusion(f32[13,32,1152,1,1]{1,0,2,4,3:T(8,128)S(1)} %fusion.45, s32[3,3,16]{2,1,0:T(4,128)S(1)} %copy-done.13, s32[1152]{0:T(1024)S(1)} %copy-done.11), kind=kOutput, calls=%fused_computation.10 | convolution fusion | flops 828278784 | bytes 2161728 | tf_op jit(solution)/shard_map/dot_general | solution.py:106
  149.6 3.1 %collective-permute-start.16 = (bf16[13,32,3,16]{1,0,3,2:T(8,128)(2,1)S(1)}, bf16[13,32,3,16]{1,0,3,2:T(8,128)(2,1)S(1)}, u32[]{:S(2)}, u32[]{:S(2)}) collective-permute-start(bf16[13,32,3,16]{1,0,3,2:T(8,128)(2,1)S(1)} %get-tuple-element.13), channel_id=1, source_target_pairs={{0,1},{1,2},{2,3},{3,4},{4,5},{5,6},{6,7},{7,8},{8,9},{9,10},{10,1... | collective-permute-start | bytes 119816 | tf_op jit(solution)/shard_map/ppermute | solution.py:37
  152.7 6.0 %collective-permute-start.17 = (bf16[13,32,3,16]{1,0,3,2:T(8,128)(2,1)S(1)}, bf16[13,32,3,16]{1,0,3,2:T(8,128)(2,1)S(1)}, u32[]{:S(2)}, u32[]{:S(2)}) collective-permute-start(bf16[13,32,3,16]{1,0,3,2:T(8,128)(2,1)S(1)} %get-tuple-element.14), channel_id=1, source_target_pairs={{0,31},{1,0},{2,1},{3,2},{4,3},{5,4},{6,5},{7,6},{8,7},{9,8},{10,9... | collective-permute-start | bytes 119816 | tf_op jit(solution)/shard_map/ppermute | solution.py:37
  158.8 5.8 %collective-permute-start.15 = (bf16[3,1,13,32,16]{3,2,4,1,0:T(8,128)(2,1)S(1)}, bf16[3,1,13,32,16]{3,2,4,1,0:T(8,128)(2,1)S(1)}, u32[]{:S(2)}, u32[]{:S(2)}) collective-permute-start(bf16[3,1,13,32,16]{3,2,4,1,0:T(8,128)(2,1)S(1)} %pad_maximum_fusion.4), channel_id=1, source_target_pairs={{1,0},{2,1},{3,2},{4,3},{5,4},{6,5},{7,6},{8,7},{9,8},{10,9},{11,1... | collective-permute-start | bytes 119816 | tf_op jit(solution)/shard_map/ppermute | solution.py:27
  164.6 1.9 collective-permute-start.14
  166.6 1.9 collective-permute-start.18
  168.5 7.7 %collective-permute-start.19 = (f32[13,32,16]{1,0,2:T(8,128)S(1)}, f32[13,32,16]{1,0,2:T(8,128)S(1)}, u32[]{:S(2)}, u32[]{:S(2)}) collective-permute-start(f32[13,32,16]{1,0,2:T(8,128)S(1)} %get-tuple-element.20), channel_id=1, source_target_pairs={{0,480},{32,0},{64,32},{96,64},{128,96},{160,128},{192,160},{224,1... | collective-permute-start | bytes 79880 | tf_op jit(solution)/shard_map/ppermute | solution.py:37
  176.5 4.8 %gather_fusion.4 = bf16[1152,13,32]{2,1,0:T(8,128)(2,1)} fusion(bf16[13,32,144]{1,0,2:T(8,128)(2,1)S(1)} %bitcast.261, s32[2048]{0:T(1024)S(1)} %pad_clamp_fusion.3), kind=kCustom, calls=%fused_computation.2.clone | custom fusion | bytes 1921536 | tf_op jit(solution)/shard_map/jit(_take)/gather | solution.py:163
  181.3 6.6 %fusion.42 = f32[13,32,1152]{1,0,2:T(8,128)S(1)} fusion(bf16[13,13,1152]{1,0,2:T(8,128)(2,1)} %copy.42, bf16[1152,13,32]{2,1,0:T(8,128)(2,1)} %gather_fusion.4, pred[1152]{0:T(1024)(128)(4,1)S(1)} %get-tuple-element.9), kind=kOutput, calls=%fused_computation.46 | convolution fusion | flops 12939264 | bytes 3265920 | tf_op jit(solution)/shard_map/oqp,qvp->ovp/dot_general | solution.py:97
  187.9 4.5 %fusion.8 = f32[13,32,16]{1,2,0:T(8,128)S(1)} fusion(f32[13,32,1152]{1,0,2:T(8,128)S(1)} %fusion.42, s32[1152]{0:T(1024)S(1)} %bitcast.264), kind=kOutput, calls=%fused_computation.16 | convolution fusion | flops 92030976 | bytes 1948160 | tf_op jit(solution)/shard_map/dot_general | solution.py:106
  192.7 3.4 %collective-permute-start.21 = (bf16[1,1,13,32,16]{3,2,4,1,0:T(8,128)(2,1)S(1)}, bf16[1,1,13,32,16]{3,2,4,1,0:T(8,128)(2,1)S(1)}, u32[]{:S(2)}, u32[]{:S(2)}) collective-permute-start(bf16[1,1,13,32,16]{3,2,4,1,0:T(8,128)(2,1)S(1)} %bitcast.246), channel_id=1, source_target_pairs={{32,0},{64,32},{96,64},{128,96},{160,128},{192,160},{224,192},{256... | collective-permute-start | bytes 39944 | tf_op jit(solution)/shard_map/ppermute | solution.py:27
  196.0 2.1 collective-permute-start.20
  198.1 4.8 %gather_fusion.7 = bf16[1152,13,32]{2,1,0:T(8,128)(2,1)} fusion(bf16[13,32,16]{1,0,2:T(8,128)(2,1)S(1)} %fusion.76, s32[2048]{0:T(1024)S(1)} %copy-done.6), kind=kCustom, calls=%fused_computation.5.clone | custom fusion | bytes 1921536 | tf_op jit(solution)/shard_map/jit(_take)/gather | solution.py:165
  203.0 6.6 %fusion.51 = f32[13,32,1152,1,1]{1,0,2,4,3:T(8,128)S(1)} fusion(bf16[13,13,1152]{0,1,2:T(8,128)(2,1)} %copy.45, bf16[1152,13,32]{2,1,0:T(8,128)(2,1)} %gather_fusion.7, pred[1152]{0:T(1024)(128)(4,1)S(1)} %copy-done.9), kind=kOutput, calls=%fused_computation.49 | convolution fusion | flops 12939264 | bytes 3265920 | tf_op jit(solution)/shard_map/oqp,ovp->qvp/dot_general | solution.py:96
  209.6 5.2 %fusion = f32[13,32,3,3,16]{1,4,3,2,0:T(8,128)S(1)} fusion(f32[13,32,1152,1,1]{1,0,2,4,3:T(8,128)S(1)} %fusion.51, s32[3,3,16]{2,1,0:T(4,128)S(1)} %copy-done.14, s32[1152]{0:T(1024)S(1)} %copy-done.11), kind=kOutput, calls=%fused_computation.8 | convolution fusion | flops 828278784 | bytes 2161728 | tf_op jit(solution)/shard_map/dot_general | solution.py:106
  215.6 1.9 collective-permute-start.24
  217.5 4.9 %collective-permute-start.25 = (bf16[13,32,3,16]{1,0,3,2:T(8,128)(2,1)S(1)}, bf16[13,32,3,16]{1,0,3,2:T(8,128)(2,1)S(1)}, u32[]{:S(2)}, u32[]{:S(2)}) collective-permute-start(bf16[13,32,3,16]{1,0,3,2:T(8,128)(2,1)S(1)} %get-tuple-element.12), channel_id=1, source_target_pairs={{0,31},{1,0},{2,1},{3,2},{4,3},{5,4},{6,5},{7,6},{8,7},{9,8},{10,9... | collective-permute-start | bytes 119816 | tf_op jit(solution)/shard_map/ppermute | solution.py:37
  222.5 5.8 %collective-permute-start.23 = (bf16[3,1,13,32,16]{3,2,4,1,0:T(8,128)(2,1)S(1)}, bf16[3,1,13,32,16]{3,2,4,1,0:T(8,128)(2,1)S(1)}, u32[]{:S(2)}, u32[]{:S(2)}) collective-permute-start(bf16[3,1,13,32,16]{3,2,4,1,0:T(8,128)(2,1)S(1)} %pad_maximum_fusion.5), channel_id=1, source_target_pairs={{1,0},{2,1},{3,2},{4,3},{5,4},{6,5},{7,6},{8,7},{9,8},{10,9},{11,1... | collective-permute-start | bytes 119816 | tf_op jit(solution)/shard_map/ppermute | solution.py:27
  228.2 1.9 collective-permute-start.22
  230.3 1.9 collective-permute-start.26
  232.2 7.5 %collective-permute-start.27 = (f32[13,32,16]{1,0,2:T(8,128)S(1)}, f32[13,32,16]{1,0,2:T(8,128)S(1)}, u32[]{:S(2)}, u32[]{:S(2)}) collective-permute-start(f32[13,32,16]{1,0,2:T(8,128)S(1)} %get-tuple-element.18), channel_id=1, source_target_pairs={{0,480},{32,0},{64,32},{96,64},{128,96},{160,128},{192,160},{224,1... | collective-permute-start | bytes 79880 | tf_op jit(solution)/shard_map/ppermute | solution.py:37
  239.9 4.8 %gather_fusion.6 = bf16[1152,13,32]{2,1,0:T(8,128)(2,1)} fusion(bf16[13,32,144]{1,0,2:T(8,128)(2,1)S(1)} %bitcast.260, s32[2048]{0:T(1024)S(1)} %pad_clamp_fusion.3), kind=kCustom, calls=%fused_computation.3.clone | custom fusion | bytes 1921536 | tf_op jit(solution)/shard_map/jit(_take)/gather | solution.py:163
  244.7 6.7 %fusion.48 = f32[13,32,1152]{1,0,2:T(8,128)S(1)} fusion(bf16[13,13,1152]{1,0,2:T(8,128)(2,1)} %copy.42, bf16[1152,13,32]{2,1,0:T(8,128)(2,1)} %gather_fusion.6, pred[1152]{0:T(1024)(128)(4,1)S(1)} %get-tuple-element.9), kind=kOutput, calls=%fused_computation.48 | convolution fusion | flops 12939264 | bytes 3265920 | tf_op jit(solution)/shard_map/oqp,qvp->ovp/dot_general | solution.py:97
  251.4 4.5 %fusion.6 = f32[13,32,16]{1,2,0:T(8,128)S(1)} fusion(f32[13,32,1152]{1,0,2:T(8,128)S(1)} %fusion.48, s32[1152]{0:T(1024)S(1)} %bitcast.265), kind=kOutput, calls=%fused_computation.14 | convolution fusion | flops 92030976 | bytes 1948160 | tf_op jit(solution)/shard_map/dot_general | solution.py:106
  (110 shorter events, 8.9 us)
Async XLA Ops:
  0.0 60.2 %copy-start = (bf16[256,256]{1,0:T(8,128)(2,1)S(1)}, bf16[256,256]{1,0:T(8,128)(2,1)}, u32[]{:S(2)}) copy-start(bf16[256,256]{1,0:T(8,128)(2,1)} %param.30) | copy-start | bytes 393220
  1.0 42.8 %collective-permute-start.5 = (bf16[1,1,16,256]{3,2,1,0:T(8,128)(2,1)S(1)}, bf16[1,1,16,256]{3,2,1,0:T(8,128)(2,1)S(1)}, u32[]{:S(2)}, u32[]{:S(2)}) collective-permute-start(bf16[1,1,16,256]{3,2,1,0:T(8,128)(2,1)S(1)} %bitcast.266), channel_id=1, source_target_pairs={{32,0},{64,32},{96,64},{128,96},{160,128},{192,160},{224,192},{256... | collective-permute-start | bytes 24584 | tf_op jit(solution)/shard_map/ppermute | solution.py:27
  14.9 28.8 %collective-permute-start.4 = (bf16[1,1,16,256]{3,2,1,0:T(8,128)(2,1)S(1)}, bf16[1,1,16,256]{3,2,1,0:T(8,128)(2,1)S(1)}, u32[]{:S(2)}, u32[]{:S(2)}) collective-permute-start(bf16[1,1,16,256]{3,2,1,0:T(8,128)(2,1)S(1)} %bitcast.267), channel_id=1, source_target_pairs={{0,32},{32,64},{64,96},{96,128},{128,160},{160,192},{192,224},{224... | collective-permute-start | bytes 24584 | tf_op jit(solution)/shard_map/ppermute | solution.py:25
  17.7 31.7 %collective-permute-start.1 = (bf16[1,1,13,32,16]{3,2,4,1,0:T(8,128)(2,1)S(1)}, bf16[1,1,13,32,16]{3,2,4,1,0:T(8,128)(2,1)S(1)}, u32[]{:S(2)}, u32[]{:S(2)}) collective-permute-start(bf16[1,1,13,32,16]{3,2,4,1,0:T(8,128)(2,1)S(1)} %bitcast.254), channel_id=1, source_target_pairs={{32,0},{64,32},{96,64},{128,96},{160,128},{192,160},{224,192},{256... | collective-permute-start | bytes 39944 | tf_op jit(solution)/shard_map/ppermute | solution.py:27
  24.7 24.7 %collective-permute-start = (bf16[1,1,13,32,16]{3,2,4,1,0:T(8,128)(2,1)S(1)}, bf16[1,1,13,32,16]{3,2,4,1,0:T(8,128)(2,1)S(1)}, u32[]{:S(2)}, u32[]{:S(2)}) collective-permute-start(bf16[1,1,13,32,16]{3,2,4,1,0:T(8,128)(2,1)S(1)} %bitcast.255), channel_id=1, source_target_pairs={{0,32},{32,64},{64,96},{96,128},{128,160},{160,192},{192,224},{224... | collective-permute-start | bytes 39944 | tf_op jit(solution)/shard_map/ppermute | solution.py:25
  27.9 39.2 %copy-start.8 = (pred[1152]{0:T(1024)(128)(4,1)}, pred[1152]{0:T(1024)(128)(4,1)S(1)}, u32[]{:S(2)}) copy-start(pred[1152]{0:T(1024)(128)(4,1)S(1)} %compare_and_fusion) | copy-start | bytes 3460
  29.4 9.5 %copy-start.5 = (s32[2048]{0:T(1024)}, s32[2048]{0:T(1024)S(1)}, u32[]{:S(2)}) copy-start(s32[2048]{0:T(1024)S(1)} %pad_clamp_fusion) | copy-start | bytes 24580
  31.8 42.0 %copy-start.10 = (s32[1152]{0:T(1024)}, s32[1152]{0:T(1024)S(1)}, u32[]{:S(2)}) copy-start(s32[1152]{0:T(1024)S(1)} %get-tuple-element.10) | copy-start | bytes 13828
  35.6 20.4 %copy-start.7 = (bf16[256,256]{1,0:T(8,128)(2,1)S(1)}, bf16[256,256]{1,0:T(8,128)(2,1)}, u32[]{:S(2)}) copy-start(bf16[256,256]{1,0:T(8,128)(2,1)} %param.29) | copy-start | bytes 393220
  43.8 12.2 %collective-permute-start.7 = (bf16[3,1,16,256]{3,2,1,0:T(8,128)(2,1)S(1)}, bf16[3,1,16,256]{3,2,1,0:T(8,128)(2,1)S(1)}, u32[]{:S(2)}, u32[]{:S(2)}) collective-permute-start(bf16[3,1,16,256]{3,2,1,0:T(8,128)(2,1)S(1)} %pad_maximum_fusion.7), channel_id=1, source_target_pairs={{1,0},{2,1},{3,2},{4,3},{5,4},{6,5},{7,6},{8,7},{9,8},{10,9},{11,1... | collective-permute-start | bytes 73736 | tf_op jit(solution)/shard_map/ppermute | solution.py:27
  47.2 8.8 %collective-permute-start.6 = (bf16[3,1,16,256]{3,2,1,0:T(8,128)(2,1)S(1)}, bf16[3,1,16,256]{3,2,1,0:T(8,128)(2,1)S(1)}, u32[]{:S(2)}, u32[]{:S(2)}) collective-permute-start(bf16[3,1,16,256]{3,2,1,0:T(8,128)(2,1)S(1)} %pad_maximum_fusion.7), channel_id=1, source_target_pairs={{0,1},{1,2},{2,3},{3,4},{4,5},{5,6},{6,7},{7,8},{8,9},{9,10},{10,1... | collective-permute-start | bytes 73736 | tf_op jit(solution)/shard_map/ppermute | solution.py:25
  49.4 10.2 %copy-start.3 = (bf16[1,1,13,32,16]{3,2,4,1,0:T(8,128)(2,1)}, bf16[1,1,13,32,16]{3,2,4,1,0:T(8,128)(2,1)S(1)}, u32[]{:S(2)}) copy-start(bf16[1,1,13,32,16]{3,2,4,1,0:T(8,128)(2,1)S(1)} %collective-permute-done) | copy-start | bytes 39940
  50.1 43.6 %collective-permute-start.3 = (bf16[3,1,13,32,16]{3,2,4,1,0:T(8,128)(2,1)}, bf16[3,1,13,32,16]{3,2,4,1,0:T(8,128)(2,1)}, u32[]{:S(2)}, u32[]{:S(2)}) collective-permute-start(bf16[3,1,13,32,16]{3,2,4,1,0:T(8,128)(2,1)} %pad_maximum_fusion.3), channel_id=1, source_target_pairs={{1,0},{2,1},{3,2},{4,3},{5,4},{6,5},{7,6},{8,7},{9,8},{10,9},{11,1... | collective-permute-start | bytes 119816 | tf_op jit(solution)/shard_map/ppermute | solution.py:27
  53.9 39.8 %collective-permute-start.2 = (bf16[3,1,13,32,16]{3,2,4,1,0:T(8,128)(2,1)}, bf16[3,1,13,32,16]{3,2,4,1,0:T(8,128)(2,1)}, u32[]{:S(2)}, u32[]{:S(2)}) collective-permute-start(bf16[3,1,13,32,16]{3,2,4,1,0:T(8,128)(2,1)} %pad_maximum_fusion.3), channel_id=1, source_target_pairs={{0,1},{1,2},{2,3},{3,4},{4,5},{5,6},{6,7},{7,8},{8,9},{9,10},{10,1... | collective-permute-start | bytes 119816 | tf_op jit(solution)/shard_map/ppermute | solution.py:25
  56.2 3.3 %copy-start.15 = (bf16[16,256]{1,0:T(8,128)(2,1)S(1)}, bf16[16,256]{1,0:T(8,128)(2,1)}, u32[]{:S(2)}) copy-start(bf16[16,256]{1,0:T(8,128)(2,1)} %param.27) | copy-start | bytes 24580
  56.2 3.3 %copy-start.16 = (f32[16]{0:T(128)S(1)}, f32[16]{0:T(128)}, u32[]{:S(2)}) copy-start(f32[16]{0:T(128)} %iota_multiply_fusion) | copy-start | bytes 196
  59.5 1.0 copy-start.12
  67.2 6.6 %copy-start.13 = (s32[3,3,16]{2,1,0:T(4,128)S(1)}, s32[3,3,16]{2,1,0:T(4,128)}, u32[]{:S(2)}) copy-start(s32[3,3,16]{2,1,0:T(4,128)} %multiply_add_fusion) | copy-start | bytes 1732
  79.0 14.7 %copy-start.4 = (bf16[1,1,13,32,16]{3,2,4,1,0:T(8,128)(2,1)S(1)}, bf16[1,1,13,32,16]{3,2,4,1,0:T(8,128)(2,1)}, u32[]{:S(2)}) copy-start(bf16[1,1,13,32,16]{3,2,4,1,0:T(8,128)(2,1)} %copy-done.3) | copy-start | bytes 39940
  85.8 25.2 %collective-permute-start.8 = (bf16[13,32,3,16]{1,0,3,2:T(8,128)(2,1)}, bf16[13,32,3,16]{1,0,3,2:T(8,128)(2,1)S(1)}, u32[]{:S(2)}, u32[]{:S(2)}) collective-permute-start(bf16[13,32,3,16]{1,0,3,2:T(8,128)(2,1)} %get-tuple-element.15), channel_id=1, source_target_pairs={{0,1},{1,2},{2,3},{3,4},{4,5},{5,6},{6,7},{7,8},{8,9},{9,10},{10,1... | collective-permute-start | bytes 119816 | tf_op jit(solution)/shard_map/ppermute | solution.py:37
  88.4 22.6 %collective-permute-start.9 = (bf16[13,32,3,16]{1,0,3,2:T(8,128)(2,1)S(1)}, bf16[13,32,3,16]{1,0,3,2:T(8,128)(2,1)S(1)}, u32[]{:S(2)}, u32[]{:S(2)}) collective-permute-start(bf16[13,32,3,16]{1,0,3,2:T(8,128)(2,1)S(1)} %get-tuple-element.16), channel_id=1, source_target_pairs={{0,31},{1,0},{2,1},{3,2},{4,3},{5,4},{6,5},{7,6},{8,7},{9,8},{10,9... | collective-permute-start | bytes 119816 | tf_op jit(solution)/shard_map/ppermute | solution.py:37
  106.4 14.2 %copy-start.2 = (bf16[1,1,16,13,32]{4,2,3,1,0:T(8,128)(2,1)S(1)}, bf16[1,1,16,13,32]{4,2,3,1,0:T(8,128)(2,1)}, u32[]{:S(2)}) copy-start(bf16[1,1,16,13,32]{4,2,3,1,0:T(8,128)(2,1)} %param.22) | copy-start | bytes 39940
  106.4 25.7 %copy-start.6 = (s32[2048]{0:T(1024)S(1)}, s32[2048]{0:T(1024)}, u32[]{:S(2)}) copy-start(s32[2048]{0:T(1024)} %copy-done.5) | copy-start | bytes 24580
  106.4 30.6 %copy-start.9 = (pred[1152]{0:T(1024)(128)(4,1)S(1)}, pred[1152]{0:T(1024)(128)(4,1)}, u32[]{:S(2)}) copy-start(pred[1152]{0:T(1024)(128)(4,1)} %copy-done.8) | copy-start | bytes 3460
  111.1 9.9 %collective-permute-start.10 = (f32[13,32,16]{1,0,2:T(8,128)S(1)}, f32[13,32,16]{1,0,2:T(8,128)S(1)}, u32[]{:S(2)}, u32[]{:S(2)}) collective-permute-start(f32[13,32,16]{1,0,2:T(8,128)S(1)} %get-tuple-element.21), channel_id=1, source_target_pairs={{0,32},{32,64},{64,96},{96,128},{128,160},{160,192},{192,224},{224... | collective-permute-start | bytes 79880 | tf_op jit(solution)/shard_map/ppermute | solution.py:37
  113.0 9.5 %collective-permute-start.11 = (f32[13,32,16]{1,0,2:T(8,128)S(1)}, f32[13,32,16]{1,0,2:T(8,128)S(1)}, u32[]{:S(2)}, u32[]{:S(2)}) collective-permute-start(f32[13,32,16]{1,0,2:T(8,128)S(1)} %get-tuple-element.22), channel_id=1, source_target_pairs={{0,480},{32,0},{64,32},{96,64},{128,96},{160,128},{192,160},{224,1... | collective-permute-start | bytes 79880 | tf_op jit(solution)/shard_map/ppermute | solution.py:37
  122.6 36.2 %collective-permute-start.13 = (bf16[1,1,13,32,16]{3,2,4,1,0:T(8,128)(2,1)S(1)}, bf16[1,1,13,32,16]{3,2,4,1,0:T(8,128)(2,1)S(1)}, u32[]{:S(2)}, u32[]{:S(2)}) collective-permute-start(bf16[1,1,13,32,16]{3,2,4,1,0:T(8,128)(2,1)S(1)} %bitcast.250), channel_id=1, source_target_pairs={{32,0},{64,32},{96,64},{128,96},{160,128},{192,160},{224,192},{256... | collective-permute-start | bytes 39944 | tf_op jit(solution)/shard_map/ppermute | solution.py:27
  130.0 28.8 %collective-permute-start.12 = (bf16[1,1,13,32,16]{3,2,4,1,0:T(8,128)(2,1)S(1)}, bf16[1,1,13,32,16]{3,2,4,1,0:T(8,128)(2,1)S(1)}, u32[]{:S(2)}, u32[]{:S(2)}) collective-permute-start(bf16[1,1,13,32,16]{3,2,4,1,0:T(8,128)(2,1)S(1)} %bitcast.251), channel_id=1, source_target_pairs={{0,32},{32,64},{64,96},{96,128},{128,160},{160,192},{192,224},{224... | collective-permute-start | bytes 39944 | tf_op jit(solution)/shard_map/ppermute | solution.py:25
  137.0 6.7 %copy-start.11 = (s32[1152]{0:T(1024)S(1)}, s32[1152]{0:T(1024)}, u32[]{:S(2)}) copy-start(s32[1152]{0:T(1024)} %copy-done.10) | copy-start | bytes 13828
  149.6 16.9 %collective-permute-start.16 = (bf16[13,32,3,16]{1,0,3,2:T(8,128)(2,1)S(1)}, bf16[13,32,3,16]{1,0,3,2:T(8,128)(2,1)S(1)}, u32[]{:S(2)}, u32[]{:S(2)}) collective-permute-start(bf16[13,32,3,16]{1,0,3,2:T(8,128)(2,1)S(1)} %get-tuple-element.13), channel_id=1, source_target_pairs={{0,1},{1,2},{2,3},{3,4},{4,5},{5,6},{6,7},{7,8},{8,9},{9,10},{10,1... | collective-permute-start | bytes 119816 | tf_op jit(solution)/shard_map/ppermute | solution.py:37
  152.7 13.8 %collective-permute-start.17 = (bf16[13,32,3,16]{1,0,3,2:T(8,128)(2,1)S(1)}, bf16[13,32,3,16]{1,0,3,2:T(8,128)(2,1)S(1)}, u32[]{:S(2)}, u32[]{:S(2)}) collective-permute-start(bf16[13,32,3,16]{1,0,3,2:T(8,128)(2,1)S(1)} %get-tuple-element.14), channel_id=1, source_target_pairs={{0,31},{1,0},{2,1},{3,2},{4,3},{5,4},{6,5},{7,6},{8,7},{9,8},{10,9... | collective-permute-start | bytes 119816 | tf_op jit(solution)/shard_map/ppermute | solution.py:37
  158.8 17.5 %collective-permute-start.15 = (bf16[3,1,13,32,16]{3,2,4,1,0:T(8,128)(2,1)S(1)}, bf16[3,1,13,32,16]{3,2,4,1,0:T(8,128)(2,1)S(1)}, u32[]{:S(2)}, u32[]{:S(2)}) collective-permute-start(bf16[3,1,13,32,16]{3,2,4,1,0:T(8,128)(2,1)S(1)} %pad_maximum_fusion.4), channel_id=1, source_target_pairs={{1,0},{2,1},{3,2},{4,3},{5,4},{6,5},{7,6},{8,7},{9,8},{10,9},{11,1... | collective-permute-start | bytes 119816 | tf_op jit(solution)/shard_map/ppermute | solution.py:27
  164.6 11.7 %collective-permute-start.14 = (bf16[3,1,13,32,16]{3,2,4,1,0:T(8,128)(2,1)S(1)}, bf16[3,1,13,32,16]{3,2,4,1,0:T(8,128)(2,1)S(1)}, u32[]{:S(2)}, u32[]{:S(2)}) collective-permute-start(bf16[3,1,13,32,16]{3,2,4,1,0:T(8,128)(2,1)S(1)} %pad_maximum_fusion.4), channel_id=1, source_target_pairs={{0,1},{1,2},{2,3},{3,4},{4,5},{5,6},{6,7},{7,8},{8,9},{9,10},{10,1... | collective-permute-start | bytes 119816 | tf_op jit(solution)/shard_map/ppermute | solution.py:25
  166.6 25.9 %collective-permute-start.18 = (f32[13,32,16]{1,0,2:T(8,128)S(1)}, f32[13,32,16]{1,0,2:T(8,128)S(1)}, u32[]{:S(2)}, u32[]{:S(2)}) collective-permute-start(f32[13,32,16]{1,0,2:T(8,128)S(1)} %get-tuple-element.19), channel_id=1, source_target_pairs={{0,32},{32,64},{64,96},{96,128},{128,160},{160,192},{192,224},{224... | collective-permute-start | bytes 79880 | tf_op jit(solution)/shard_map/ppermute | solution.py:37
  168.5 23.9 %collective-permute-start.19 = (f32[13,32,16]{1,0,2:T(8,128)S(1)}, f32[13,32,16]{1,0,2:T(8,128)S(1)}, u32[]{:S(2)}, u32[]{:S(2)}) collective-permute-start(f32[13,32,16]{1,0,2:T(8,128)S(1)} %get-tuple-element.20), channel_id=1, source_target_pairs={{0,480},{32,0},{64,32},{96,64},{128,96},{160,128},{192,160},{224,1... | collective-permute-start | bytes 79880 | tf_op jit(solution)/shard_map/ppermute | solution.py:37
  192.7 29.7 %collective-permute-start.21 = (bf16[1,1,13,32,16]{3,2,4,1,0:T(8,128)(2,1)S(1)}, bf16[1,1,13,32,16]{3,2,4,1,0:T(8,128)(2,1)S(1)}, u32[]{:S(2)}, u32[]{:S(2)}) collective-permute-start(bf16[1,1,13,32,16]{3,2,4,1,0:T(8,128)(2,1)S(1)} %bitcast.246), channel_id=1, source_target_pairs={{32,0},{64,32},{96,64},{128,96},{160,128},{192,160},{224,192},{256... | collective-permute-start | bytes 39944 | tf_op jit(solution)/shard_map/ppermute | solution.py:27
  196.0 26.4 %collective-permute-start.20 = (bf16[1,1,13,32,16]{3,2,4,1,0:T(8,128)(2,1)S(1)}, bf16[1,1,13,32,16]{3,2,4,1,0:T(8,128)(2,1)S(1)}, u32[]{:S(2)}, u32[]{:S(2)}) collective-permute-start(bf16[1,1,13,32,16]{3,2,4,1,0:T(8,128)(2,1)S(1)} %bitcast.247), channel_id=1, source_target_pairs={{0,32},{32,64},{64,96},{96,128},{128,160},{160,192},{192,224},{224... | collective-permute-start | bytes 39944 | tf_op jit(solution)/shard_map/ppermute | solution.py:25
  203.0 6.7 %copy-start.14 = (s32[3,3,16]{2,1,0:T(4,128)S(1)}, s32[3,3,16]{2,1,0:T(4,128)}, u32[]{:S(2)}) copy-start(s32[3,3,16]{2,1,0:T(4,128)} %multiply_add_fusion) | copy-start | bytes 1732
  215.6 14.6 %collective-permute-start.24 = (bf16[13,32,3,16]{1,0,3,2:T(8,128)(2,1)S(1)}, bf16[13,32,3,16]{1,0,3,2:T(8,128)(2,1)S(1)}, u32[]{:S(2)}, u32[]{:S(2)}) collective-permute-start(bf16[13,32,3,16]{1,0,3,2:T(8,128)(2,1)S(1)} %get-tuple-element.11), channel_id=1, source_target_pairs={{0,1},{1,2},{2,3},{3,4},{4,5},{5,6},{6,7},{7,8},{8,9},{9,10},{10,1... | collective-permute-start | bytes 119816 | tf_op jit(solution)/shard_map/ppermute | solution.py:37
  217.5 12.7 %collective-permute-start.25 = (bf16[13,32,3,16]{1,0,3,2:T(8,128)(2,1)S(1)}, bf16[13,32,3,16]{1,0,3,2:T(8,128)(2,1)S(1)}, u32[]{:S(2)}, u32[]{:S(2)}) collective-permute-start(bf16[13,32,3,16]{1,0,3,2:T(8,128)(2,1)S(1)} %get-tuple-element.12), channel_id=1, source_target_pairs={{0,31},{1,0},{2,1},{3,2},{4,3},{5,4},{6,5},{7,6},{8,7},{9,8},{10,9... | collective-permute-start | bytes 119816 | tf_op jit(solution)/shard_map/ppermute | solution.py:37
  222.5 17.2 %collective-permute-start.23 = (bf16[3,1,13,32,16]{3,2,4,1,0:T(8,128)(2,1)S(1)}, bf16[3,1,13,32,16]{3,2,4,1,0:T(8,128)(2,1)S(1)}, u32[]{:S(2)}, u32[]{:S(2)}) collective-permute-start(bf16[3,1,13,32,16]{3,2,4,1,0:T(8,128)(2,1)S(1)} %pad_maximum_fusion.5), channel_id=1, source_target_pairs={{1,0},{2,1},{3,2},{4,3},{5,4},{6,5},{7,6},{8,7},{9,8},{10,9},{11,1... | collective-permute-start | bytes 119816 | tf_op jit(solution)/shard_map/ppermute | solution.py:27
  228.2 11.5 %collective-permute-start.22 = (bf16[3,1,13,32,16]{3,2,4,1,0:T(8,128)(2,1)S(1)}, bf16[3,1,13,32,16]{3,2,4,1,0:T(8,128)(2,1)S(1)}, u32[]{:S(2)}, u32[]{:S(2)}) collective-permute-start(bf16[3,1,13,32,16]{3,2,4,1,0:T(8,128)(2,1)S(1)} %pad_maximum_fusion.5), channel_id=1, source_target_pairs={{0,1},{1,2},{2,3},{3,4},{4,5},{5,6},{6,7},{7,8},{8,9},{9,10},{10,1... | collective-permute-start | bytes 119816 | tf_op jit(solution)/shard_map/ppermute | solution.py:25
  230.3 25.8 %collective-permute-start.26 = (f32[13,32,16]{1,0,2:T(8,128)S(1)}, f32[13,32,16]{1,0,2:T(8,128)S(1)}, u32[]{:S(2)}, u32[]{:S(2)}) collective-permute-start(f32[13,32,16]{1,0,2:T(8,128)S(1)} %get-tuple-element.17), channel_id=1, source_target_pairs={{0,32},{32,64},{64,96},{96,128},{128,160},{160,192},{192,224},{224... | collective-permute-start | bytes 79880 | tf_op jit(solution)/shard_map/ppermute | solution.py:37
  232.2 23.9 %collective-permute-start.27 = (f32[13,32,16]{1,0,2:T(8,128)S(1)}, f32[13,32,16]{1,0,2:T(8,128)S(1)}, u32[]{:S(2)}, u32[]{:S(2)}) collective-permute-start(f32[13,32,16]{1,0,2:T(8,128)S(1)} %get-tuple-element.18), channel_id=1, source_target_pairs={{0,480},{32,0},{64,32},{96,64},{128,96},{160,128},{192,160},{224,1... | collective-permute-start | bytes 79880 | tf_op jit(solution)/shard_map/ppermute | solution.py:37
  244.7 12.1 %copy-start.1 = (bf16[256,256]{1,0:T(8,128)(2,1)S(1)}, bf16[256,256]{1,0:T(8,128)(2,1)}, u32[]{:S(2)}) copy-start(bf16[256,256]{1,0:T(8,128)(2,1)} %param.30) | copy-start | bytes 393220
where the time goes:
time: 261 us; the launch traced here: 257 us
  starting transfers between devices  119 us (46%)
  matrix products  75.2 us (29%)
  local copies, waits for them, and re-layouts  51 us (20%)
  other arithmetic  8.91 us (3%)
    ppermute x12, starting transfers between devices, shifted(): return lax.ppermute(value, axis, pairs)  52.3 us
    ppermute x8, starting transfers between devices, padded(): lax.ppermute(head, axis, [((i + 1) % count, i) for i in range(count)])  50.4 us
    dot_general x6, matrix products, scatter_rows(): summed = jnp.dot(flat, hot_table, precision=lax.Precision.HIGHEST)  29.2 us
    dot_general x6, matrix products, orbital_product(): jnp.einsum('oqp,qvp->ovp', blocks, vectors, preferred_element_type=jnp.fl...  20.4 us
    dot_general x3, matrix products, orbital_product(): jnp.einsum('oqp,ovp->qvp', blocks, vectors, preferred_element_type=jnp.fl...  19.9 us
    ppermute x8, starting transfers between devices, padded(): lax.ppermute(tail, axis, [(i, (i + 1) % count) for i in range(count)])  16.2 us
    gather x3, local copies, waits for them, and re-layouts, apply(): jnp.take(vector_rows, source_indices, axis=2)  14.5 us
    gather x3, local copies, waits for them, and re-layouts, apply(): jnp.take(rim, target_indices, axis=2)  14.5 us
  transfers between devices with their start and end apart: 28, of which 2 were waited for; matrix products, arithmetic and copies ran while one was open for 52% of the time, Pallas kernels for 0%

commit v1 on v0

v1 whole, which is shorter than its diff:
```python
import math

import jax
import jax.numpy as jnp
from jax import lax
from jax.sharding import PartitionSpec as P

NEIGHBOUR_SLOTS = 72
RBF = 16
ORBITAL_COUNT = 13
FILTER = 3


cutoff = 8.0
onsite_scale = 0.15

f32 = jnp.float32
bf16 = jnp.bfloat16


def shifted(value, axis, steps):
    count = lax.axis_size(axis)
    pairs = [(source, (source + steps) % count) for source in range(count)]
    return lax.ppermute(value, axis, pairs)


def bf16_parts(value):
    high = lax.reduce_precision(value, exponent_bits=8, mantissa_bits=7)
    rest = value - high
    middle = lax.reduce_precision(rest, exponent_bits=8, mantissa_bits=7)
    low = rest - middle
    return high.astype(bf16), middle.astype(bf16), low.astype(bf16)


def halo(flat):
    from_west = shifted(flat, "gx", 1)
    from_east = shifted(flat, "gx", -1)
    strip = jnp.stack([from_west, flat, from_east]).reshape(-1)
    from_south = shifted(strip, "gy", 1).reshape(3, -1)
    from_north = shifted(strip, "gy", -1).reshape(3, -1)
    strip = strip.reshape(3, -1)
    return jnp.stack([from_south, strip, from_north], axis=1).reshape(9, -1)


def first_halo(common, pairs):
    n = common.shape[0]
    m = pairs.shape[1]
    to_east = jnp.concatenate([common, pairs[6:9].reshape(-1)])
    to_west = jnp.concatenate([common, pairs[0:3].reshape(-1)])
    from_west = shifted(to_east, "gx", 1)
    from_east = shifted(to_west, "gx", -1)
    strip_common = jnp.stack([from_west[:n], common, from_east[:n]])
    strip_pairs = jnp.stack(
        [
            from_west[n:].reshape(3, m),
            pairs[3:6],
            from_east[n:].reshape(3, m),
        ]
    )
    to_north = jnp.concatenate([strip_common.reshape(-1), strip_pairs[:, 2].reshape(-1)])
    to_south = jnp.concatenate([strip_common.reshape(-1), strip_pairs[:, 0].reshape(-1)])
    from_south = shifted(to_north, "gy", 1)
    from_north = shifted(to_south, "gy", -1)
    all_common = jnp.stack(
        [from_south[: 3 * n].reshape(3, n), strip_common, from_north[: 3 * n].reshape(3, n)],
        axis=1,
    ).reshape(9, n)
    incoming = jnp.stack(
        [
            from_south[3 * n :].reshape(3, m),
            strip_pairs[:, 1],
            from_north[3 * n :].reshape(3, m),
        ],
        axis=1,
    ).reshape(9, m)
    return all_common, incoming


def pair_blocks(before_rows, distance, live_flags, radial_weight, mixing_weight, gate_weight, output_weight):
    centres = cutoff * jnp.arange(RBF, dtype=f32) / (RBF - 1)
    spacing = cutoff / (RBF - 1)
    basis = jnp.exp(-jnp.square((distance[:, None] - centres[None, :]) / spacing)).astype(bf16)
    cutoff_envelope = jnp.square(1.0 - jnp.square(distance / cutoff))
    before = before_rows + jnp.dot(basis, radial_weight, preferred_element_type=f32)
    edge = jax.nn.silu(before).astype(bf16)
    opened = jax.nn.silu(jnp.dot(edge, mixing_weight, preferred_element_type=f32))
    mixed = (opened * jnp.dot(edge, gate_weight, preferred_element_type=f32)).astype(bf16)
    raw_out = jnp.dot(mixed, output_weight, preferred_element_type=f32)
    scale_factor = 1.5 / math.sqrt(NEIGHBOUR_SLOTS * ORBITAL_COUNT) * cutoff_envelope * live_flags
    return (raw_out * scale_factor[:, None]).astype(bf16)


def on_device(
    features,
    atom_kinds,
    kind_table,
    band_vectors,
    pair_offsets,
    pair_source,
    pair_target,
    pair_live_mask,
    radial_weight,
    w_source,
    w_target,
    mixing_weight,
    gate_weight,
    output_weight,
    w_site,
):
    atom_count = features.shape[2]
    feat = features.shape[3]
    vec = band_vectors.shape[4]
    orb = ORBITAL_COUNT
    slots = pair_source.shape[3]
    kind_hot = (
        atom_kinds[0, 0][:, None] == jnp.arange(kind_table.shape[0], dtype=jnp.int32)[None, :]
    ).astype(f32)
    embedded = jnp.dot(kind_hot, kind_table, precision=lax.Precision.HIGHEST)
    atoms = (features[0, 0].astype(f32) + embedded).astype(bf16)

    offsets = pair_offsets[0, 0]
    distance = jnp.sqrt(offsets[0] * offsets[0] + offsets[1] * offsets[1] + offsets[2] * offsets[2])
    source = pair_source[0, 0]
    target = pair_target[0, 0]
    live = pair_live_mask[0, 0]
    high, middle, low = bf16_parts(distance)
    pair_data = jnp.stack(
        [source.astype(bf16), target.astype(bf16), live.astype(bf16), high, middle, low], axis=-1
    ).reshape(9, slots * 6)

    first = band_vectors[0, 0]
    common = jnp.concatenate([atoms.reshape(-1), first.reshape(-1)])
    all_common, incoming = first_halo(common, pair_data)
    n_atoms = atom_count * feat
    ring_atoms = all_common[:, :n_atoms].reshape(9 * atom_count, feat)
    ring_first = all_common[:, n_atoms:]

    incoming = incoming.reshape(9, slots, 6).astype(f32)
    in_source = incoming[..., 0].astype(jnp.int32)
    in_target = incoming[..., 1].astype(jnp.int32)
    in_live = incoming[..., 2]
    in_distance = (incoming[..., 3] + incoming[..., 4]) + incoming[..., 5]

    places = jnp.arange(9, dtype=jnp.int32)[:, None] * atom_count
    centre = 4 * atom_count
    row_source = jnp.concatenate([(centre + source).reshape(-1), (places + in_source).reshape(-1)])
    row_target = jnp.concatenate([(places + target).reshape(-1), (centre + in_target).reshape(-1)])
    all_distance = jnp.concatenate([distance.reshape(-1), in_distance.reshape(-1)])
    all_live = jnp.concatenate([live.reshape(-1).astype(f32), in_live.reshape(-1)])

    source_projection = jnp.dot(ring_atoms, w_source, preferred_element_type=f32)
    target_projection = jnp.dot(ring_atoms, w_target, preferred_element_type=f32)
    table = jnp.concatenate([source_projection, target_projection])
    table_parts = jnp.concatenate(bf16_parts(table), axis=1)
    ring = 9 * atom_count
    columns = jnp.arange(2 * ring, dtype=jnp.int32)[None, :]
    pick = (
        (columns == row_source[:, None]) | (columns == (row_target[:, None] + ring))
    ).astype(bf16)
    picked = jnp.dot(pick, table_parts, preferred_element_type=f32)
    before_rows = (picked[:, :feat] + picked[:, feat : 2 * feat]) + picked[:, 2 * feat :]

    hopping = pair_blocks(
        before_rows, all_distance, all_live, radial_weight, mixing_weight, gate_weight, output_weight
    )
    own_hopping = hopping[: 9 * slots].reshape(9, slots, orb * orb)
    in_hopping = jnp.swapaxes(
        hopping[9 * slots :].reshape(9, slots, orb, orb), 2, 3
    ).reshape(9, slots, orb * orb)

    pair_ids = jnp.arange(atom_count * atom_count, dtype=jnp.int32)[None, None, :]
    own_key = source * atom_count + target
    in_key = in_target * atom_count + in_source
    own_hot = (own_key[:, :, None] == pair_ids).astype(bf16)
    in_hot = (in_key[:, :, None] == pair_ids).astype(bf16)
    summed = jnp.einsum("tsp,tsb->tpb", own_hot, own_hopping, preferred_element_type=f32)
    summed = summed + jnp.einsum("tsp,tsb->tpb", in_hot, in_hopping, preferred_element_type=f32)

    square = jnp.dot(atoms, w_site, preferred_element_type=f32).reshape(-1, orb, orb)
    onsite = (onsite_scale * 0.5 * (square + jnp.swapaxes(square, 1, 2))).astype(bf16)
    eye = jnp.eye(atom_count, dtype=f32)
    onsite_full = (eye[:, :, None, None] * onsite.astype(f32)[:, None, :, :]).reshape(
        atom_count * atom_count, orb * orb
    )
    summed = summed.at[4].add(onsite_full)
    dense = jnp.transpose(
        summed.reshape(9, atom_count, atom_count, orb, orb), (1, 3, 0, 2, 4)
    ).reshape(atom_count * orb, 9 * atom_count * orb)

    def apply(ring_vectors):
        wide = ring_vectors.reshape(9 * atom_count * orb, vec).astype(f32)
        out = jnp.dot(dense, wide, precision=lax.Precision.HIGHEST, preferred_element_type=f32)
        return out.reshape(atom_count, orb, vec)

    previous = first.astype(f32)
    current = apply(ring_first)
    for repeat in range(FILTER - 1):
        ring_now = halo(current.astype(bf16).reshape(-1))
        upcoming = 2.0 * apply(ring_now) - previous
        previous, current = (current, upcoming)
    return current[None, None]


def solution(mesh):
    in_specs = (
        P("gx", "gy", None, None),
        P("gx", "gy", None),
        P(),
        P("gx", "gy", None, None, None),
        P("gx", "gy", None, None, None),
        P("gx", "gy", None, None),
        P("gx", "gy", None, None),
        P("gx", "gy", None, None),
        P(),
        P(),
        P(),
        P(),
        P(),
        P(),
        P(),
    )
    out_specs = P("gx", "gy", None, None, None)
    return jax.shard_map(
        on_device, mesh=mesh, in_specs=in_specs, out_specs=out_specs, check_vma=False
    )
```

time: 261 us -> 131 us (0.50)
  the two profiles are of different devices: /device:TPU:1 before, /device:TPU:27 now
where the time goes in v1:
time: 131 us; the launch traced here: 130 us
  starting transfers between devices  50.3 us (38%)
  local copies, waits for them, and re-layouts  42.3 us (32%)
  waiting for transfers between devices  17.5 us (13%)
  matrix products  12.4 us (9%)
  other arithmetic  6.81 us (5%)
    ppermute x12, starting transfers between devices, shifted(): return lax.ppermute(value, axis, pairs)  50.3 us
    reshape x2, local copies, waits for them, and re-layouts, on_device(): summed.reshape(9, atom_count, atom_count, orb, orb)  23.8 us
    ppermute x12, waiting for transfers between devices, shifted(): return lax.ppermute(value, axis, pairs)  17.5 us
    dot_general x1, local copies, waits for them, and re-layouts, apply(): jnp.dot(dense, wide, precision=lax.Precision.HIGHEST, preferred_element_t...  9.55 us
    dot_general x3, matrix products, apply(): jnp.dot(dense, wide, precision=lax.Precision.HIGHEST, preferred_element_t...  3.17 us
  transfers between devices with their start and end apart: 12, of which 5 were waited for; matrix products, arithmetic and copies ran while one was open for 4% of the time, Pallas kernels for 0%

profile of v1, /device:TPU:27, one launch (start us, length us, event | category | flops | bytes accessed | tf_op | source)
XLA Modules:
  0.0 130.1 jit_solution(15532852661606694357)
XLA Ops:
  0.0 0.8 fusion.50
  0.8 0.7 constant_dynamic-update-slice_fusion.5
  1.5 0.7 convert_element_type.171
  2.1 0.7 constant_dynamic-update-slice_fusion.4
  2.9 0.2 copy.83
  3.1 0.2 reshape.406
  3.3 0.2 copy.84
  3.5 0.2 reshape.407
  3.6 0.9 fusion.13
  4.6 0.8 copy.77
  5.5 4.0 %collective-permute-start = (bf16[13056]{0:T(1024)(128)(2,1)S(1)}, bf16[13056]{0:T(1024)(128)(2,1)S(1)}, u32[]{:S(2)}, u32[]{:S(2)}) collective-permute-start(bf16[13056]{0:T(1024)(128)(2,1)S(1)} %get-tuple-element.39), channel_id=1, source_target_pairs={{0,32},{32,64},{64,96},{96,128},{128,160},{160,192},{192,224},{224... | collective-permute-start | bytes 78344 | tf_op jit(solution)/shard_map/ppermute | solution.py:24
  9.5 10.1 %collective-permute-start.1 = (bf16[13056]{0:T(1024)(128)(2,1)S(1)}, bf16[13056]{0:T(1024)(128)(2,1)S(1)}, u32[]{:S(2)}, u32[]{:S(2)}) collective-permute-start(bf16[13056]{0:T(1024)(128)(2,1)S(1)} %get-tuple-element.38), channel_id=1, source_target_pairs={{0,480},{32,0},{64,32},{96,64},{128,96},{160,128},{192,160},{224,1... | collective-permute-start | bytes 78344 | tf_op jit(solution)/shard_map/ppermute | solution.py:24
  19.7 0.7 add_reduce_fusion.2
  20.4 0.7 convert_reduce_fusion
  21.2 1.0 fusion.55
  22.3 0.2 copy.91
  22.6 0.2 copy.85
  22.8 0.2 stack.65
  23.0 0.2 copy.92
  23.1 0.4 mul.179
  23.6 0.6 mul.180
  24.5 0.2 pad_maximum_fusion.4
  24.8 6.1 %collective-permute-start.2 = (bf16[34560]{0:T(1024)(128)(2,1)S(1)}, bf16[34560]{0:T(1024)(128)(2,1)S(1)}, u32[]{:S(2)}, u32[]{:S(2)}) collective-permute-start(bf16[34560]{0:T(1024)(128)(2,1)S(1)} %get-tuple-element.33), channel_id=1, source_target_pairs={{0,1},{1,2},{2,3},{3,4},{4,5},{5,6},{6,7},{7,8},{8,9},{9,10},{10,1... | collective-permute-start | bytes 207368 | tf_op jit(solution)/shard_map/ppermute | solution.py:24
  30.9 2.1 %collective-permute-start.3 = (bf16[34560]{0:T(1024)(128)(2,1)S(1)}, bf16[34560]{0:T(1024)(128)(2,1)S(1)}, u32[]{:S(2)}, u32[]{:S(2)}) collective-permute-start(bf16[34560]{0:T(1024)(128)(2,1)S(1)} %get-tuple-element.34), channel_id=1, source_target_pairs={{0,31},{1,0},{2,1},{3,2},{4,3},{5,4},{6,5},{7,6},{8,7},{9,8},{10,9... | collective-permute-start | bytes 207368 | tf_op jit(solution)/shard_map/ppermute | solution.py:24
  33.0 0.2 fusion.75
  33.2 5.4 %collective-permute-done.3 = bf16[34560]{0:T(1024)(128)(2,1)S(1)} collective-permute-done((bf16[34560]{0:T(1024)(128)(2,1)S(1)}, bf16[34560]{0:T(1024)(128)(2,1)S(1)}, u32[]{:S(2)}, u32[]{:S(2)}) %collective-permute-start.3) | collective-permute-done | bytes 69152 | tf_op jit(solution)/shard_map/ppermute | solution.py:24
  38.7 0.5 reshape.422
  39.2 0.7 add_reduce_fusion
  40.0 1.0 slice_reduce_fusion
  41.1 0.2 pad_maximum_fusion.1
  41.4 0.2 reshape.409
  41.7 0.2 copy-done.4
  41.9 0.2 fusion.52
  42.1 0.2 fusion.53
  42.4 2.2 %fusion.3 = f32[2304,768]{1,0:T(8,128)S(1)} fusion(s32[2304]{0:T(1024)S(1)} %get-tuple-element.52, s32[2304]{0:T(1024)S(1)} %get-tuple-element.51, bf16[288,256]{1,0:T(8,128)(2,1)S(1)} %get-tuple-element.32, bf16[288,256]{1,0:T(8,128)(2,1)S(1)} %get-tuple-element.31, bf16[288,256]{1,0:T(8,128)(2,1)S(1)} %get-tuple-element.30), kind=kOutput, calls=%fused_computation.8 | convolution fusion | flops 1022533632 | bytes 7538688 | tf_op jit(solution)/shard_map/dot_general | solution.py:160
  44.7 1.0 multiply_convert_fusion
  45.7 0.5 fusion.54
  46.2 0.6 copy-done.2
  46.8 2.3 %fusion.1 = bf16[2304,169]{0,1:T(8,128)(2,1)S(1)} fusion(bf16[256,169]{0,1:T(8,128)(2,1)} %param.30, bf16[2304,256]{1,0:T(8,128)(2,1)} %copy-done.2, bf16[256,256]{1,0:T(8,128)(2,1)} %param.29, f32[2304,256]{1,0:T(8,128)S(1)} %fusion.54, f32[2304]{0:T(1024)S(1)} %get-tuple-element.24), kind=kOutput, calls=%fused_computation.4 | convolution fusion | flops 505668096 | bytes 4544512 | tf_op jit(solution)/shard_map/dot_general | solution.py:88
  49.1 0.2 reshape.411
  49.4 0.2 reshape.412
  49.9 0.5 fusion.8
  50.3 0.5 convolution_add_fusion.1
  50.9 6.9 %reshape.415 = f32[9,16,16,13,13]{2,1,4,3,0:T(8,128)} reshape(f32[9,256,169]{1,2,0:T(8,128)S(1)} %fusion.29) | data formatting | bytes 3115008 | tf_op jit(solution)/shard_map/reshape | solution.py:187
  57.7 17.0 %copy.93 = f32[9,16,16,13,13]{4,2,0,1,3:T(8,128)} copy(f32[9,16,16,13,13]{2,1,4,3,0:T(8,128)} %reshape.415) | data formatting | bytes 3115008 | tf_op jit(solution)/shard_map/reshape | solution.py:187
  74.7 9.5 %dot_general.55 = f32[16,13,1872]{2,0,1:T(8,128)S(1)} reshape(f32[16,13,9,16,13]{4,3,2,0,1:T(8,128)} %bitcast.110) | data formatting | bytes 3115008 | tf_op jit(solution)/shard_map/dot_general | solution.py:192
  84.3 0.3 reshape.416
  84.6 0.8 fusion.51
  85.5 1.9 %collective-permute-start.4 = (bf16[6656]{0:T(1024)(128)(2,1)S(1)}, bf16[6656]{0:T(1024)(128)(2,1)S(1)}, u32[]{:S(2)}, u32[]{:S(2)}) collective-permute-start(bf16[6656]{0:T(1024)(128)(2,1)S(1)} %reshape.417), channel_id=1, source_target_pairs={{0,32},{32,64},{64,96},{96,128},{128,160},{160,192},{192,224},{224... | collective-permute-start | bytes 39944 | tf_op jit(solution)/shard_map/ppermute | solution.py:24
  87.5 7.0 %collective-permute-start.5 = (bf16[6656]{0:T(1024)(128)(2,1)S(1)}, bf16[6656]{0:T(1024)(128)(2,1)S(1)}, u32[]{:S(2)}, u32[]{:S(2)}) collective-permute-start(bf16[6656]{0:T(1024)(128)(2,1)S(1)} %reshape.417), channel_id=1, source_target_pairs={{0,480},{32,0},{64,32},{96,64},{128,96},{160,128},{192,160},{224,1... | collective-permute-start | bytes 39944 | tf_op jit(solution)/shard_map/ppermute | solution.py:24
  94.6 0.7 collective-permute-done.5
  95.5 3.0 %collective-permute-start.6 = (bf16[19968]{0:T(1024)(128)(2,1)S(1)}, bf16[19968]{0:T(1024)(128)(2,1)S(1)}, u32[]{:S(2)}, u32[]{:S(2)}) collective-permute-start(bf16[19968]{0:T(1024)(128)(2,1)S(1)} %reshape.418), channel_id=1, source_target_pairs={{0,1},{1,2},{2,3},{3,4},{4,5},{5,6},{6,7},{7,8},{8,9},{9,10},{10,1... | collective-permute-start | bytes 119816 | tf_op jit(solution)/shard_map/ppermute | solution.py:24
  98.5 1.9 %collective-permute-start.7 = (bf16[19968]{0:T(1024)(128)(2,1)S(1)}, bf16[19968]{0:T(1024)(128)(2,1)S(1)}, u32[]{:S(2)}, u32[]{:S(2)}) collective-permute-start(bf16[19968]{0:T(1024)(128)(2,1)S(1)} %reshape.418), channel_id=1, source_target_pairs={{0,31},{1,0},{2,1},{3,2},{4,3},{5,4},{6,5},{7,6},{8,7},{9,8},{10,9... | collective-permute-start | bytes 119816 | tf_op jit(solution)/shard_map/ppermute | solution.py:24
  100.5 5.4 %collective-permute-done.7 = bf16[19968]{0:T(1024)(128)(2,1)S(1)} collective-permute-done((bf16[19968]{0:T(1024)(128)(2,1)S(1)}, bf16[19968]{0:T(1024)(128)(2,1)S(1)}, u32[]{:S(2)}, u32[]{:S(2)}) %collective-permute-start.7) | collective-permute-done | bytes 39968 | tf_op jit(solution)/shard_map/ppermute | solution.py:24
  106.1 0.3 reshape_reshape.7
  106.5 0.8 fusion.12
  107.4 1.9 %collective-permute-start.8 = (bf16[6656]{0:T(1024)(128)(2,1)S(1)}, bf16[6656]{0:T(1024)(128)(2,1)S(1)}, u32[]{:S(2)}, u32[]{:S(2)}) collective-permute-start(bf16[6656]{0:T(1024)(128)(2,1)S(1)} %reshape.419), channel_id=1, source_target_pairs={{0,32},{32,64},{64,96},{96,128},{128,160},{160,192},{192,224},{224... | collective-permute-start | bytes 39944 | tf_op jit(solution)/shard_map/ppermute | solution.py:24
  109.4 7.0 %collective-permute-start.9 = (bf16[6656]{0:T(1024)(128)(2,1)S(1)}, bf16[6656]{0:T(1024)(128)(2,1)S(1)}, u32[]{:S(2)}, u32[]{:S(2)}) collective-permute-start(bf16[6656]{0:T(1024)(128)(2,1)S(1)} %reshape.419), channel_id=1, source_target_pairs={{0,480},{32,0},{64,32},{96,64},{128,96},{160,128},{192,160},{224,1... | collective-permute-start | bytes 39944 | tf_op jit(solution)/shard_map/ppermute | solution.py:24
  116.5 0.7 collective-permute-done.9
  117.3 3.3 %collective-permute-start.10 = (bf16[19968]{0:T(1024)(128)(2,1)S(1)}, bf16[19968]{0:T(1024)(128)(2,1)S(1)}, u32[]{:S(2)}, u32[]{:S(2)}) collective-permute-start(bf16[19968]{0:T(1024)(128)(2,1)S(1)} %reshape.420), channel_id=1, source_target_pairs={{0,1},{1,2},{2,3},{3,4},{4,5},{5,6},{6,7},{7,8},{8,9},{9,10},{10,1... | collective-permute-start | bytes 119816 | tf_op jit(solution)/shard_map/ppermute | solution.py:24
  120.7 1.9 %collective-permute-start.11 = (bf16[19968]{0:T(1024)(128)(2,1)S(1)}, bf16[19968]{0:T(1024)(128)(2,1)S(1)}, u32[]{:S(2)}, u32[]{:S(2)}) collective-permute-start(bf16[19968]{0:T(1024)(128)(2,1)S(1)} %reshape.420), channel_id=1, source_target_pairs={{0,31},{1,0},{2,1},{3,2},{4,3},{5,4},{6,5},{7,6},{8,7},{9,8},{10,9... | collective-permute-start | bytes 119816 | tf_op jit(solution)/shard_map/ppermute | solution.py:24
  122.7 5.4 %collective-permute-done.11 = bf16[19968]{0:T(1024)(128)(2,1)S(1)} collective-permute-done((bf16[19968]{0:T(1024)(128)(2,1)S(1)}, bf16[19968]{0:T(1024)(128)(2,1)S(1)}, u32[]{:S(2)}, u32[]{:S(2)}) %collective-permute-start.11) | collective-permute-done | bytes 39968 | tf_op jit(solution)/shard_map/ppermute | solution.py:24
  128.3 0.3 reshape_reshape.8
  128.6 1.5 %fusion.11 = f32[1,1,16,13,32]{4,2,3,1,0:T(8,128)} fusion(f32[16,13,32]{2,0,1:T(8,128)S(1)} %get-tuple-element.50, f32[16,13,1872]{2,0,1:T(8,128)S(1)} %dot_general.55, bf16[1872,32]{1,0:T(8,128)(2,1)S(1)} %reshape_reshape.8), kind=kOutput, calls=%fused_computation.23 | convolution fusion | flops 149533696 | bytes 1730560 | tf_op jit(solution)/shard_map/dot_general | solution.py:192
  (98 shorter events, 3.2 us)
Async XLA Ops:
  0.0 45.7 %copy-start = (bf16[256,256]{1,0:T(8,128)(2,1)S(1)}, bf16[256,256]{1,0:T(8,128)(2,1)}, u32[]{:S(2)}) copy-start(bf16[256,256]{1,0:T(8,128)(2,1)} %param.28) | copy-start | bytes 393220
  5.5 18.7 %collective-permute-start = (bf16[13056]{0:T(1024)(128)(2,1)S(1)}, bf16[13056]{0:T(1024)(128)(2,1)S(1)}, u32[]{:S(2)}, u32[]{:S(2)}) collective-permute-start(bf16[13056]{0:T(1024)(128)(2,1)S(1)} %get-tuple-element.39), channel_id=1, source_target_pairs={{0,32},{32,64},{64,96},{96,128},{128,160},{160,192},{192,224},{224... | collective-permute-start | bytes 78344 | tf_op jit(solution)/shard_map/ppermute | solution.py:24
  9.5 14.7 %collective-permute-start.1 = (bf16[13056]{0:T(1024)(128)(2,1)S(1)}, bf16[13056]{0:T(1024)(128)(2,1)S(1)}, u32[]{:S(2)}, u32[]{:S(2)}) collective-permute-start(bf16[13056]{0:T(1024)(128)(2,1)S(1)} %get-tuple-element.38), channel_id=1, source_target_pairs={{0,480},{32,0},{64,32},{96,64},{128,96},{160,128},{192,160},{224,1... | collective-permute-start | bytes 78344 | tf_op jit(solution)/shard_map/ppermute | solution.py:24
  24.8 8.4 %collective-permute-start.2 = (bf16[34560]{0:T(1024)(128)(2,1)S(1)}, bf16[34560]{0:T(1024)(128)(2,1)S(1)}, u32[]{:S(2)}, u32[]{:S(2)}) collective-permute-start(bf16[34560]{0:T(1024)(128)(2,1)S(1)} %get-tuple-element.33), channel_id=1, source_target_pairs={{0,1},{1,2},{2,3},{3,4},{4,5},{5,6},{6,7},{7,8},{8,9},{9,10},{10,1... | collective-permute-start | bytes 207368 | tf_op jit(solution)/shard_map/ppermute | solution.py:24
  30.9 7.7 %collective-permute-start.3 = (bf16[34560]{0:T(1024)(128)(2,1)S(1)}, bf16[34560]{0:T(1024)(128)(2,1)S(1)}, u32[]{:S(2)}, u32[]{:S(2)}) collective-permute-start(bf16[34560]{0:T(1024)(128)(2,1)S(1)} %get-tuple-element.34), channel_id=1, source_target_pairs={{0,31},{1,0},{2,1},{3,2},{4,3},{5,4},{6,5},{7,6},{8,7},{9,8},{10,9... | collective-permute-start | bytes 207368 | tf_op jit(solution)/shard_map/ppermute | solution.py:24
  41.0 0.9 copy-start.4
  41.0 1.0 copy-start.5
  41.6 3.1 %copy-start.1 = (bf16[9,10752]{1,0:T(8,128)(2,1)}, bf16[9,10752]{1,0:T(8,128)(2,1)S(1)}, u32[]{:S(2)}) copy-start(bf16[9,10752]{1,0:T(8,128)(2,1)S(1)} %reshape.409) | copy-start | bytes 580612
  42.4 2.3 %copy-start.6 = (bf16[16,256]{1,0:T(8,128)(2,1)S(1)}, bf16[16,256]{1,0:T(8,128)(2,1)}, u32[]{:S(2)}) copy-start(bf16[16,256]{1,0:T(8,128)(2,1)} %param.25) | copy-start | bytes 24580
  45.7 1.0 copy-start.2
  74.7 9.6 %slice-start = ((bf16[9,10752]{1,0:T(8,128)(2,1)}), bf16[9,6656]{1,0:T(8,128)(2,1)S(1)}, s32[]{:S(2)}) async-start(bf16[9,10752]{1,0:T(8,128)(2,1)} %copy-done.1), calls=%async_computation | async-start | bytes 425984 | tf_op jit(solution)/shard_map/slice | solution.py:136
  85.4 21.0 %copy-start.3 = (bf16[1,1,16,13,32]{4,2,3,1,0:T(8,128)(2,1)S(1)}, bf16[1,1,16,13,32]{4,2,3,1,0:T(8,128)(2,1)}, u32[]{:S(2)}) copy-start(bf16[1,1,16,13,32]{4,2,3,1,0:T(8,128)(2,1)} %param.20) | copy-start | bytes 39940
  85.5 9.0 %collective-permute-start.4 = (bf16[6656]{0:T(1024)(128)(2,1)S(1)}, bf16[6656]{0:T(1024)(128)(2,1)S(1)}, u32[]{:S(2)}, u32[]{:S(2)}) collective-permute-start(bf16[6656]{0:T(1024)(128)(2,1)S(1)} %reshape.417), channel_id=1, source_target_pairs={{0,32},{32,64},{64,96},{96,128},{128,160},{160,192},{192,224},{224... | collective-permute-start | bytes 39944 | tf_op jit(solution)/shard_map/ppermute | solution.py:24
  87.5 7.8 %collective-permute-start.5 = (bf16[6656]{0:T(1024)(128)(2,1)S(1)}, bf16[6656]{0:T(1024)(128)(2,1)S(1)}, u32[]{:S(2)}, u32[]{:S(2)}) collective-permute-start(bf16[6656]{0:T(1024)(128)(2,1)S(1)} %reshape.417), channel_id=1, source_target_pairs={{0,480},{32,0},{64,32},{96,64},{128,96},{160,128},{192,160},{224,1... | collective-permute-start | bytes 39944 | tf_op jit(solution)/shard_map/ppermute | solution.py:24
  95.5 5.0 %collective-permute-start.6 = (bf16[19968]{0:T(1024)(128)(2,1)S(1)}, bf16[19968]{0:T(1024)(128)(2,1)S(1)}, u32[]{:S(2)}, u32[]{:S(2)}) collective-permute-start(bf16[19968]{0:T(1024)(128)(2,1)S(1)} %reshape.418), channel_id=1, source_target_pairs={{0,1},{1,2},{2,3},{3,4},{4,5},{5,6},{6,7},{7,8},{8,9},{9,10},{10,1... | collective-permute-start | bytes 119816 | tf_op jit(solution)/shard_map/ppermute | solution.py:24
  98.5 7.4 %collective-permute-start.7 = (bf16[19968]{0:T(1024)(128)(2,1)S(1)}, bf16[19968]{0:T(1024)(128)(2,1)S(1)}, u32[]{:S(2)}, u32[]{:S(2)}) collective-permute-start(bf16[19968]{0:T(1024)(128)(2,1)S(1)} %reshape.418), channel_id=1, source_target_pairs={{0,31},{1,0},{2,1},{3,2},{4,3},{5,4},{6,5},{7,6},{8,7},{9,8},{10,9... | collective-permute-start | bytes 119816 | tf_op jit(solution)/shard_map/ppermute | solution.py:24
  107.4 9.0 %collective-permute-start.8 = (bf16[6656]{0:T(1024)(128)(2,1)S(1)}, bf16[6656]{0:T(1024)(128)(2,1)S(1)}, u32[]{:S(2)}, u32[]{:S(2)}) collective-permute-start(bf16[6656]{0:T(1024)(128)(2,1)S(1)} %reshape.419), channel_id=1, source_target_pairs={{0,32},{32,64},{64,96},{96,128},{128,160},{160,192},{192,224},{224... | collective-permute-start | bytes 39944 | tf_op jit(solution)/shard_map/ppermute | solution.py:24
  109.4 7.8 %collective-permute-start.9 = (bf16[6656]{0:T(1024)(128)(2,1)S(1)}, bf16[6656]{0:T(1024)(128)(2,1)S(1)}, u32[]{:S(2)}, u32[]{:S(2)}) collective-permute-start(bf16[6656]{0:T(1024)(128)(2,1)S(1)} %reshape.419), channel_id=1, source_target_pairs={{0,480},{32,0},{64,32},{96,64},{128,96},{160,128},{192,160},{224,1... | collective-permute-start | bytes 39944 | tf_op jit(solution)/shard_map/ppermute | solution.py:24
  117.3 5.4 %collective-permute-start.10 = (bf16[19968]{0:T(1024)(128)(2,1)S(1)}, bf16[19968]{0:T(1024)(128)(2,1)S(1)}, u32[]{:S(2)}, u32[]{:S(2)}) collective-permute-start(bf16[19968]{0:T(1024)(128)(2,1)S(1)} %reshape.420), channel_id=1, source_target_pairs={{0,1},{1,2},{2,3},{3,4},{4,5},{5,6},{6,7},{7,8},{8,9},{9,10},{10,1... | collective-permute-start | bytes 119816 | tf_op jit(solution)/shard_map/ppermute | solution.py:24
  120.7 7.4 %collective-permute-start.11 = (bf16[19968]{0:T(1024)(128)(2,1)S(1)}, bf16[19968]{0:T(1024)(128)(2,1)S(1)}, u32[]{:S(2)}, u32[]{:S(2)}) collective-permute-start(bf16[19968]{0:T(1024)(128)(2,1)S(1)} %reshape.420), channel_id=1, source_target_pairs={{0,31},{1,0},{2,1},{3,2},{4,3},{5,4},{6,5},{7,6},{8,7},{9,8},{10,9... | collective-permute-start | bytes 119816 | tf_op jit(solution)/shard_map/ppermute | solution.py:24

commit v2 on v1

--- a/solution.py
+++ b/solution.py
@@ -76,7 +76,7 @@
     return all_common, incoming
 
 
-def pair_blocks(before_rows, distance, live_flags, radial_weight, mixing_weight, gate_weight, output_weight):
+def pair_mixed(before_rows, distance, live_flags, radial_weight, mixing_weight, gate_weight):
     centres = cutoff * jnp.arange(RBF, dtype=f32) / (RBF - 1)
     spacing = cutoff / (RBF - 1)
     basis = jnp.exp(-jnp.square((distance[:, None] - centres[None, :]) / spacing)).astype(bf16)
@@ -85,9 +85,8 @@
     edge = jax.nn.silu(before).astype(bf16)
     opened = jax.nn.silu(jnp.dot(edge, mixing_weight, preferred_element_type=f32))
     mixed = (opened * jnp.dot(edge, gate_weight, preferred_element_type=f32)).astype(bf16)
-    raw_out = jnp.dot(mixed, output_weight, preferred_element_type=f32)
     scale_factor = 1.5 / math.sqrt(NEIGHBOUR_SLOTS * ORBITAL_COUNT) * cutoff_envelope * live_flags
-    return (raw_out * scale_factor[:, None]).astype(bf16)
+    return mixed, scale_factor
 
 
 def on_device(
@@ -128,7 +127,7 @@
         [source.astype(bf16), target.astype(bf16), live.astype(bf16), high, middle, low], axis=-1
     ).reshape(9, slots * 6)
 
-    first = band_vectors[0, 0]
+    first = jnp.transpose(band_vectors[0, 0], (1, 0, 2))
     common = jnp.concatenate([atoms.reshape(-1), first.reshape(-1)])
     all_common, incoming = first_halo(common, pair_data)
     n_atoms = atom_count * feat
@@ -160,37 +159,40 @@
     picked = jnp.dot(pick, table_parts, preferred_element_type=f32)
     before_rows = (picked[:, :feat] + picked[:, feat : 2 * feat]) + picked[:, 2 * feat :]
 
-    hopping = pair_blocks(
-        before_rows, all_distance, all_live, radial_weight, mixing_weight, gate_weight, output_weight
-    )
-    own_hopping = hopping[: 9 * slots].reshape(9, slots, orb * orb)
-    in_hopping = jnp.swapaxes(
-        hopping[9 * slots :].reshape(9, slots, orb, orb), 2, 3
-    ).reshape(9, slots, orb * orb)
-
-    pair_ids = jnp.arange(atom_count * atom_count, dtype=jnp.int32)[None, None, :]
-    own_key = source * atom_count + target
-    in_key = in_target * atom_count + in_source
-    own_hot = (own_key[:, :, None] == pair_ids).astype(bf16)
-    in_hot = (in_key[:, :, None] == pair_ids).astype(bf16)
-    summed = jnp.einsum("tsp,tsb->tpb", own_hot, own_hopping, preferred_element_type=f32)
-    summed = summed + jnp.einsum("tsp,tsb->tpb", in_hot, in_hopping, preferred_element_type=f32)
+    mixed, scale = pair_mixed(
+        before_rows, all_distance, all_live, radial_weight, mixing_weight, gate_weight
+    )
+    weight_blocks = output_weight.reshape(feat, orb, orb)
+    own_weight = jnp.swapaxes(weight_blocks, 1, 2).reshape(feat, orb * orb)
+    own_raw = jnp.einsum("fb,sf->bs", own_weight, mixed[: 9 * slots], preferred_element_type=f32)
+    in_raw = jnp.einsum("fb,sf->bs", output_weight, mixed[9 * slots :], preferred_element_type=f32)
+    blocks_t = (jnp.concatenate([own_raw, in_raw], axis=1) * scale[None, :]).astype(bf16)
 
     square = jnp.dot(atoms, w_site, preferred_element_type=f32).reshape(-1, orb, orb)
     onsite = (onsite_scale * 0.5 * (square + jnp.swapaxes(square, 1, 2))).astype(bf16)
-    eye = jnp.eye(atom_count, dtype=f32)
-    onsite_full = (eye[:, :, None, None] * onsite.astype(f32)[:, None, :, :]).reshape(
-        atom_count * atom_count, orb * orb
-    )
-    summed = summed.at[4].add(onsite_full)
-    dense = jnp.transpose(
-        summed.reshape(9, atom_count, atom_count, orb, orb), (1, 3, 0, 2, 4)
-    ).reshape(atom_count * orb, 9 * atom_count * orb)
+    onsite_t = jnp.transpose(onsite, (2, 1, 0)).reshape(orb * orb, atom_count)
+    blocks_t = jnp.concatenate([blocks_t, onsite_t], axis=1)
+
+    own_atoms = jnp.arange(atom_count, dtype=jnp.int32)
+    row_atom = jnp.concatenate([source.reshape(-1), in_target.reshape(-1), own_atoms])
+    column_atom = jnp.concatenate(
+        [(places + target).reshape(-1), (places + in_source).reshape(-1), centre + own_atoms]
+    )
+    row_hot = (own_atoms[:, None] == row_atom[None, :]).astype(bf16)
+    spread = (blocks_t[:, None, :] * row_hot[None, :, :]).reshape(orb * orb * atom_count, -1)
+    column_hot = (column_atom[:, None] == jnp.arange(ring, dtype=jnp.int32)[None, :]).astype(bf16)
+    dense = jnp.dot(spread, column_hot, preferred_element_type=f32).reshape(
+        orb, orb * atom_count, ring
+    )
+    dense_parts = jnp.concatenate(bf16_parts(dense), axis=2)
 
     def apply(ring_vectors):
-        wide = ring_vectors.reshape(9 * atom_count * orb, vec).astype(f32)
-        out = jnp.dot(dense, wide, precision=lax.Precision.HIGHEST, preferred_element_type=f32)
-        return out.reshape(atom_count, orb, vec)
+        by_orbital = jnp.swapaxes(ring_vectors.reshape(9, orb, atom_count, vec), 0, 1).reshape(
+            orb, ring, vec
+        )
+        tripled = jnp.concatenate([by_orbital, by_orbital, by_orbital], axis=1)
+        out = jnp.einsum("qak,qkv->qav", dense_parts, tripled, preferred_element_type=f32)
+        return out.sum(axis=0).reshape(orb, atom_count, vec)
 
     previous = first.astype(f32)
     current = apply(ring_first)
@@ -198,6 +200,7 @@
         ring_now = halo(current.astype(bf16).reshape(-1))
         upcoming = 2.0 * apply(ring_now) - previous
         previous, current = (current, upcoming)
+    current = jnp.transpose(current, (1, 0, 2))
     return current[None, None]
 
 

time: 131 us -> 112 us (0.85)
  the two profiles are of different devices: /device:TPU:27 before, /device:TPU:32 now
where the time goes in v2:
time: 112 us; the launch traced here: 111 us
  starting transfers between devices  46.4 us (41%)
  waiting for transfers between devices  27 us (24%)
  matrix products  16.8 us (15%)
  other arithmetic  9.95 us (9%)
  local copies, waits for them, and re-layouts  9.94 us (9%)
    ppermute x12, starting transfers between devices, shifted(): return lax.ppermute(value, axis, pairs)  46.4 us
    ppermute x12, waiting for transfers between devices, shifted(): return lax.ppermute(value, axis, pairs)  27 us
    dot_general x3, matrix products, apply(): jnp.einsum('qak,qkv->qav', dense_parts, tripled, preferred_element_type=f32)  4.81 us
    dot_general x1, matrix products, on_device(): jnp.dot(spread, column_hot, preferred_element_type=f32)  4.56 us
    unnamed x6, other arithmetic  2.84 us
    mul x1, other arithmetic, on_device(): blocks_t[:, None, :] * row_hot[None, :, :]  2.42 us
  transfers between devices with their start and end apart: 12, of which 6 were waited for; matrix products, arithmetic and copies ran while one was open for 5% of the time, Pallas kernels for 0%

profile of v2, /device:TPU:32, one launch (start us, length us, event | category | flops | bytes accessed | tf_op | source)
XLA Modules:
  0.0 110.9 jit_solution(12629905216275428424)
XLA Ops:
  0.0 0.7 convert_element_type.182
  0.7 0.9 fusion.14
  1.7 0.7 fusion.63
  2.4 0.9 reshape.372
  3.3 0.7 constant_dynamic-update-slice_fusion.5
  4.0 0.7 constant_dynamic-update-slice_fusion.4
  4.8 0.2 copy.104
  5.0 0.2 reshape.374
  5.1 0.2 copy.103
  5.3 0.2 reshape.373
  5.5 13.4 %collective-permute-start.1 = (bf16[13056]{0:T(1024)(128)(2,1)S(1)}, bf16[13056]{0:T(1024)(128)(2,1)S(1)}, u32[]{:S(2)}, u32[]{:S(2)}) collective-permute-start(bf16[13056]{0:T(1024)(128)(2,1)S(1)} %get-tuple-element.26), channel_id=1, source_target_pairs={{0,480},{32,0},{64,32},{96,64},{128,96},{160,128},{192,160},{224,1... | collective-permute-start | bytes 78344 | tf_op jit(solution)/shard_map/ppermute | solution.py:24
  18.9 1.9 %collective-permute-start = (bf16[13056]{0:T(1024)(128)(2,1)S(1)}, bf16[13056]{0:T(1024)(128)(2,1)S(1)}, u32[]{:S(2)}, u32[]{:S(2)}) collective-permute-start(bf16[13056]{0:T(1024)(128)(2,1)S(1)} %get-tuple-element.27), channel_id=1, source_target_pairs={{0,32},{32,64},{64,96},{96,128},{128,160},{160,192},{192,224},{224... | collective-permute-start | bytes 78344 | tf_op jit(solution)/shard_map/ppermute | solution.py:24
  20.9 0.7 convert_reduce_fusion
  21.6 0.7 reduce.2
  22.3 1.0 fusion.68
  23.5 0.2 copy.110
  23.7 0.7 reduce.4
  24.5 0.2 copy.105
  24.6 0.2 stack.65
  24.8 0.9 reshape.378
  25.9 0.2 copy.137
  26.2 2.1 %collective-permute-done = bf16[13056]{0:T(1024)(128)(2,1)S(1)} collective-permute-done((bf16[13056]{0:T(1024)(128)(2,1)S(1)}, bf16[13056]{0:T(1024)(128)(2,1)S(1)}, u32[]{:S(2)}, u32[]{:S(2)}) %collective-permute-start) | collective-permute-done | bytes 26144 | tf_op jit(solution)/shard_map/ppermute | solution.py:24
  28.5 0.2 pad_maximum_fusion.6
  28.7 1.9 %collective-permute-start.2 = (bf16[34560]{0:T(1024)(128)(2,1)S(1)}, bf16[34560]{0:T(1024)(128)(2,1)S(1)}, u32[]{:S(2)}, u32[]{:S(2)}) collective-permute-start(bf16[34560]{0:T(1024)(128)(2,1)S(1)} %get-tuple-element.21), channel_id=1, source_target_pairs={{0,1},{1,2},{2,3},{3,4},{4,5},{5,6},{6,7},{7,8},{8,9},{9,10},{10,1... | collective-permute-start | bytes 207368 | tf_op jit(solution)/shard_map/ppermute | solution.py:24
  30.7 5.8 %collective-permute-start.3 = (bf16[34560]{0:T(1024)(128)(2,1)S(1)}, bf16[34560]{0:T(1024)(128)(2,1)S(1)}, u32[]{:S(2)}, u32[]{:S(2)}) collective-permute-start(bf16[34560]{0:T(1024)(128)(2,1)S(1)} %get-tuple-element.22), channel_id=1, source_target_pairs={{0,31},{1,0},{2,1},{3,2},{4,3},{5,4},{6,5},{7,6},{8,7},{9,8},{10,9... | collective-permute-start | bytes 207368 | tf_op jit(solution)/shard_map/ppermute | solution.py:24
  36.6 1.7 %collective-permute-done.3 = bf16[34560]{0:T(1024)(128)(2,1)S(1)} collective-permute-done((bf16[34560]{0:T(1024)(128)(2,1)S(1)}, bf16[34560]{0:T(1024)(128)(2,1)S(1)}, u32[]{:S(2)}, u32[]{:S(2)}) %collective-permute-start.3) | collective-permute-done | bytes 69152 | tf_op jit(solution)/shard_map/ppermute | solution.py:24
  38.4 0.2 pad_maximum_fusion.3
  38.7 0.2 reshape.376
  39.1 0.5 reshape.390
  39.6 1.0 slice_reduce_fusion
  40.6 0.5 fusion.20
  41.2 0.2 fusion.66
  41.4 0.2 fusion.65
  41.6 0.3 reshape.382
  41.9 0.3 copy.114
  42.5 2.2 %fusion.2 = f32[2304,768]{1,0:T(8,128)S(1)} fusion(s32[2304]{0:T(1024)S(1)} %add_add_fusion, s32[2304]{0:T(1024)S(1)} %pad_add_fusion, bf16[288,256]{1,0:T(8,128)(2,1)S(1)} %get-tuple-element.20, bf16[288,256]{1,0:T(8,128)(2,1)S(1)} %get-tuple-element.19, bf16[288,256]{1,0:T(8,128)(2,1)S(1)} %get-tuple-element.18), kind=kOutput, calls=%fused_computation.7 | convolution fusion | flops 1022533632 | bytes 7538688 | tf_op jit(solution)/shard_map/dot_general | solution.py:159
  44.7 0.9 multiply_convert_fusion
  45.7 0.5 fusion.67
  46.2 0.4 copy-done.5
  46.6 0.8 fusion
  47.5 0.3 convolution_bitcast_fusion
  47.9 0.3 convolution_bitcast_fusion.1
  48.4 2.4 %broadcast_multiply_fusion = bf16[169,16,2320]{2,1,0:T(8,128)(2,1)S(1)} fusion(bf16[16,2320]{1,0:T(8,128)(2,1)S(1)} %fusion.42, bf16[169,2320]{1,0:T(8,128)(2,1)S(1)} %pad_maximum_fusion.1), kind=kLoop, calls=%fused_computation | loop fusion | flops 6273280 | bytes 13404960 | tf_op jit(solution)/shard_map/mul | solution.py:182
  50.8 4.6 %reduce-precision_convert_fusion.1 = (bf16[13,208,144]{1,2,0:T(8,128)(2,1)S(1)}, bf16[13,208,144]{1,2,0:T(8,128)(2,1)S(1)}, bf16[13,208,144]{1,2,0:T(8,128)(2,1)S(1)}) fusion(bf16[13,208,2320]{2,1,0:T(8,128)(2,1)S(1)} %bitcast.120, s32[2320]{0:T(1024)S(1)} %pad_add_fusion.2), kind=kOutput, calls=%fused_computation.12 | convolution fusion | flops 1809764352 | bytes 14892096 | tf_op jit(solution)/shard_map/dot_general | solution.py:184
  55.4 0.8 fusion.64
  56.6 5.6 %collective-permute-start.5 = (bf16[6656]{0:T(1024)(128)(2,1)S(1)}, bf16[6656]{0:T(1024)(128)(2,1)S(1)}, u32[]{:S(2)}, u32[]{:S(2)}) collective-permute-start(bf16[6656]{0:T(1024)(128)(2,1)S(1)} %convert_element_type.208), channel_id=1, source_target_pairs={{0,480},{32,0},{64,32},{96,64},{128,96},{160,128},{192,160},{224,1... | collective-permute-start | bytes 39944 | tf_op jit(solution)/shard_map/ppermute | solution.py:24
  62.2 1.9 %collective-permute-start.4 = (bf16[6656]{0:T(1024)(128)(2,1)S(1)}, bf16[6656]{0:T(1024)(128)(2,1)S(1)}, u32[]{:S(2)}, u32[]{:S(2)}) collective-permute-start(bf16[6656]{0:T(1024)(128)(2,1)S(1)} %convert_element_type.208), channel_id=1, source_target_pairs={{0,32},{32,64},{64,96},{96,128},{128,160},{160,192},{192,224},{224... | collective-permute-start | bytes 39944 | tf_op jit(solution)/shard_map/ppermute | solution.py:24
  64.3 7.2 %collective-permute-done.4 = bf16[6656]{0:T(1024)(128)(2,1)S(1)} collective-permute-done((bf16[6656]{0:T(1024)(128)(2,1)S(1)}, bf16[6656]{0:T(1024)(128)(2,1)S(1)}, u32[]{:S(2)}, u32[]{:S(2)}) %collective-permute-start.4) | collective-permute-done | bytes 13344 | tf_op jit(solution)/shard_map/ppermute | solution.py:24
  71.6 3.8 %collective-permute-start.7 = (bf16[19968]{0:T(1024)(128)(2,1)S(1)}, bf16[19968]{0:T(1024)(128)(2,1)S(1)}, u32[]{:S(2)}, u32[]{:S(2)}) collective-permute-start(bf16[19968]{0:T(1024)(128)(2,1)S(1)} %reshape.384), channel_id=1, source_target_pairs={{0,31},{1,0},{2,1},{3,2},{4,3},{5,4},{6,5},{7,6},{8,7},{9,8},{10,9... | collective-permute-start | bytes 119816 | tf_op jit(solution)/shard_map/ppermute | solution.py:24
  75.4 1.9 %collective-permute-start.6 = (bf16[19968]{0:T(1024)(128)(2,1)S(1)}, bf16[19968]{0:T(1024)(128)(2,1)S(1)}, u32[]{:S(2)}, u32[]{:S(2)}) collective-permute-start(bf16[19968]{0:T(1024)(128)(2,1)S(1)} %reshape.384), channel_id=1, source_target_pairs={{0,1},{1,2},{2,3},{3,4},{4,5},{5,6},{6,7},{7,8},{8,9},{9,10},{10,1... | collective-permute-start | bytes 119816 | tf_op jit(solution)/shard_map/ppermute | solution.py:24
  77.5 5.4 %collective-permute-done.6 = bf16[19968]{0:T(1024)(128)(2,1)S(1)} collective-permute-done((bf16[19968]{0:T(1024)(128)(2,1)S(1)}, bf16[19968]{0:T(1024)(128)(2,1)S(1)}, u32[]{:S(2)}, u32[]{:S(2)}) %collective-permute-start.6) | collective-permute-done | bytes 39968 | tf_op jit(solution)/shard_map/ppermute | solution.py:24
  83.0 0.3 reshape_reshape.7
  83.4 0.3 copy.122
  83.7 2.0 %fusion.12 = f32[208,32]{0,1:T(8,128)S(1)} fusion(bf16[13,144,32]{1,2,0:T(8,128)(2,1)S(1)} %copy.122, bf16[13,208,144]{1,2,0:T(8,128)(2,1)S(1)} %get-tuple-element.16, bf16[13,208,144]{1,2,0:T(8,128)(2,1)} %copy-done.7, bf16[13,208,144]{1,2,0:T(8,128)(2,1)S(1)} %get-tuple-element.15), kind=kOutput, calls=%fused_computation.29 | convolution fusion | flops 82853888 | bytes 2482688 | tf_op jit(solution)/shard_map/qak,qkv->qav/dot_general | solution.py:194
  85.9 2.5 %collective-permute-start.9 = (bf16[6656]{0:T(1024)(128)(2,1)S(1)}, bf16[6656]{0:T(1024)(128)(2,1)S(1)}, u32[]{:S(2)}, u32[]{:S(2)}) collective-permute-start(bf16[6656]{0:T(1024)(128)(2,1)S(1)} %reshape.386), channel_id=1, source_target_pairs={{0,480},{32,0},{64,32},{96,64},{128,96},{160,128},{192,160},{224,1... | collective-permute-start | bytes 39944 | tf_op jit(solution)/shard_map/ppermute | solution.py:24
  88.5 3.3 %collective-permute-start.8 = (bf16[6656]{0:T(1024)(128)(2,1)S(1)}, bf16[6656]{0:T(1024)(128)(2,1)S(1)}, u32[]{:S(2)}, u32[]{:S(2)}) collective-permute-start(bf16[6656]{0:T(1024)(128)(2,1)S(1)} %reshape.386), channel_id=1, source_target_pairs={{0,32},{32,64},{64,96},{96,128},{128,160},{160,192},{192,224},{224... | collective-permute-start | bytes 39944 | tf_op jit(solution)/shard_map/ppermute | solution.py:24
  91.9 5.8 %collective-permute-done.8 = bf16[6656]{0:T(1024)(128)(2,1)S(1)} collective-permute-done((bf16[6656]{0:T(1024)(128)(2,1)S(1)}, bf16[6656]{0:T(1024)(128)(2,1)S(1)}, u32[]{:S(2)}, u32[]{:S(2)}) %collective-permute-start.8) | collective-permute-done | bytes 13344 | tf_op jit(solution)/shard_map/ppermute | solution.py:24
  97.9 1.9 %collective-permute-start.11 = (bf16[19968]{0:T(1024)(128)(2,1)S(1)}, bf16[19968]{0:T(1024)(128)(2,1)S(1)}, u32[]{:S(2)}, u32[]{:S(2)}) collective-permute-start(bf16[19968]{0:T(1024)(128)(2,1)S(1)} %reshape.387), channel_id=1, source_target_pairs={{0,31},{1,0},{2,1},{3,2},{4,3},{5,4},{6,5},{7,6},{8,7},{9,8},{10,9... | collective-permute-start | bytes 119816 | tf_op jit(solution)/shard_map/ppermute | solution.py:24
  99.8 2.4 %collective-permute-start.10 = (bf16[19968]{0:T(1024)(128)(2,1)S(1)}, bf16[19968]{0:T(1024)(128)(2,1)S(1)}, u32[]{:S(2)}, u32[]{:S(2)}) collective-permute-start(bf16[19968]{0:T(1024)(128)(2,1)S(1)} %reshape.387), channel_id=1, source_target_pairs={{0,1},{1,2},{2,3},{3,4},{4,5},{5,6},{6,7},{7,8},{8,9},{9,10},{10,1... | collective-permute-start | bytes 119816 | tf_op jit(solution)/shard_map/ppermute | solution.py:24
  102.4 4.9 %collective-permute-done.10 = bf16[19968]{0:T(1024)(128)(2,1)S(1)} collective-permute-done((bf16[19968]{0:T(1024)(128)(2,1)S(1)}, bf16[19968]{0:T(1024)(128)(2,1)S(1)}, u32[]{:S(2)}, u32[]{:S(2)}) %collective-permute-start.10) | collective-permute-done | bytes 39968 | tf_op jit(solution)/shard_map/ppermute | solution.py:24
  107.5 0.3 reshape_reshape.8
  107.8 0.3 copy.129
  108.1 2.0 %fusion.13 = f32[208,32]{0,1:T(8,128)S(1)} fusion(f32[208,32]{0,1:T(8,128)S(1)} %get-tuple-element.35, bf16[13,144,32]{1,2,0:T(8,128)(2,1)S(1)} %copy.129, bf16[13,208,144]{1,2,0:T(8,128)(2,1)S(1)} %get-tuple-element.16, bf16[13,208,144]{1,2,0:T(8,128)(2,1)} %copy-done.7, bf16[13,208,144]{1,2,0:T(8,128)(2,1)S(1)} %get-tuple-element.15), kind=kOutput, calls=%fused_computation.31 | convolution fusion | flops 82860544 | bytes 2509312 | tf_op jit(solution)/shard_map/qak,qkv->qav/dot_general | solution.py:194
  110.1 0.7 copy.133
  (108 shorter events, 3.6 us)
Async XLA Ops:
  0.0 45.7 %copy-start = (bf16[256,256]{1,0:T(8,128)(2,1)S(1)}, bf16[256,256]{1,0:T(8,128)(2,1)}, u32[]{:S(2)}) copy-start(bf16[256,256]{1,0:T(8,128)(2,1)} %param.26) | copy-start | bytes 393220
  5.5 20.6 %collective-permute-start.1 = (bf16[13056]{0:T(1024)(128)(2,1)S(1)}, bf16[13056]{0:T(1024)(128)(2,1)S(1)}, u32[]{:S(2)}, u32[]{:S(2)}) collective-permute-start(bf16[13056]{0:T(1024)(128)(2,1)S(1)} %get-tuple-element.26), channel_id=1, source_target_pairs={{0,480},{32,0},{64,32},{96,64},{128,96},{160,128},{192,160},{224,1... | collective-permute-start | bytes 78344 | tf_op jit(solution)/shard_map/ppermute | solution.py:24
  18.9 9.4 %collective-permute-start = (bf16[13056]{0:T(1024)(128)(2,1)S(1)}, bf16[13056]{0:T(1024)(128)(2,1)S(1)}, u32[]{:S(2)}, u32[]{:S(2)}) collective-permute-start(bf16[13056]{0:T(1024)(128)(2,1)S(1)} %get-tuple-element.27), channel_id=1, source_target_pairs={{0,32},{32,64},{64,96},{96,128},{128,160},{160,192},{192,224},{224... | collective-permute-start | bytes 78344 | tf_op jit(solution)/shard_map/ppermute | solution.py:24
  28.7 7.9 %collective-permute-start.2 = (bf16[34560]{0:T(1024)(128)(2,1)S(1)}, bf16[34560]{0:T(1024)(128)(2,1)S(1)}, u32[]{:S(2)}, u32[]{:S(2)}) collective-permute-start(bf16[34560]{0:T(1024)(128)(2,1)S(1)} %get-tuple-element.21), channel_id=1, source_target_pairs={{0,1},{1,2},{2,3},{3,4},{4,5},{5,6},{6,7},{7,8},{8,9},{9,10},{10,1... | collective-permute-start | bytes 207368 | tf_op jit(solution)/shard_map/ppermute | solution.py:24
  30.7 7.7 %collective-permute-start.3 = (bf16[34560]{0:T(1024)(128)(2,1)S(1)}, bf16[34560]{0:T(1024)(128)(2,1)S(1)}, u32[]{:S(2)}, u32[]{:S(2)}) collective-permute-start(bf16[34560]{0:T(1024)(128)(2,1)S(1)} %get-tuple-element.22), channel_id=1, source_target_pairs={{0,31},{1,0},{2,1},{3,2},{4,3},{5,4},{6,5},{7,6},{8,7},{9,8},{10,9... | collective-permute-start | bytes 207368 | tf_op jit(solution)/shard_map/ppermute | solution.py:24
  38.9 2.3 %copy-start.3 = (bf16[256,256]{1,0:T(8,128)(2,1)S(1)}, bf16[256,256]{1,0:T(8,128)(2,1)}, u32[]{:S(2)}) copy-start(bf16[256,256]{1,0:T(8,128)(2,1)} %param.25) | copy-start | bytes 393220
  39.1 2.3 %copy-start.4 = (bf16[256,256]{1,0:T(8,128)(2,1)S(1)}, bf16[256,256]{1,0:T(8,128)(2,1)}, u32[]{:S(2)}) copy-start(bf16[256,256]{1,0:T(8,128)(2,1)} %param.24) | copy-start | bytes 393220
  42.5 2.3 %copy-start.6 = (bf16[16,256]{1,0:T(8,128)(2,1)S(1)}, bf16[16,256]{1,0:T(8,128)(2,1)}, u32[]{:S(2)}) copy-start(bf16[16,256]{1,0:T(8,128)(2,1)} %param.23) | copy-start | bytes 24580
  45.7 0.9 copy-start.5
  46.6 0.9 copy-start.1
  55.4 1.0 copy-start.7
  56.6 7.7 %collective-permute-start.5 = (bf16[6656]{0:T(1024)(128)(2,1)S(1)}, bf16[6656]{0:T(1024)(128)(2,1)S(1)}, u32[]{:S(2)}, u32[]{:S(2)}) collective-permute-start(bf16[6656]{0:T(1024)(128)(2,1)S(1)} %convert_element_type.208), channel_id=1, source_target_pairs={{0,480},{32,0},{64,32},{96,64},{128,96},{160,128},{192,160},{224,1... | collective-permute-start | bytes 39944 | tf_op jit(solution)/shard_map/ppermute | solution.py:24
  62.2 9.2 %collective-permute-start.4 = (bf16[6656]{0:T(1024)(128)(2,1)S(1)}, bf16[6656]{0:T(1024)(128)(2,1)S(1)}, u32[]{:S(2)}, u32[]{:S(2)}) collective-permute-start(bf16[6656]{0:T(1024)(128)(2,1)S(1)} %convert_element_type.208), channel_id=1, source_target_pairs={{0,32},{32,64},{64,96},{96,128},{128,160},{160,192},{192,224},{224... | collective-permute-start | bytes 39944 | tf_op jit(solution)/shard_map/ppermute | solution.py:24
  71.6 5.8 %collective-permute-start.7 = (bf16[19968]{0:T(1024)(128)(2,1)S(1)}, bf16[19968]{0:T(1024)(128)(2,1)S(1)}, u32[]{:S(2)}, u32[]{:S(2)}) collective-permute-start(bf16[19968]{0:T(1024)(128)(2,1)S(1)} %reshape.384), channel_id=1, source_target_pairs={{0,31},{1,0},{2,1},{3,2},{4,3},{5,4},{6,5},{7,6},{8,7},{9,8},{10,9... | collective-permute-start | bytes 119816 | tf_op jit(solution)/shard_map/ppermute | solution.py:24
  75.4 7.4 %collective-permute-start.6 = (bf16[19968]{0:T(1024)(128)(2,1)S(1)}, bf16[19968]{0:T(1024)(128)(2,1)S(1)}, u32[]{:S(2)}, u32[]{:S(2)}) collective-permute-start(bf16[19968]{0:T(1024)(128)(2,1)S(1)} %reshape.384), channel_id=1, source_target_pairs={{0,1},{1,2},{2,3},{3,4},{4,5},{5,6},{6,7},{7,8},{8,9},{9,10},{10,1... | collective-permute-start | bytes 119816 | tf_op jit(solution)/shard_map/ppermute | solution.py:24
  83.7 2.1 %copy-start.2 = (bf16[1,1,16,13,32]{4,2,3,1,0:T(8,128)(2,1)S(1)}, bf16[1,1,16,13,32]{4,2,3,1,0:T(8,128)(2,1)}, u32[]{:S(2)}) copy-start(bf16[1,1,16,13,32]{4,2,3,1,0:T(8,128)(2,1)} %param.18) | copy-start | bytes 39940
  85.9 6.0 %collective-permute-start.9 = (bf16[6656]{0:T(1024)(128)(2,1)S(1)}, bf16[6656]{0:T(1024)(128)(2,1)S(1)}, u32[]{:S(2)}, u32[]{:S(2)}) collective-permute-start(bf16[6656]{0:T(1024)(128)(2,1)S(1)} %reshape.386), channel_id=1, source_target_pairs={{0,480},{32,0},{64,32},{96,64},{128,96},{160,128},{192,160},{224,1... | collective-permute-start | bytes 39944 | tf_op jit(solution)/shard_map/ppermute | solution.py:24
  88.5 9.2 %collective-permute-start.8 = (bf16[6656]{0:T(1024)(128)(2,1)S(1)}, bf16[6656]{0:T(1024)(128)(2,1)S(1)}, u32[]{:S(2)}, u32[]{:S(2)}) collective-permute-start(bf16[6656]{0:T(1024)(128)(2,1)S(1)} %reshape.386), channel_id=1, source_target_pairs={{0,32},{32,64},{64,96},{96,128},{128,160},{160,192},{192,224},{224... | collective-permute-start | bytes 39944 | tf_op jit(solution)/shard_map/ppermute | solution.py:24
  97.9 4.5 %collective-permute-start.11 = (bf16[19968]{0:T(1024)(128)(2,1)S(1)}, bf16[19968]{0:T(1024)(128)(2,1)S(1)}, u32[]{:S(2)}, u32[]{:S(2)}) collective-permute-start(bf16[19968]{0:T(1024)(128)(2,1)S(1)} %reshape.387), channel_id=1, source_target_pairs={{0,31},{1,0},{2,1},{3,2},{4,3},{5,4},{6,5},{7,6},{8,7},{9,8},{10,9... | collective-permute-start | bytes 119816 | tf_op jit(solution)/shard_map/ppermute | solution.py:24
  99.8 7.4 %collective-permute-start.10 = (bf16[19968]{0:T(1024)(128)(2,1)S(1)}, bf16[19968]{0:T(1024)(128)(2,1)S(1)}, u32[]{:S(2)}, u32[]{:S(2)}) collective-permute-start(bf16[19968]{0:T(1024)(128)(2,1)S(1)} %reshape.387), channel_id=1, source_target_pairs={{0,1},{1,2},{2,3},{3,4},{4,5},{5,6},{6,7},{7,8},{8,9},{9,10},{10,1... | collective-permute-start | bytes 119816 | tf_op jit(solution)/shard_map/ppermute | solution.py:24

commit v3 on v2

--- a/solution.py
+++ b/solution.py
@@ -32,48 +32,44 @@
     return high.astype(bf16), middle.astype(bf16), low.astype(bf16)
 
 
+def neighbour_shift(value, dx, dy):
+    nx = lax.axis_size("gx")
+    ny = lax.axis_size("gy")
+    if dx == 0:
+        return shifted(value, "gy", dy)
+    if dy == 0:
+        return shifted(value, "gx", dx)
+    pairs = [
+        (a * ny + b, ((a + dx) % nx) * ny + (b + dy) % ny) for a in range(nx) for b in range(ny)
+    ]
+    return lax.ppermute(value, ("gx", "gy"), pairs)
+
+
 def halo(flat):
-    from_west = shifted(flat, "gx", 1)
-    from_east = shifted(flat, "gx", -1)
-    strip = jnp.stack([from_west, flat, from_east]).reshape(-1)
-    from_south = shifted(strip, "gy", 1).reshape(3, -1)
-    from_north = shifted(strip, "gy", -1).reshape(3, -1)
-    strip = strip.reshape(3, -1)
-    return jnp.stack([from_south, strip, from_north], axis=1).reshape(9, -1)
+    places = []
+    for u in range(9):
+        if u == 4:
+            places.append(flat)
+        else:
+            t = 8 - u
+            places.append(neighbour_shift(flat, t // 3 - 1, t % 3 - 1))
+    return jnp.stack(places)
 
 
 def first_halo(common, pairs):
     n = common.shape[0]
-    m = pairs.shape[1]
-    to_east = jnp.concatenate([common, pairs[6:9].reshape(-1)])
-    to_west = jnp.concatenate([common, pairs[0:3].reshape(-1)])
-    from_west = shifted(to_east, "gx", 1)
-    from_east = shifted(to_west, "gx", -1)
-    strip_common = jnp.stack([from_west[:n], common, from_east[:n]])
-    strip_pairs = jnp.stack(
-        [
-            from_west[n:].reshape(3, m),
-            pairs[3:6],
-            from_east[n:].reshape(3, m),
-        ]
-    )
-    to_north = jnp.concatenate([strip_common.reshape(-1), strip_pairs[:, 2].reshape(-1)])
-    to_south = jnp.concatenate([strip_common.reshape(-1), strip_pairs[:, 0].reshape(-1)])
-    from_south = shifted(to_north, "gy", 1)
-    from_north = shifted(to_south, "gy", -1)
-    all_common = jnp.stack(
-        [from_south[: 3 * n].reshape(3, n), strip_common, from_north[: 3 * n].reshape(3, n)],
-        axis=1,
-    ).reshape(9, n)
-    incoming = jnp.stack(
-        [
-            from_south[3 * n :].reshape(3, m),
-            strip_pairs[:, 1],
-            from_north[3 * n :].reshape(3, m),
-        ],
-        axis=1,
-    ).reshape(9, m)
-    return all_common, incoming
+    all_common = []
+    incoming = []
+    for u in range(9):
+        t = 8 - u
+        if u == 4:
+            all_common.append(common)
+            incoming.append(pairs[4])
+        else:
+            got = neighbour_shift(jnp.concatenate([common, pairs[t]]), t // 3 - 1, t % 3 - 1)
+            all_common.append(got[:n])
+            incoming.append(got[n:])
+    return jnp.stack(all_common), jnp.stack(incoming)
 
 
 def pair_mixed(before_rows, distance, live_flags, radial_weight, mixing_weight, gate_weight):

time: 112 us -> 172 us (1.54)
  the two profiles are of different devices: /device:TPU:32 before, /device:TPU:4 now
where the time goes in v3:
time: 172 us; the launch traced here: 171 us
  starting transfers between devices  100 us (58%)
  waiting for transfers between devices  32.2 us (19%)
  matrix products  16.8 us (10%)
  local copies, waits for them, and re-layouts  12.8 us (7%)
  other arithmetic  7.89 us (5%)
    ppermute x12, starting transfers between devices, shifted(): return lax.ppermute(value, axis, pairs)  53.5 us
    ppermute x12, starting transfers between devices, neighbour_shift(): return lax.ppermute(value, ('gx', 'gy'), pairs)  46.9 us
    ppermute x12, waiting for transfers between devices, shifted(): return lax.ppermute(value, axis, pairs)  18.9 us
    ppermute x12, waiting for transfers between devices, neighbour_shift(): return lax.ppermute(value, ('gx', 'gy'), pairs)  13.2 us
    dot_general x3, matrix products, apply(): jnp.einsum('qak,qkv->qav', dense_parts, tripled, preferred_element_type=f32)  4.81 us
    dot_general x1, matrix products, on_device(): jnp.dot(spread, column_hot, preferred_element_type=f32)  4.57 us
    unnamed x7, other arithmetic  3.53 us
  transfers between devices with their start and end apart: 24, of which 6 were waited for; matrix products, arithmetic and copies ran while one was open for 5% of the time, Pallas kernels for 0%

profile of v3, /device:TPU:4, one launch (start us, length us, event | category | flops | bytes accessed | tf_op | source)
XLA Modules:
  0.0 171.3 jit_solution(8788433110743379501)
XLA Ops:
  0.0 1.0 fusion.14
  1.0 0.8 fusion.59
  1.7 0.9 reshape.451
  2.7 0.7 constant_dynamic-update-slice_fusion.5
  3.4 0.7 constant_dynamic-update-slice_fusion.4
  4.0 0.7 constant_dynamic-update-slice_fusion.3
  5.4 10.9 %collective-permute-start.6 = (bf16[11520]{0:T(1024)(128)(2,1)S(1)}, bf16[11520]{0:T(1024)(128)(2,1)S(1)}, u32[]{:S(2)}, u32[]{:S(2)}) collective-permute-start(bf16[11520]{0:T(1024)(128)(2,1)S(1)} %get-tuple-element.35), channel_id=1, source_target_pairs={{0,480},{32,0},{64,32},{96,64},{128,96},{160,128},{192,160},{224,1... | collective-permute-start | bytes 69128 | tf_op jit(solution)/shard_map/ppermute | solution.py:24
  16.3 1.9 %collective-permute-start = (bf16[11520]{0:T(1024)(128)(2,1)S(1)}, bf16[11520]{0:T(1024)(128)(2,1)S(1)}, u32[]{:S(2)}, u32[]{:S(2)}) collective-permute-start(bf16[11520]{0:T(1024)(128)(2,1)S(1)} %get-tuple-element.36), channel_id=1, source_target_pairs={{0,33},{1,34},{2,35},{3,36},{4,37},{5,38},{6,39},{7,40},{8,41},{9,... | collective-permute-start | bytes 69128 | tf_op jit(solution)/shard_map/ppermute | solution.py:45
  20.0 7.9 %collective-permute-start.7 = (bf16[11520]{0:T(1024)(128)(2,1)S(1)}, bf16[11520]{0:T(1024)(128)(2,1)S(1)}, u32[]{:S(2)}, u32[]{:S(2)}) collective-permute-start(bf16[11520]{0:T(1024)(128)(2,1)S(1)} %get-tuple-element.29), channel_id=1, source_target_pairs={{0,511},{1,480},{2,481},{3,482},{4,483},{5,484},{6,485},{7,486},{8... | collective-permute-start | bytes 69128 | tf_op jit(solution)/shard_map/ppermute | solution.py:45
  27.9 1.9 %collective-permute-start.1 = (bf16[11520]{0:T(1024)(128)(2,1)S(1)}, bf16[11520]{0:T(1024)(128)(2,1)S(1)}, u32[]{:S(2)}, u32[]{:S(2)}) collective-permute-start(bf16[11520]{0:T(1024)(128)(2,1)S(1)} %get-tuple-element.30), channel_id=1, source_target_pairs={{0,32},{32,64},{64,96},{96,128},{128,160},{160,192},{192,224},{224... | collective-permute-start | bytes 69128 | tf_op jit(solution)/shard_map/ppermute | solution.py:24
  29.8 2.1 %collective-permute-start.2 = (bf16[11520]{0:T(1024)(128)(2,1)S(1)}, bf16[11520]{0:T(1024)(128)(2,1)S(1)}, u32[]{:S(2)}, u32[]{:S(2)}) collective-permute-start(bf16[11520]{0:T(1024)(128)(2,1)S(1)} %get-tuple-element.31), channel_id=1, source_target_pairs={{0,63},{1,32},{2,33},{3,34},{4,35},{5,36},{6,37},{7,38},{8,39},{9,... | collective-permute-start | bytes 69128 | tf_op jit(solution)/shard_map/ppermute | solution.py:45
  32.0 0.7 convert_reduce_fusion
  32.7 0.7 reduce
  33.4 1.0 fusion.65
  34.6 0.2 copy.125
  34.8 2.1 %collective-permute-start.3 = (bf16[11520]{0:T(1024)(128)(2,1)S(1)}, bf16[11520]{0:T(1024)(128)(2,1)S(1)}, u32[]{:S(2)}, u32[]{:S(2)}) collective-permute-start(bf16[11520]{0:T(1024)(128)(2,1)S(1)} %get-tuple-element.32), channel_id=1, source_target_pairs={{0,1},{1,2},{2,3},{3,4},{4,5},{5,6},{6,7},{7,8},{8,9},{9,10},{10,1... | collective-permute-start | bytes 69128 | tf_op jit(solution)/shard_map/ppermute | solution.py:24
  36.9 5.8 %collective-permute-start.4 = (bf16[11520]{0:T(1024)(128)(2,1)S(1)}, bf16[11520]{0:T(1024)(128)(2,1)S(1)}, u32[]{:S(2)}, u32[]{:S(2)}) collective-permute-start(bf16[11520]{0:T(1024)(128)(2,1)S(1)} %get-tuple-element.33), channel_id=1, source_target_pairs={{0,31},{1,0},{2,1},{3,2},{4,3},{5,4},{6,5},{7,6},{8,7},{9,8},{10,9... | collective-permute-start | bytes 69128 | tf_op jit(solution)/shard_map/ppermute | solution.py:24
  42.7 5.9 %collective-permute-start.5 = (bf16[11520]{0:T(1024)(128)(2,1)S(1)}, bf16[11520]{0:T(1024)(128)(2,1)S(1)}, u32[]{:S(2)}, u32[]{:S(2)}) collective-permute-start(bf16[11520]{0:T(1024)(128)(2,1)S(1)} %get-tuple-element.34), channel_id=1, source_target_pairs={{0,481},{1,482},{2,483},{3,484},{4,485},{5,486},{6,487},{7,488},{8... | collective-permute-start | bytes 69128 | tf_op jit(solution)/shard_map/ppermute | solution.py:45
  48.6 0.7 reduce.1
  49.3 0.9 reshape.453
  50.3 0.2 copy.150
  51.0 0.7 stack.117
  54.1 0.2 fusion.63
  54.3 0.2 fusion.62
  54.5 0.3 reshape.457
  54.8 0.3 copy.129
  55.3 2.2 %fusion.2 = f32[2304,768]{1,0:T(8,128)S(1)} fusion(s32[2304]{0:T(1024)S(1)} %get-tuple-element.41, s32[2304]{0:T(1024)S(1)} %get-tuple-element.40, bf16[288,256]{1,0:T(8,128)(2,1)S(1)} %get-tuple-element.14, bf16[288,256]{1,0:T(8,128)(2,1)S(1)} %get-tuple-element.13, bf16[288,256]{1,0:T(8,128)(2,1)S(1)} %get-tuple-element.12), kind=kOutput, calls=%fused_computation.7 | convolution fusion | flops 1022533632 | bytes 7538688 | tf_op jit(solution)/shard_map/dot_general | solution.py:155
  57.6 0.9 multiply_convert_fusion
  58.5 0.5 fusion.64
  59.0 0.4 copy-done.5
  59.4 0.8 fusion
  60.3 0.3 convolution_bitcast_fusion
  60.7 0.3 convolution_bitcast_fusion.1
  61.2 2.4 %broadcast_multiply_fusion = bf16[169,16,2320]{2,1,0:T(8,128)(2,1)S(1)} fusion(bf16[16,2320]{1,0:T(8,128)(2,1)S(1)} %fusion.39, bf16[169,2320]{1,0:T(8,128)(2,1)S(1)} %pad_maximum_fusion.1), kind=kLoop, calls=%fused_computation | loop fusion | flops 6273280 | bytes 13404960 | tf_op jit(solution)/shard_map/mul | solution.py:178
  63.6 4.6 %reduce-precision_convert_fusion.1 = (bf16[13,208,144]{1,2,0:T(8,128)(2,1)S(1)}, bf16[13,208,144]{1,2,0:T(8,128)(2,1)S(1)}, bf16[13,208,144]{1,2,0:T(8,128)(2,1)S(1)}) fusion(bf16[13,208,2320]{2,1,0:T(8,128)(2,1)S(1)} %bitcast.113, s32[2320]{0:T(1024)S(1)} %pad_add_fusion.2), kind=kOutput, calls=%fused_computation.12 | convolution fusion | flops 1809764352 | bytes 14892096 | tf_op jit(solution)/shard_map/dot_general | solution.py:180
  68.2 0.8 fusion.61
  69.0 0.2 copy-done.7
  69.4 1.9 %collective-permute-start.8 = (bf16[6656]{0:T(1024)(128)(2,1)S(1)}, bf16[6656]{0:T(1024)(128)(2,1)S(1)}, u32[]{:S(2)}, u32[]{:S(2)}) collective-permute-start(bf16[6656]{0:T(1024)(128)(2,1)S(1)} %convert_element_type.205), channel_id=1, source_target_pairs={{0,33},{1,34},{2,35},{3,36},{4,37},{5,38},{6,39},{7,40},{8,41},{9,... | collective-permute-start | bytes 39944 | tf_op jit(solution)/shard_map/ppermute | solution.py:45
  71.3 9.5 %collective-permute-start.15 = (bf16[6656]{0:T(1024)(128)(2,1)S(1)}, bf16[6656]{0:T(1024)(128)(2,1)S(1)}, u32[]{:S(2)}, u32[]{:S(2)}) collective-permute-start(bf16[6656]{0:T(1024)(128)(2,1)S(1)} %convert_element_type.205), channel_id=1, source_target_pairs={{0,511},{1,480},{2,481},{3,482},{4,483},{5,484},{6,485},{7,486},{8... | collective-permute-start | bytes 39944 | tf_op jit(solution)/shard_map/ppermute | solution.py:45
  80.8 8.9 %collective-permute-start.14 = (bf16[6656]{0:T(1024)(128)(2,1)S(1)}, bf16[6656]{0:T(1024)(128)(2,1)S(1)}, u32[]{:S(2)}, u32[]{:S(2)}) collective-permute-start(bf16[6656]{0:T(1024)(128)(2,1)S(1)} %convert_element_type.205), channel_id=1, source_target_pairs={{0,480},{32,0},{64,32},{96,64},{128,96},{160,128},{192,160},{224,1... | collective-permute-start | bytes 39944 | tf_op jit(solution)/shard_map/ppermute | solution.py:24
  89.7 1.9 %collective-permute-start.13 = (bf16[6656]{0:T(1024)(128)(2,1)S(1)}, bf16[6656]{0:T(1024)(128)(2,1)S(1)}, u32[]{:S(2)}, u32[]{:S(2)}) collective-permute-start(bf16[6656]{0:T(1024)(128)(2,1)S(1)} %convert_element_type.205), channel_id=1, source_target_pairs={{0,481},{1,482},{2,483},{3,484},{4,485},{5,486},{6,487},{7,488},{8... | collective-permute-start | bytes 39944 | tf_op jit(solution)/shard_map/ppermute | solution.py:45
  91.6 4.9 %collective-permute-start.12 = (bf16[6656]{0:T(1024)(128)(2,1)S(1)}, bf16[6656]{0:T(1024)(128)(2,1)S(1)}, u32[]{:S(2)}, u32[]{:S(2)}) collective-permute-start(bf16[6656]{0:T(1024)(128)(2,1)S(1)} %convert_element_type.205), channel_id=1, source_target_pairs={{0,31},{1,0},{2,1},{3,2},{4,3},{5,4},{6,5},{7,6},{8,7},{9,8},{10,9... | collective-permute-start | bytes 39944 | tf_op jit(solution)/shard_map/ppermute | solution.py:24
  96.6 4.2 %collective-permute-start.9 = (bf16[6656]{0:T(1024)(128)(2,1)S(1)}, bf16[6656]{0:T(1024)(128)(2,1)S(1)}, u32[]{:S(2)}, u32[]{:S(2)}) collective-permute-start(bf16[6656]{0:T(1024)(128)(2,1)S(1)} %convert_element_type.205), channel_id=1, source_target_pairs={{0,32},{32,64},{64,96},{96,128},{128,160},{160,192},{192,224},{224... | collective-permute-start | bytes 39944 | tf_op jit(solution)/shard_map/ppermute | solution.py:24
  100.9 5.0 %collective-permute-done.9 = bf16[6656]{0:T(1024)(128)(2,1)S(1)} collective-permute-done((bf16[6656]{0:T(1024)(128)(2,1)S(1)}, bf16[6656]{0:T(1024)(128)(2,1)S(1)}, u32[]{:S(2)}, u32[]{:S(2)}) %collective-permute-start.9) | collective-permute-done | bytes 13344 | tf_op jit(solution)/shard_map/ppermute | solution.py:24
  105.9 2.1 %collective-permute-start.10 = (bf16[6656]{0:T(1024)(128)(2,1)S(1)}, bf16[6656]{0:T(1024)(128)(2,1)S(1)}, u32[]{:S(2)}, u32[]{:S(2)}) collective-permute-start(bf16[6656]{0:T(1024)(128)(2,1)S(1)} %convert_element_type.205), channel_id=1, source_target_pairs={{0,63},{1,32},{2,33},{3,34},{4,35},{5,36},{6,37},{7,38},{8,39},{9,... | collective-permute-start | bytes 39944 | tf_op jit(solution)/shard_map/ppermute | solution.py:45
  108.2 6.6 %collective-permute-done.10 = bf16[6656]{0:T(1024)(128)(2,1)S(1)} collective-permute-done((bf16[6656]{0:T(1024)(128)(2,1)S(1)}, bf16[6656]{0:T(1024)(128)(2,1)S(1)}, u32[]{:S(2)}, u32[]{:S(2)}) %collective-permute-start.10) | collective-permute-done | bytes 13344 | tf_op jit(solution)/shard_map/ppermute | solution.py:45
  114.8 1.9 %collective-permute-start.11 = (bf16[6656]{0:T(1024)(128)(2,1)S(1)}, bf16[6656]{0:T(1024)(128)(2,1)S(1)}, u32[]{:S(2)}, u32[]{:S(2)}) collective-permute-start(bf16[6656]{0:T(1024)(128)(2,1)S(1)} %convert_element_type.205), channel_id=1, source_target_pairs={{0,1},{1,2},{2,3},{3,4},{4,5},{5,6},{6,7},{7,8},{8,9},{9,10},{10,1... | collective-permute-start | bytes 39944 | tf_op jit(solution)/shard_map/ppermute | solution.py:24
  116.8 5.1 %collective-permute-done.11 = bf16[6656]{0:T(1024)(128)(2,1)S(1)} collective-permute-done((bf16[6656]{0:T(1024)(128)(2,1)S(1)}, bf16[6656]{0:T(1024)(128)(2,1)S(1)}, u32[]{:S(2)}, u32[]{:S(2)}) %collective-permute-start.11) | collective-permute-done | bytes 13344 | tf_op jit(solution)/shard_map/ppermute | solution.py:24
  122.6 0.3 copy.136
  122.9 2.0 %fusion.12 = f32[208,32]{0,1:T(8,128)S(1)} fusion(bf16[13,144,32]{1,2,0:T(8,128)(2,1)S(1)} %copy.136, bf16[13,208,144]{1,2,0:T(8,128)(2,1)S(1)} %get-tuple-element.10, bf16[13,208,144]{1,2,0:T(8,128)(2,1)} %copy-done.7, bf16[13,208,144]{1,2,0:T(8,128)(2,1)S(1)} %get-tuple-element.9), kind=kOutput, calls=%fused_computation.29 | convolution fusion | flops 82853888 | bytes 2482688 | tf_op jit(solution)/shard_map/qak,qkv->qav/dot_general | solution.py:190
  125.2 1.9 %collective-permute-start.16 = (bf16[6656]{0:T(1024)(128)(2,1)S(1)}, bf16[6656]{0:T(1024)(128)(2,1)S(1)}, u32[]{:S(2)}, u32[]{:S(2)}) collective-permute-start(bf16[6656]{0:T(1024)(128)(2,1)S(1)} %reshape.460), channel_id=1, source_target_pairs={{0,33},{1,34},{2,35},{3,36},{4,37},{5,38},{6,39},{7,40},{8,41},{9,... | collective-permute-start | bytes 39944 | tf_op jit(solution)/shard_map/ppermute | solution.py:45
  127.1 7.9 %collective-permute-start.23 = (bf16[6656]{0:T(1024)(128)(2,1)S(1)}, bf16[6656]{0:T(1024)(128)(2,1)S(1)}, u32[]{:S(2)}, u32[]{:S(2)}) collective-permute-start(bf16[6656]{0:T(1024)(128)(2,1)S(1)} %reshape.460), channel_id=1, source_target_pairs={{0,511},{1,480},{2,481},{3,482},{4,483},{5,484},{6,485},{7,486},{8... | collective-permute-start | bytes 39944 | tf_op jit(solution)/shard_map/ppermute | solution.py:45
  134.9 1.9 %collective-permute-start.22 = (bf16[6656]{0:T(1024)(128)(2,1)S(1)}, bf16[6656]{0:T(1024)(128)(2,1)S(1)}, u32[]{:S(2)}, u32[]{:S(2)}) collective-permute-start(bf16[6656]{0:T(1024)(128)(2,1)S(1)} %reshape.460), channel_id=1, source_target_pairs={{0,480},{32,0},{64,32},{96,64},{128,96},{160,128},{192,160},{224,1... | collective-permute-start | bytes 39944 | tf_op jit(solution)/shard_map/ppermute | solution.py:24
  136.9 1.9 %collective-permute-start.21 = (bf16[6656]{0:T(1024)(128)(2,1)S(1)}, bf16[6656]{0:T(1024)(128)(2,1)S(1)}, u32[]{:S(2)}, u32[]{:S(2)}) collective-permute-start(bf16[6656]{0:T(1024)(128)(2,1)S(1)} %reshape.460), channel_id=1, source_target_pairs={{0,481},{1,482},{2,483},{3,484},{4,485},{5,486},{6,487},{7,488},{8... | collective-permute-start | bytes 39944 | tf_op jit(solution)/shard_map/ppermute | solution.py:45
  138.8 3.7 %collective-permute-start.20 = (bf16[6656]{0:T(1024)(128)(2,1)S(1)}, bf16[6656]{0:T(1024)(128)(2,1)S(1)}, u32[]{:S(2)}, u32[]{:S(2)}) collective-permute-start(bf16[6656]{0:T(1024)(128)(2,1)S(1)} %reshape.460), channel_id=1, source_target_pairs={{0,31},{1,0},{2,1},{3,2},{4,3},{5,4},{6,5},{7,6},{8,7},{9,8},{10,9... | collective-permute-start | bytes 39944 | tf_op jit(solution)/shard_map/ppermute | solution.py:24
  142.5 5.4 %collective-permute-start.17 = (bf16[6656]{0:T(1024)(128)(2,1)S(1)}, bf16[6656]{0:T(1024)(128)(2,1)S(1)}, u32[]{:S(2)}, u32[]{:S(2)}) collective-permute-start(bf16[6656]{0:T(1024)(128)(2,1)S(1)} %reshape.460), channel_id=1, source_target_pairs={{0,32},{32,64},{64,96},{96,128},{128,160},{160,192},{192,224},{224... | collective-permute-start | bytes 39944 | tf_op jit(solution)/shard_map/ppermute | solution.py:24
  148.1 3.7 %collective-permute-done.17 = bf16[6656]{0:T(1024)(128)(2,1)S(1)} collective-permute-done((bf16[6656]{0:T(1024)(128)(2,1)S(1)}, bf16[6656]{0:T(1024)(128)(2,1)S(1)}, u32[]{:S(2)}, u32[]{:S(2)}) %collective-permute-start.17) | collective-permute-done | bytes 13344 | tf_op jit(solution)/shard_map/ppermute | solution.py:24
  151.7 1.9 %collective-permute-start.18 = (bf16[6656]{0:T(1024)(128)(2,1)S(1)}, bf16[6656]{0:T(1024)(128)(2,1)S(1)}, u32[]{:S(2)}, u32[]{:S(2)}) collective-permute-start(bf16[6656]{0:T(1024)(128)(2,1)S(1)} %reshape.460), channel_id=1, source_target_pairs={{0,63},{1,32},{2,33},{3,34},{4,35},{5,36},{6,37},{7,38},{8,39},{9,... | collective-permute-start | bytes 39944 | tf_op jit(solution)/shard_map/ppermute | solution.py:45
  153.8 6.6 %collective-permute-done.18 = bf16[6656]{0:T(1024)(128)(2,1)S(1)} collective-permute-done((bf16[6656]{0:T(1024)(128)(2,1)S(1)}, bf16[6656]{0:T(1024)(128)(2,1)S(1)}, u32[]{:S(2)}, u32[]{:S(2)}) %collective-permute-start.18) | collective-permute-done | bytes 13344 | tf_op jit(solution)/shard_map/ppermute | solution.py:45
  160.4 1.9 %collective-permute-start.19 = (bf16[6656]{0:T(1024)(128)(2,1)S(1)}, bf16[6656]{0:T(1024)(128)(2,1)S(1)}, u32[]{:S(2)}, u32[]{:S(2)}) collective-permute-start(bf16[6656]{0:T(1024)(128)(2,1)S(1)} %reshape.460), channel_id=1, source_target_pairs={{0,1},{1,2},{2,3},{3,4},{4,5},{5,6},{6,7},{7,8},{8,9},{9,10},{10,1... | collective-permute-start | bytes 39944 | tf_op jit(solution)/shard_map/ppermute | solution.py:24
  162.4 5.1 %collective-permute-done.19 = bf16[6656]{0:T(1024)(128)(2,1)S(1)} collective-permute-done((bf16[6656]{0:T(1024)(128)(2,1)S(1)}, bf16[6656]{0:T(1024)(128)(2,1)S(1)}, u32[]{:S(2)}, u32[]{:S(2)}) %collective-permute-start.19) | collective-permute-done | bytes 13344 | tf_op jit(solution)/shard_map/ppermute | solution.py:24
  168.2 0.3 copy.142
  168.5 2.0 %fusion.13 = f32[208,32]{0,1:T(8,128)S(1)} fusion(f32[208,32]{0,1:T(8,128)S(1)} %get-tuple-element.39, bf16[13,144,32]{1,2,0:T(8,128)(2,1)S(1)} %copy.142, bf16[13,208,144]{1,2,0:T(8,128)(2,1)S(1)} %get-tuple-element.10, bf16[13,208,144]{1,2,0:T(8,128)(2,1)} %copy-done.7, bf16[13,208,144]{1,2,0:T(8,128)(2,1)S(1)} %get-tuple-element.9), kind=kOutput, calls=%fused_computation.31 | convolution fusion | flops 82860544 | bytes 2509312 | tf_op jit(solution)/shard_map/qak,qkv->qav/dot_general | solution.py:190
  170.5 0.7 copy.146
  (164 shorter events, 7.9 us)
Async XLA Ops:
  0.0 58.5 %copy-start = (bf16[256,256]{1,0:T(8,128)(2,1)S(1)}, bf16[256,256]{1,0:T(8,128)(2,1)}, u32[]{:S(2)}) copy-start(bf16[256,256]{1,0:T(8,128)(2,1)} %param.26) | copy-start | bytes 393220
  5.4 29.4 %collective-permute-start.6 = (bf16[11520]{0:T(1024)(128)(2,1)S(1)}, bf16[11520]{0:T(1024)(128)(2,1)S(1)}, u32[]{:S(2)}, u32[]{:S(2)}) collective-permute-start(bf16[11520]{0:T(1024)(128)(2,1)S(1)} %get-tuple-element.35), channel_id=1, source_target_pairs={{0,480},{32,0},{64,32},{96,64},{128,96},{160,128},{192,160},{224,1... | collective-permute-start | bytes 69128 | tf_op jit(solution)/shard_map/ppermute | solution.py:24
  16.3 20.6 %collective-permute-start = (bf16[11520]{0:T(1024)(128)(2,1)S(1)}, bf16[11520]{0:T(1024)(128)(2,1)S(1)}, u32[]{:S(2)}, u32[]{:S(2)}) collective-permute-start(bf16[11520]{0:T(1024)(128)(2,1)S(1)} %get-tuple-element.36), channel_id=1, source_target_pairs={{0,33},{1,34},{2,35},{3,36},{4,37},{5,38},{6,39},{7,40},{8,41},{9,... | collective-permute-start | bytes 69128 | tf_op jit(solution)/shard_map/ppermute | solution.py:45
  20.0 22.7 %collective-permute-start.7 = (bf16[11520]{0:T(1024)(128)(2,1)S(1)}, bf16[11520]{0:T(1024)(128)(2,1)S(1)}, u32[]{:S(2)}, u32[]{:S(2)}) collective-permute-start(bf16[11520]{0:T(1024)(128)(2,1)S(1)} %get-tuple-element.29), channel_id=1, source_target_pairs={{0,511},{1,480},{2,481},{3,482},{4,483},{5,484},{6,485},{7,486},{8... | collective-permute-start | bytes 69128 | tf_op jit(solution)/shard_map/ppermute | solution.py:45
  27.9 22.8 %collective-permute-start.1 = (bf16[11520]{0:T(1024)(128)(2,1)S(1)}, bf16[11520]{0:T(1024)(128)(2,1)S(1)}, u32[]{:S(2)}, u32[]{:S(2)}) collective-permute-start(bf16[11520]{0:T(1024)(128)(2,1)S(1)} %get-tuple-element.30), channel_id=1, source_target_pairs={{0,32},{32,64},{64,96},{96,128},{128,160},{160,192},{192,224},{224... | collective-permute-start | bytes 69128 | tf_op jit(solution)/shard_map/ppermute | solution.py:24
  29.8 21.0 %collective-permute-start.2 = (bf16[11520]{0:T(1024)(128)(2,1)S(1)}, bf16[11520]{0:T(1024)(128)(2,1)S(1)}, u32[]{:S(2)}, u32[]{:S(2)}) collective-permute-start(bf16[11520]{0:T(1024)(128)(2,1)S(1)} %get-tuple-element.31), channel_id=1, source_target_pairs={{0,63},{1,32},{2,33},{3,34},{4,35},{5,36},{6,37},{7,38},{8,39},{9,... | collective-permute-start | bytes 69128 | tf_op jit(solution)/shard_map/ppermute | solution.py:45
  34.8 19.3 %copy-start.3 = (bf16[256,256]{1,0:T(8,128)(2,1)S(1)}, bf16[256,256]{1,0:T(8,128)(2,1)}, u32[]{:S(2)}) copy-start(bf16[256,256]{1,0:T(8,128)(2,1)} %param.25) | copy-start | bytes 393220
  34.8 19.5 %copy-start.4 = (bf16[256,256]{1,0:T(8,128)(2,1)S(1)}, bf16[256,256]{1,0:T(8,128)(2,1)}, u32[]{:S(2)}) copy-start(bf16[256,256]{1,0:T(8,128)(2,1)} %param.24) | copy-start | bytes 393220
  34.8 16.0 %collective-permute-start.3 = (bf16[11520]{0:T(1024)(128)(2,1)S(1)}, bf16[11520]{0:T(1024)(128)(2,1)S(1)}, u32[]{:S(2)}, u32[]{:S(2)}) collective-permute-start(bf16[11520]{0:T(1024)(128)(2,1)S(1)} %get-tuple-element.32), channel_id=1, source_target_pairs={{0,1},{1,2},{2,3},{3,4},{4,5},{5,6},{6,7},{7,8},{8,9},{9,10},{10,1... | collective-permute-start | bytes 69128 | tf_op jit(solution)/shard_map/ppermute | solution.py:24
  36.9 14.0 %collective-permute-start.4 = (bf16[11520]{0:T(1024)(128)(2,1)S(1)}, bf16[11520]{0:T(1024)(128)(2,1)S(1)}, u32[]{:S(2)}, u32[]{:S(2)}) collective-permute-start(bf16[11520]{0:T(1024)(128)(2,1)S(1)} %get-tuple-element.33), channel_id=1, source_target_pairs={{0,31},{1,0},{2,1},{3,2},{4,3},{5,4},{6,5},{7,6},{8,7},{9,8},{10,9... | collective-permute-start | bytes 69128 | tf_op jit(solution)/shard_map/ppermute | solution.py:24
  42.7 8.2 %collective-permute-start.5 = (bf16[11520]{0:T(1024)(128)(2,1)S(1)}, bf16[11520]{0:T(1024)(128)(2,1)S(1)}, u32[]{:S(2)}, u32[]{:S(2)}) collective-permute-start(bf16[11520]{0:T(1024)(128)(2,1)S(1)} %get-tuple-element.34), channel_id=1, source_target_pairs={{0,481},{1,482},{2,483},{3,484},{4,485},{5,486},{6,487},{7,488},{8... | collective-permute-start | bytes 69128 | tf_op jit(solution)/shard_map/ppermute | solution.py:45
  55.3 2.3 %copy-start.6 = (bf16[16,256]{1,0:T(8,128)(2,1)S(1)}, bf16[16,256]{1,0:T(8,128)(2,1)}, u32[]{:S(2)}) copy-start(bf16[16,256]{1,0:T(8,128)(2,1)} %param.23) | copy-start | bytes 24580
  58.5 0.9 copy-start.5
  59.4 0.9 copy-start.1
  68.2 1.0 copy-start.7
  69.4 27.2 %collective-permute-start.8 = (bf16[6656]{0:T(1024)(128)(2,1)S(1)}, bf16[6656]{0:T(1024)(128)(2,1)S(1)}, u32[]{:S(2)}, u32[]{:S(2)}) collective-permute-start(bf16[6656]{0:T(1024)(128)(2,1)S(1)} %convert_element_type.205), channel_id=1, source_target_pairs={{0,33},{1,34},{2,35},{3,36},{4,37},{5,38},{6,39},{7,40},{8,41},{9,... | collective-permute-start | bytes 39944 | tf_op jit(solution)/shard_map/ppermute | solution.py:45
  71.3 51.1 %collective-permute-start.15 = (bf16[6656]{0:T(1024)(128)(2,1)S(1)}, bf16[6656]{0:T(1024)(128)(2,1)S(1)}, u32[]{:S(2)}, u32[]{:S(2)}) collective-permute-start(bf16[6656]{0:T(1024)(128)(2,1)S(1)} %convert_element_type.205), channel_id=1, source_target_pairs={{0,511},{1,480},{2,481},{3,482},{4,483},{5,484},{6,485},{7,486},{8... | collective-permute-start | bytes 39944 | tf_op jit(solution)/shard_map/ppermute | solution.py:45
  80.8 41.5 %collective-permute-start.14 = (bf16[6656]{0:T(1024)(128)(2,1)S(1)}, bf16[6656]{0:T(1024)(128)(2,1)S(1)}, u32[]{:S(2)}, u32[]{:S(2)}) collective-permute-start(bf16[6656]{0:T(1024)(128)(2,1)S(1)} %convert_element_type.205), channel_id=1, source_target_pairs={{0,480},{32,0},{64,32},{96,64},{128,96},{160,128},{192,160},{224,1... | collective-permute-start | bytes 39944 | tf_op jit(solution)/shard_map/ppermute | solution.py:24
  89.7 32.5 %collective-permute-start.13 = (bf16[6656]{0:T(1024)(128)(2,1)S(1)}, bf16[6656]{0:T(1024)(128)(2,1)S(1)}, u32[]{:S(2)}, u32[]{:S(2)}) collective-permute-start(bf16[6656]{0:T(1024)(128)(2,1)S(1)} %convert_element_type.205), channel_id=1, source_target_pairs={{0,481},{1,482},{2,483},{3,484},{4,485},{5,486},{6,487},{7,488},{8... | collective-permute-start | bytes 39944 | tf_op jit(solution)/shard_map/ppermute | solution.py:45
  91.6 30.4 %collective-permute-start.12 = (bf16[6656]{0:T(1024)(128)(2,1)S(1)}, bf16[6656]{0:T(1024)(128)(2,1)S(1)}, u32[]{:S(2)}, u32[]{:S(2)}) collective-permute-start(bf16[6656]{0:T(1024)(128)(2,1)S(1)} %convert_element_type.205), channel_id=1, source_target_pairs={{0,31},{1,0},{2,1},{3,2},{4,3},{5,4},{6,5},{7,6},{8,7},{9,8},{10,9... | collective-permute-start | bytes 39944 | tf_op jit(solution)/shard_map/ppermute | solution.py:24
  96.6 9.4 %collective-permute-start.9 = (bf16[6656]{0:T(1024)(128)(2,1)S(1)}, bf16[6656]{0:T(1024)(128)(2,1)S(1)}, u32[]{:S(2)}, u32[]{:S(2)}) collective-permute-start(bf16[6656]{0:T(1024)(128)(2,1)S(1)} %convert_element_type.205), channel_id=1, source_target_pairs={{0,32},{32,64},{64,96},{96,128},{128,160},{160,192},{192,224},{224... | collective-permute-start | bytes 39944 | tf_op jit(solution)/shard_map/ppermute | solution.py:24
  105.9 8.9 %collective-permute-start.10 = (bf16[6656]{0:T(1024)(128)(2,1)S(1)}, bf16[6656]{0:T(1024)(128)(2,1)S(1)}, u32[]{:S(2)}, u32[]{:S(2)}) collective-permute-start(bf16[6656]{0:T(1024)(128)(2,1)S(1)} %convert_element_type.205), channel_id=1, source_target_pairs={{0,63},{1,32},{2,33},{3,34},{4,35},{5,36},{6,37},{7,38},{8,39},{9,... | collective-permute-start | bytes 39944 | tf_op jit(solution)/shard_map/ppermute | solution.py:45
  114.8 7.1 %collective-permute-start.11 = (bf16[6656]{0:T(1024)(128)(2,1)S(1)}, bf16[6656]{0:T(1024)(128)(2,1)S(1)}, u32[]{:S(2)}, u32[]{:S(2)}) collective-permute-start(bf16[6656]{0:T(1024)(128)(2,1)S(1)} %convert_element_type.205), channel_id=1, source_target_pairs={{0,1},{1,2},{2,3},{3,4},{4,5},{5,6},{6,7},{7,8},{8,9},{9,10},{10,1... | collective-permute-start | bytes 39944 | tf_op jit(solution)/shard_map/ppermute | solution.py:24
  122.9 2.1 %copy-start.2 = (bf16[1,1,16,13,32]{4,2,3,1,0:T(8,128)(2,1)S(1)}, bf16[1,1,16,13,32]{4,2,3,1,0:T(8,128)(2,1)}, u32[]{:S(2)}) copy-start(bf16[1,1,16,13,32]{4,2,3,1,0:T(8,128)(2,1)} %param.18) | copy-start | bytes 39940
  125.2 17.4 %collective-permute-start.16 = (bf16[6656]{0:T(1024)(128)(2,1)S(1)}, bf16[6656]{0:T(1024)(128)(2,1)S(1)}, u32[]{:S(2)}, u32[]{:S(2)}) collective-permute-start(bf16[6656]{0:T(1024)(128)(2,1)S(1)} %reshape.460), channel_id=1, source_target_pairs={{0,33},{1,34},{2,35},{3,36},{4,37},{5,38},{6,39},{7,40},{8,41},{9,... | collective-permute-start | bytes 39944 | tf_op jit(solution)/shard_map/ppermute | solution.py:45
  127.1 41.0 %collective-permute-start.23 = (bf16[6656]{0:T(1024)(128)(2,1)S(1)}, bf16[6656]{0:T(1024)(128)(2,1)S(1)}, u32[]{:S(2)}, u32[]{:S(2)}) collective-permute-start(bf16[6656]{0:T(1024)(128)(2,1)S(1)} %reshape.460), channel_id=1, source_target_pairs={{0,511},{1,480},{2,481},{3,482},{4,483},{5,484},{6,485},{7,486},{8... | collective-permute-start | bytes 39944 | tf_op jit(solution)/shard_map/ppermute | solution.py:45
  134.9 33.0 %collective-permute-start.22 = (bf16[6656]{0:T(1024)(128)(2,1)S(1)}, bf16[6656]{0:T(1024)(128)(2,1)S(1)}, u32[]{:S(2)}, u32[]{:S(2)}) collective-permute-start(bf16[6656]{0:T(1024)(128)(2,1)S(1)} %reshape.460), channel_id=1, source_target_pairs={{0,480},{32,0},{64,32},{96,64},{128,96},{160,128},{192,160},{224,1... | collective-permute-start | bytes 39944 | tf_op jit(solution)/shard_map/ppermute | solution.py:24
  136.9 30.9 %collective-permute-start.21 = (bf16[6656]{0:T(1024)(128)(2,1)S(1)}, bf16[6656]{0:T(1024)(128)(2,1)S(1)}, u32[]{:S(2)}, u32[]{:S(2)}) collective-permute-start(bf16[6656]{0:T(1024)(128)(2,1)S(1)} %reshape.460), channel_id=1, source_target_pairs={{0,481},{1,482},{2,483},{3,484},{4,485},{5,486},{6,487},{7,488},{8... | collective-permute-start | bytes 39944 | tf_op jit(solution)/shard_map/ppermute | solution.py:45
  138.8 28.8 %collective-permute-start.20 = (bf16[6656]{0:T(1024)(128)(2,1)S(1)}, bf16[6656]{0:T(1024)(128)(2,1)S(1)}, u32[]{:S(2)}, u32[]{:S(2)}) collective-permute-start(bf16[6656]{0:T(1024)(128)(2,1)S(1)} %reshape.460), channel_id=1, source_target_pairs={{0,31},{1,0},{2,1},{3,2},{4,3},{5,4},{6,5},{7,6},{8,7},{9,8},{10,9... | collective-permute-start | bytes 39944 | tf_op jit(solution)/shard_map/ppermute | solution.py:24
  142.5 9.2 %collective-permute-start.17 = (bf16[6656]{0:T(1024)(128)(2,1)S(1)}, bf16[6656]{0:T(1024)(128)(2,1)S(1)}, u32[]{:S(2)}, u32[]{:S(2)}) collective-permute-start(bf16[6656]{0:T(1024)(128)(2,1)S(1)} %reshape.460), channel_id=1, source_target_pairs={{0,32},{32,64},{64,96},{96,128},{128,160},{160,192},{192,224},{224... | collective-permute-start | bytes 39944 | tf_op jit(solution)/shard_map/ppermute | solution.py:24
  151.7 8.6 %collective-permute-start.18 = (bf16[6656]{0:T(1024)(128)(2,1)S(1)}, bf16[6656]{0:T(1024)(128)(2,1)S(1)}, u32[]{:S(2)}, u32[]{:S(2)}) collective-permute-start(bf16[6656]{0:T(1024)(128)(2,1)S(1)} %reshape.460), channel_id=1, source_target_pairs={{0,63},{1,32},{2,33},{3,34},{4,35},{5,36},{6,37},{7,38},{8,39},{9,... | collective-permute-start | bytes 39944 | tf_op jit(solution)/shard_map/ppermute | solution.py:45
  160.4 7.1 %collective-permute-start.19 = (bf16[6656]{0:T(1024)(128)(2,1)S(1)}, bf16[6656]{0:T(1024)(128)(2,1)S(1)}, u32[]{:S(2)}, u32[]{:S(2)}) collective-permute-start(bf16[6656]{0:T(1024)(128)(2,1)S(1)} %reshape.460), channel_id=1, source_target_pairs={{0,1},{1,2},{2,3},{3,4},{4,5},{5,6},{6,7},{7,8},{8,9},{9,10},{10,1... | collective-permute-start | bytes 39944 | tf_op jit(solution)/shard_map/ppermute | solution.py:24

commit v4 on v2

--- a/solution.py
+++ b/solution.py
@@ -73,7 +73,8 @@
         ],
         axis=1,
     ).reshape(9, m)
-    return all_common, incoming
+    strip_incoming = strip_pairs[:, 1]
+    return strip_common, strip_incoming, all_common, incoming
 
 
 def pair_mixed(before_rows, distance, live_flags, radial_weight, mixing_weight, gate_weight):
@@ -123,67 +124,101 @@
     target = pair_target[0, 0]
     live = pair_live_mask[0, 0]
     high, middle, low = bf16_parts(distance)
+    fields = 6
     pair_data = jnp.stack(
-        [source.astype(bf16), target.astype(bf16), live.astype(bf16), high, middle, low], axis=-1
-    ).reshape(9, slots * 6)
+        [source.astype(bf16), target.astype(bf16), live.astype(bf16), high, middle, low], axis=1
+    ).reshape(9, fields * slots)
 
     first = jnp.transpose(band_vectors[0, 0], (1, 0, 2))
     common = jnp.concatenate([atoms.reshape(-1), first.reshape(-1)])
-    all_common, incoming = first_halo(common, pair_data)
+    strip_common, strip_incoming, all_common, incoming = first_halo(common, pair_data)
     n_atoms = atom_count * feat
     ring_atoms = all_common[:, :n_atoms].reshape(9 * atom_count, feat)
     ring_first = all_common[:, n_atoms:]
-
-    incoming = incoming.reshape(9, slots, 6).astype(f32)
-    in_source = incoming[..., 0].astype(jnp.int32)
-    in_target = incoming[..., 1].astype(jnp.int32)
-    in_live = incoming[..., 2]
-    in_distance = (incoming[..., 3] + incoming[..., 4]) + incoming[..., 5]
-
-    places = jnp.arange(9, dtype=jnp.int32)[:, None] * atom_count
-    centre = 4 * atom_count
-    row_source = jnp.concatenate([(centre + source).reshape(-1), (places + in_source).reshape(-1)])
-    row_target = jnp.concatenate([(places + target).reshape(-1), (centre + in_target).reshape(-1)])
-    all_distance = jnp.concatenate([distance.reshape(-1), in_distance.reshape(-1)])
-    all_live = jnp.concatenate([live.reshape(-1).astype(f32), in_live.reshape(-1)])
-
-    source_projection = jnp.dot(ring_atoms, w_source, preferred_element_type=f32)
-    target_projection = jnp.dot(ring_atoms, w_target, preferred_element_type=f32)
-    table = jnp.concatenate([source_projection, target_projection])
-    table_parts = jnp.concatenate(bf16_parts(table), axis=1)
+    strip_atoms = strip_common[:, :n_atoms].reshape(3 * atom_count, feat)
+
+    def unpack(received):
+        received = received.reshape(-1, fields, slots).astype(f32)
+        got_source = received[:, 0].astype(jnp.int32)
+        got_target = received[:, 1].astype(jnp.int32)
+        got_distance = (received[:, 3] + received[:, 4]) + received[:, 5]
+        return got_source, got_target, received[:, 2], got_distance
+
     ring = 9 * atom_count
-    columns = jnp.arange(2 * ring, dtype=jnp.int32)[None, :]
-    pick = (
-        (columns == row_source[:, None]) | (columns == (row_target[:, None] + ring))
-    ).astype(bf16)
-    picked = jnp.dot(pick, table_parts, preferred_element_type=f32)
-    before_rows = (picked[:, :feat] + picked[:, feat : 2 * feat]) + picked[:, 2 * feat :]
-
-    mixed, scale = pair_mixed(
-        before_rows, all_distance, all_live, radial_weight, mixing_weight, gate_weight
-    )
     weight_blocks = output_weight.reshape(feat, orb, orb)
     own_weight = jnp.swapaxes(weight_blocks, 1, 2).reshape(feat, orb * orb)
-    own_raw = jnp.einsum("fb,sf->bs", own_weight, mixed[: 9 * slots], preferred_element_type=f32)
-    in_raw = jnp.einsum("fb,sf->bs", output_weight, mixed[9 * slots :], preferred_element_type=f32)
-    blocks_t = (jnp.concatenate([own_raw, in_raw], axis=1) * scale[None, :]).astype(bf16)
+    own_atoms = jnp.arange(atom_count, dtype=jnp.int32)
+
+    def group_dense(table_atoms, own_sets, in_source, in_target, in_distance, in_live, in_places, extra):
+        width = table_atoms.shape[0]
+        if width == ring:
+            block_of = {u: u for u in range(9)}
+        else:
+            block_of = {1: 0, 4: 1, 7: 2}
+        own_block = jnp.array([block_of[t] for t in own_sets], jnp.int32)[:, None] * atom_count
+        in_block = jnp.array([block_of[u] for u in in_places], jnp.int32)[:, None] * atom_count
+        centre_block = block_of[4] * atom_count
+        own_ring = jnp.array(own_sets, jnp.int32)[:, None] * atom_count
+        in_ring = jnp.array(in_places, jnp.int32)[:, None] * atom_count
+        own_source = source[jnp.array(own_sets)]
+        own_target = target[jnp.array(own_sets)]
+        row_source = jnp.concatenate(
+            [(centre_block + own_source).reshape(-1), (in_block + in_source).reshape(-1)]
+        )
+        row_target = jnp.concatenate(
+            [(own_block + own_target).reshape(-1), (centre_block + in_target).reshape(-1)]
+        )
+        group_distance = jnp.concatenate(
+            [distance[jnp.array(own_sets)].reshape(-1), in_distance.reshape(-1)]
+        )
+        group_live = jnp.concatenate(
+            [live[jnp.array(own_sets)].reshape(-1).astype(f32), in_live.reshape(-1)]
+        )
+        source_projection = jnp.dot(table_atoms, w_source, preferred_element_type=f32)
+        target_projection = jnp.dot(table_atoms, w_target, preferred_element_type=f32)
+        table = jnp.concatenate([source_projection, target_projection])
+        table_parts = jnp.concatenate(bf16_parts(table), axis=1)
+        columns = jnp.arange(2 * width, dtype=jnp.int32)[None, :]
+        pick = (
+            (columns == row_source[:, None]) | (columns == (row_target[:, None] + width))
+        ).astype(bf16)
+        picked = jnp.dot(pick, table_parts, preferred_element_type=f32)
+        before_rows = (picked[:, :feat] + picked[:, feat : 2 * feat]) + picked[:, 2 * feat :]
+        mixed, scale = pair_mixed(
+            before_rows, group_distance, group_live, radial_weight, mixing_weight, gate_weight
+        )
+        own_count = len(own_sets) * slots
+        own_raw = jnp.einsum("fb,sf->bs", own_weight, mixed[:own_count], preferred_element_type=f32)
+        in_raw = jnp.einsum("fb,sf->bs", output_weight, mixed[own_count:], preferred_element_type=f32)
+        blocks_t = (jnp.concatenate([own_raw, in_raw], axis=1) * scale[None, :]).astype(bf16)
+        row_atom = jnp.concatenate([own_source.reshape(-1), in_target.reshape(-1)])
+        column_atom = jnp.concatenate(
+            [(own_ring + own_target).reshape(-1), (in_ring + in_source).reshape(-1)]
+        )
+        if extra is not None:
+            blocks_t = jnp.concatenate([blocks_t, extra], axis=1)
+            row_atom = jnp.concatenate([row_atom, own_atoms])
+            column_atom = jnp.concatenate([column_atom, 4 * atom_count + own_atoms])
+        row_hot = (own_atoms[:, None] == row_atom[None, :]).astype(bf16)
+        spread = (blocks_t[:, None, :] * row_hot[None, :, :]).reshape(orb * orb * atom_count, -1)
+        column_hot = (column_atom[:, None] == jnp.arange(ring, dtype=jnp.int32)[None, :]).astype(bf16)
+        return jnp.dot(spread, column_hot, preferred_element_type=f32)
 
     square = jnp.dot(atoms, w_site, preferred_element_type=f32).reshape(-1, orb, orb)
     onsite = (onsite_scale * 0.5 * (square + jnp.swapaxes(square, 1, 2))).astype(bf16)
     onsite_t = jnp.transpose(onsite, (2, 1, 0)).reshape(orb * orb, atom_count)
-    blocks_t = jnp.concatenate([blocks_t, onsite_t], axis=1)
-
-    own_atoms = jnp.arange(atom_count, dtype=jnp.int32)
-    row_atom = jnp.concatenate([source.reshape(-1), in_target.reshape(-1), own_atoms])
-    column_atom = jnp.concatenate(
-        [(places + target).reshape(-1), (places + in_source).reshape(-1), centre + own_atoms]
-    )
-    row_hot = (own_atoms[:, None] == row_atom[None, :]).astype(bf16)
-    spread = (blocks_t[:, None, :] * row_hot[None, :, :]).reshape(orb * orb * atom_count, -1)
-    column_hot = (column_atom[:, None] == jnp.arange(ring, dtype=jnp.int32)[None, :]).astype(bf16)
-    dense = jnp.dot(spread, column_hot, preferred_element_type=f32).reshape(
-        orb, orb * atom_count, ring
-    )
+
+    strip_places = (1, 4, 7)
+    s_source, s_target, s_live, s_distance = unpack(strip_incoming)
+    dense = group_dense(
+        strip_atoms, strip_places, s_source, s_target, s_distance, s_live, strip_places, onsite_t
+    )
+    rest_places = (0, 2, 3, 5, 6, 8)
+    r_source, r_target, r_live, r_distance = unpack(incoming[jnp.array(rest_places)])
+    dense = dense + group_dense(
+        ring_atoms, rest_places, r_source, r_target, r_distance, r_live, rest_places, None
+    )
+    dense = dense.reshape(orb, orb * atom_count, ring)
     dense_parts = jnp.concatenate(bf16_parts(dense), axis=2)
 
     def apply(ring_vectors):

time: 112 us -> 123 us (1.098)
  the two profiles are of different devices: /device:TPU:32 before, /device:TPU:4 now
where the time goes in v4:
time: 123 us; the launch traced here: 122 us
  starting transfers between devices  46.4 us (38%)
  waiting for transfers between devices  22.6 us (18%)
  local copies, waits for them, and re-layouts  19.1 us (16%)
  matrix products  18.9 us (15%)
  other arithmetic  13.7 us (11%)
    ppermute x12, starting transfers between devices, shifted(): return lax.ppermute(value, axis, pairs)  46.4 us
    ppermute x12, waiting for transfers between devices, shifted(): return lax.ppermute(value, axis, pairs)  22.6 us
    dot_general x3, matrix products, apply(): jnp.einsum('qak,qkv->qav', dense_parts, tripled, preferred_element_type=f32)  6 us
    dot_general x2, matrix products, group_dense(): return jnp.dot(spread, column_hot, preferred_element_type=f32)  4.4 us
    convert_element_type x3, other arithmetic, bf16_parts(): return (high.astype(bf16), middle.astype(bf16), low.astype(bf16))  3.98 us
    mul x2, other arithmetic, group_dense(): blocks_t[:, None, :] * row_hot[None, :, :]  3.57 us
    reshape x1, local copies, waits for them, and re-layouts, on_device(): dense = dense.reshape(orb, orb * atom_count, ring)  3.52 us
    unnamed x28, local copies, waits for them, and re-layouts  2.79 us
  transfers between devices with their start and end apart: 12, of which 4 were waited for; matrix products, arithmetic and copies ran while one was open for 14% of the time, Pallas kernels for 0%

profile of v4, /device:TPU:4, one launch (start us, length us, event | category | flops | bytes accessed | tf_op | source)
XLA Modules:
  0.0 121.7 jit_solution(12709088650279027442)
XLA Ops:
  0.0 0.7 constant_dynamic-update-slice_fusion.5
  0.8 0.7 fusion.88
  1.5 0.7 constant_dynamic-update-slice_fusion.4
  2.2 0.7 constant_dynamic-update-slice_fusion.3
  3.0 0.9 reshape.543
  3.9 0.9 fusion.12
  4.9 10.9 %collective-permute-start.1 = (bf16[13056]{0:T(1024)(128)(2,1)S(1)}, bf16[13056]{0:T(1024)(128)(2,1)S(1)}, u32[]{:S(2)}, u32[]{:S(2)}) collective-permute-start(bf16[13056]{0:T(1024)(128)(2,1)S(1)} %get-tuple-element.32), channel_id=1, source_target_pairs={{0,480},{32,0},{64,32},{96,64},{128,96},{160,128},{192,160},{224,1... | collective-permute-start | bytes 78344 | tf_op jit(solution)/shard_map/ppermute | solution.py:24
  15.8 1.9 %collective-permute-start = (bf16[13056]{0:T(1024)(128)(2,1)S(1)}, bf16[13056]{0:T(1024)(128)(2,1)S(1)}, u32[]{:S(2)}, u32[]{:S(2)}) collective-permute-start(bf16[13056]{0:T(1024)(128)(2,1)S(1)} %get-tuple-element.31), channel_id=1, source_target_pairs={{0,32},{32,64},{64,96},{96,128},{128,160},{160,192},{192,224},{224... | collective-permute-start | bytes 78344 | tf_op jit(solution)/shard_map/ppermute | solution.py:24
  17.7 0.7 copy.203
  18.4 0.7 copy.202
  19.1 0.7 copy.201
  19.8 0.7 pad_clamp_fusion
  20.5 0.6 gather_fusion.4
  21.0 0.6 gather_fusion.6
  21.6 0.6 gather_fusion
  22.2 0.6 gather_fusion.1
  22.7 0.6 gather_fusion.8
  23.3 0.6 gather_fusion.3
  23.9 1.0 fusion.93
  25.3 0.7 add_bitcast_fusion
  26.0 0.7 add_bitcast_fusion.1
  26.7 0.6 gather_fusion.7
  27.3 0.6 gather_fusion.2
  27.9 0.9 reshape.548
  30.0 6.1 %collective-permute-start.3 = (bf16[34560]{0:T(1024)(128)(2,1)S(1)}, bf16[34560]{0:T(1024)(128)(2,1)S(1)}, u32[]{:S(2)}, u32[]{:S(2)}) collective-permute-start(bf16[34560]{0:T(1024)(128)(2,1)S(1)} %get-tuple-element.27), channel_id=1, source_target_pairs={{0,31},{1,0},{2,1},{3,2},{4,3},{5,4},{6,5},{7,6},{8,7},{9,8},{10,9... | collective-permute-start | bytes 207368 | tf_op jit(solution)/shard_map/ppermute | solution.py:24
  36.1 1.9 %collective-permute-start.2 = (bf16[34560]{0:T(1024)(128)(2,1)S(1)}, bf16[34560]{0:T(1024)(128)(2,1)S(1)}, u32[]{:S(2)}, u32[]{:S(2)}) collective-permute-start(bf16[34560]{0:T(1024)(128)(2,1)S(1)} %get-tuple-element.26), channel_id=1, source_target_pairs={{0,1},{1,2},{2,3},{3,4},{4,5},{5,6},{6,7},{7,8},{8,9},{9,10},{10,1... | collective-permute-start | bytes 207368 | tf_op jit(solution)/shard_map/ppermute | solution.py:24
  38.6 0.6 fusion.40
  39.2 0.5 multiply_convert_fusion.1
  40.1 0.3 fusion.6
  40.4 0.5 copy-done.2
  41.5 2.9 %broadcast_multiply_fusion.1 = bf16[169,16,784]{2,1,0:T(8,128)(2,1)} fusion(bf16[16,784]{1,0:T(8,128)(2,1)S(1)} %fusion.57, bf16[169,784]{1,0:T(8,128)(2,1)S(1)} %pad_maximum_fusion.1), kind=kLoop, calls=%fused_computation.19 | loop fusion | flops 2119936 | bytes 4529952 | tf_op jit(solution)/shard_map/mul | solution.py:203
  45.6 0.6 gather_fusion.5
  46.5 1.6 %fusion.2 = f32[1536,768]{1,0:T(8,128)S(1)} fusion(s32[1536]{0:T(1024)S(1)} %get-tuple-element.42, s32[1536]{0:T(1024)S(1)} %get-tuple-element.43, bf16[288,256]{1,0:T(8,128)(2,1)S(1)} %get-tuple-element.22, bf16[288,256]{1,0:T(8,128)(2,1)S(1)} %get-tuple-element.21, bf16[288,256]{1,0:T(8,128)(2,1)S(1)} %get-tuple-element.20), kind=kOutput, calls=%fused_computation.23 | convolution fusion | flops 682131456 | bytes 5173248 | tf_op jit(solution)/shard_map/dot_general | solution.py:185
  48.0 0.8 multiply_convert_fusion
  48.8 0.4 fusion.96
  49.2 0.5 fusion
  49.7 0.3 convolution_bitcast_fusion
  50.0 0.3 convolution_bitcast_fusion.1
  50.5 0.7 broadcast_multiply_fusion
  51.1 2.7 %fusion.5 = f32[2704,144]{0,1:T(8,128)S(1)} fusion(bf16[2704,1536]{1,0:T(8,128)(2,1)S(1)} %bitcast.168, s32[1536]{0:T(1024)S(1)} %get-tuple-element.41), kind=kOutput, calls=%fused_computation.29 | convolution fusion | flops 1196384256 | bytes 9870336 | tf_op jit(solution)/shard_map/dot_general | solution.py:205
  53.9 1.7 %convolution_add_fusion = f32[2704,144]{0,1:T(8,128)S(1)} fusion(f32[2704,144]{0,1:T(8,128)S(1)} %fusion.5, bf16[2704,784]{1,0:T(8,128)(2,1)S(1)} %bitcast.171, s32[784]{0:T(1024)S(1)} %pad_add_fusion.6), kind=kOutput, calls=%fused_computation.10 | convolution fusion | flops 611043840 | bytes 7358016 | tf_op jit(solution)/shard_map/dot_general | solution.py:205
  55.6 3.5 %reshape.557 = f32[13,208,144]{1,0,2:T(8,128)} reshape(f32[2704,144]{0,1:T(8,128)S(1)} %convolution_add_fusion) | data formatting | bytes 3115008 | tf_op jit(solution)/shard_map/reshape | solution.py:221
  59.1 3.9 %reduce-precision_convert_fusion.1 = (bf16[13,208,144]{1,2,0:T(8,128)(2,1)S(1)}, bf16[13,208,144]{1,2,0:T(8,128)(2,1)S(1)}, bf16[13,208,144]{1,2,0:T(8,128)(2,1)}) fusion(f32[13,208,144]{1,0,2:T(8,128)} %reshape.557), kind=kLoop, calls=%fused_computation.17 | loop fusion | flops 2725632 | bytes 3893760 | tf_op jit(solution)/shard_map/convert_element_type | solution.py:32
  63.3 0.3 copy.130
  63.6 2.0 %fusion.89 = (bf16[208,32]{0,1:T(8,128)(2,1)S(1)}, f32[208,32]{0,1:T(8,128)S(1)}) fusion(bf16[13,208,144]{1,2,0:T(8,128)(2,1)} %get-tuple-element.19, bf16[13,208,144]{1,2,0:T(8,128)(2,1)S(1)} %get-tuple-element.18, bf16[13,208,144]{1,2,0:T(8,128)(2,1)S(1)} %get-tuple-element.17, bf16[13,144,32]{1,2,0:T(8,128)(2,1)S(1)} %copy.130), kind=kOutput, calls=%fused_computation.224 | convolution fusion | flops 82853888 | bytes 2496000 | tf_op jit(solution)/shard_map/qak,qkv->qav/dot_general | solution.py:229
  65.9 6.7 %collective-permute-start.5 = (bf16[6656]{0:T(1024)(128)(2,1)S(1)}, bf16[6656]{0:T(1024)(128)(2,1)S(1)}, u32[]{:S(2)}, u32[]{:S(2)}) collective-permute-start(bf16[6656]{0:T(1024)(128)(2,1)S(1)} %convert_element_type.291), channel_id=1, source_target_pairs={{0,480},{32,0},{64,32},{96,64},{128,96},{160,128},{192,160},{224,1... | collective-permute-start | bytes 39944 | tf_op jit(solution)/shard_map/ppermute | solution.py:24
  72.5 1.9 %collective-permute-start.4 = (bf16[6656]{0:T(1024)(128)(2,1)S(1)}, bf16[6656]{0:T(1024)(128)(2,1)S(1)}, u32[]{:S(2)}, u32[]{:S(2)}) collective-permute-start(bf16[6656]{0:T(1024)(128)(2,1)S(1)} %convert_element_type.291), channel_id=1, source_target_pairs={{0,32},{32,64},{64,96},{96,128},{128,160},{160,192},{192,224},{224... | collective-permute-start | bytes 39944 | tf_op jit(solution)/shard_map/ppermute | solution.py:24
  74.6 7.2 %collective-permute-done.4 = bf16[6656]{0:T(1024)(128)(2,1)S(1)} collective-permute-done((bf16[6656]{0:T(1024)(128)(2,1)S(1)}, bf16[6656]{0:T(1024)(128)(2,1)S(1)}, u32[]{:S(2)}, u32[]{:S(2)}) %collective-permute-start.4) | collective-permute-done | bytes 13344 | tf_op jit(solution)/shard_map/ppermute | solution.py:24
  81.9 4.9 %collective-permute-start.7 = (bf16[19968]{0:T(1024)(128)(2,1)S(1)}, bf16[19968]{0:T(1024)(128)(2,1)S(1)}, u32[]{:S(2)}, u32[]{:S(2)}) collective-permute-start(bf16[19968]{0:T(1024)(128)(2,1)S(1)} %reshape.560), channel_id=1, source_target_pairs={{0,31},{1,0},{2,1},{3,2},{4,3},{5,4},{6,5},{7,6},{8,7},{9,8},{10,9... | collective-permute-start | bytes 119816 | tf_op jit(solution)/shard_map/ppermute | solution.py:24
  86.9 1.9 %collective-permute-start.6 = (bf16[19968]{0:T(1024)(128)(2,1)S(1)}, bf16[19968]{0:T(1024)(128)(2,1)S(1)}, u32[]{:S(2)}, u32[]{:S(2)}) collective-permute-start(bf16[19968]{0:T(1024)(128)(2,1)S(1)} %reshape.560), channel_id=1, source_target_pairs={{0,1},{1,2},{2,3},{3,4},{4,5},{5,6},{6,7},{7,8},{8,9},{9,10},{10,1... | collective-permute-start | bytes 119816 | tf_op jit(solution)/shard_map/ppermute | solution.py:24
  88.9 5.4 %collective-permute-done.6 = bf16[19968]{0:T(1024)(128)(2,1)S(1)} collective-permute-done((bf16[19968]{0:T(1024)(128)(2,1)S(1)}, bf16[19968]{0:T(1024)(128)(2,1)S(1)}, u32[]{:S(2)}, u32[]{:S(2)}) %collective-permute-start.6) | collective-permute-done | bytes 39968 | tf_op jit(solution)/shard_map/ppermute | solution.py:24
  94.5 0.3 reshape_reshape.6
  94.9 0.3 copy.138
  95.2 2.0 %fusion.10 = f32[208,32]{0,1:T(8,128)S(1)} fusion(bf16[13,144,32]{1,2,0:T(8,128)(2,1)S(1)} %copy.138, bf16[13,208,144]{1,2,0:T(8,128)(2,1)} %get-tuple-element.19, bf16[13,208,144]{1,2,0:T(8,128)(2,1)S(1)} %get-tuple-element.18, bf16[13,208,144]{1,2,0:T(8,128)(2,1)S(1)} %get-tuple-element.17), kind=kOutput, calls=%fused_computation.42 | convolution fusion | flops 82853888 | bytes 2482688 | tf_op jit(solution)/shard_map/qak,qkv->qav/dot_general | solution.py:229
  97.4 1.9 %collective-permute-start.9 = (bf16[6656]{0:T(1024)(128)(2,1)S(1)}, bf16[6656]{0:T(1024)(128)(2,1)S(1)}, u32[]{:S(2)}, u32[]{:S(2)}) collective-permute-start(bf16[6656]{0:T(1024)(128)(2,1)S(1)} %reshape.562), channel_id=1, source_target_pairs={{0,480},{32,0},{64,32},{96,64},{128,96},{160,128},{192,160},{224,1... | collective-permute-start | bytes 39944 | tf_op jit(solution)/shard_map/ppermute | solution.py:24
  99.3 3.9 %collective-permute-start.8 = (bf16[6656]{0:T(1024)(128)(2,1)S(1)}, bf16[6656]{0:T(1024)(128)(2,1)S(1)}, u32[]{:S(2)}, u32[]{:S(2)}) collective-permute-start(bf16[6656]{0:T(1024)(128)(2,1)S(1)} %reshape.562), channel_id=1, source_target_pairs={{0,32},{32,64},{64,96},{96,128},{128,160},{160,192},{192,224},{224... | collective-permute-start | bytes 39944 | tf_op jit(solution)/shard_map/ppermute | solution.py:24
  103.4 5.2 %collective-permute-done.8 = bf16[6656]{0:T(1024)(128)(2,1)S(1)} collective-permute-done((bf16[6656]{0:T(1024)(128)(2,1)S(1)}, bf16[6656]{0:T(1024)(128)(2,1)S(1)}, u32[]{:S(2)}, u32[]{:S(2)}) %collective-permute-start.8) | collective-permute-done | bytes 13344 | tf_op jit(solution)/shard_map/ppermute | solution.py:24
  108.7 1.9 %collective-permute-start.11 = (bf16[19968]{0:T(1024)(128)(2,1)S(1)}, bf16[19968]{0:T(1024)(128)(2,1)S(1)}, u32[]{:S(2)}, u32[]{:S(2)}) collective-permute-start(bf16[19968]{0:T(1024)(128)(2,1)S(1)} %reshape.563), channel_id=1, source_target_pairs={{0,31},{1,0},{2,1},{3,2},{4,3},{5,4},{6,5},{7,6},{8,7},{9,8},{10,9... | collective-permute-start | bytes 119816 | tf_op jit(solution)/shard_map/ppermute | solution.py:24
  110.7 2.4 %collective-permute-start.10 = (bf16[19968]{0:T(1024)(128)(2,1)S(1)}, bf16[19968]{0:T(1024)(128)(2,1)S(1)}, u32[]{:S(2)}, u32[]{:S(2)}) collective-permute-start(bf16[19968]{0:T(1024)(128)(2,1)S(1)} %reshape.563), channel_id=1, source_target_pairs={{0,1},{1,2},{2,3},{3,4},{4,5},{5,6},{6,7},{7,8},{8,9},{9,10},{10,1... | collective-permute-start | bytes 119816 | tf_op jit(solution)/shard_map/ppermute | solution.py:24
  113.2 4.9 %collective-permute-done.10 = bf16[19968]{0:T(1024)(128)(2,1)S(1)} collective-permute-done((bf16[19968]{0:T(1024)(128)(2,1)S(1)}, bf16[19968]{0:T(1024)(128)(2,1)S(1)}, u32[]{:S(2)}, u32[]{:S(2)}) %collective-permute-start.10) | collective-permute-done | bytes 39968 | tf_op jit(solution)/shard_map/ppermute | solution.py:24
  118.3 0.3 reshape_reshape.7
  118.7 0.3 copy.145
  119.0 2.0 %fusion.11 = f32[208,32]{0,1:T(8,128)S(1)} fusion(f32[208,32]{0,1:T(8,128)S(1)} %get-tuple-element.49, bf16[13,144,32]{1,2,0:T(8,128)(2,1)S(1)} %copy.145, bf16[13,208,144]{1,2,0:T(8,128)(2,1)} %get-tuple-element.19, bf16[13,208,144]{1,2,0:T(8,128)(2,1)S(1)} %get-tuple-element.18, bf16[13,208,144]{1,2,0:T(8,128)(2,1)S(1)} %get-tuple-element.17), kind=kOutput, calls=%fused_computation.44 | convolution fusion | flops 82860544 | bytes 2509312 | tf_op jit(solution)/shard_map/qak,qkv->qav/dot_general | solution.py:229
  121.0 0.7 copy.149
  (155 shorter events, 6.5 us)
Async XLA Ops:
  0.0 39.7 %copy-start = (bf16[256,256]{1,0:T(8,128)(2,1)S(1)}, bf16[256,256]{1,0:T(8,128)(2,1)}, u32[]{:S(2)}) copy-start(bf16[256,256]{1,0:T(8,128)(2,1)} %param.43) | copy-start | bytes 393220
  0.0 38.0 %copy-start.6 = (s32[3]{0:T(128)S(1)}, s32[3]{0:T(128)}, u32[]{:S(2)}) copy-start(s32[3]{0:T(128)} %constant.68) | copy-start | bytes 40
  0.0 38.2 %copy-start.3 = (bf16[256,256]{1,0:T(8,128)(2,1)S(1)}, bf16[256,256]{1,0:T(8,128)(2,1)}, u32[]{:S(2)}) copy-start(bf16[256,256]{1,0:T(8,128)(2,1)} %param.42) | copy-start | bytes 393220
  0.0 38.3 %copy-start.4 = (bf16[256,256]{1,0:T(8,128)(2,1)S(1)}, bf16[256,256]{1,0:T(8,128)(2,1)}, u32[]{:S(2)}) copy-start(bf16[256,256]{1,0:T(8,128)(2,1)} %param.41) | copy-start | bytes 393220
  4.9 24.3 %collective-permute-start.1 = (bf16[13056]{0:T(1024)(128)(2,1)S(1)}, bf16[13056]{0:T(1024)(128)(2,1)S(1)}, u32[]{:S(2)}, u32[]{:S(2)}) collective-permute-start(bf16[13056]{0:T(1024)(128)(2,1)S(1)} %get-tuple-element.32), channel_id=1, source_target_pairs={{0,480},{32,0},{64,32},{96,64},{128,96},{160,128},{192,160},{224,1... | collective-permute-start | bytes 78344 | tf_op jit(solution)/shard_map/ppermute | solution.py:24
  15.8 13.4 %collective-permute-start = (bf16[13056]{0:T(1024)(128)(2,1)S(1)}, bf16[13056]{0:T(1024)(128)(2,1)S(1)}, u32[]{:S(2)}, u32[]{:S(2)}) collective-permute-start(bf16[13056]{0:T(1024)(128)(2,1)S(1)} %get-tuple-element.31), channel_id=1, source_target_pairs={{0,32},{32,64},{64,96},{96,128},{128,160},{160,192},{192,224},{224... | collective-permute-start | bytes 78344 | tf_op jit(solution)/shard_map/ppermute | solution.py:24
  29.1 10.0 %copy-start.9 = (bf16[16,256]{1,0:T(8,128)(2,1)S(1)}, bf16[16,256]{1,0:T(8,128)(2,1)}, u32[]{:S(2)}) copy-start(bf16[16,256]{1,0:T(8,128)(2,1)} %param.40) | copy-start | bytes 24580
  30.0 14.4 %collective-permute-start.3 = (bf16[34560]{0:T(1024)(128)(2,1)S(1)}, bf16[34560]{0:T(1024)(128)(2,1)S(1)}, u32[]{:S(2)}, u32[]{:S(2)}) collective-permute-start(bf16[34560]{0:T(1024)(128)(2,1)S(1)} %get-tuple-element.27), channel_id=1, source_target_pairs={{0,31},{1,0},{2,1},{3,2},{4,3},{5,4},{6,5},{7,6},{8,7},{9,8},{10,9... | collective-permute-start | bytes 207368 | tf_op jit(solution)/shard_map/ppermute | solution.py:24
  36.1 8.4 %collective-permute-start.2 = (bf16[34560]{0:T(1024)(128)(2,1)S(1)}, bf16[34560]{0:T(1024)(128)(2,1)S(1)}, u32[]{:S(2)}, u32[]{:S(2)}) collective-permute-start(bf16[34560]{0:T(1024)(128)(2,1)S(1)} %get-tuple-element.26), channel_id=1, source_target_pairs={{0,1},{1,2},{2,3},{3,4},{4,5},{5,6},{6,7},{7,8},{8,9},{9,10},{10,1... | collective-permute-start | bytes 207368 | tf_op jit(solution)/shard_map/ppermute | solution.py:24
  39.2 0.9 copy-start.8
  40.1 0.9 copy-start.2
  44.4 1.9 %copy-start.7 = (s32[6]{0:T(128)S(1)}, s32[6]{0:T(128)}, u32[]{:S(2)}) copy-start(s32[6]{0:T(128)} %constant.73) | copy-start | bytes 76
  45.0 5.3 %copy-start.1 = (bf16[9,10752]{1,0:T(8,128)(2,1)}, bf16[9,10752]{1,0:T(8,128)(2,1)S(1)}, u32[]{:S(2)}) copy-start(bf16[9,10752]{1,0:T(8,128)(2,1)S(1)} %reshape.554) | copy-start | bytes 580612
  50.4 3.4 %slice-start = ((s8[4845568]{0:T(1024)(128)(4,1)}), s8[4194304]{0:T(1024)(128)(4,1)S(1)}, s32[]{:S(2)}) async-start(s8[4845568]{0:T(1024)(128)(4,1)} %bitcast.169), calls=%async_computation | async-start | bytes 8388608
  51.1 2.7 %slice-start.1 = ((s8[4845568]{0:T(1024)(128)(4,1)}), s8[651264]{0:T(1024)(128)(4,1)S(1)}, s32[]{:S(2)}) async-start(s8[4845568]{0:T(1024)(128)(4,1)} %bitcast.169), calls=%async_computation.1 | async-start | bytes 1302528
  59.1 3.9 %slice-start.2 = ((bf16[9,10752]{1,0:T(8,128)(2,1)}), bf16[9,6656]{1,0:T(8,128)(2,1)S(1)}, s32[]{:S(2)}) async-start(bf16[9,10752]{1,0:T(8,128)(2,1)} %copy-done.1), calls=%async_computation.2 | async-start | bytes 425984 | tf_op jit(solution)/shard_map/slice | solution.py:137
  65.9 8.7 %collective-permute-start.5 = (bf16[6656]{0:T(1024)(128)(2,1)S(1)}, bf16[6656]{0:T(1024)(128)(2,1)S(1)}, u32[]{:S(2)}, u32[]{:S(2)}) collective-permute-start(bf16[6656]{0:T(1024)(128)(2,1)S(1)} %convert_element_type.291), channel_id=1, source_target_pairs={{0,480},{32,0},{64,32},{96,64},{128,96},{160,128},{192,160},{224,1... | collective-permute-start | bytes 39944 | tf_op jit(solution)/shard_map/ppermute | solution.py:24
  72.5 9.2 %collective-permute-start.4 = (bf16[6656]{0:T(1024)(128)(2,1)S(1)}, bf16[6656]{0:T(1024)(128)(2,1)S(1)}, u32[]{:S(2)}, u32[]{:S(2)}) collective-permute-start(bf16[6656]{0:T(1024)(128)(2,1)S(1)} %convert_element_type.291), channel_id=1, source_target_pairs={{0,32},{32,64},{64,96},{96,128},{128,160},{160,192},{192,224},{224... | collective-permute-start | bytes 39944 | tf_op jit(solution)/shard_map/ppermute | solution.py:24
  81.9 7.0 %collective-permute-start.7 = (bf16[19968]{0:T(1024)(128)(2,1)S(1)}, bf16[19968]{0:T(1024)(128)(2,1)S(1)}, u32[]{:S(2)}, u32[]{:S(2)}) collective-permute-start(bf16[19968]{0:T(1024)(128)(2,1)S(1)} %reshape.560), channel_id=1, source_target_pairs={{0,31},{1,0},{2,1},{3,2},{4,3},{5,4},{6,5},{7,6},{8,7},{9,8},{10,9... | collective-permute-start | bytes 119816 | tf_op jit(solution)/shard_map/ppermute | solution.py:24
  86.9 7.4 %collective-permute-start.6 = (bf16[19968]{0:T(1024)(128)(2,1)S(1)}, bf16[19968]{0:T(1024)(128)(2,1)S(1)}, u32[]{:S(2)}, u32[]{:S(2)}) collective-permute-start(bf16[19968]{0:T(1024)(128)(2,1)S(1)} %reshape.560), channel_id=1, source_target_pairs={{0,1},{1,2},{2,3},{3,4},{4,5},{5,6},{6,7},{7,8},{8,9},{9,10},{10,1... | collective-permute-start | bytes 119816 | tf_op jit(solution)/shard_map/ppermute | solution.py:24
  95.2 2.1 %copy-start.5 = (bf16[1,1,16,13,32]{4,2,3,1,0:T(8,128)(2,1)S(1)}, bf16[1,1,16,13,32]{4,2,3,1,0:T(8,128)(2,1)}, u32[]{:S(2)}) copy-start(bf16[1,1,16,13,32]{4,2,3,1,0:T(8,128)(2,1)} %param.35) | copy-start | bytes 39940
  97.4 6.0 %collective-permute-start.9 = (bf16[6656]{0:T(1024)(128)(2,1)S(1)}, bf16[6656]{0:T(1024)(128)(2,1)S(1)}, u32[]{:S(2)}, u32[]{:S(2)}) collective-permute-start(bf16[6656]{0:T(1024)(128)(2,1)S(1)} %reshape.562), channel_id=1, source_target_pairs={{0,480},{32,0},{64,32},{96,64},{128,96},{160,128},{192,160},{224,1... | collective-permute-start | bytes 39944 | tf_op jit(solution)/shard_map/ppermute | solution.py:24
  99.3 9.2 %collective-permute-start.8 = (bf16[6656]{0:T(1024)(128)(2,1)S(1)}, bf16[6656]{0:T(1024)(128)(2,1)S(1)}, u32[]{:S(2)}, u32[]{:S(2)}) collective-permute-start(bf16[6656]{0:T(1024)(128)(2,1)S(1)} %reshape.562), channel_id=1, source_target_pairs={{0,32},{32,64},{64,96},{96,128},{128,160},{160,192},{192,224},{224... | collective-permute-start | bytes 39944 | tf_op jit(solution)/shard_map/ppermute | solution.py:24
  108.7 4.5 %collective-permute-start.11 = (bf16[19968]{0:T(1024)(128)(2,1)S(1)}, bf16[19968]{0:T(1024)(128)(2,1)S(1)}, u32[]{:S(2)}, u32[]{:S(2)}) collective-permute-start(bf16[19968]{0:T(1024)(128)(2,1)S(1)} %reshape.563), channel_id=1, source_target_pairs={{0,31},{1,0},{2,1},{3,2},{4,3},{5,4},{6,5},{7,6},{8,7},{9,8},{10,9... | collective-permute-start | bytes 119816 | tf_op jit(solution)/shard_map/ppermute | solution.py:24
  110.7 7.4 %collective-permute-start.10 = (bf16[19968]{0:T(1024)(128)(2,1)S(1)}, bf16[19968]{0:T(1024)(128)(2,1)S(1)}, u32[]{:S(2)}, u32[]{:S(2)}) collective-permute-start(bf16[19968]{0:T(1024)(128)(2,1)S(1)} %reshape.563), channel_id=1, source_target_pairs={{0,1},{1,2},{2,3},{3,4},{4,5},{5,6},{6,7},{7,8},{8,9},{9,10},{10,1... | collective-permute-start | bytes 119816 | tf_op jit(solution)/shard_map/ppermute | solution.py:24

commit v5 on v2

--- a/solution.py
+++ b/solution.py
@@ -124,21 +124,20 @@
     live = pair_live_mask[0, 0]
     high, middle, low = bf16_parts(distance)
     pair_data = jnp.stack(
-        [source.astype(bf16), target.astype(bf16), live.astype(bf16), high, middle, low], axis=-1
-    ).reshape(9, slots * 6)
-
-    first = jnp.transpose(band_vectors[0, 0], (1, 0, 2))
-    common = jnp.concatenate([atoms.reshape(-1), first.reshape(-1)])
+        [source.astype(bf16), target.astype(bf16), live.astype(bf16), high, middle, low], axis=1
+    ).reshape(9, 6 * slots)
+
+    common = jnp.concatenate([atoms.reshape(-1), band_vectors[0, 0].reshape(-1)])
     all_common, incoming = first_halo(common, pair_data)
     n_atoms = atom_count * feat
     ring_atoms = all_common[:, :n_atoms].reshape(9 * atom_count, feat)
     ring_first = all_common[:, n_atoms:]
 
-    incoming = incoming.reshape(9, slots, 6).astype(f32)
-    in_source = incoming[..., 0].astype(jnp.int32)
-    in_target = incoming[..., 1].astype(jnp.int32)
-    in_live = incoming[..., 2]
-    in_distance = (incoming[..., 3] + incoming[..., 4]) + incoming[..., 5]
+    incoming = incoming.reshape(9, 6, slots).astype(f32)
+    in_source = incoming[:, 0].astype(jnp.int32)
+    in_target = incoming[:, 1].astype(jnp.int32)
+    in_live = incoming[:, 2]
+    in_distance = (incoming[:, 3] + incoming[:, 4]) + incoming[:, 5]
 
     places = jnp.arange(9, dtype=jnp.int32)[:, None] * atom_count
     centre = 4 * atom_count
@@ -184,17 +183,22 @@
     dense = jnp.dot(spread, column_hot, preferred_element_type=f32).reshape(
         orb, orb * atom_count, ring
     )
-    dense_parts = jnp.concatenate(bf16_parts(dense), axis=2)
+    dense_high, dense_middle, _ = bf16_parts(dense)
+    dense_parts = jnp.concatenate([dense_high, dense_middle], axis=2)
 
     def apply(ring_vectors):
         by_orbital = jnp.swapaxes(ring_vectors.reshape(9, orb, atom_count, vec), 0, 1).reshape(
             orb, ring, vec
         )
-        tripled = jnp.concatenate([by_orbital, by_orbital, by_orbital], axis=1)
-        out = jnp.einsum("qak,qkv->qav", dense_parts, tripled, preferred_element_type=f32)
+        doubled = jnp.concatenate([by_orbital, by_orbital], axis=1)
+        out = jnp.einsum("qak,qkv->qav", dense_parts, doubled, preferred_element_type=f32)
         return out.sum(axis=0).reshape(orb, atom_count, vec)
 
+    first = jnp.transpose(band_vectors[0, 0], (1, 0, 2))
     previous = first.astype(f32)
+    ring_first = jnp.transpose(
+        ring_first.reshape(9, atom_count, orb, vec), (0, 2, 1, 3)
+    ).reshape(9, -1)
     current = apply(ring_first)
     for repeat in range(FILTER - 1):
         ring_now = halo(current.astype(bf16).reshape(-1))

time: 112 us -> 103 us (0.920)
  matrix products: 16.8 us -> 14 us
  waiting for transfers between devices: 27 us -> 24.7 us
  other arithmetic: 9.95 us -> 8.48 us
  local copies, waits for them, and re-layouts: 9.94 us -> 8.73 us
    dot_general x3, matrix products: 4.81 us -> 1.74 us  [apply(): jnp.einsum('qak,qkv->qav', dense_parts, doubled, preferred_element_type=f32)]
    ppermute x12, waiting for transfers between devices: 27 us -> 24.7 us  [shifted(): return lax.ppermute(value, axis, pairs)]
  transfers between devices with their start and end apart: 12 -> 12, of which waited for: 6 -> 5; matrix products, arithmetic and copies ran while one was open for 5% -> 5% of each run, Pallas kernels for 0% -> 0%
where the time goes in v5:
time: 103 us; the launch traced here: 102 us
  starting transfers between devices  45.3 us (44%)
  waiting for transfers between devices  24.7 us (24%)
  matrix products  14 us (14%)
  local copies, waits for them, and re-layouts  8.73 us (8%)
  other arithmetic  8.48 us (8%)
    ppermute x12, starting transfers between devices, shifted(): return lax.ppermute(value, axis, pairs)  45.3 us
    ppermute x12, waiting for transfers between devices, shifted(): return lax.ppermute(value, axis, pairs)  24.7 us
    dot_general x1, matrix products, on_device(): jnp.dot(spread, column_hot, preferred_element_type=f32)  4.87 us
    unnamed x6, other arithmetic  2.83 us
    mul x1, other arithmetic, on_device(): blocks_t[:, None, :] * row_hot[None, :, :]  2.42 us
    dot_general x1, matrix products, on_device(): picked = jnp.dot(pick, table_parts, preferred_element_type=f32)  2.24 us
  transfers between devices with their start and end apart: 12, of which 5 were waited for; matrix products, arithmetic and copies ran while one was open for 5% of the time, Pallas kernels for 0%

profile of v5, /device:TPU:32, one launch (start us, length us, event | category | flops | bytes accessed | tf_op | source)
XLA Modules:
  0.0 102.1 jit_solution(14553898363093303745)
XLA Ops:
  0.0 0.7 convert_element_type.185
  0.7 0.9 fusion.15
  1.7 0.7 fusion.60
  2.4 0.7 constant_dynamic-update-slice_fusion.5
  3.1 0.7 constant_dynamic-update-slice_fusion.4
  3.9 0.8 copy.82
  4.8 0.1 reshape_squeeze.12
  4.9 4.3 %collective-permute-start = (bf16[13056]{0:T(1024)(128)(2,1)S(1)}, bf16[13056]{0:T(1024)(128)(2,1)S(1)}, u32[]{:S(2)}, u32[]{:S(2)}) collective-permute-start(bf16[13056]{0:T(1024)(128)(2,1)S(1)} %get-tuple-element.25), channel_id=1, source_target_pairs={{0,32},{32,64},{64,96},{96,128},{128,160},{160,192},{192,224},{224... | collective-permute-start | bytes 78344 | tf_op jit(solution)/shard_map/ppermute | solution.py:24
  9.2 11.0 %collective-permute-start.1 = (bf16[13056]{0:T(1024)(128)(2,1)S(1)}, bf16[13056]{0:T(1024)(128)(2,1)S(1)}, u32[]{:S(2)}, u32[]{:S(2)}) collective-permute-start(bf16[13056]{0:T(1024)(128)(2,1)S(1)} %get-tuple-element.26), channel_id=1, source_target_pairs={{0,480},{32,0},{64,32},{96,64},{128,96},{160,128},{192,160},{224,1... | collective-permute-start | bytes 78344 | tf_op jit(solution)/shard_map/ppermute | solution.py:24
  20.2 0.7 convert_reduce_fusion
  21.0 0.7 reduce.2
  21.7 1.0 %fusion.65 = f32[16,169]{1,0:T(8,128)S(1)} fusion(bf16[16,256]{1,0:T(8,128)(2,1)S(1)} %fusion.15, bf16[256,169]{0,1:T(8,128)(2,1)} %param.29), kind=kOutput, calls=%fused_computation.144 | convolution fusion | flops 1384448 | bytes 105536 | tf_op jit(solution)/shard_map/dot_general | solution.py:170
  22.7 0.1 reshape.378
  22.8 0.2 copy.94
  23.1 0.7 reduce.4
  23.8 0.9 reshape.376
  24.9 0.2 copy.112
  25.4 0.2 pad_maximum_fusion.9
  25.7 1.9 %collective-permute-start.2 = (bf16[34560]{0:T(1024)(128)(2,1)S(1)}, bf16[34560]{0:T(1024)(128)(2,1)S(1)}, u32[]{:S(2)}, u32[]{:S(2)}) collective-permute-start(bf16[34560]{0:T(1024)(128)(2,1)S(1)} %get-tuple-element.20), channel_id=1, source_target_pairs={{0,1},{1,2},{2,3},{3,4},{4,5},{5,6},{6,7},{7,8},{8,9},{9,10},{10,1... | collective-permute-start | bytes 207368 | tf_op jit(solution)/shard_map/ppermute | solution.py:24
  27.6 5.8 %collective-permute-start.3 = (bf16[34560]{0:T(1024)(128)(2,1)S(1)}, bf16[34560]{0:T(1024)(128)(2,1)S(1)}, u32[]{:S(2)}, u32[]{:S(2)}) collective-permute-start(bf16[34560]{0:T(1024)(128)(2,1)S(1)} %get-tuple-element.21), channel_id=1, source_target_pairs={{0,31},{1,0},{2,1},{3,2},{4,3},{5,4},{6,5},{7,6},{8,7},{9,8},{10,9... | collective-permute-start | bytes 207368 | tf_op jit(solution)/shard_map/ppermute | solution.py:24
  33.4 0.2 fusion.83
  33.6 1.7 %collective-permute-done.3 = bf16[34560]{0:T(1024)(128)(2,1)S(1)} collective-permute-done((bf16[34560]{0:T(1024)(128)(2,1)S(1)}, bf16[34560]{0:T(1024)(128)(2,1)S(1)}, u32[]{:S(2)}, u32[]{:S(2)}) %collective-permute-start.3) | collective-permute-done | bytes 69152 | tf_op jit(solution)/shard_map/ppermute | solution.py:24
  35.5 0.2 pad_maximum_fusion.6
  35.8 0.1 copy.92
  35.9 0.2 reshape.374
  36.3 0.2 fusion.63
  36.5 0.2 fusion.62
  36.7 0.6 reshape.380
  37.3 0.5 copy.98
  37.9 2.2 %fusion.2 = f32[2304,768]{1,0:T(8,128)S(1)} fusion(s32[2304]{0:T(1024)S(1)} %add_add_fusion, s32[2304]{0:T(1024)S(1)} %pad_add_fusion, bf16[288,256]{1,0:T(8,128)(2,1)S(1)} %get-tuple-element.19, bf16[288,256]{1,0:T(8,128)(2,1)S(1)} %get-tuple-element.18, bf16[288,256]{1,0:T(8,128)(2,1)S(1)} %get-tuple-element.17), kind=kOutput, calls=%fused_computation.7 | convolution fusion | flops 1022533632 | bytes 7538688 | tf_op jit(solution)/shard_map/dot_general | solution.py:158
  40.1 0.9 multiply_convert_fusion
  41.1 0.5 fusion.64
  41.5 0.4 copy-done.5
  42.0 0.8 fusion
  42.8 0.1 copy-done.1
  42.9 0.3 convolution_bitcast_fusion
  43.2 0.3 convolution_bitcast_fusion.1
  43.8 2.4 %broadcast_multiply_fusion = bf16[169,16,2320]{2,1,0:T(8,128)(2,1)S(1)} fusion(bf16[16,2320]{1,0:T(8,128)(2,1)S(1)} %fusion.34, bf16[169,2320]{1,0:T(8,128)(2,1)S(1)} %pad_maximum_fusion.1), kind=kLoop, calls=%fused_computation | loop fusion | flops 6273280 | bytes 13404960 | tf_op jit(solution)/shard_map/mul | solution.py:181
  46.2 4.9 %reduce-precision_convert_fusion = (bf16[13,208,144]{1,2,0:T(8,128)(2,1)S(1)}, bf16[13,208,144]{1,2,0:T(8,128)(2,1)S(1)}) fusion(bf16[13,208,2320]{2,1,0:T(8,128)(2,1)S(1)} %bitcast.130, s32[2320]{0:T(1024)S(1)} %pad_add_fusion.2), kind=kOutput, calls=%fused_computation.9 | convolution fusion | flops 1808985600 | bytes 14113344 | tf_op jit(solution)/shard_map/dot_general | solution.py:183
  51.1 0.6 fusion.61
  51.6 0.1 copy.100
  51.8 0.1 convert_element_type.210
  51.9 4.3 %collective-permute-start.5 = (bf16[6656]{0:T(1024)(128)(2,1)S(1)}, bf16[6656]{0:T(1024)(128)(2,1)S(1)}, u32[]{:S(2)}, u32[]{:S(2)}) collective-permute-start(bf16[6656]{0:T(1024)(128)(2,1)S(1)} %convert_element_type.210), channel_id=1, source_target_pairs={{0,480},{32,0},{64,32},{96,64},{128,96},{160,128},{192,160},{224,1... | collective-permute-start | bytes 39944 | tf_op jit(solution)/shard_map/ppermute | solution.py:24
  56.2 1.9 %collective-permute-start.4 = (bf16[6656]{0:T(1024)(128)(2,1)S(1)}, bf16[6656]{0:T(1024)(128)(2,1)S(1)}, u32[]{:S(2)}, u32[]{:S(2)}) collective-permute-start(bf16[6656]{0:T(1024)(128)(2,1)S(1)} %convert_element_type.210), channel_id=1, source_target_pairs={{0,32},{32,64},{64,96},{96,128},{128,160},{160,192},{192,224},{224... | collective-permute-start | bytes 39944 | tf_op jit(solution)/shard_map/ppermute | solution.py:24
  58.3 7.2 %collective-permute-done.4 = bf16[6656]{0:T(1024)(128)(2,1)S(1)} collective-permute-done((bf16[6656]{0:T(1024)(128)(2,1)S(1)}, bf16[6656]{0:T(1024)(128)(2,1)S(1)}, u32[]{:S(2)}, u32[]{:S(2)}) %collective-permute-start.4) | collective-permute-done | bytes 13344 | tf_op jit(solution)/shard_map/ppermute | solution.py:24
  65.6 3.8 %collective-permute-start.7 = (bf16[19968]{0:T(1024)(128)(2,1)S(1)}, bf16[19968]{0:T(1024)(128)(2,1)S(1)}, u32[]{:S(2)}, u32[]{:S(2)}) collective-permute-start(bf16[19968]{0:T(1024)(128)(2,1)S(1)} %reshape.382), channel_id=1, source_target_pairs={{0,31},{1,0},{2,1},{3,2},{4,3},{5,4},{6,5},{7,6},{8,7},{9,8},{10,9... | collective-permute-start | bytes 119816 | tf_op jit(solution)/shard_map/ppermute | solution.py:24
  69.4 2.1 %collective-permute-start.6 = (bf16[19968]{0:T(1024)(128)(2,1)S(1)}, bf16[19968]{0:T(1024)(128)(2,1)S(1)}, u32[]{:S(2)}, u32[]{:S(2)}) collective-permute-start(bf16[19968]{0:T(1024)(128)(2,1)S(1)} %reshape.382), channel_id=1, source_target_pairs={{0,1},{1,2},{2,3},{3,4},{4,5},{5,6},{6,7},{7,8},{8,9},{9,10},{10,1... | collective-permute-start | bytes 119816 | tf_op jit(solution)/shard_map/ppermute | solution.py:24
  71.7 5.2 %collective-permute-done.6 = bf16[19968]{0:T(1024)(128)(2,1)S(1)} collective-permute-done((bf16[19968]{0:T(1024)(128)(2,1)S(1)}, bf16[19968]{0:T(1024)(128)(2,1)S(1)}, u32[]{:S(2)}, u32[]{:S(2)}) %collective-permute-start.6) | collective-permute-done | bytes 39968 | tf_op jit(solution)/shard_map/ppermute | solution.py:24
  76.9 0.1 pad_maximum_fusion.7
  77.1 0.3 reshape_reshape.7
  77.5 0.3 copy.104
  77.8 0.6 fusion.13
  78.3 0.1 copy.106
  78.6 2.5 %collective-permute-start.9 = (bf16[6656]{0:T(1024)(128)(2,1)S(1)}, bf16[6656]{0:T(1024)(128)(2,1)S(1)}, u32[]{:S(2)}, u32[]{:S(2)}) collective-permute-start(bf16[6656]{0:T(1024)(128)(2,1)S(1)} %reshape.384), channel_id=1, source_target_pairs={{0,480},{32,0},{64,32},{96,64},{128,96},{160,128},{192,160},{224,1... | collective-permute-start | bytes 39944 | tf_op jit(solution)/shard_map/ppermute | solution.py:24
  81.1 3.3 %collective-permute-start.8 = (bf16[6656]{0:T(1024)(128)(2,1)S(1)}, bf16[6656]{0:T(1024)(128)(2,1)S(1)}, u32[]{:S(2)}, u32[]{:S(2)}) collective-permute-start(bf16[6656]{0:T(1024)(128)(2,1)S(1)} %reshape.384), channel_id=1, source_target_pairs={{0,32},{32,64},{64,96},{96,128},{128,160},{160,192},{192,224},{224... | collective-permute-start | bytes 39944 | tf_op jit(solution)/shard_map/ppermute | solution.py:24
  84.6 5.8 %collective-permute-done.8 = bf16[6656]{0:T(1024)(128)(2,1)S(1)} collective-permute-done((bf16[6656]{0:T(1024)(128)(2,1)S(1)}, bf16[6656]{0:T(1024)(128)(2,1)S(1)}, u32[]{:S(2)}, u32[]{:S(2)}) %collective-permute-start.8) | collective-permute-done | bytes 13344 | tf_op jit(solution)/shard_map/ppermute | solution.py:24
  90.5 1.9 %collective-permute-start.11 = (bf16[19968]{0:T(1024)(128)(2,1)S(1)}, bf16[19968]{0:T(1024)(128)(2,1)S(1)}, u32[]{:S(2)}, u32[]{:S(2)}) collective-permute-start(bf16[19968]{0:T(1024)(128)(2,1)S(1)} %reshape.385), channel_id=1, source_target_pairs={{0,31},{1,0},{2,1},{3,2},{4,3},{5,4},{6,5},{7,6},{8,7},{9,8},{10,9... | collective-permute-start | bytes 119816 | tf_op jit(solution)/shard_map/ppermute | solution.py:24
  92.5 2.4 %collective-permute-start.10 = (bf16[19968]{0:T(1024)(128)(2,1)S(1)}, bf16[19968]{0:T(1024)(128)(2,1)S(1)}, u32[]{:S(2)}, u32[]{:S(2)}) collective-permute-start(bf16[19968]{0:T(1024)(128)(2,1)S(1)} %reshape.385), channel_id=1, source_target_pairs={{0,1},{1,2},{2,3},{3,4},{4,5},{5,6},{6,7},{7,8},{8,9},{9,10},{10,1... | collective-permute-start | bytes 119816 | tf_op jit(solution)/shard_map/ppermute | solution.py:24
  95.0 4.9 %collective-permute-done.10 = bf16[19968]{0:T(1024)(128)(2,1)S(1)} collective-permute-done((bf16[19968]{0:T(1024)(128)(2,1)S(1)}, bf16[19968]{0:T(1024)(128)(2,1)S(1)}, u32[]{:S(2)}, u32[]{:S(2)}) %collective-permute-start.10) | collective-permute-done | bytes 39968 | tf_op jit(solution)/shard_map/ppermute | solution.py:24
  99.9 0.1 pad_maximum_fusion.8
  100.1 0.3 reshape_reshape.8
  100.5 0.3 copy.109
  100.8 0.6 fusion.14
  101.4 0.8 copy.111
  (102 shorter events, 2.5 us)
Async XLA Ops:
  0.0 41.1 %copy-start = (bf16[256,256]{1,0:T(8,128)(2,1)S(1)}, bf16[256,256]{1,0:T(8,128)(2,1)}, u32[]{:S(2)}) copy-start(bf16[256,256]{1,0:T(8,128)(2,1)} %param.26) | copy-start | bytes 393220
  4.9 20.2 %collective-permute-start = (bf16[13056]{0:T(1024)(128)(2,1)S(1)}, bf16[13056]{0:T(1024)(128)(2,1)S(1)}, u32[]{:S(2)}, u32[]{:S(2)}) collective-permute-start(bf16[13056]{0:T(1024)(128)(2,1)S(1)} %get-tuple-element.25), channel_id=1, source_target_pairs={{0,32},{32,64},{64,96},{96,128},{128,160},{160,192},{192,224},{224... | collective-permute-start | bytes 78344 | tf_op jit(solution)/shard_map/ppermute | solution.py:24
  9.2 16.0 %collective-permute-start.1 = (bf16[13056]{0:T(1024)(128)(2,1)S(1)}, bf16[13056]{0:T(1024)(128)(2,1)S(1)}, u32[]{:S(2)}, u32[]{:S(2)}) collective-permute-start(bf16[13056]{0:T(1024)(128)(2,1)S(1)} %get-tuple-element.26), channel_id=1, source_target_pairs={{0,480},{32,0},{64,32},{96,64},{128,96},{160,128},{192,160},{224,1... | collective-permute-start | bytes 78344 | tf_op jit(solution)/shard_map/ppermute | solution.py:24
  25.2 11.2 %copy-start.3 = (bf16[256,256]{1,0:T(8,128)(2,1)S(1)}, bf16[256,256]{1,0:T(8,128)(2,1)}, u32[]{:S(2)}) copy-start(bf16[256,256]{1,0:T(8,128)(2,1)} %param.25) | copy-start | bytes 393220
  25.4 11.1 %copy-start.4 = (bf16[256,256]{1,0:T(8,128)(2,1)S(1)}, bf16[256,256]{1,0:T(8,128)(2,1)}, u32[]{:S(2)}) copy-start(bf16[256,256]{1,0:T(8,128)(2,1)} %param.24) | copy-start | bytes 393220
  25.7 7.9 %collective-permute-start.2 = (bf16[34560]{0:T(1024)(128)(2,1)S(1)}, bf16[34560]{0:T(1024)(128)(2,1)S(1)}, u32[]{:S(2)}, u32[]{:S(2)}) collective-permute-start(bf16[34560]{0:T(1024)(128)(2,1)S(1)} %get-tuple-element.20), channel_id=1, source_target_pairs={{0,1},{1,2},{2,3},{3,4},{4,5},{5,6},{6,7},{7,8},{8,9},{9,10},{10,1... | collective-permute-start | bytes 207368 | tf_op jit(solution)/shard_map/ppermute | solution.py:24
  27.6 7.7 %collective-permute-start.3 = (bf16[34560]{0:T(1024)(128)(2,1)S(1)}, bf16[34560]{0:T(1024)(128)(2,1)S(1)}, u32[]{:S(2)}, u32[]{:S(2)}) collective-permute-start(bf16[34560]{0:T(1024)(128)(2,1)S(1)} %get-tuple-element.21), channel_id=1, source_target_pairs={{0,31},{1,0},{2,1},{3,2},{4,3},{5,4},{6,5},{7,6},{8,7},{9,8},{10,9... | collective-permute-start | bytes 207368 | tf_op jit(solution)/shard_map/ppermute | solution.py:24
  37.8 2.3 %copy-start.6 = (bf16[16,256]{1,0:T(8,128)(2,1)S(1)}, bf16[16,256]{1,0:T(8,128)(2,1)}, u32[]{:S(2)}) copy-start(bf16[16,256]{1,0:T(8,128)(2,1)} %param.23) | copy-start | bytes 24580
  41.1 0.9 copy-start.5
  42.0 0.9 copy-start.1
  51.9 6.4 %collective-permute-start.5 = (bf16[6656]{0:T(1024)(128)(2,1)S(1)}, bf16[6656]{0:T(1024)(128)(2,1)S(1)}, u32[]{:S(2)}, u32[]{:S(2)}) collective-permute-start(bf16[6656]{0:T(1024)(128)(2,1)S(1)} %convert_element_type.210), channel_id=1, source_target_pairs={{0,480},{32,0},{64,32},{96,64},{128,96},{160,128},{192,160},{224,1... | collective-permute-start | bytes 39944 | tf_op jit(solution)/shard_map/ppermute | solution.py:24
  56.2 9.2 %collective-permute-start.4 = (bf16[6656]{0:T(1024)(128)(2,1)S(1)}, bf16[6656]{0:T(1024)(128)(2,1)S(1)}, u32[]{:S(2)}, u32[]{:S(2)}) collective-permute-start(bf16[6656]{0:T(1024)(128)(2,1)S(1)} %convert_element_type.210), channel_id=1, source_target_pairs={{0,32},{32,64},{64,96},{96,128},{128,160},{160,192},{192,224},{224... | collective-permute-start | bytes 39944 | tf_op jit(solution)/shard_map/ppermute | solution.py:24
  65.6 6.0 %collective-permute-start.7 = (bf16[19968]{0:T(1024)(128)(2,1)S(1)}, bf16[19968]{0:T(1024)(128)(2,1)S(1)}, u32[]{:S(2)}, u32[]{:S(2)}) collective-permute-start(bf16[19968]{0:T(1024)(128)(2,1)S(1)} %reshape.382), channel_id=1, source_target_pairs={{0,31},{1,0},{2,1},{3,2},{4,3},{5,4},{6,5},{7,6},{8,7},{9,8},{10,9... | collective-permute-start | bytes 119816 | tf_op jit(solution)/shard_map/ppermute | solution.py:24
  69.4 7.4 %collective-permute-start.6 = (bf16[19968]{0:T(1024)(128)(2,1)S(1)}, bf16[19968]{0:T(1024)(128)(2,1)S(1)}, u32[]{:S(2)}, u32[]{:S(2)}) collective-permute-start(bf16[19968]{0:T(1024)(128)(2,1)S(1)} %reshape.382), channel_id=1, source_target_pairs={{0,1},{1,2},{2,3},{3,4},{4,5},{5,6},{6,7},{7,8},{8,9},{9,10},{10,1... | collective-permute-start | bytes 119816 | tf_op jit(solution)/shard_map/ppermute | solution.py:24
  77.4 1.0 copy-start.2
  78.6 6.0 %collective-permute-start.9 = (bf16[6656]{0:T(1024)(128)(2,1)S(1)}, bf16[6656]{0:T(1024)(128)(2,1)S(1)}, u32[]{:S(2)}, u32[]{:S(2)}) collective-permute-start(bf16[6656]{0:T(1024)(128)(2,1)S(1)} %reshape.384), channel_id=1, source_target_pairs={{0,480},{32,0},{64,32},{96,64},{128,96},{160,128},{192,160},{224,1... | collective-permute-start | bytes 39944 | tf_op jit(solution)/shard_map/ppermute | solution.py:24
  81.1 9.2 %collective-permute-start.8 = (bf16[6656]{0:T(1024)(128)(2,1)S(1)}, bf16[6656]{0:T(1024)(128)(2,1)S(1)}, u32[]{:S(2)}, u32[]{:S(2)}) collective-permute-start(bf16[6656]{0:T(1024)(128)(2,1)S(1)} %reshape.384), channel_id=1, source_target_pairs={{0,32},{32,64},{64,96},{96,128},{128,160},{160,192},{192,224},{224... | collective-permute-start | bytes 39944 | tf_op jit(solution)/shard_map/ppermute | solution.py:24
  90.5 4.5 %collective-permute-start.11 = (bf16[19968]{0:T(1024)(128)(2,1)S(1)}, bf16[19968]{0:T(1024)(128)(2,1)S(1)}, u32[]{:S(2)}, u32[]{:S(2)}) collective-permute-start(bf16[19968]{0:T(1024)(128)(2,1)S(1)} %reshape.385), channel_id=1, source_target_pairs={{0,31},{1,0},{2,1},{3,2},{4,3},{5,4},{6,5},{7,6},{8,7},{9,8},{10,9... | collective-permute-start | bytes 119816 | tf_op jit(solution)/shard_map/ppermute | solution.py:24
  92.5 7.4 %collective-permute-start.10 = (bf16[19968]{0:T(1024)(128)(2,1)S(1)}, bf16[19968]{0:T(1024)(128)(2,1)S(1)}, u32[]{:S(2)}, u32[]{:S(2)}) collective-permute-start(bf16[19968]{0:T(1024)(128)(2,1)S(1)} %reshape.385), channel_id=1, source_target_pairs={{0,1},{1,2},{2,3},{3,4},{4,5},{5,6},{6,7},{7,8},{8,9},{9,10},{10,1... | collective-permute-start | bytes 119816 | tf_op jit(solution)/shard_map/ppermute | solution.py:24

commit v6 on v5

--- a/solution.py
+++ b/solution.py
@@ -73,7 +73,7 @@
         ],
         axis=1,
     ).reshape(9, m)
-    return all_common, incoming
+    return strip_common, strip_pairs[:, 1], all_common, incoming
 
 
 def pair_mixed(before_rows, distance, live_flags, radial_weight, mixing_weight, gate_weight):
@@ -128,54 +128,96 @@
     ).reshape(9, 6 * slots)
 
     common = jnp.concatenate([atoms.reshape(-1), band_vectors[0, 0].reshape(-1)])
-    all_common, incoming = first_halo(common, pair_data)
+    strip_common, strip_incoming, all_common, incoming = first_halo(common, pair_data)
     n_atoms = atom_count * feat
     ring_atoms = all_common[:, :n_atoms].reshape(9 * atom_count, feat)
     ring_first = all_common[:, n_atoms:]
-
-    incoming = incoming.reshape(9, 6, slots).astype(f32)
-    in_source = incoming[:, 0].astype(jnp.int32)
-    in_target = incoming[:, 1].astype(jnp.int32)
-    in_live = incoming[:, 2]
-    in_distance = (incoming[:, 3] + incoming[:, 4]) + incoming[:, 5]
-
-    places = jnp.arange(9, dtype=jnp.int32)[:, None] * atom_count
-    centre = 4 * atom_count
-    row_source = jnp.concatenate([(centre + source).reshape(-1), (places + in_source).reshape(-1)])
-    row_target = jnp.concatenate([(places + target).reshape(-1), (centre + in_target).reshape(-1)])
-    all_distance = jnp.concatenate([distance.reshape(-1), in_distance.reshape(-1)])
-    all_live = jnp.concatenate([live.reshape(-1).astype(f32), in_live.reshape(-1)])
-
-    source_projection = jnp.dot(ring_atoms, w_source, preferred_element_type=f32)
-    target_projection = jnp.dot(ring_atoms, w_target, preferred_element_type=f32)
-    table = jnp.concatenate([source_projection, target_projection])
-    table_parts = jnp.concatenate(bf16_parts(table), axis=1)
+    strip_atoms = strip_common[:, :n_atoms].reshape(3 * atom_count, feat)
+
+    def unpack(received):
+        received = received.reshape(-1, 6, slots).astype(f32)
+        got_distance = (received[:, 3] + received[:, 4]) + received[:, 5]
+        return (
+            received[:, 0].astype(jnp.int32),
+            received[:, 1].astype(jnp.int32),
+            received[:, 2],
+            got_distance,
+        )
+
+    def rest(values):
+        return jnp.concatenate([values[0::3], values[2::3]])
+
     ring = 9 * atom_count
-    columns = jnp.arange(2 * ring, dtype=jnp.int32)[None, :]
-    pick = (
-        (columns == row_source[:, None]) | (columns == (row_target[:, None] + ring))
-    ).astype(bf16)
-    picked = jnp.dot(pick, table_parts, preferred_element_type=f32)
-    before_rows = (picked[:, :feat] + picked[:, feat : 2 * feat]) + picked[:, 2 * feat :]
-
-    mixed, scale = pair_mixed(
-        before_rows, all_distance, all_live, radial_weight, mixing_weight, gate_weight
-    )
     weight_blocks = output_weight.reshape(feat, orb, orb)
     own_weight = jnp.swapaxes(weight_blocks, 1, 2).reshape(feat, orb * orb)
-    own_raw = jnp.einsum("fb,sf->bs", own_weight, mixed[: 9 * slots], preferred_element_type=f32)
-    in_raw = jnp.einsum("fb,sf->bs", output_weight, mixed[9 * slots :], preferred_element_type=f32)
-    blocks_t = (jnp.concatenate([own_raw, in_raw], axis=1) * scale[None, :]).astype(bf16)
+
+    def group_blocks(table_atoms, own_index, in_index, own_sets, in_sets):
+        own_source, own_target, own_live, own_distance = own_sets
+        in_source, in_target, in_live, in_distance = in_sets
+        width = table_atoms.shape[0]
+        centre_index = atom_count * (width // (2 * atom_count))
+        row_source = jnp.concatenate(
+            [(centre_index + own_source).reshape(-1), (in_index + in_source).reshape(-1)]
+        )
+        row_target = jnp.concatenate(
+            [(own_index + own_target).reshape(-1), (centre_index + in_target).reshape(-1)]
+        )
+        group_distance = jnp.concatenate([own_distance.reshape(-1), in_distance.reshape(-1)])
+        group_live = jnp.concatenate([own_live.reshape(-1), in_live.reshape(-1)])
+        source_projection = jnp.dot(table_atoms, w_source, preferred_element_type=f32)
+        target_projection = jnp.dot(table_atoms, w_target, preferred_element_type=f32)
+        table = jnp.concatenate([source_projection, target_projection])
+        table_parts = jnp.concatenate(bf16_parts(table), axis=1)
+        columns = jnp.arange(2 * width, dtype=jnp.int32)[None, :]
+        pick = (
+            (columns == row_source[:, None]) | (columns == (row_target[:, None] + width))
+        ).astype(bf16)
+        picked = jnp.dot(pick, table_parts, preferred_element_type=f32)
+        before_rows = (picked[:, :feat] + picked[:, feat : 2 * feat]) + picked[:, 2 * feat :]
+        mixed, scale = pair_mixed(
+            before_rows, group_distance, group_live, radial_weight, mixing_weight, gate_weight
+        )
+        own_count = own_source.size
+        own_raw = jnp.einsum("fb,sf->bs", own_weight, mixed[:own_count], preferred_element_type=f32)
+        in_raw = jnp.einsum("fb,sf->bs", output_weight, mixed[own_count:], preferred_element_type=f32)
+        return (jnp.concatenate([own_raw, in_raw], axis=1) * scale[None, :]).astype(bf16)
+
+    live_f = live.astype(f32)
+    strip_sets = (source[1::3], target[1::3], live_f[1::3], distance[1::3])
+    strip_in = unpack(strip_incoming)
+    three = jnp.arange(3, dtype=jnp.int32)[:, None] * atom_count
+    strip_blocks = group_blocks(strip_atoms, three, three, strip_sets, strip_in)
+
+    rest_sets = (rest(source), rest(target), rest(live_f), rest(distance))
+    rest_in = unpack(rest(incoming))
+    rest_places = rest(jnp.arange(9, dtype=jnp.int32))[:, None] * atom_count
+    rest_blocks = group_blocks(ring_atoms, rest_places, rest_places, rest_sets, rest_in)
 
     square = jnp.dot(atoms, w_site, preferred_element_type=f32).reshape(-1, orb, orb)
     onsite = (onsite_scale * 0.5 * (square + jnp.swapaxes(square, 1, 2))).astype(bf16)
     onsite_t = jnp.transpose(onsite, (2, 1, 0)).reshape(orb * orb, atom_count)
-    blocks_t = jnp.concatenate([blocks_t, onsite_t], axis=1)
+    blocks_t = jnp.concatenate([strip_blocks, rest_blocks, onsite_t], axis=1)
 
     own_atoms = jnp.arange(atom_count, dtype=jnp.int32)
-    row_atom = jnp.concatenate([source.reshape(-1), in_target.reshape(-1), own_atoms])
+    strip_places = jnp.array([1, 4, 7], jnp.int32)[:, None] * atom_count
+    centre = 4 * atom_count
+    row_atom = jnp.concatenate(
+        [
+            strip_sets[0].reshape(-1),
+            strip_in[1].reshape(-1),
+            rest_sets[0].reshape(-1),
+            rest_in[1].reshape(-1),
+            own_atoms,
+        ]
+    )
     column_atom = jnp.concatenate(
-        [(places + target).reshape(-1), (places + in_source).reshape(-1), centre + own_atoms]
+        [
+            (strip_places + strip_sets[1]).reshape(-1),
+            (strip_places + strip_in[0]).reshape(-1),
+            (rest_places + rest_sets[1]).reshape(-1),
+            (rest_places + rest_in[0]).reshape(-1),
+            centre + own_atoms,
+        ]
     )
     row_hot = (own_atoms[:, None] == row_atom[None, :]).astype(bf16)
     spread = (blocks_t[:, None, :] * row_hot[None, :, :]).reshape(orb * orb * atom_count, -1)

time: 103 us -> 103 us (level)
  local copies, waits for them, and re-layouts: 8.73 us -> 11.8 us
  waiting for transfers between devices: 24.7 us -> 23 us
  starting transfers between devices: 45.3 us -> 43.7 us
  matrix products: 14 us -> 15.2 us
    unnamed x17 -> x33, local copies, waits for them, and re-layouts: 1.42 us -> 3.74 us
    ppermute x12, waiting for transfers between devices: 24.7 us -> 23 us  [shifted(): return lax.ppermute(value, axis, pairs)]
    ppermute x12, starting transfers between devices: 45.3 us -> 43.7 us  [shifted(): return lax.ppermute(value, axis, pairs)]
    dot_general x5 -> x10, matrix products: 3.28 us -> 3.83 us  [the longest x2 2.14 us: group_blocks(): picked = jnp.dot(pick, table_parts, preferred_element_type=f32)]
    unnamed x6 -> x9, other arithmetic: 2.83 us -> 2.29 us
  transfers between devices with their start and end apart: 12 -> 12, of which waited for: 5 -> 4; matrix products, arithmetic and copies ran while one was open for 5% -> 8% of each run, Pallas kernels for 0% -> 0%
where the time goes in v6:
time: 103 us; the launch traced here: 102 us
  starting transfers between devices  43.7 us (42%)
  waiting for transfers between devices  23 us (22%)
  matrix products  15.2 us (15%)
  local copies, waits for them, and re-layouts  11.8 us (11%)
  other arithmetic  7.57 us (7%)
    ppermute x12, starting transfers between devices, shifted(): return lax.ppermute(value, axis, pairs)  43.7 us
    ppermute x12, waiting for transfers between devices, shifted(): return lax.ppermute(value, axis, pairs)  23 us
    dot_general x1, matrix products, on_device(): jnp.dot(spread, column_hot, preferred_element_type=f32)  4.87 us
    unnamed x33, local copies, waits for them, and re-layouts  3.74 us
    mul x1, other arithmetic, on_device(): blocks_t[:, None, :] * row_hot[None, :, :]  2.42 us
    unnamed x9, other arithmetic  2.29 us
    dot_general x2, matrix products, group_blocks(): picked = jnp.dot(pick, table_parts, preferred_element_type=f32)  2.14 us
  transfers between devices with their start and end apart: 12, of which 4 were waited for; matrix products, arithmetic and copies ran while one was open for 8% of the time, Pallas kernels for 0%

profile of v6, /device:TPU:32, one launch (start us, length us, event | category | flops | bytes accessed | tf_op | source)
XLA Modules:
  0.0 102.3 jit_solution(5180198971389569249)
XLA Ops:
  0.0 1.0 fusion.15
  1.0 0.8 fusion.85
  1.8 0.7 fusion.84
  2.5 0.7 constant_dynamic-update-slice_fusion.5
  3.2 0.7 constant_dynamic-update-slice_fusion.4
  4.0 0.8 copy.83
  5.0 4.3 %collective-permute-start = (bf16[13056]{0:T(1024)(128)(2,1)S(1)}, bf16[13056]{0:T(1024)(128)(2,1)S(1)}, u32[]{:S(2)}, u32[]{:S(2)}) collective-permute-start(bf16[13056]{0:T(1024)(128)(2,1)S(1)} %get-tuple-element.34), channel_id=1, source_target_pairs={{0,32},{32,64},{64,96},{96,128},{128,160},{160,192},{192,224},{224... | collective-permute-start | bytes 78344 | tf_op jit(solution)/shard_map/ppermute | solution.py:24
  9.3 11.0 %collective-permute-start.1 = (bf16[13056]{0:T(1024)(128)(2,1)S(1)}, bf16[13056]{0:T(1024)(128)(2,1)S(1)}, u32[]{:S(2)}, u32[]{:S(2)}) collective-permute-start(bf16[13056]{0:T(1024)(128)(2,1)S(1)} %get-tuple-element.35), channel_id=1, source_target_pairs={{0,480},{32,0},{64,32},{96,64},{128,96},{160,128},{192,160},{224,1... | collective-permute-start | bytes 78344 | tf_op jit(solution)/shard_map/ppermute | solution.py:24
  20.4 0.7 copy.158
  21.0 0.7 copy.157
  22.1 1.0 fusion.93
  23.2 0.2 copy.95
  23.5 0.7 constant_dynamic-update-slice_fusion.7
  24.5 0.9 reshape.494
  25.5 0.2 copy.113
  26.1 0.2 pad_maximum_fusion.10
  26.3 0.2 fusion.122
  26.8 0.2 fusion.87
  27.0 1.9 %collective-permute-start.2 = (bf16[34560]{0:T(1024)(128)(2,1)S(1)}, bf16[34560]{0:T(1024)(128)(2,1)S(1)}, u32[]{:S(2)}, u32[]{:S(2)}) collective-permute-start(bf16[34560]{0:T(1024)(128)(2,1)S(1)} %get-tuple-element.29), channel_id=1, source_target_pairs={{0,1},{1,2},{2,3},{3,4},{4,5},{5,6},{6,7},{7,8},{8,9},{9,10},{10,1... | collective-permute-start | bytes 207368 | tf_op jit(solution)/shard_map/ppermute | solution.py:24
  28.9 5.8 %collective-permute-start.3 = (bf16[34560]{0:T(1024)(128)(2,1)S(1)}, bf16[34560]{0:T(1024)(128)(2,1)S(1)}, u32[]{:S(2)}, u32[]{:S(2)}) collective-permute-start(bf16[34560]{0:T(1024)(128)(2,1)S(1)} %get-tuple-element.30), channel_id=1, source_target_pairs={{0,31},{1,0},{2,1},{3,2},{4,3},{5,4},{6,5},{7,6},{8,7},{9,8},{10,9... | collective-permute-start | bytes 207368 | tf_op jit(solution)/shard_map/ppermute | solution.py:24
  34.8 0.6 fusion.27
  35.4 0.5 multiply_convert_fusion.1
  35.9 0.3 fusion.89
  36.3 0.3 fusion.9
  36.7 0.5 copy-done.2
  37.2 0.2 convolution_bitcast_fusion.2
  37.5 0.2 convolution_bitcast_fusion.3
  38.2 0.2 pad_maximum_fusion.6
  38.6 0.2 reshape.498
  38.8 0.2 fusion.91
  39.0 0.2 fusion.90
  39.4 1.6 %fusion.2 = f32[1536,768]{1,0:T(8,128)S(1)} fusion(s32[1536]{0:T(1024)S(1)} %add_add_fusion, s32[1536]{0:T(1024)S(1)} %pad_add_fusion, bf16[288,256]{1,0:T(8,128)(2,1)S(1)} %get-tuple-element.25, bf16[288,256]{1,0:T(8,128)(2,1)S(1)} %get-tuple-element.24, bf16[288,256]{1,0:T(8,128)(2,1)S(1)} %get-tuple-element.23), kind=kOutput, calls=%fused_computation.9 | convolution fusion | flops 682131456 | bytes 5173248 | tf_op jit(solution)/shard_map/dot_general | solution.py:175
  40.9 0.8 multiply_convert_fusion
  41.7 0.4 fusion.92
  42.1 0.6 fusion
  42.6 0.3 convolution_bitcast_fusion.1
  42.9 0.3 convolution_bitcast_fusion
  43.3 0.3 slice-done
  43.6 0.6 reshape.505
  44.1 0.5 copy.99
  44.8 2.4 %broadcast_multiply_fusion = bf16[169,16,2320]{2,1,0:T(8,128)(2,1)S(1)} fusion(bf16[16,2320]{1,0:T(8,128)(2,1)S(1)} %fusion.43, bf16[169,2320]{1,0:T(8,128)(2,1)S(1)} %pad_maximum_fusion.1), kind=kLoop, calls=%fused_computation | loop fusion | flops 6273280 | bytes 13404960 | tf_op jit(solution)/shard_map/mul | solution.py:223
  47.2 4.9 %reduce-precision_convert_fusion = (bf16[13,208,144]{1,2,0:T(8,128)(2,1)S(1)}, bf16[13,208,144]{1,2,0:T(8,128)(2,1)S(1)}) fusion(bf16[13,208,2320]{2,1,0:T(8,128)(2,1)S(1)} %bitcast.192, s32[2320]{0:T(1024)S(1)} %constant_dynamic-update-slice_fusion.9), kind=kOutput, calls=%fused_computation.4 | convolution fusion | flops 1808985600 | bytes 14113344 | tf_op jit(solution)/shard_map/dot_general | solution.py:225
  52.1 0.6 fusion.86
  52.7 0.3 copy-done.11
  53.0 0.3 copy-done.9
  53.6 4.1 %collective-permute-start.5 = (bf16[6656]{0:T(1024)(128)(2,1)S(1)}, bf16[6656]{0:T(1024)(128)(2,1)S(1)}, u32[]{:S(2)}, u32[]{:S(2)}) collective-permute-start(bf16[6656]{0:T(1024)(128)(2,1)S(1)} %convert_element_type.267), channel_id=1, source_target_pairs={{0,480},{32,0},{64,32},{96,64},{128,96},{160,128},{192,160},{224,1... | collective-permute-start | bytes 39944 | tf_op jit(solution)/shard_map/ppermute | solution.py:24
  57.6 1.9 %collective-permute-start.4 = (bf16[6656]{0:T(1024)(128)(2,1)S(1)}, bf16[6656]{0:T(1024)(128)(2,1)S(1)}, u32[]{:S(2)}, u32[]{:S(2)}) collective-permute-start(bf16[6656]{0:T(1024)(128)(2,1)S(1)} %convert_element_type.267), channel_id=1, source_target_pairs={{0,32},{32,64},{64,96},{96,128},{128,160},{160,192},{192,224},{224... | collective-permute-start | bytes 39944 | tf_op jit(solution)/shard_map/ppermute | solution.py:24
  59.7 7.2 %collective-permute-done.4 = bf16[6656]{0:T(1024)(128)(2,1)S(1)} collective-permute-done((bf16[6656]{0:T(1024)(128)(2,1)S(1)}, bf16[6656]{0:T(1024)(128)(2,1)S(1)}, u32[]{:S(2)}, u32[]{:S(2)}) %collective-permute-start.4) | collective-permute-done | bytes 13344 | tf_op jit(solution)/shard_map/ppermute | solution.py:24
  67.0 2.5 %collective-permute-start.7 = (bf16[19968]{0:T(1024)(128)(2,1)S(1)}, bf16[19968]{0:T(1024)(128)(2,1)S(1)}, u32[]{:S(2)}, u32[]{:S(2)}) collective-permute-start(bf16[19968]{0:T(1024)(128)(2,1)S(1)} %reshape.507), channel_id=1, source_target_pairs={{0,31},{1,0},{2,1},{3,2},{4,3},{5,4},{6,5},{7,6},{8,7},{9,8},{10,9... | collective-permute-start | bytes 119816 | tf_op jit(solution)/shard_map/ppermute | solution.py:24
  69.5 2.1 %collective-permute-start.6 = (bf16[19968]{0:T(1024)(128)(2,1)S(1)}, bf16[19968]{0:T(1024)(128)(2,1)S(1)}, u32[]{:S(2)}, u32[]{:S(2)}) collective-permute-start(bf16[19968]{0:T(1024)(128)(2,1)S(1)} %reshape.507), channel_id=1, source_target_pairs={{0,1},{1,2},{2,3},{3,4},{4,5},{5,6},{6,7},{7,8},{8,9},{9,10},{10,1... | collective-permute-start | bytes 119816 | tf_op jit(solution)/shard_map/ppermute | solution.py:24
  71.8 5.2 %collective-permute-done.6 = bf16[19968]{0:T(1024)(128)(2,1)S(1)} collective-permute-done((bf16[19968]{0:T(1024)(128)(2,1)S(1)}, bf16[19968]{0:T(1024)(128)(2,1)S(1)}, u32[]{:S(2)}, u32[]{:S(2)}) %collective-permute-start.6) | collective-permute-done | bytes 39968 | tf_op jit(solution)/shard_map/ppermute | solution.py:24
  77.2 0.3 reshape_reshape.6
  77.5 0.3 copy.105
  77.9 0.6 fusion.13
  78.8 2.5 %collective-permute-start.9 = (bf16[6656]{0:T(1024)(128)(2,1)S(1)}, bf16[6656]{0:T(1024)(128)(2,1)S(1)}, u32[]{:S(2)}, u32[]{:S(2)}) collective-permute-start(bf16[6656]{0:T(1024)(128)(2,1)S(1)} %reshape.509), channel_id=1, source_target_pairs={{0,480},{32,0},{64,32},{96,64},{128,96},{160,128},{192,160},{224,1... | collective-permute-start | bytes 39944 | tf_op jit(solution)/shard_map/ppermute | solution.py:24
  81.3 3.3 %collective-permute-start.8 = (bf16[6656]{0:T(1024)(128)(2,1)S(1)}, bf16[6656]{0:T(1024)(128)(2,1)S(1)}, u32[]{:S(2)}, u32[]{:S(2)}) collective-permute-start(bf16[6656]{0:T(1024)(128)(2,1)S(1)} %reshape.509), channel_id=1, source_target_pairs={{0,32},{32,64},{64,96},{96,128},{128,160},{160,192},{192,224},{224... | collective-permute-start | bytes 39944 | tf_op jit(solution)/shard_map/ppermute | solution.py:24
  84.8 5.8 %collective-permute-done.8 = bf16[6656]{0:T(1024)(128)(2,1)S(1)} collective-permute-done((bf16[6656]{0:T(1024)(128)(2,1)S(1)}, bf16[6656]{0:T(1024)(128)(2,1)S(1)}, u32[]{:S(2)}, u32[]{:S(2)}) %collective-permute-start.8) | collective-permute-done | bytes 13344 | tf_op jit(solution)/shard_map/ppermute | solution.py:24
  90.7 1.9 %collective-permute-start.11 = (bf16[19968]{0:T(1024)(128)(2,1)S(1)}, bf16[19968]{0:T(1024)(128)(2,1)S(1)}, u32[]{:S(2)}, u32[]{:S(2)}) collective-permute-start(bf16[19968]{0:T(1024)(128)(2,1)S(1)} %reshape.510), channel_id=1, source_target_pairs={{0,31},{1,0},{2,1},{3,2},{4,3},{5,4},{6,5},{7,6},{8,7},{9,8},{10,9... | collective-permute-start | bytes 119816 | tf_op jit(solution)/shard_map/ppermute | solution.py:24
  92.7 2.4 %collective-permute-start.10 = (bf16[19968]{0:T(1024)(128)(2,1)S(1)}, bf16[19968]{0:T(1024)(128)(2,1)S(1)}, u32[]{:S(2)}, u32[]{:S(2)}) collective-permute-start(bf16[19968]{0:T(1024)(128)(2,1)S(1)} %reshape.510), channel_id=1, source_target_pairs={{0,1},{1,2},{2,3},{3,4},{4,5},{5,6},{6,7},{7,8},{8,9},{9,10},{10,1... | collective-permute-start | bytes 119816 | tf_op jit(solution)/shard_map/ppermute | solution.py:24
  95.2 4.9 %collective-permute-done.10 = bf16[19968]{0:T(1024)(128)(2,1)S(1)} collective-permute-done((bf16[19968]{0:T(1024)(128)(2,1)S(1)}, bf16[19968]{0:T(1024)(128)(2,1)S(1)}, u32[]{:S(2)}, u32[]{:S(2)}) %collective-permute-start.10) | collective-permute-done | bytes 39968 | tf_op jit(solution)/shard_map/ppermute | solution.py:24
  100.3 0.3 reshape_reshape.7
  100.7 0.3 copy.110
  101.0 0.6 fusion.14
  101.6 0.8 copy.112
  (162 shorter events, 4.8 us)
Async XLA Ops:
  0.0 35.9 %copy-start = (bf16[256,256]{1,0:T(8,128)(2,1)S(1)}, bf16[256,256]{1,0:T(8,128)(2,1)}, u32[]{:S(2)}) copy-start(bf16[256,256]{1,0:T(8,128)(2,1)} %param.27) | copy-start | bytes 393220
  0.0 26.6 %copy-start.3 = (bf16[256,256]{1,0:T(8,128)(2,1)S(1)}, bf16[256,256]{1,0:T(8,128)(2,1)}, u32[]{:S(2)}) copy-start(bf16[256,256]{1,0:T(8,128)(2,1)} %param.26) | copy-start | bytes 393220
  1.0 25.8 %copy-start.4 = (bf16[256,256]{1,0:T(8,128)(2,1)S(1)}, bf16[256,256]{1,0:T(8,128)(2,1)}, u32[]{:S(2)}) copy-start(bf16[256,256]{1,0:T(8,128)(2,1)} %param.25) | copy-start | bytes 393220
  5.0 29.7 %copy-start.6 = (s32[3]{0:T(128)S(1)}, s32[3]{0:T(128)}, u32[]{:S(2)}) copy-start(s32[3]{0:T(128)} %constant.53) | copy-start | bytes 40
  5.0 20.8 %collective-permute-start = (bf16[13056]{0:T(1024)(128)(2,1)S(1)}, bf16[13056]{0:T(1024)(128)(2,1)S(1)}, u32[]{:S(2)}, u32[]{:S(2)}) collective-permute-start(bf16[13056]{0:T(1024)(128)(2,1)S(1)} %get-tuple-element.34), channel_id=1, source_target_pairs={{0,32},{32,64},{64,96},{96,128},{128,160},{160,192},{192,224},{224... | collective-permute-start | bytes 78344 | tf_op jit(solution)/shard_map/ppermute | solution.py:24
  9.3 16.5 %collective-permute-start.1 = (bf16[13056]{0:T(1024)(128)(2,1)S(1)}, bf16[13056]{0:T(1024)(128)(2,1)S(1)}, u32[]{:S(2)}, u32[]{:S(2)}) collective-permute-start(bf16[13056]{0:T(1024)(128)(2,1)S(1)} %get-tuple-element.35), channel_id=1, source_target_pairs={{0,480},{32,0},{64,32},{96,64},{128,96},{160,128},{192,160},{224,1... | collective-permute-start | bytes 78344 | tf_op jit(solution)/shard_map/ppermute | solution.py:24
  26.5 9.0 %copy-start.8 = (bf16[16,256]{1,0:T(8,128)(2,1)S(1)}, bf16[16,256]{1,0:T(8,128)(2,1)}, u32[]{:S(2)}) copy-start(bf16[16,256]{1,0:T(8,128)(2,1)} %param.24) | copy-start | bytes 24580
  27.0 10.8 %collective-permute-start.2 = (bf16[34560]{0:T(1024)(128)(2,1)S(1)}, bf16[34560]{0:T(1024)(128)(2,1)S(1)}, u32[]{:S(2)}, u32[]{:S(2)}) collective-permute-start(bf16[34560]{0:T(1024)(128)(2,1)S(1)} %get-tuple-element.29), channel_id=1, source_target_pairs={{0,1},{1,2},{2,3},{3,4},{4,5},{5,6},{6,7},{7,8},{8,9},{9,10},{10,1... | collective-permute-start | bytes 207368 | tf_op jit(solution)/shard_map/ppermute | solution.py:24
  28.9 9.0 %collective-permute-start.3 = (bf16[34560]{0:T(1024)(128)(2,1)S(1)}, bf16[34560]{0:T(1024)(128)(2,1)S(1)}, u32[]{:S(2)}, u32[]{:S(2)}) collective-permute-start(bf16[34560]{0:T(1024)(128)(2,1)S(1)} %get-tuple-element.30), channel_id=1, source_target_pairs={{0,31},{1,0},{2,1},{3,2},{4,3},{5,4},{6,5},{7,6},{8,7},{9,8},{10,9... | collective-permute-start | bytes 207368 | tf_op jit(solution)/shard_map/ppermute | solution.py:24
  35.4 0.9 copy-start.7
  36.3 0.9 copy-start.2
  38.7 2.2 %copy-start.1 = (bf16[9,10752]{1,0:T(8,128)(2,1)}, bf16[9,10752]{1,0:T(8,128)(2,1)S(1)}, u32[]{:S(2)}) copy-start(bf16[9,10752]{1,0:T(8,128)(2,1)S(1)} %reshape.498) | copy-start | bytes 580612
  42.6 0.9 slice-start
  52.1 0.9 copy-start.11
  52.1 1.3 %copy-start.9 = (bf16[13,208,144]{1,2,0:T(8,128)(2,1)}, bf16[13,208,144]{1,2,0:T(8,128)(2,1)S(1)}, u32[]{:S(2)}) copy-start(bf16[13,208,144]{1,2,0:T(8,128)(2,1)S(1)} %get-tuple-element.21) | copy-start | bytes 2336260
  53.4 24.5 %copy-start.12 = (bf16[13,208,144]{1,2,0:T(8,128)(2,1)S(1)}, bf16[13,208,144]{1,2,0:T(8,128)(2,1)}, u32[]{:S(2)}) copy-start(bf16[13,208,144]{1,2,0:T(8,128)(2,1)} %copy-done.11) | copy-start | bytes 2336260
  53.5 24.4 %copy-start.10 = (bf16[13,208,144]{1,2,0:T(8,128)(2,1)S(1)}, bf16[13,208,144]{1,2,0:T(8,128)(2,1)}, u32[]{:S(2)}) copy-start(bf16[13,208,144]{1,2,0:T(8,128)(2,1)} %copy-done.9) | copy-start | bytes 2336260
  53.6 6.1 %collective-permute-start.5 = (bf16[6656]{0:T(1024)(128)(2,1)S(1)}, bf16[6656]{0:T(1024)(128)(2,1)S(1)}, u32[]{:S(2)}, u32[]{:S(2)}) collective-permute-start(bf16[6656]{0:T(1024)(128)(2,1)S(1)} %convert_element_type.267), channel_id=1, source_target_pairs={{0,480},{32,0},{64,32},{96,64},{128,96},{160,128},{192,160},{224,1... | collective-permute-start | bytes 39944 | tf_op jit(solution)/shard_map/ppermute | solution.py:24
  57.6 9.2 %collective-permute-start.4 = (bf16[6656]{0:T(1024)(128)(2,1)S(1)}, bf16[6656]{0:T(1024)(128)(2,1)S(1)}, u32[]{:S(2)}, u32[]{:S(2)}) collective-permute-start(bf16[6656]{0:T(1024)(128)(2,1)S(1)} %convert_element_type.267), channel_id=1, source_target_pairs={{0,32},{32,64},{64,96},{96,128},{128,160},{160,192},{192,224},{224... | collective-permute-start | bytes 39944 | tf_op jit(solution)/shard_map/ppermute | solution.py:24
  67.0 4.7 %collective-permute-start.7 = (bf16[19968]{0:T(1024)(128)(2,1)S(1)}, bf16[19968]{0:T(1024)(128)(2,1)S(1)}, u32[]{:S(2)}, u32[]{:S(2)}) collective-permute-start(bf16[19968]{0:T(1024)(128)(2,1)S(1)} %reshape.507), channel_id=1, source_target_pairs={{0,31},{1,0},{2,1},{3,2},{4,3},{5,4},{6,5},{7,6},{8,7},{9,8},{10,9... | collective-permute-start | bytes 119816 | tf_op jit(solution)/shard_map/ppermute | solution.py:24
  69.5 7.4 %collective-permute-start.6 = (bf16[19968]{0:T(1024)(128)(2,1)S(1)}, bf16[19968]{0:T(1024)(128)(2,1)S(1)}, u32[]{:S(2)}, u32[]{:S(2)}) collective-permute-start(bf16[19968]{0:T(1024)(128)(2,1)S(1)} %reshape.507), channel_id=1, source_target_pairs={{0,1},{1,2},{2,3},{3,4},{4,5},{5,6},{6,7},{7,8},{8,9},{9,10},{10,1... | collective-permute-start | bytes 119816 | tf_op jit(solution)/shard_map/ppermute | solution.py:24
  77.9 0.8 copy-start.5
  78.8 6.0 %collective-permute-start.9 = (bf16[6656]{0:T(1024)(128)(2,1)S(1)}, bf16[6656]{0:T(1024)(128)(2,1)S(1)}, u32[]{:S(2)}, u32[]{:S(2)}) collective-permute-start(bf16[6656]{0:T(1024)(128)(2,1)S(1)} %reshape.509), channel_id=1, source_target_pairs={{0,480},{32,0},{64,32},{96,64},{128,96},{160,128},{192,160},{224,1... | collective-permute-start | bytes 39944 | tf_op jit(solution)/shard_map/ppermute | solution.py:24
  81.3 9.2 %collective-permute-start.8 = (bf16[6656]{0:T(1024)(128)(2,1)S(1)}, bf16[6656]{0:T(1024)(128)(2,1)S(1)}, u32[]{:S(2)}, u32[]{:S(2)}) collective-permute-start(bf16[6656]{0:T(1024)(128)(2,1)S(1)} %reshape.509), channel_id=1, source_target_pairs={{0,32},{32,64},{64,96},{96,128},{128,160},{160,192},{192,224},{224... | collective-permute-start | bytes 39944 | tf_op jit(solution)/shard_map/ppermute | solution.py:24
  90.7 4.5 %collective-permute-start.11 = (bf16[19968]{0:T(1024)(128)(2,1)S(1)}, bf16[19968]{0:T(1024)(128)(2,1)S(1)}, u32[]{:S(2)}, u32[]{:S(2)}) collective-permute-start(bf16[19968]{0:T(1024)(128)(2,1)S(1)} %reshape.510), channel_id=1, source_target_pairs={{0,31},{1,0},{2,1},{3,2},{4,3},{5,4},{6,5},{7,6},{8,7},{9,8},{10,9... | collective-permute-start | bytes 119816 | tf_op jit(solution)/shard_map/ppermute | solution.py:24
  92.7 7.4 %collective-permute-start.10 = (bf16[19968]{0:T(1024)(128)(2,1)S(1)}, bf16[19968]{0:T(1024)(128)(2,1)S(1)}, u32[]{:S(2)}, u32[]{:S(2)}) collective-permute-start(bf16[19968]{0:T(1024)(128)(2,1)S(1)} %reshape.510), channel_id=1, source_target_pairs={{0,1},{1,2},{2,3},{3,4},{4,5},{5,6},{6,7},{7,8},{8,9},{9,10},{10,1... | collective-permute-start | bytes 119816 | tf_op jit(solution)/shard_map/ppermute | solution.py:24

commit v7 on v6

--- a/solution.py
+++ b/solution.py
@@ -122,10 +122,16 @@
     source = pair_source[0, 0]
     target = pair_target[0, 0]
     live = pair_live_mask[0, 0]
-    high, middle, low = bf16_parts(distance)
-    pair_data = jnp.stack(
-        [source.astype(bf16), target.astype(bf16), live.astype(bf16), high, middle, low], axis=1
-    ).reshape(9, 6 * slots)
+    high = lax.reduce_precision(distance, exponent_bits=8, mantissa_bits=7)
+    rest_distance = distance - high
+    middle = lax.reduce_precision(rest_distance, exponent_bits=8, mantissa_bits=7)
+    low = rest_distance - middle
+    field = lax.broadcasted_iota(jnp.int32, (9, 6, slots), 1)
+    fields = [source.astype(f32), target.astype(f32), live.astype(f32), high, middle, low]
+    pair_data = fields[5][:, None, :]
+    for index in range(4, -1, -1):
+        pair_data = jnp.where(field == index, fields[index][:, None, :], pair_data)
+    pair_data = pair_data.astype(bf16).reshape(9, 6 * slots)
 
     common = jnp.concatenate([atoms.reshape(-1), band_vectors[0, 0].reshape(-1)])
     strip_common, strip_incoming, all_common, incoming = first_halo(common, pair_data)

time: 103 us -> 105 us (1.019)
  waiting for transfers between devices: 23 us -> 26.3 us
  local copies, waits for them, and re-layouts: 11.8 us -> 9.72 us
    ppermute x12, waiting for transfers between devices: 23 us -> 26.3 us  [shifted(): return lax.ppermute(value, axis, pairs)]
    unnamed x33, local copies, waits for them, and re-layouts: 3.74 us -> 2.36 us
    unnamed x9 -> x6, other arithmetic: 2.29 us -> 1.59 us
  transfers between devices with their start and end apart: 12 -> 12, of which waited for: 4 -> 5; matrix products, arithmetic and copies ran while one was open for 8% -> 7% of each run, Pallas kernels for 0% -> 0%
where the time goes in v7:
time: 105 us; the launch traced here: 104 us
  starting transfers between devices  44 us (42%)
  waiting for transfers between devices  26.3 us (25%)
  matrix products  15.1 us (14%)
  local copies, waits for them, and re-layouts  9.72 us (9%)
  other arithmetic  7.69 us (7%)
    ppermute x12, starting transfers between devices, shifted(): return lax.ppermute(value, axis, pairs)  44 us
    ppermute x12, waiting for transfers between devices, shifted(): return lax.ppermute(value, axis, pairs)  26.3 us
    dot_general x1, matrix products, on_device(): jnp.dot(spread, column_hot, preferred_element_type=f32)  4.84 us
    mul x1, other arithmetic, on_device(): blocks_t[:, None, :] * row_hot[None, :, :]  2.42 us
    unnamed x33, local copies, waits for them, and re-layouts  2.36 us
    dot_general x2, matrix products, group_blocks(): picked = jnp.dot(pick, table_parts, preferred_element_type=f32)  2.15 us
  transfers between devices with their start and end apart: 12, of which 5 were waited for; matrix products, arithmetic and copies ran while one was open for 7% of the time, Pallas kernels for 0%

profile of v7, /device:TPU:32, one launch (start us, length us, event | category | flops | bytes accessed | tf_op | source)
XLA Modules:
  0.0 103.9 jit_solution(14254245000346986695)
XLA Ops:
  0.0 0.8 add_sqrt_fusion
  0.8 0.7 convert_element_type.180
  1.5 1.0 fusion.15
  2.5 0.7 copy_bitcast_fusion.3
  3.4 0.8 copy.63
  4.3 13.4 %collective-permute-start.1 = (bf16[13056]{0:T(1024)(128)(2,1)S(1)}, bf16[13056]{0:T(1024)(128)(2,1)S(1)}, u32[]{:S(2)}, u32[]{:S(2)}) collective-permute-start(bf16[13056]{0:T(1024)(128)(2,1)S(1)} %get-tuple-element.29), channel_id=1, source_target_pairs={{0,480},{32,0},{64,32},{96,64},{128,96},{160,128},{192,160},{224,1... | collective-permute-start | bytes 78344 | tf_op jit(solution)/shard_map/ppermute | solution.py:24
  17.8 1.9 %collective-permute-start = (bf16[13056]{0:T(1024)(128)(2,1)S(1)}, bf16[13056]{0:T(1024)(128)(2,1)S(1)}, u32[]{:S(2)}, u32[]{:S(2)}) collective-permute-start(bf16[13056]{0:T(1024)(128)(2,1)S(1)} %get-tuple-element.30), channel_id=1, source_target_pairs={{0,32},{32,64},{64,96},{96,128},{128,160},{160,192},{192,224},{224... | collective-permute-start | bytes 78344 | tf_op jit(solution)/shard_map/ppermute | solution.py:24
  20.0 1.0 fusion.87
  21.2 0.2 copy.68
  21.5 0.7 constant_dynamic-update-slice_fusion.4
  22.5 0.9 reshape.426
  23.5 0.2 copy.86
  23.8 3.3 %collective-permute-done = bf16[13056]{0:T(1024)(128)(2,1)S(1)} collective-permute-done((bf16[13056]{0:T(1024)(128)(2,1)S(1)}, bf16[13056]{0:T(1024)(128)(2,1)S(1)}, u32[]{:S(2)}, u32[]{:S(2)}) %collective-permute-start) | collective-permute-done | bytes 26144 | tf_op jit(solution)/shard_map/ppermute | solution.py:24
  27.4 0.2 pad_maximum_fusion.10
  27.6 0.2 fusion.116
  28.0 0.1 fusion.82
  28.1 0.2 fusion.81
  28.3 1.9 %collective-permute-start.2 = (bf16[34560]{0:T(1024)(128)(2,1)S(1)}, bf16[34560]{0:T(1024)(128)(2,1)S(1)}, u32[]{:S(2)}, u32[]{:S(2)}) collective-permute-start(bf16[34560]{0:T(1024)(128)(2,1)S(1)} %get-tuple-element.27), channel_id=1, source_target_pairs={{0,1},{1,2},{2,3},{3,4},{4,5},{5,6},{6,7},{7,8},{8,9},{9,10},{10,1... | collective-permute-start | bytes 207368 | tf_op jit(solution)/shard_map/ppermute | solution.py:24
  30.2 5.8 %collective-permute-start.3 = (bf16[34560]{0:T(1024)(128)(2,1)S(1)}, bf16[34560]{0:T(1024)(128)(2,1)S(1)}, u32[]{:S(2)}, u32[]{:S(2)}) collective-permute-start(bf16[34560]{0:T(1024)(128)(2,1)S(1)} %get-tuple-element.28), channel_id=1, source_target_pairs={{0,31},{1,0},{2,1},{3,2},{4,3},{5,4},{6,5},{7,6},{8,7},{9,8},{10,9... | collective-permute-start | bytes 207368 | tf_op jit(solution)/shard_map/ppermute | solution.py:24
  36.2 0.6 fusion.27
  36.8 0.5 multiply_convert_fusion.1
  37.3 0.3 fusion.83
  37.7 0.3 fusion.9
  38.0 0.5 copy-done.2
  38.6 0.2 convolution_bitcast_fusion.2
  38.8 0.2 convolution_bitcast_fusion.3
  39.5 0.2 pad_maximum_fusion.6
  39.9 0.2 reshape.430
  40.2 0.2 fusion.85
  40.3 0.2 fusion.84
  40.7 1.6 %fusion.2 = f32[1536,768]{1,0:T(8,128)S(1)} fusion(s32[1536]{0:T(1024)S(1)} %add_add_fusion, s32[1536]{0:T(1024)S(1)} %pad_add_fusion, bf16[288,256]{1,0:T(8,128)(2,1)S(1)} %get-tuple-element.23, bf16[288,256]{1,0:T(8,128)(2,1)S(1)} %get-tuple-element.22, bf16[288,256]{1,0:T(8,128)(2,1)S(1)} %get-tuple-element.21), kind=kOutput, calls=%fused_computation.9 | convolution fusion | flops 682131456 | bytes 5173248 | tf_op jit(solution)/shard_map/dot_general | solution.py:181
  42.3 0.8 multiply_convert_fusion
  43.0 0.4 fusion.86
  43.4 0.5 fusion
  44.0 0.3 convolution_bitcast_fusion.1
  44.3 0.3 convolution_bitcast_fusion
  44.6 0.3 slice-done
  44.9 0.6 reshape.437
  45.5 0.5 copy.72
  46.1 2.4 %broadcast_multiply_fusion = bf16[169,16,2320]{2,1,0:T(8,128)(2,1)S(1)} fusion(bf16[16,2320]{1,0:T(8,128)(2,1)S(1)} %fusion.43, bf16[169,2320]{1,0:T(8,128)(2,1)S(1)} %pad_maximum_fusion.1), kind=kLoop, calls=%fused_computation | loop fusion | flops 6273280 | bytes 13404960 | tf_op jit(solution)/shard_map/mul | solution.py:229
  48.5 4.8 %reduce-precision_convert_fusion = (bf16[13,208,144]{1,2,0:T(8,128)(2,1)S(1)}, bf16[13,208,144]{1,2,0:T(8,128)(2,1)S(1)}) fusion(bf16[13,208,2320]{2,1,0:T(8,128)(2,1)S(1)} %bitcast.177, s32[2320]{0:T(1024)S(1)} %constant_dynamic-update-slice_fusion.6), kind=kOutput, calls=%fused_computation.4 | convolution fusion | flops 1808985600 | bytes 14113344 | tf_op jit(solution)/shard_map/dot_general | solution.py:231
  53.4 0.6 fusion.80
  54.0 0.4 copy-done.11
  54.3 0.3 copy-done.9
  54.9 4.4 %collective-permute-start.5 = (bf16[6656]{0:T(1024)(128)(2,1)S(1)}, bf16[6656]{0:T(1024)(128)(2,1)S(1)}, u32[]{:S(2)}, u32[]{:S(2)}) collective-permute-start(bf16[6656]{0:T(1024)(128)(2,1)S(1)} %convert_element_type.214), channel_id=1, source_target_pairs={{0,480},{32,0},{64,32},{96,64},{128,96},{160,128},{192,160},{224,1... | collective-permute-start | bytes 39944 | tf_op jit(solution)/shard_map/ppermute | solution.py:24
  59.3 1.9 %collective-permute-start.4 = (bf16[6656]{0:T(1024)(128)(2,1)S(1)}, bf16[6656]{0:T(1024)(128)(2,1)S(1)}, u32[]{:S(2)}, u32[]{:S(2)}) collective-permute-start(bf16[6656]{0:T(1024)(128)(2,1)S(1)} %convert_element_type.214), channel_id=1, source_target_pairs={{0,32},{32,64},{64,96},{96,128},{128,160},{160,192},{192,224},{224... | collective-permute-start | bytes 39944 | tf_op jit(solution)/shard_map/ppermute | solution.py:24
  61.3 7.2 %collective-permute-done.4 = bf16[6656]{0:T(1024)(128)(2,1)S(1)} collective-permute-done((bf16[6656]{0:T(1024)(128)(2,1)S(1)}, bf16[6656]{0:T(1024)(128)(2,1)S(1)}, u32[]{:S(2)}, u32[]{:S(2)}) %collective-permute-start.4) | collective-permute-done | bytes 13344 | tf_op jit(solution)/shard_map/ppermute | solution.py:24
  68.7 2.4 %collective-permute-start.7 = (bf16[19968]{0:T(1024)(128)(2,1)S(1)}, bf16[19968]{0:T(1024)(128)(2,1)S(1)}, u32[]{:S(2)}, u32[]{:S(2)}) collective-permute-start(bf16[19968]{0:T(1024)(128)(2,1)S(1)} %reshape.439), channel_id=1, source_target_pairs={{0,31},{1,0},{2,1},{3,2},{4,3},{5,4},{6,5},{7,6},{8,7},{9,8},{10,9... | collective-permute-start | bytes 119816 | tf_op jit(solution)/shard_map/ppermute | solution.py:24
  71.1 2.1 %collective-permute-start.6 = (bf16[19968]{0:T(1024)(128)(2,1)S(1)}, bf16[19968]{0:T(1024)(128)(2,1)S(1)}, u32[]{:S(2)}, u32[]{:S(2)}) collective-permute-start(bf16[19968]{0:T(1024)(128)(2,1)S(1)} %reshape.439), channel_id=1, source_target_pairs={{0,1},{1,2},{2,3},{3,4},{4,5},{5,6},{6,7},{7,8},{8,9},{9,10},{10,1... | collective-permute-start | bytes 119816 | tf_op jit(solution)/shard_map/ppermute | solution.py:24
  73.3 5.2 %collective-permute-done.6 = bf16[19968]{0:T(1024)(128)(2,1)S(1)} collective-permute-done((bf16[19968]{0:T(1024)(128)(2,1)S(1)}, bf16[19968]{0:T(1024)(128)(2,1)S(1)}, u32[]{:S(2)}, u32[]{:S(2)}) %collective-permute-start.6) | collective-permute-done | bytes 39968 | tf_op jit(solution)/shard_map/ppermute | solution.py:24
  78.5 0.1 pad_maximum_fusion.7
  78.8 0.3 reshape_reshape.6
  79.1 0.3 copy.78
  79.4 0.6 fusion.13
  80.3 2.5 %collective-permute-start.9 = (bf16[6656]{0:T(1024)(128)(2,1)S(1)}, bf16[6656]{0:T(1024)(128)(2,1)S(1)}, u32[]{:S(2)}, u32[]{:S(2)}) collective-permute-start(bf16[6656]{0:T(1024)(128)(2,1)S(1)} %reshape.441), channel_id=1, source_target_pairs={{0,480},{32,0},{64,32},{96,64},{128,96},{160,128},{192,160},{224,1... | collective-permute-start | bytes 39944 | tf_op jit(solution)/shard_map/ppermute | solution.py:24
  82.9 3.3 %collective-permute-start.8 = (bf16[6656]{0:T(1024)(128)(2,1)S(1)}, bf16[6656]{0:T(1024)(128)(2,1)S(1)}, u32[]{:S(2)}, u32[]{:S(2)}) collective-permute-start(bf16[6656]{0:T(1024)(128)(2,1)S(1)} %reshape.441), channel_id=1, source_target_pairs={{0,32},{32,64},{64,96},{96,128},{128,160},{160,192},{192,224},{224... | collective-permute-start | bytes 39944 | tf_op jit(solution)/shard_map/ppermute | solution.py:24
  86.3 5.8 %collective-permute-done.8 = bf16[6656]{0:T(1024)(128)(2,1)S(1)} collective-permute-done((bf16[6656]{0:T(1024)(128)(2,1)S(1)}, bf16[6656]{0:T(1024)(128)(2,1)S(1)}, u32[]{:S(2)}, u32[]{:S(2)}) %collective-permute-start.8) | collective-permute-done | bytes 13344 | tf_op jit(solution)/shard_map/ppermute | solution.py:24
  92.3 1.9 %collective-permute-start.11 = (bf16[19968]{0:T(1024)(128)(2,1)S(1)}, bf16[19968]{0:T(1024)(128)(2,1)S(1)}, u32[]{:S(2)}, u32[]{:S(2)}) collective-permute-start(bf16[19968]{0:T(1024)(128)(2,1)S(1)} %reshape.442), channel_id=1, source_target_pairs={{0,31},{1,0},{2,1},{3,2},{4,3},{5,4},{6,5},{7,6},{8,7},{9,8},{10,9... | collective-permute-start | bytes 119816 | tf_op jit(solution)/shard_map/ppermute | solution.py:24
  94.2 2.4 %collective-permute-start.10 = (bf16[19968]{0:T(1024)(128)(2,1)S(1)}, bf16[19968]{0:T(1024)(128)(2,1)S(1)}, u32[]{:S(2)}, u32[]{:S(2)}) collective-permute-start(bf16[19968]{0:T(1024)(128)(2,1)S(1)} %reshape.442), channel_id=1, source_target_pairs={{0,1},{1,2},{2,3},{3,4},{4,5},{5,6},{6,7},{7,8},{8,9},{9,10},{10,1... | collective-permute-start | bytes 119816 | tf_op jit(solution)/shard_map/ppermute | solution.py:24
  96.8 4.9 %collective-permute-done.10 = bf16[19968]{0:T(1024)(128)(2,1)S(1)} collective-permute-done((bf16[19968]{0:T(1024)(128)(2,1)S(1)}, bf16[19968]{0:T(1024)(128)(2,1)S(1)}, u32[]{:S(2)}, u32[]{:S(2)}) %collective-permute-start.10) | collective-permute-done | bytes 39968 | tf_op jit(solution)/shard_map/ppermute | solution.py:24
  101.9 0.3 reshape_reshape.7
  102.2 0.3 copy.83
  102.5 0.6 fusion.14
  103.1 0.8 copy.85
  (164 shorter events, 4.6 us)
Async XLA Ops:
  0.0 37.3 %copy-start = (bf16[256,256]{1,0:T(8,128)(2,1)S(1)}, bf16[256,256]{1,0:T(8,128)(2,1)}, u32[]{:S(2)}) copy-start(bf16[256,256]{1,0:T(8,128)(2,1)} %param.27) | copy-start | bytes 393220
  0.0 27.9 %copy-start.3 = (bf16[256,256]{1,0:T(8,128)(2,1)S(1)}, bf16[256,256]{1,0:T(8,128)(2,1)}, u32[]{:S(2)}) copy-start(bf16[256,256]{1,0:T(8,128)(2,1)} %param.26) | copy-start | bytes 393220
  1.5 26.6 %copy-start.4 = (bf16[256,256]{1,0:T(8,128)(2,1)S(1)}, bf16[256,256]{1,0:T(8,128)(2,1)}, u32[]{:S(2)}) copy-start(bf16[256,256]{1,0:T(8,128)(2,1)} %param.25) | copy-start | bytes 393220
  4.3 31.7 %copy-start.6 = (s32[3]{0:T(128)S(1)}, s32[3]{0:T(128)}, u32[]{:S(2)}) copy-start(s32[3]{0:T(128)} %constant.63) | copy-start | bytes 40
  4.3 19.4 %collective-permute-start.1 = (bf16[13056]{0:T(1024)(128)(2,1)S(1)}, bf16[13056]{0:T(1024)(128)(2,1)S(1)}, u32[]{:S(2)}, u32[]{:S(2)}) collective-permute-start(bf16[13056]{0:T(1024)(128)(2,1)S(1)} %get-tuple-element.29), channel_id=1, source_target_pairs={{0,480},{32,0},{64,32},{96,64},{128,96},{160,128},{192,160},{224,1... | collective-permute-start | bytes 78344 | tf_op jit(solution)/shard_map/ppermute | solution.py:24
  17.8 9.4 %collective-permute-start = (bf16[13056]{0:T(1024)(128)(2,1)S(1)}, bf16[13056]{0:T(1024)(128)(2,1)S(1)}, u32[]{:S(2)}, u32[]{:S(2)}) collective-permute-start(bf16[13056]{0:T(1024)(128)(2,1)S(1)} %get-tuple-element.30), channel_id=1, source_target_pairs={{0,32},{32,64},{64,96},{96,128},{128,160},{160,192},{192,224},{224... | collective-permute-start | bytes 78344 | tf_op jit(solution)/shard_map/ppermute | solution.py:24
  27.8 9.0 %copy-start.8 = (bf16[16,256]{1,0:T(8,128)(2,1)S(1)}, bf16[16,256]{1,0:T(8,128)(2,1)}, u32[]{:S(2)}) copy-start(bf16[16,256]{1,0:T(8,128)(2,1)} %param.24) | copy-start | bytes 24580
  28.3 10.9 %collective-permute-start.2 = (bf16[34560]{0:T(1024)(128)(2,1)S(1)}, bf16[34560]{0:T(1024)(128)(2,1)S(1)}, u32[]{:S(2)}, u32[]{:S(2)}) collective-permute-start(bf16[34560]{0:T(1024)(128)(2,1)S(1)} %get-tuple-element.27), channel_id=1, source_target_pairs={{0,1},{1,2},{2,3},{3,4},{4,5},{5,6},{6,7},{7,8},{8,9},{9,10},{10,1... | collective-permute-start | bytes 207368 | tf_op jit(solution)/shard_map/ppermute | solution.py:24
  30.2 9.0 %collective-permute-start.3 = (bf16[34560]{0:T(1024)(128)(2,1)S(1)}, bf16[34560]{0:T(1024)(128)(2,1)S(1)}, u32[]{:S(2)}, u32[]{:S(2)}) collective-permute-start(bf16[34560]{0:T(1024)(128)(2,1)S(1)} %get-tuple-element.28), channel_id=1, source_target_pairs={{0,31},{1,0},{2,1},{3,2},{4,3},{5,4},{6,5},{7,6},{8,7},{9,8},{10,9... | collective-permute-start | bytes 207368 | tf_op jit(solution)/shard_map/ppermute | solution.py:24
  36.8 0.9 copy-start.7
  37.7 0.9 copy-start.2
  40.1 2.2 %copy-start.1 = (bf16[9,10752]{1,0:T(8,128)(2,1)}, bf16[9,10752]{1,0:T(8,128)(2,1)S(1)}, u32[]{:S(2)}) copy-start(bf16[9,10752]{1,0:T(8,128)(2,1)S(1)} %reshape.430) | copy-start | bytes 580612
  44.0 0.9 slice-start
  53.4 1.0 copy-start.11
  53.4 1.3 %copy-start.9 = (bf16[13,208,144]{1,2,0:T(8,128)(2,1)}, bf16[13,208,144]{1,2,0:T(8,128)(2,1)S(1)}, u32[]{:S(2)}) copy-start(bf16[13,208,144]{1,2,0:T(8,128)(2,1)S(1)} %get-tuple-element.19) | copy-start | bytes 2336260
  54.6 24.8 %copy-start.12 = (bf16[13,208,144]{1,2,0:T(8,128)(2,1)S(1)}, bf16[13,208,144]{1,2,0:T(8,128)(2,1)}, u32[]{:S(2)}) copy-start(bf16[13,208,144]{1,2,0:T(8,128)(2,1)} %copy-done.11) | copy-start | bytes 2336260
  54.8 24.6 %copy-start.10 = (bf16[13,208,144]{1,2,0:T(8,128)(2,1)S(1)}, bf16[13,208,144]{1,2,0:T(8,128)(2,1)}, u32[]{:S(2)}) copy-start(bf16[13,208,144]{1,2,0:T(8,128)(2,1)} %copy-done.9) | copy-start | bytes 2336260
  54.9 6.4 %collective-permute-start.5 = (bf16[6656]{0:T(1024)(128)(2,1)S(1)}, bf16[6656]{0:T(1024)(128)(2,1)S(1)}, u32[]{:S(2)}, u32[]{:S(2)}) collective-permute-start(bf16[6656]{0:T(1024)(128)(2,1)S(1)} %convert_element_type.214), channel_id=1, source_target_pairs={{0,480},{32,0},{64,32},{96,64},{128,96},{160,128},{192,160},{224,1... | collective-permute-start | bytes 39944 | tf_op jit(solution)/shard_map/ppermute | solution.py:24
  59.3 9.2 %collective-permute-start.4 = (bf16[6656]{0:T(1024)(128)(2,1)S(1)}, bf16[6656]{0:T(1024)(128)(2,1)S(1)}, u32[]{:S(2)}, u32[]{:S(2)}) collective-permute-start(bf16[6656]{0:T(1024)(128)(2,1)S(1)} %convert_element_type.214), channel_id=1, source_target_pairs={{0,32},{32,64},{64,96},{96,128},{128,160},{160,192},{192,224},{224... | collective-permute-start | bytes 39944 | tf_op jit(solution)/shard_map/ppermute | solution.py:24
  68.7 4.7 %collective-permute-start.7 = (bf16[19968]{0:T(1024)(128)(2,1)S(1)}, bf16[19968]{0:T(1024)(128)(2,1)S(1)}, u32[]{:S(2)}, u32[]{:S(2)}) collective-permute-start(bf16[19968]{0:T(1024)(128)(2,1)S(1)} %reshape.439), channel_id=1, source_target_pairs={{0,31},{1,0},{2,1},{3,2},{4,3},{5,4},{6,5},{7,6},{8,7},{9,8},{10,9... | collective-permute-start | bytes 119816 | tf_op jit(solution)/shard_map/ppermute | solution.py:24
  71.1 7.4 %collective-permute-start.6 = (bf16[19968]{0:T(1024)(128)(2,1)S(1)}, bf16[19968]{0:T(1024)(128)(2,1)S(1)}, u32[]{:S(2)}, u32[]{:S(2)}) collective-permute-start(bf16[19968]{0:T(1024)(128)(2,1)S(1)} %reshape.439), channel_id=1, source_target_pairs={{0,1},{1,2},{2,3},{3,4},{4,5},{5,6},{6,7},{7,8},{8,9},{9,10},{10,1... | collective-permute-start | bytes 119816 | tf_op jit(solution)/shard_map/ppermute | solution.py:24
  79.4 0.8 copy-start.5
  80.3 6.0 %collective-permute-start.9 = (bf16[6656]{0:T(1024)(128)(2,1)S(1)}, bf16[6656]{0:T(1024)(128)(2,1)S(1)}, u32[]{:S(2)}, u32[]{:S(2)}) collective-permute-start(bf16[6656]{0:T(1024)(128)(2,1)S(1)} %reshape.441), channel_id=1, source_target_pairs={{0,480},{32,0},{64,32},{96,64},{128,96},{160,128},{192,160},{224,1... | collective-permute-start | bytes 39944 | tf_op jit(solution)/shard_map/ppermute | solution.py:24
  82.9 9.2 %collective-permute-start.8 = (bf16[6656]{0:T(1024)(128)(2,1)S(1)}, bf16[6656]{0:T(1024)(128)(2,1)S(1)}, u32[]{:S(2)}, u32[]{:S(2)}) collective-permute-start(bf16[6656]{0:T(1024)(128)(2,1)S(1)} %reshape.441), channel_id=1, source_target_pairs={{0,32},{32,64},{64,96},{96,128},{128,160},{160,192},{192,224},{224... | collective-permute-start | bytes 39944 | tf_op jit(solution)/shard_map/ppermute | solution.py:24
  92.3 4.5 %collective-permute-start.11 = (bf16[19968]{0:T(1024)(128)(2,1)S(1)}, bf16[19968]{0:T(1024)(128)(2,1)S(1)}, u32[]{:S(2)}, u32[]{:S(2)}) collective-permute-start(bf16[19968]{0:T(1024)(128)(2,1)S(1)} %reshape.442), channel_id=1, source_target_pairs={{0,31},{1,0},{2,1},{3,2},{4,3},{5,4},{6,5},{7,6},{8,7},{9,8},{10,9... | collective-permute-start | bytes 119816 | tf_op jit(solution)/shard_map/ppermute | solution.py:24
  94.2 7.4 %collective-permute-start.10 = (bf16[19968]{0:T(1024)(128)(2,1)S(1)}, bf16[19968]{0:T(1024)(128)(2,1)S(1)}, u32[]{:S(2)}, u32[]{:S(2)}) collective-permute-start(bf16[19968]{0:T(1024)(128)(2,1)S(1)} %reshape.442), channel_id=1, source_target_pairs={{0,1},{1,2},{2,3},{3,4},{4,5},{5,6},{6,7},{7,8},{8,9},{9,10},{10,1... | collective-permute-start | bytes 119816 | tf_op jit(solution)/shard_map/ppermute | solution.py:24

commit v8 on v7

--- a/solution.py
+++ b/solution.py
@@ -32,12 +32,27 @@
     return high.astype(bf16), middle.astype(bf16), low.astype(bf16)
 
 
+def gy_swaps(to_south, to_north):
+    count = lax.axis_size("gy")
+    even = lax.axis_index("gy") % 2 == 0
+    on_chip = lax.ppermute(
+        jnp.where(even, to_north, to_south), "gy", [(i, i ^ 1) for i in range(count)]
+    )
+    across = lax.ppermute(
+        jnp.where(even, to_south, to_north),
+        "gy",
+        [(i, (i + 1) % count if i % 2 else (i - 1) % count) for i in range(count)],
+    )
+    return jnp.where(even, across, on_chip), jnp.where(even, on_chip, across)
+
+
 def halo(flat):
     from_west = shifted(flat, "gx", 1)
     from_east = shifted(flat, "gx", -1)
     strip = jnp.stack([from_west, flat, from_east]).reshape(-1)
-    from_south = shifted(strip, "gy", 1).reshape(3, -1)
-    from_north = shifted(strip, "gy", -1).reshape(3, -1)
+    from_south, from_north = gy_swaps(strip, strip)
+    from_south = from_south.reshape(3, -1)
+    from_north = from_north.reshape(3, -1)
     strip = strip.reshape(3, -1)
     return jnp.stack([from_south, strip, from_north], axis=1).reshape(9, -1)
 
@@ -59,8 +74,7 @@
     )
     to_north = jnp.concatenate([strip_common.reshape(-1), strip_pairs[:, 2].reshape(-1)])
     to_south = jnp.concatenate([strip_common.reshape(-1), strip_pairs[:, 0].reshape(-1)])
-    from_south = shifted(to_north, "gy", 1)
-    from_north = shifted(to_south, "gy", -1)
+    from_south, from_north = gy_swaps(to_south, to_north)
     all_common = jnp.stack(
         [from_south[: 3 * n].reshape(3, n), strip_common, from_north[: 3 * n].reshape(3, n)],
         axis=1,

time: 105 us -> 104 us (level)
  the two profiles are of different devices: /device:TPU:32 before, /device:TPU:1 now
where the time goes in v8:
time: 104 us
  starting transfers between devices  48.8 us (47%)
  waiting for transfers between devices  19.1 us (18%)
  matrix products  15.1 us (15%)
  local copies, waits for them, and re-layouts  11.8 us (11%)
  other arithmetic  7.72 us (7%)
  between operations  1.08 us (1%)
    ppermute x6, starting transfers between devices, shifted(): return lax.ppermute(value, axis, pairs)  28.7 us
    ppermute x6, waiting for transfers between devices, shifted(): return lax.ppermute(value, axis, pairs)  12.7 us
    ppermute x3, starting transfers between devices, gy_swaps(): lax.ppermute(jnp.where(even, to_north, to_south), 'gy', [(i, i ^ 1) for i...  11.9 us
    ppermute x3, starting transfers between devices, gy_swaps(): lax.ppermute(jnp.where(even, to_south, to_north), 'gy', [(i, (i + 1) % co...  8.27 us
    ppermute x3, waiting for transfers between devices, gy_swaps(): lax.ppermute(jnp.where(even, to_south, to_north), 'gy', [(i, (i + 1) % co...  6.33 us
    dot_general x1, matrix products, on_device(): jnp.dot(spread, column_hot, preferred_element_type=f32)  4.84 us
    unnamed x35, local copies, waits for them, and re-layouts  3.96 us
    mul x1, other arithmetic, on_device(): blocks_t[:, None, :] * row_hot[None, :, :]  2.42 us
  transfers between devices with their start and end apart: 12, of which 5 were waited for; matrix products, arithmetic and copies ran while one was open for 7% of the time, Pallas kernels for 0%

profile of v8, /device:TPU:1, one launch (start us, length us, event | category | flops | bytes accessed | tf_op | source)
XLA Modules:
  0.0 103.6 jit_solution(16828089131317409035)
XLA Ops:
  0.0 0.8 add_sqrt_fusion
  0.8 0.7 convert_element_type.180
  1.5 0.9 fusion.15
  2.5 0.7 copy_bitcast_fusion.3
  3.4 0.9 copy.63
  4.4 14.0 %collective-permute-start.1 = (bf16[13056]{0:T(1024)(128)(2,1)S(1)}, bf16[13056]{0:T(1024)(128)(2,1)S(1)}, u32[]{:S(2)}, u32[]{:S(2)}) collective-permute-start(bf16[13056]{0:T(1024)(128)(2,1)S(1)} %get-tuple-element.35), channel_id=1, source_target_pairs={{0,480},{32,0},{64,32},{96,64},{128,96},{160,128},{192,160},{224,1... | collective-permute-start | bytes 78344 | tf_op jit(solution)/shard_map/ppermute | solution.py:24
  18.3 1.9 %collective-permute-start = (bf16[13056]{0:T(1024)(128)(2,1)S(1)}, bf16[13056]{0:T(1024)(128)(2,1)S(1)}, u32[]{:S(2)}, u32[]{:S(2)}) collective-permute-start(bf16[13056]{0:T(1024)(128)(2,1)S(1)} %get-tuple-element.36), channel_id=1, source_target_pairs={{0,32},{32,64},{64,96},{96,128},{128,160},{160,192},{192,224},{224... | collective-permute-start | bytes 78344 | tf_op jit(solution)/shard_map/ppermute | solution.py:24
  20.6 1.0 fusion.87
  21.8 0.2 copy.68
  22.1 0.7 constant_dynamic-update-slice_fusion.4
  23.1 0.9 reshape.426
  24.1 0.2 copy.86
  24.4 2.1 %collective-permute-done = bf16[13056]{0:T(1024)(128)(2,1)S(1)} collective-permute-done((bf16[13056]{0:T(1024)(128)(2,1)S(1)}, bf16[13056]{0:T(1024)(128)(2,1)S(1)}, u32[]{:S(2)}, u32[]{:S(2)}) %collective-permute-start) | collective-permute-done | bytes 26144 | tf_op jit(solution)/shard_map/ppermute | solution.py:24
  26.9 0.2 pad_maximum_fusion.10
  27.4 0.8 dynamic-update-slice.10
  28.2 0.8 dynamic-update-slice.12
  29.3 0.2 dynamic-update-slice.13
  29.5 0.2 dynamic-update-slice.11
  29.7 4.2 %collective-permute-start.2 = (bf16[34560]{0:T(1024)(128)(2,1)S(1)}, bf16[34560]{0:T(1024)(128)(2,1)S(1)}, u32[]{:S(2)}, u32[]{:S(2)}) collective-permute-start(bf16[34560]{0:T(1024)(128)(2,1)S(1)} %get-tuple-element.26), channel_id=1, source_target_pairs={{0,31},{1,2},{2,1},{3,4},{4,3},{5,6},{6,5},{7,8},{8,7},{9,10},{10,... | collective-permute-start | bytes 207368 | tf_op jit(solution)/shard_map/ppermute | solution.py:41
  34.0 3.4 %collective-permute-start.3 = (bf16[34560]{0:T(1024)(128)(2,1)S(1)}, bf16[34560]{0:T(1024)(128)(2,1)S(1)}, u32[]{:S(2)}, u32[]{:S(2)}) collective-permute-start(bf16[34560]{0:T(1024)(128)(2,1)S(1)} %get-tuple-element.27), channel_id=1, source_target_pairs={{0,1},{1,0},{2,3},{3,2},{4,5},{5,4},{6,7},{7,6},{8,9},{9,8},{10,11... | collective-permute-start | bytes 207368 | tf_op jit(solution)/shard_map/ppermute | solution.py:38
  37.5 0.6 fusion.27
  38.2 0.5 multiply_convert_fusion.1
  38.7 0.3 fusion.83
  39.1 0.3 fusion.9
  39.4 0.5 copy-done.2
  39.9 0.2 convolution_bitcast_fusion.2
  40.2 0.2 convolution_bitcast_fusion.3
  41.0 0.2 pad_maximum_fusion.6
  41.3 0.2 reshape.430
  41.6 0.2 fusion.85
  41.7 0.2 fusion.84
  42.1 1.6 %fusion.2 = f32[1536,768]{1,0:T(8,128)S(1)} fusion(s32[1536]{0:T(1024)S(1)} %add_add_fusion, s32[1536]{0:T(1024)S(1)} %pad_add_fusion, bf16[288,256]{1,0:T(8,128)(2,1)S(1)} %get-tuple-element.23, bf16[288,256]{1,0:T(8,128)(2,1)S(1)} %get-tuple-element.22, bf16[288,256]{1,0:T(8,128)(2,1)S(1)} %get-tuple-element.21), kind=kOutput, calls=%fused_computation.9 | convolution fusion | flops 682131456 | bytes 5173248 | tf_op jit(solution)/shard_map/dot_general | solution.py:195
  43.7 0.8 multiply_convert_fusion
  44.5 0.4 fusion.86
  44.8 0.5 fusion
  45.4 0.3 convolution_bitcast_fusion.1
  45.7 0.3 convolution_bitcast_fusion
  46.0 0.3 slice-done
  46.3 0.6 reshape.437
  46.9 0.5 copy.72
  47.5 2.4 %broadcast_multiply_fusion = bf16[169,16,2320]{2,1,0:T(8,128)(2,1)S(1)} fusion(bf16[16,2320]{1,0:T(8,128)(2,1)S(1)} %fusion.43, bf16[169,2320]{1,0:T(8,128)(2,1)S(1)} %pad_maximum_fusion.1), kind=kLoop, calls=%fused_computation | loop fusion | flops 6273280 | bytes 13404960 | tf_op jit(solution)/shard_map/mul | solution.py:243
  49.9 4.8 %reduce-precision_convert_fusion = (bf16[13,208,144]{1,2,0:T(8,128)(2,1)S(1)}, bf16[13,208,144]{1,2,0:T(8,128)(2,1)S(1)}) fusion(bf16[13,208,2320]{2,1,0:T(8,128)(2,1)S(1)} %bitcast.177, s32[2320]{0:T(1024)S(1)} %constant_dynamic-update-slice_fusion.6), kind=kOutput, calls=%fused_computation.4 | convolution fusion | flops 1808985600 | bytes 14113344 | tf_op jit(solution)/shard_map/dot_general | solution.py:245
  54.8 0.6 fusion.80
  55.4 0.4 copy-done.11
  55.7 0.3 copy-done.9
  56.3 5.6 %collective-permute-start.5 = (bf16[6656]{0:T(1024)(128)(2,1)S(1)}, bf16[6656]{0:T(1024)(128)(2,1)S(1)}, u32[]{:S(2)}, u32[]{:S(2)}) collective-permute-start(bf16[6656]{0:T(1024)(128)(2,1)S(1)} %convert_element_type.214), channel_id=1, source_target_pairs={{0,480},{32,0},{64,32},{96,64},{128,96},{160,128},{192,160},{224,1... | collective-permute-start | bytes 39944 | tf_op jit(solution)/shard_map/ppermute | solution.py:24
  61.9 1.9 %collective-permute-start.4 = (bf16[6656]{0:T(1024)(128)(2,1)S(1)}, bf16[6656]{0:T(1024)(128)(2,1)S(1)}, u32[]{:S(2)}, u32[]{:S(2)}) collective-permute-start(bf16[6656]{0:T(1024)(128)(2,1)S(1)} %convert_element_type.214), channel_id=1, source_target_pairs={{0,32},{32,64},{64,96},{96,128},{128,160},{160,192},{192,224},{224... | collective-permute-start | bytes 39944 | tf_op jit(solution)/shard_map/ppermute | solution.py:24
  63.9 6.0 %collective-permute-done.4 = bf16[6656]{0:T(1024)(128)(2,1)S(1)} collective-permute-done((bf16[6656]{0:T(1024)(128)(2,1)S(1)}, bf16[6656]{0:T(1024)(128)(2,1)S(1)}, u32[]{:S(2)}, u32[]{:S(2)}) %collective-permute-start.4) | collective-permute-done | bytes 13344 | tf_op jit(solution)/shard_map/ppermute | solution.py:24
  70.1 3.3 %collective-permute-start.7 = (bf16[19968]{0:T(1024)(128)(2,1)S(1)}, bf16[19968]{0:T(1024)(128)(2,1)S(1)}, u32[]{:S(2)}, u32[]{:S(2)}) collective-permute-start(bf16[19968]{0:T(1024)(128)(2,1)S(1)} %reshape.439), channel_id=1, source_target_pairs={{0,1},{1,0},{2,3},{3,2},{4,5},{5,4},{6,7},{7,6},{8,9},{9,8},{10,11... | collective-permute-start | bytes 119816 | tf_op jit(solution)/shard_map/ppermute | solution.py:38
  73.5 2.1 %collective-permute-start.6 = (bf16[19968]{0:T(1024)(128)(2,1)S(1)}, bf16[19968]{0:T(1024)(128)(2,1)S(1)}, u32[]{:S(2)}, u32[]{:S(2)}) collective-permute-start(bf16[19968]{0:T(1024)(128)(2,1)S(1)} %reshape.439), channel_id=1, source_target_pairs={{0,31},{1,2},{2,1},{3,4},{4,3},{5,6},{6,5},{7,8},{8,7},{9,10},{10,... | collective-permute-start | bytes 119816 | tf_op jit(solution)/shard_map/ppermute | solution.py:41
  75.7 3.1 %collective-permute-done.6 = bf16[19968]{0:T(1024)(128)(2,1)S(1)} collective-permute-done((bf16[19968]{0:T(1024)(128)(2,1)S(1)}, bf16[19968]{0:T(1024)(128)(2,1)S(1)}, u32[]{:S(2)}, u32[]{:S(2)}) %collective-permute-start.6) | collective-permute-done | bytes 39968 | tf_op jit(solution)/shard_map/ppermute | solution.py:41
  79.1 0.3 reshape_reshape.6
  79.4 0.3 copy.78
  79.7 0.6 fusion.13
  80.6 1.9 %collective-permute-start.9 = (bf16[6656]{0:T(1024)(128)(2,1)S(1)}, bf16[6656]{0:T(1024)(128)(2,1)S(1)}, u32[]{:S(2)}, u32[]{:S(2)}) collective-permute-start(bf16[6656]{0:T(1024)(128)(2,1)S(1)} %reshape.441), channel_id=1, source_target_pairs={{0,480},{32,0},{64,32},{96,64},{128,96},{160,128},{192,160},{224,1... | collective-permute-start | bytes 39944 | tf_op jit(solution)/shard_map/ppermute | solution.py:24
  82.6 3.4 %collective-permute-start.8 = (bf16[6656]{0:T(1024)(128)(2,1)S(1)}, bf16[6656]{0:T(1024)(128)(2,1)S(1)}, u32[]{:S(2)}, u32[]{:S(2)}) collective-permute-start(bf16[6656]{0:T(1024)(128)(2,1)S(1)} %reshape.441), channel_id=1, source_target_pairs={{0,32},{32,64},{64,96},{96,128},{128,160},{160,192},{192,224},{224... | collective-permute-start | bytes 39944 | tf_op jit(solution)/shard_map/ppermute | solution.py:24
  86.1 4.6 %collective-permute-done.8 = bf16[6656]{0:T(1024)(128)(2,1)S(1)} collective-permute-done((bf16[6656]{0:T(1024)(128)(2,1)S(1)}, bf16[6656]{0:T(1024)(128)(2,1)S(1)}, u32[]{:S(2)}, u32[]{:S(2)}) %collective-permute-start.8) | collective-permute-done | bytes 13344 | tf_op jit(solution)/shard_map/ppermute | solution.py:24
  90.8 5.2 %collective-permute-start.11 = (bf16[19968]{0:T(1024)(128)(2,1)S(1)}, bf16[19968]{0:T(1024)(128)(2,1)S(1)}, u32[]{:S(2)}, u32[]{:S(2)}) collective-permute-start(bf16[19968]{0:T(1024)(128)(2,1)S(1)} %reshape.442), channel_id=1, source_target_pairs={{0,1},{1,0},{2,3},{3,2},{4,5},{5,4},{6,7},{7,6},{8,9},{9,8},{10,11... | collective-permute-start | bytes 119816 | tf_op jit(solution)/shard_map/ppermute | solution.py:38
  96.0 1.9 %collective-permute-start.10 = (bf16[19968]{0:T(1024)(128)(2,1)S(1)}, bf16[19968]{0:T(1024)(128)(2,1)S(1)}, u32[]{:S(2)}, u32[]{:S(2)}) collective-permute-start(bf16[19968]{0:T(1024)(128)(2,1)S(1)} %reshape.442), channel_id=1, source_target_pairs={{0,31},{1,2},{2,1},{3,4},{4,3},{5,6},{6,5},{7,8},{8,7},{9,10},{10,... | collective-permute-start | bytes 119816 | tf_op jit(solution)/shard_map/ppermute | solution.py:41
  98.1 3.3 %collective-permute-done.10 = bf16[19968]{0:T(1024)(128)(2,1)S(1)} collective-permute-done((bf16[19968]{0:T(1024)(128)(2,1)S(1)}, bf16[19968]{0:T(1024)(128)(2,1)S(1)}, u32[]{:S(2)}, u32[]{:S(2)}) %collective-permute-start.10) | collective-permute-done | bytes 39968 | tf_op jit(solution)/shard_map/ppermute | solution.py:41
  101.6 0.3 reshape_reshape.7
  102.0 0.3 copy.83
  102.3 0.6 fusion.14
  102.9 0.8 copy.85
  (173 shorter events, 5.2 us)
Async XLA Ops:
  0.0 38.7 %copy-start = (bf16[256,256]{1,0:T(8,128)(2,1)S(1)}, bf16[256,256]{1,0:T(8,128)(2,1)}, u32[]{:S(2)}) copy-start(bf16[256,256]{1,0:T(8,128)(2,1)} %param.27) | copy-start | bytes 393220
  2.5 26.5 %copy-start.3 = (bf16[256,256]{1,0:T(8,128)(2,1)S(1)}, bf16[256,256]{1,0:T(8,128)(2,1)}, u32[]{:S(2)}) copy-start(bf16[256,256]{1,0:T(8,128)(2,1)} %param.26) | copy-start | bytes 393220
  3.4 25.7 %copy-start.4 = (bf16[256,256]{1,0:T(8,128)(2,1)S(1)}, bf16[256,256]{1,0:T(8,128)(2,1)}, u32[]{:S(2)}) copy-start(bf16[256,256]{1,0:T(8,128)(2,1)} %param.25) | copy-start | bytes 393220
  4.4 20.0 %collective-permute-start.1 = (bf16[13056]{0:T(1024)(128)(2,1)S(1)}, bf16[13056]{0:T(1024)(128)(2,1)S(1)}, u32[]{:S(2)}, u32[]{:S(2)}) collective-permute-start(bf16[13056]{0:T(1024)(128)(2,1)S(1)} %get-tuple-element.35), channel_id=1, source_target_pairs={{0,480},{32,0},{64,32},{96,64},{128,96},{160,128},{192,160},{224,1... | collective-permute-start | bytes 78344 | tf_op jit(solution)/shard_map/ppermute | solution.py:24
  18.3 8.2 %collective-permute-start = (bf16[13056]{0:T(1024)(128)(2,1)S(1)}, bf16[13056]{0:T(1024)(128)(2,1)S(1)}, u32[]{:S(2)}, u32[]{:S(2)}) collective-permute-start(bf16[13056]{0:T(1024)(128)(2,1)S(1)} %get-tuple-element.36), channel_id=1, source_target_pairs={{0,32},{32,64},{64,96},{96,128},{128,160},{160,192},{192,224},{224... | collective-permute-start | bytes 78344 | tf_op jit(solution)/shard_map/ppermute | solution.py:24
  21.7 15.7 %copy-start.6 = (s32[3]{0:T(128)S(1)}, s32[3]{0:T(128)}, u32[]{:S(2)}) copy-start(s32[3]{0:T(128)} %constant.82) | copy-start | bytes 40
  27.4 10.8 %copy-start.8 = (bf16[16,256]{1,0:T(8,128)(2,1)S(1)}, bf16[16,256]{1,0:T(8,128)(2,1)}, u32[]{:S(2)}) copy-start(bf16[16,256]{1,0:T(8,128)(2,1)} %param.24) | copy-start | bytes 24580
  29.7 10.8 %collective-permute-start.2 = (bf16[34560]{0:T(1024)(128)(2,1)S(1)}, bf16[34560]{0:T(1024)(128)(2,1)S(1)}, u32[]{:S(2)}, u32[]{:S(2)}) collective-permute-start(bf16[34560]{0:T(1024)(128)(2,1)S(1)} %get-tuple-element.26), channel_id=1, source_target_pairs={{0,31},{1,2},{2,1},{3,4},{4,3},{5,6},{6,5},{7,8},{8,7},{9,10},{10,... | collective-permute-start | bytes 207368 | tf_op jit(solution)/shard_map/ppermute | solution.py:41
  34.0 6.6 %collective-permute-start.3 = (bf16[34560]{0:T(1024)(128)(2,1)S(1)}, bf16[34560]{0:T(1024)(128)(2,1)S(1)}, u32[]{:S(2)}, u32[]{:S(2)}) collective-permute-start(bf16[34560]{0:T(1024)(128)(2,1)S(1)} %get-tuple-element.27), channel_id=1, source_target_pairs={{0,1},{1,0},{2,3},{3,2},{4,5},{5,4},{6,7},{7,6},{8,9},{9,8},{10,11... | collective-permute-start | bytes 207368 | tf_op jit(solution)/shard_map/ppermute | solution.py:38
  38.2 0.9 copy-start.7
  39.1 0.9 copy-start.2
  41.5 2.2 %copy-start.1 = (bf16[9,10752]{1,0:T(8,128)(2,1)}, bf16[9,10752]{1,0:T(8,128)(2,1)S(1)}, u32[]{:S(2)}) copy-start(bf16[9,10752]{1,0:T(8,128)(2,1)S(1)} %reshape.430) | copy-start | bytes 580612
  45.4 0.9 slice-start
  54.8 1.0 copy-start.11
  54.8 1.3 %copy-start.9 = (bf16[13,208,144]{1,2,0:T(8,128)(2,1)}, bf16[13,208,144]{1,2,0:T(8,128)(2,1)S(1)}, u32[]{:S(2)}) copy-start(bf16[13,208,144]{1,2,0:T(8,128)(2,1)S(1)} %get-tuple-element.19) | copy-start | bytes 2336260
  56.3 23.4 %copy-start.10 = (bf16[13,208,144]{1,2,0:T(8,128)(2,1)S(1)}, bf16[13,208,144]{1,2,0:T(8,128)(2,1)}, u32[]{:S(2)}) copy-start(bf16[13,208,144]{1,2,0:T(8,128)(2,1)} %copy-done.9) | copy-start | bytes 2336260
  56.3 23.4 %copy-start.12 = (bf16[13,208,144]{1,2,0:T(8,128)(2,1)S(1)}, bf16[13,208,144]{1,2,0:T(8,128)(2,1)}, u32[]{:S(2)}) copy-start(bf16[13,208,144]{1,2,0:T(8,128)(2,1)} %copy-done.11) | copy-start | bytes 2336260
  56.3 7.6 %collective-permute-start.5 = (bf16[6656]{0:T(1024)(128)(2,1)S(1)}, bf16[6656]{0:T(1024)(128)(2,1)S(1)}, u32[]{:S(2)}, u32[]{:S(2)}) collective-permute-start(bf16[6656]{0:T(1024)(128)(2,1)S(1)} %convert_element_type.214), channel_id=1, source_target_pairs={{0,480},{32,0},{64,32},{96,64},{128,96},{160,128},{192,160},{224,1... | collective-permute-start | bytes 39944 | tf_op jit(solution)/shard_map/ppermute | solution.py:24
  61.9 8.1 %collective-permute-start.4 = (bf16[6656]{0:T(1024)(128)(2,1)S(1)}, bf16[6656]{0:T(1024)(128)(2,1)S(1)}, u32[]{:S(2)}, u32[]{:S(2)}) collective-permute-start(bf16[6656]{0:T(1024)(128)(2,1)S(1)} %convert_element_type.214), channel_id=1, source_target_pairs={{0,32},{32,64},{64,96},{96,128},{128,160},{160,192},{192,224},{224... | collective-permute-start | bytes 39944 | tf_op jit(solution)/shard_map/ppermute | solution.py:24
  70.1 5.6 %collective-permute-start.7 = (bf16[19968]{0:T(1024)(128)(2,1)S(1)}, bf16[19968]{0:T(1024)(128)(2,1)S(1)}, u32[]{:S(2)}, u32[]{:S(2)}) collective-permute-start(bf16[19968]{0:T(1024)(128)(2,1)S(1)} %reshape.439), channel_id=1, source_target_pairs={{0,1},{1,0},{2,3},{3,2},{4,5},{5,4},{6,7},{7,6},{8,9},{9,8},{10,11... | collective-permute-start | bytes 119816 | tf_op jit(solution)/shard_map/ppermute | solution.py:38
  73.5 5.3 %collective-permute-start.6 = (bf16[19968]{0:T(1024)(128)(2,1)S(1)}, bf16[19968]{0:T(1024)(128)(2,1)S(1)}, u32[]{:S(2)}, u32[]{:S(2)}) collective-permute-start(bf16[19968]{0:T(1024)(128)(2,1)S(1)} %reshape.439), channel_id=1, source_target_pairs={{0,31},{1,2},{2,1},{3,4},{4,3},{5,6},{6,5},{7,8},{8,7},{9,10},{10,... | collective-permute-start | bytes 119816 | tf_op jit(solution)/shard_map/ppermute | solution.py:41
  79.7 0.8 copy-start.5
  80.6 5.4 %collective-permute-start.9 = (bf16[6656]{0:T(1024)(128)(2,1)S(1)}, bf16[6656]{0:T(1024)(128)(2,1)S(1)}, u32[]{:S(2)}, u32[]{:S(2)}) collective-permute-start(bf16[6656]{0:T(1024)(128)(2,1)S(1)} %reshape.441), channel_id=1, source_target_pairs={{0,480},{32,0},{64,32},{96,64},{128,96},{160,128},{192,160},{224,1... | collective-permute-start | bytes 39944 | tf_op jit(solution)/shard_map/ppermute | solution.py:24
  82.6 8.1 %collective-permute-start.8 = (bf16[6656]{0:T(1024)(128)(2,1)S(1)}, bf16[6656]{0:T(1024)(128)(2,1)S(1)}, u32[]{:S(2)}, u32[]{:S(2)}) collective-permute-start(bf16[6656]{0:T(1024)(128)(2,1)S(1)} %reshape.441), channel_id=1, source_target_pairs={{0,32},{32,64},{64,96},{96,128},{128,160},{160,192},{192,224},{224... | collective-permute-start | bytes 39944 | tf_op jit(solution)/shard_map/ppermute | solution.py:24
  90.8 7.2 %collective-permute-start.11 = (bf16[19968]{0:T(1024)(128)(2,1)S(1)}, bf16[19968]{0:T(1024)(128)(2,1)S(1)}, u32[]{:S(2)}, u32[]{:S(2)}) collective-permute-start(bf16[19968]{0:T(1024)(128)(2,1)S(1)} %reshape.442), channel_id=1, source_target_pairs={{0,1},{1,0},{2,3},{3,2},{4,5},{5,4},{6,7},{7,6},{8,9},{9,8},{10,11... | collective-permute-start | bytes 119816 | tf_op jit(solution)/shard_map/ppermute | solution.py:38
  96.0 5.3 %collective-permute-start.10 = (bf16[19968]{0:T(1024)(128)(2,1)S(1)}, bf16[19968]{0:T(1024)(128)(2,1)S(1)}, u32[]{:S(2)}, u32[]{:S(2)}) collective-permute-start(bf16[19968]{0:T(1024)(128)(2,1)S(1)} %reshape.442), channel_id=1, source_target_pairs={{0,31},{1,2},{2,1},{3,4},{4,3},{5,6},{6,5},{7,8},{8,7},{9,10},{10,... | collective-permute-start | bytes 119816 | tf_op jit(solution)/shard_map/ppermute | solution.py:41

commit v9 on v6

--- a/solution.py
+++ b/solution.py
@@ -236,12 +236,23 @@
         out = jnp.einsum("qak,qkv->qav", dense_parts, doubled, preferred_element_type=f32)
         return out.sum(axis=0).reshape(orb, atom_count, vec)
 
+    def first_apply(ring_vectors):
+        by_orbital = jnp.swapaxes(ring_vectors.reshape(9, orb, atom_count, vec), 0, 1).reshape(
+            orb, ring, vec
+        )
+        gathered = jnp.einsum("qcv,sc->qvs", by_orbital, column_hot, preferred_element_type=f32)
+        blocks3 = blocks_t.reshape(orb, orb, -1).astype(f32)
+        products = jnp.sum(blocks3[:, :, None, :] * gathered[:, None, :, :], axis=0)
+        parts = jnp.concatenate(bf16_parts(products), axis=0)
+        out = jnp.einsum("pvs,rs->prv", parts, row_hot, preferred_element_type=f32)
+        return out.reshape(3, orb, atom_count, vec).sum(axis=0)
+
     first = jnp.transpose(band_vectors[0, 0], (1, 0, 2))
     previous = first.astype(f32)
     ring_first = jnp.transpose(
         ring_first.reshape(9, atom_count, orb, vec), (0, 2, 1, 3)
     ).reshape(9, -1)
-    current = apply(ring_first)
+    current = first_apply(ring_first)
     for repeat in range(FILTER - 1):
         ring_now = halo(current.astype(bf16).reshape(-1))
         upcoming = 2.0 * apply(ring_now) - previous

time: 103 us -> 134 us (1.30)
  other arithmetic: 7.57 us -> 30.6 us
  matrix products: 15.2 us -> 24.8 us
  waiting for transfers between devices: 23 us -> 17.4 us
  starting transfers between devices: 43.7 us -> 47.6 us
    reduce_sum x0 -> x2, other arithmetic: none -> 13.2 us  [the longest x1 13.1 us: first_apply(): products = jnp.sum(blocks3[:, :, None, :] * gathered[:, None, :, :], axis=0)]
    dot_general x0 -> x2, matrix products: none -> 10.2 us  [the longest x1 6.43 us: first_apply(): out = jnp.einsum('pvs,rs->prv', parts, row_hot, preferred_element_type=f32)]
    ppermute x12, waiting for transfers between devices: 23 us -> 17.4 us  [shifted(): return lax.ppermute(value, axis, pairs)]
    concatenate x0 -> x1, other arithmetic: none -> 5.15 us  [first_apply(): parts = jnp.concatenate(bf16_parts(products), axis=0)]
    ppermute x12, starting transfers between devices: 43.7 us -> 47.6 us  [shifted(): return lax.ppermute(value, axis, pairs)]
    convert_element_type x2 -> x3, other arithmetic: 0.09 us -> 3.13 us  [bf16_parts(): return (high.astype(bf16), middle.astype(bf16), low.astype(bf16))]
    unnamed x33 -> x31, local copies, waits for them, and re-layouts: 3.74 us -> 3.06 us
  transfers between devices with their start and end apart: 12 -> 12, of which waited for: 4 -> 3; matrix products, arithmetic and copies ran while one was open for 8% -> 12% of each run, Pallas kernels for 0% -> 0%
where the time goes in v9:
time: 134 us; the launch traced here: 133 us
  starting transfers between devices  47.6 us (36%)
  other arithmetic  30.6 us (23%)
  matrix products  24.8 us (19%)
  waiting for transfers between devices  17.4 us (13%)
  local copies, waits for them, and re-layouts  11.2 us (8%)
    ppermute x12, starting transfers between devices, shifted(): return lax.ppermute(value, axis, pairs)  47.6 us
    ppermute x12, waiting for transfers between devices, shifted(): return lax.ppermute(value, axis, pairs)  17.4 us
    reduce_sum x1, other arithmetic, first_apply(): products = jnp.sum(blocks3[:, :, None, :] * gathered[:, None, :, :], axis=0)  13.1 us
    dot_general x1, matrix products, first_apply(): out = jnp.einsum('pvs,rs->prv', parts, row_hot, preferred_element_type=f32)  6.43 us
    concatenate x1, other arithmetic, first_apply(): parts = jnp.concatenate(bf16_parts(products), axis=0)  5.15 us
    dot_general x1, matrix products, on_device(): jnp.dot(spread, column_hot, preferred_element_type=f32)  4.88 us
    dot_general x1, matrix products, first_apply(): jnp.einsum('qcv,sc->qvs', by_orbital, column_hot, preferred_element_type=...  3.75 us
    convert_element_type x3, other arithmetic, bf16_parts(): return (high.astype(bf16), middle.astype(bf16), low.astype(bf16))  3.13 us
  transfers between devices with their start and end apart: 12, of which 3 were waited for; matrix products, arithmetic and copies ran while one was open for 12% of the time, Pallas kernels for 0%

profile of v9, /device:TPU:32, one launch (start us, length us, event | category | flops | bytes accessed | tf_op | source)
XLA Modules:
  0.0 132.7 jit_solution(11774214478678818726)
XLA Ops:
  0.0 1.0 fusion.27
  1.0 0.8 fusion.99
  1.8 0.7 fusion.98
  2.5 0.7 constant_dynamic-update-slice_fusion.5
  3.2 0.7 constant_dynamic-update-slice_fusion.4
  4.0 0.8 copy.111
  5.0 4.3 %collective-permute-start = (bf16[13056]{0:T(1024)(128)(2,1)S(1)}, bf16[13056]{0:T(1024)(128)(2,1)S(1)}, u32[]{:S(2)}, u32[]{:S(2)}) collective-permute-start(bf16[13056]{0:T(1024)(128)(2,1)S(1)} %get-tuple-element.37), channel_id=1, source_target_pairs={{0,32},{32,64},{64,96},{96,128},{128,160},{160,192},{192,224},{224... | collective-permute-start | bytes 78344 | tf_op jit(solution)/shard_map/ppermute | solution.py:24
  9.3 11.0 %collective-permute-start.1 = (bf16[13056]{0:T(1024)(128)(2,1)S(1)}, bf16[13056]{0:T(1024)(128)(2,1)S(1)}, u32[]{:S(2)}, u32[]{:S(2)}) collective-permute-start(bf16[13056]{0:T(1024)(128)(2,1)S(1)} %get-tuple-element.38), channel_id=1, source_target_pairs={{0,480},{32,0},{64,32},{96,64},{128,96},{160,128},{192,160},{224,1... | collective-permute-start | bytes 78344 | tf_op jit(solution)/shard_map/ppermute | solution.py:24
  20.4 0.7 copy.193
  21.0 0.7 copy.194
  22.1 1.0 fusion.106
  23.2 0.2 copy.123
  23.5 0.7 constant_dynamic-update-slice_fusion.7
  24.5 0.9 reshape.550
  25.5 0.2 copy.142
  26.1 0.2 pad_maximum_fusion.18
  27.0 1.9 %collective-permute-start.2 = (bf16[34560]{0:T(1024)(128)(2,1)S(1)}, bf16[34560]{0:T(1024)(128)(2,1)S(1)}, u32[]{:S(2)}, u32[]{:S(2)}) collective-permute-start(bf16[34560]{0:T(1024)(128)(2,1)S(1)} %get-tuple-element.32), channel_id=1, source_target_pairs={{0,1},{1,2},{2,3},{3,4},{4,5},{5,6},{6,7},{7,8},{8,9},{9,10},{10,1... | collective-permute-start | bytes 207368 | tf_op jit(solution)/shard_map/ppermute | solution.py:24
  28.9 5.8 %collective-permute-start.3 = (bf16[34560]{0:T(1024)(128)(2,1)S(1)}, bf16[34560]{0:T(1024)(128)(2,1)S(1)}, u32[]{:S(2)}, u32[]{:S(2)}) collective-permute-start(bf16[34560]{0:T(1024)(128)(2,1)S(1)} %get-tuple-element.33), channel_id=1, source_target_pairs={{0,31},{1,0},{2,1},{3,2},{4,3},{5,4},{6,5},{7,6},{8,7},{9,8},{10,9... | collective-permute-start | bytes 207368 | tf_op jit(solution)/shard_map/ppermute | solution.py:24
  34.8 0.6 fusion.42
  35.4 0.5 multiply_convert_fusion.1
  36.0 0.3 fusion.102
  36.3 0.3 fusion.15
  36.7 0.5 copy-done.3
  37.2 0.2 convolution_bitcast_fusion.2
  37.5 0.2 convolution_bitcast_fusion.3
  37.8 0.8 fusion.32
  39.1 0.2 pad_maximum_fusion.14
  39.4 0.2 reshape.554
  39.7 0.2 fusion.104
  39.9 0.2 fusion.103
  40.2 1.6 %fusion.5 = f32[1536,768]{1,0:T(8,128)S(1)} fusion(s32[1536]{0:T(1024)S(1)} %add_add_fusion, s32[1536]{0:T(1024)S(1)} %pad_add_fusion, bf16[288,256]{1,0:T(8,128)(2,1)S(1)} %get-tuple-element.28, bf16[288,256]{1,0:T(8,128)(2,1)S(1)} %get-tuple-element.27, bf16[288,256]{1,0:T(8,128)(2,1)S(1)} %get-tuple-element.26), kind=kOutput, calls=%fused_computation.18 | convolution fusion | flops 682131456 | bytes 5173248 | tf_op jit(solution)/shard_map/dot_general | solution.py:175
  41.8 0.8 multiply_convert_fusion
  42.6 0.4 fusion.105
  42.9 0.5 fusion.3
  43.5 0.3 convolution_bitcast_fusion.1
  43.8 0.3 convolution_bitcast_fusion
  44.2 0.3 slice-done
  44.4 1.4 %reshape.561 = bf16[9,16,13,32]{3,2,1,0:T(8,128)(2,1)} reshape(bf16[9,6656]{1,0:T(8,128)(2,1)S(1)} %slice-done) | data formatting | bytes 239616 | tf_op jit(solution)/shard_map/reshape | solution.py:253
  46.1 3.7 %fusion.10 = f32[13,32,2320]{2,1,0:T(8,128)} fusion(s32[2320]{0:T(1024)} %copy-done.7, bf16[13,144,32]{2,0,1:T(8,128)(2,1)} %bitcast.194), kind=kOutput, calls=%fused_computation.27 | convolution fusion | flops 278288640 | bytes 3989568 | tf_op jit(solution)/shard_map/qcv,sc->qvs/dot_general | solution.py:243
  50.1 13.1 %multiply_reduce_fusion = f32[13,32,2320]{2,1,0:T(8,128)} fusion(f32[13,32,2320]{2,1,0:T(8,128)} %fusion.10, f32[13,13,2320]{2,1,0:T(8,128)S(1)} %maximum_convert_fusion), kind=kLoop, calls=%fused_computation | loop fusion | flops 24128000 | bytes 9289280 | tf_op jit(solution)/shard_map/reduce_sum | solution.py:245
  63.2 3.0 %reduce-precision_convert_fusion.1 = (bf16[13,32,2320]{2,1,0:T(8,128)(2,1)S(1)}, bf16[13,32,2320]{2,1,0:T(8,128)(2,1)S(1)}, bf16[13,32,2320]{2,1,0:T(8,128)(2,1)S(1)}) fusion(f32[13,32,2320]{2,1,0:T(8,128)} %multiply_reduce_fusion), kind=kLoop, calls=%fused_computation.8 | loop fusion | flops 6755840 | bytes 9651200 | tf_op jit(solution)/shard_map/convert_element_type | solution.py:32
  66.3 5.1 %pad_maximum_fusion = bf16[39,32,2320]{2,1,0:T(8,128)(2,1)} fusion(bf16[13,32,2320]{2,1,0:T(8,128)(2,1)S(1)} %get-tuple-element.22, bf16[13,32,2320]{2,1,0:T(8,128)(2,1)S(1)} %get-tuple-element.23, bf16[13,32,2320]{2,1,0:T(8,128)(2,1)S(1)} %get-tuple-element.21), kind=kLoop, calls=%fused_computation.4 | loop fusion | flops 5790720 | bytes 11581440 | tf_op jit(solution)/shard_map/concatenate | solution.py:246
  71.4 6.4 %fusion.20 = f32[39,16,32]{0,1,2:T(8,128)S(1)} fusion(bf16[39,32,2320]{2,1,0:T(8,128)(2,1)} %pad_maximum_fusion, s32[2320]{0:T(1024)S(1)} %constant_dynamic-update-slice_fusion.8), kind=kOutput, calls=%fused_computation.42 | convolution fusion | flops 92688640 | bytes 5879872 | tf_op jit(solution)/shard_map/pvs,rs->prv/dot_general | solution.py:247
  77.8 0.3 copy.130
  78.3 3.9 %collective-permute-start.5 = (bf16[6656]{0:T(1024)(128)(2,1)S(1)}, bf16[6656]{0:T(1024)(128)(2,1)S(1)}, u32[]{:S(2)}, u32[]{:S(2)}) collective-permute-start(bf16[6656]{0:T(1024)(128)(2,1)S(1)} %convert_element_type.299), channel_id=1, source_target_pairs={{0,480},{32,0},{64,32},{96,64},{128,96},{160,128},{192,160},{224,1... | collective-permute-start | bytes 39944 | tf_op jit(solution)/shard_map/ppermute | solution.py:24
  82.2 1.9 %collective-permute-start.4 = (bf16[6656]{0:T(1024)(128)(2,1)S(1)}, bf16[6656]{0:T(1024)(128)(2,1)S(1)}, u32[]{:S(2)}, u32[]{:S(2)}) collective-permute-start(bf16[6656]{0:T(1024)(128)(2,1)S(1)} %convert_element_type.299), channel_id=1, source_target_pairs={{0,32},{32,64},{64,96},{96,128},{128,160},{160,192},{192,224},{224... | collective-permute-start | bytes 39944 | tf_op jit(solution)/shard_map/ppermute | solution.py:24
  84.2 2.4 %broadcast_multiply_fusion = bf16[169,16,2320]{2,1,0:T(8,128)(2,1)S(1)} fusion(bf16[16,2320]{1,0:T(8,128)(2,1)S(1)} %fusion.56, bf16[169,2320]{1,0:T(8,128)(2,1)S(1)} %pad_maximum_fusion.12), kind=kLoop, calls=%fused_computation.1 | loop fusion | flops 6273280 | bytes 13404960 | tf_op jit(solution)/shard_map/mul | solution.py:223
  86.6 4.9 %reduce-precision_convert_fusion.2 = (bf16[13,208,144]{1,2,0:T(8,128)(2,1)S(1)}, bf16[13,208,144]{1,2,0:T(8,128)(2,1)S(1)}) fusion(bf16[13,208,2320]{2,1,0:T(8,128)(2,1)S(1)} %bitcast.193, s32[2320]{0:T(1024)S(1)} %copy-done.8), kind=kOutput, calls=%fused_computation.13 | convolution fusion | flops 1808985600 | bytes 14113344 | tf_op jit(solution)/shard_map/dot_general | solution.py:225
  91.9 3.0 %collective-permute-start.7 = (bf16[19968]{0:T(1024)(128)(2,1)S(1)}, bf16[19968]{0:T(1024)(128)(2,1)S(1)}, u32[]{:S(2)}, u32[]{:S(2)}) collective-permute-start(bf16[19968]{0:T(1024)(128)(2,1)S(1)} %reshape.564), channel_id=1, source_target_pairs={{0,31},{1,0},{2,1},{3,2},{4,3},{5,4},{6,5},{7,6},{8,7},{9,8},{10,9... | collective-permute-start | bytes 119816 | tf_op jit(solution)/shard_map/ppermute | solution.py:24
  94.9 1.9 %collective-permute-start.6 = (bf16[19968]{0:T(1024)(128)(2,1)S(1)}, bf16[19968]{0:T(1024)(128)(2,1)S(1)}, u32[]{:S(2)}, u32[]{:S(2)}) collective-permute-start(bf16[19968]{0:T(1024)(128)(2,1)S(1)} %reshape.564), channel_id=1, source_target_pairs={{0,1},{1,2},{2,3},{3,4},{4,5},{5,6},{6,7},{7,8},{8,9},{9,10},{10,1... | collective-permute-start | bytes 119816 | tf_op jit(solution)/shard_map/ppermute | solution.py:24
  97.0 5.4 %collective-permute-done.6 = bf16[19968]{0:T(1024)(128)(2,1)S(1)} collective-permute-done((bf16[19968]{0:T(1024)(128)(2,1)S(1)}, bf16[19968]{0:T(1024)(128)(2,1)S(1)}, u32[]{:S(2)}, u32[]{:S(2)}) %collective-permute-start.6) | collective-permute-done | bytes 39968 | tf_op jit(solution)/shard_map/ppermute | solution.py:24
  102.6 0.3 reshape_reshape.6
  102.9 0.3 copy.133
  103.2 0.6 fusion.25
  104.2 7.5 %collective-permute-start.9 = (bf16[6656]{0:T(1024)(128)(2,1)S(1)}, bf16[6656]{0:T(1024)(128)(2,1)S(1)}, u32[]{:S(2)}, u32[]{:S(2)}) collective-permute-start(bf16[6656]{0:T(1024)(128)(2,1)S(1)} %reshape.566), channel_id=1, source_target_pairs={{0,480},{32,0},{64,32},{96,64},{128,96},{160,128},{192,160},{224,1... | collective-permute-start | bytes 39944 | tf_op jit(solution)/shard_map/ppermute | solution.py:24
  111.7 1.9 %collective-permute-start.8 = (bf16[6656]{0:T(1024)(128)(2,1)S(1)}, bf16[6656]{0:T(1024)(128)(2,1)S(1)}, u32[]{:S(2)}, u32[]{:S(2)}) collective-permute-start(bf16[6656]{0:T(1024)(128)(2,1)S(1)} %reshape.566), channel_id=1, source_target_pairs={{0,32},{32,64},{64,96},{96,128},{128,160},{160,192},{192,224},{224... | collective-permute-start | bytes 39944 | tf_op jit(solution)/shard_map/ppermute | solution.py:24
  113.7 7.2 %collective-permute-done.8 = bf16[6656]{0:T(1024)(128)(2,1)S(1)} collective-permute-done((bf16[6656]{0:T(1024)(128)(2,1)S(1)}, bf16[6656]{0:T(1024)(128)(2,1)S(1)}, u32[]{:S(2)}, u32[]{:S(2)}) %collective-permute-start.8) | collective-permute-done | bytes 13344 | tf_op jit(solution)/shard_map/ppermute | solution.py:24
  121.1 1.9 %collective-permute-start.11 = (bf16[19968]{0:T(1024)(128)(2,1)S(1)}, bf16[19968]{0:T(1024)(128)(2,1)S(1)}, u32[]{:S(2)}, u32[]{:S(2)}) collective-permute-start(bf16[19968]{0:T(1024)(128)(2,1)S(1)} %reshape.567), channel_id=1, source_target_pairs={{0,31},{1,0},{2,1},{3,2},{4,3},{5,4},{6,5},{7,6},{8,7},{9,8},{10,9... | collective-permute-start | bytes 119816 | tf_op jit(solution)/shard_map/ppermute | solution.py:24
  123.0 2.4 %collective-permute-start.10 = (bf16[19968]{0:T(1024)(128)(2,1)S(1)}, bf16[19968]{0:T(1024)(128)(2,1)S(1)}, u32[]{:S(2)}, u32[]{:S(2)}) collective-permute-start(bf16[19968]{0:T(1024)(128)(2,1)S(1)} %reshape.567), channel_id=1, source_target_pairs={{0,1},{1,2},{2,3},{3,4},{4,5},{5,6},{6,7},{7,8},{8,9},{9,10},{10,1... | collective-permute-start | bytes 119816 | tf_op jit(solution)/shard_map/ppermute | solution.py:24
  125.6 4.9 %collective-permute-done.10 = bf16[19968]{0:T(1024)(128)(2,1)S(1)} collective-permute-done((bf16[19968]{0:T(1024)(128)(2,1)S(1)}, bf16[19968]{0:T(1024)(128)(2,1)S(1)}, u32[]{:S(2)}, u32[]{:S(2)}) %collective-permute-start.10) | collective-permute-done | bytes 39968 | tf_op jit(solution)/shard_map/ppermute | solution.py:24
  130.7 0.3 reshape_reshape.7
  131.0 0.3 copy.138
  131.3 0.6 fusion.26
  132.0 0.7 subtract_bitcast_fusion
  (173 shorter events, 5.6 us)
Async XLA Ops:
  0.0 35.9 %copy-start = (bf16[256,256]{1,0:T(8,128)(2,1)S(1)}, bf16[256,256]{1,0:T(8,128)(2,1)}, u32[]{:S(2)}) copy-start(bf16[256,256]{1,0:T(8,128)(2,1)} %param.27) | copy-start | bytes 393220
  0.0 26.6 %copy-start.4 = (bf16[256,256]{1,0:T(8,128)(2,1)S(1)}, bf16[256,256]{1,0:T(8,128)(2,1)}, u32[]{:S(2)}) copy-start(bf16[256,256]{1,0:T(8,128)(2,1)} %param.26) | copy-start | bytes 393220
  0.0 26.8 %copy-start.5 = (bf16[256,256]{1,0:T(8,128)(2,1)S(1)}, bf16[256,256]{1,0:T(8,128)(2,1)}, u32[]{:S(2)}) copy-start(bf16[256,256]{1,0:T(8,128)(2,1)} %param.25) | copy-start | bytes 393220
  4.0 30.7 %copy-start.9 = (s32[3]{0:T(128)S(1)}, s32[3]{0:T(128)}, u32[]{:S(2)}) copy-start(s32[3]{0:T(128)} %constant.54) | copy-start | bytes 40
  5.0 20.8 %collective-permute-start = (bf16[13056]{0:T(1024)(128)(2,1)S(1)}, bf16[13056]{0:T(1024)(128)(2,1)S(1)}, u32[]{:S(2)}, u32[]{:S(2)}) collective-permute-start(bf16[13056]{0:T(1024)(128)(2,1)S(1)} %get-tuple-element.37), channel_id=1, source_target_pairs={{0,32},{32,64},{64,96},{96,128},{128,160},{160,192},{192,224},{224... | collective-permute-start | bytes 78344 | tf_op jit(solution)/shard_map/ppermute | solution.py:24
  9.3 16.5 %collective-permute-start.1 = (bf16[13056]{0:T(1024)(128)(2,1)S(1)}, bf16[13056]{0:T(1024)(128)(2,1)S(1)}, u32[]{:S(2)}, u32[]{:S(2)}) collective-permute-start(bf16[13056]{0:T(1024)(128)(2,1)S(1)} %get-tuple-element.38), channel_id=1, source_target_pairs={{0,480},{32,0},{64,32},{96,64},{128,96},{160,128},{192,160},{224,1... | collective-permute-start | bytes 78344 | tf_op jit(solution)/shard_map/ppermute | solution.py:24
  26.3 9.1 %copy-start.11 = (bf16[16,256]{1,0:T(8,128)(2,1)S(1)}, bf16[16,256]{1,0:T(8,128)(2,1)}, u32[]{:S(2)}) copy-start(bf16[16,256]{1,0:T(8,128)(2,1)} %param.24) | copy-start | bytes 24580
  27.0 11.7 %collective-permute-start.2 = (bf16[34560]{0:T(1024)(128)(2,1)S(1)}, bf16[34560]{0:T(1024)(128)(2,1)S(1)}, u32[]{:S(2)}, u32[]{:S(2)}) collective-permute-start(bf16[34560]{0:T(1024)(128)(2,1)S(1)} %get-tuple-element.32), channel_id=1, source_target_pairs={{0,1},{1,2},{2,3},{3,4},{4,5},{5,6},{6,7},{7,8},{8,9},{9,10},{10,1... | collective-permute-start | bytes 207368 | tf_op jit(solution)/shard_map/ppermute | solution.py:24
  28.9 9.8 %collective-permute-start.3 = (bf16[34560]{0:T(1024)(128)(2,1)S(1)}, bf16[34560]{0:T(1024)(128)(2,1)S(1)}, u32[]{:S(2)}, u32[]{:S(2)}) collective-permute-start(bf16[34560]{0:T(1024)(128)(2,1)S(1)} %get-tuple-element.33), channel_id=1, source_target_pairs={{0,31},{1,0},{2,1},{3,2},{4,3},{5,4},{6,5},{7,6},{8,7},{9,8},{10,9... | collective-permute-start | bytes 207368 | tf_op jit(solution)/shard_map/ppermute | solution.py:24
  35.4 0.9 copy-start.10
  36.3 0.9 copy-start.3
  39.6 2.2 %copy-start.1 = (bf16[9,10752]{1,0:T(8,128)(2,1)}, bf16[9,10752]{1,0:T(8,128)(2,1)S(1)}, u32[]{:S(2)}) copy-start(bf16[9,10752]{1,0:T(8,128)(2,1)S(1)} %reshape.554) | copy-start | bytes 580612
  43.5 0.9 slice-start
  44.1 1.7 %copy-start.7 = (s32[2320]{0:T(1024)}, s32[2320]{0:T(1024)S(1)}, u32[]{:S(2)}) copy-start(s32[2320]{0:T(1024)S(1)} %constant_dynamic-update-slice_fusion.9) | copy-start | bytes 27844
  71.4 12.7 %copy-start.2 = (bf16[169,768]{1,0:T(8,128)(2,1)S(1)}, bf16[169,768]{1,0:T(8,128)(2,1)}, u32[]{:S(2)}) copy-start(bf16[169,768]{1,0:T(8,128)(2,1)} %fusion.32) | copy-start | bytes 778756
  78.3 13.4 %collective-permute-start.5 = (bf16[6656]{0:T(1024)(128)(2,1)S(1)}, bf16[6656]{0:T(1024)(128)(2,1)S(1)}, u32[]{:S(2)}, u32[]{:S(2)}) collective-permute-start(bf16[6656]{0:T(1024)(128)(2,1)S(1)} %convert_element_type.299), channel_id=1, source_target_pairs={{0,480},{32,0},{64,32},{96,64},{128,96},{160,128},{192,160},{224,1... | collective-permute-start | bytes 39944 | tf_op jit(solution)/shard_map/ppermute | solution.py:24
  82.2 9.5 %collective-permute-start.4 = (bf16[6656]{0:T(1024)(128)(2,1)S(1)}, bf16[6656]{0:T(1024)(128)(2,1)S(1)}, u32[]{:S(2)}, u32[]{:S(2)}) collective-permute-start(bf16[6656]{0:T(1024)(128)(2,1)S(1)} %convert_element_type.299), channel_id=1, source_target_pairs={{0,32},{32,64},{64,96},{96,128},{128,160},{160,192},{192,224},{224... | collective-permute-start | bytes 39944 | tf_op jit(solution)/shard_map/ppermute | solution.py:24
  84.2 2.4 %copy-start.8 = (s32[2320]{0:T(1024)S(1)}, s32[2320]{0:T(1024)}, u32[]{:S(2)}) copy-start(s32[2320]{0:T(1024)} %copy-done.7) | copy-start | bytes 27844
  91.9 5.1 %collective-permute-start.7 = (bf16[19968]{0:T(1024)(128)(2,1)S(1)}, bf16[19968]{0:T(1024)(128)(2,1)S(1)}, u32[]{:S(2)}, u32[]{:S(2)}) collective-permute-start(bf16[19968]{0:T(1024)(128)(2,1)S(1)} %reshape.564), channel_id=1, source_target_pairs={{0,31},{1,0},{2,1},{3,2},{4,3},{5,4},{6,5},{7,6},{8,7},{9,8},{10,9... | collective-permute-start | bytes 119816 | tf_op jit(solution)/shard_map/ppermute | solution.py:24
  94.9 7.4 %collective-permute-start.6 = (bf16[19968]{0:T(1024)(128)(2,1)S(1)}, bf16[19968]{0:T(1024)(128)(2,1)S(1)}, u32[]{:S(2)}, u32[]{:S(2)}) collective-permute-start(bf16[19968]{0:T(1024)(128)(2,1)S(1)} %reshape.564), channel_id=1, source_target_pairs={{0,1},{1,2},{2,3},{3,4},{4,5},{5,6},{6,7},{7,8},{8,9},{9,10},{10,1... | collective-permute-start | bytes 119816 | tf_op jit(solution)/shard_map/ppermute | solution.py:24
  103.2 0.8 copy-start.6
  104.2 9.6 %collective-permute-start.9 = (bf16[6656]{0:T(1024)(128)(2,1)S(1)}, bf16[6656]{0:T(1024)(128)(2,1)S(1)}, u32[]{:S(2)}, u32[]{:S(2)}) collective-permute-start(bf16[6656]{0:T(1024)(128)(2,1)S(1)} %reshape.566), channel_id=1, source_target_pairs={{0,480},{32,0},{64,32},{96,64},{128,96},{160,128},{192,160},{224,1... | collective-permute-start | bytes 39944 | tf_op jit(solution)/shard_map/ppermute | solution.py:24
  111.7 9.2 %collective-permute-start.8 = (bf16[6656]{0:T(1024)(128)(2,1)S(1)}, bf16[6656]{0:T(1024)(128)(2,1)S(1)}, u32[]{:S(2)}, u32[]{:S(2)}) collective-permute-start(bf16[6656]{0:T(1024)(128)(2,1)S(1)} %reshape.566), channel_id=1, source_target_pairs={{0,32},{32,64},{64,96},{96,128},{128,160},{160,192},{192,224},{224... | collective-permute-start | bytes 39944 | tf_op jit(solution)/shard_map/ppermute | solution.py:24
  121.1 4.5 %collective-permute-start.11 = (bf16[19968]{0:T(1024)(128)(2,1)S(1)}, bf16[19968]{0:T(1024)(128)(2,1)S(1)}, u32[]{:S(2)}, u32[]{:S(2)}) collective-permute-start(bf16[19968]{0:T(1024)(128)(2,1)S(1)} %reshape.567), channel_id=1, source_target_pairs={{0,31},{1,0},{2,1},{3,2},{4,3},{5,4},{6,5},{7,6},{8,7},{9,8},{10,9... | collective-permute-start | bytes 119816 | tf_op jit(solution)/shard_map/ppermute | solution.py:24
  123.0 7.4 %collective-permute-start.10 = (bf16[19968]{0:T(1024)(128)(2,1)S(1)}, bf16[19968]{0:T(1024)(128)(2,1)S(1)}, u32[]{:S(2)}, u32[]{:S(2)}) collective-permute-start(bf16[19968]{0:T(1024)(128)(2,1)S(1)} %reshape.567), channel_id=1, source_target_pairs={{0,1},{1,2},{2,3},{3,4},{4,5},{5,6},{6,7},{7,8},{8,9},{9,10},{10,1... | collective-permute-start | bytes 119816 | tf_op jit(solution)/shard_map/ppermute | solution.py:24

commit v10 on v6

--- a/solution.py
+++ b/solution.py
@@ -225,15 +225,13 @@
     dense = jnp.dot(spread, column_hot, preferred_element_type=f32).reshape(
         orb, orb * atom_count, ring
     )
-    dense_high, dense_middle, _ = bf16_parts(dense)
-    dense_parts = jnp.concatenate([dense_high, dense_middle], axis=2)
+    dense_parts = dense.astype(bf16)
 
     def apply(ring_vectors):
         by_orbital = jnp.swapaxes(ring_vectors.reshape(9, orb, atom_count, vec), 0, 1).reshape(
             orb, ring, vec
         )
-        doubled = jnp.concatenate([by_orbital, by_orbital], axis=1)
-        out = jnp.einsum("qak,qkv->qav", dense_parts, doubled, preferred_element_type=f32)
+        out = jnp.einsum("qak,qkv->qav", dense_parts, by_orbital, preferred_element_type=f32)
         return out.sum(axis=0).reshape(orb, atom_count, vec)
 
     first = jnp.transpose(band_vectors[0, 0], (1, 0, 2))

time: 103 us -> 101 us (0.981)
  the two profiles are of different devices: /device:TPU:32 before, /device:TPU:27 now
where the time goes in v10:
time: 101 us
  starting transfers between devices  50.4 us (50%)
  waiting for transfers between devices  17.6 us (17%)
  matrix products  15.6 us (15%)
  local copies, waits for them, and re-layouts  9.12 us (9%)
  other arithmetic  6.88 us (7%)
    ppermute x12, starting transfers between devices, shifted(): return lax.ppermute(value, axis, pairs)  50.4 us
    ppermute x12, waiting for transfers between devices, shifted(): return lax.ppermute(value, axis, pairs)  17.6 us
    dot_general x1, matrix products, on_device(): jnp.dot(spread, column_hot, preferred_element_type=f32)  4.85 us
    mul x1, other arithmetic, on_device(): blocks_t[:, None, :] * row_hot[None, :, :]  2.42 us
    unnamed x25, local copies, waits for them, and re-layouts  2.39 us
    dot_general x3, matrix products, apply(): jnp.einsum('qak,qkv->qav', dense_parts, by_orbital, preferred_element_typ...  2.21 us
    dot_general x2, matrix products, group_blocks(): picked = jnp.dot(pick, table_parts, preferred_element_type=f32)  2.15 us
  transfers between devices with their start and end apart: 12, of which 5 were waited for; matrix products, arithmetic and copies ran while one was open for 4% of the time, Pallas kernels for 0%

profile of v10, /device:TPU:27, one launch (start us, length us, event | category | flops | bytes accessed | tf_op | source)
XLA Modules:
  0.0 100.5 jit_solution(11845338869898814999)
XLA Ops:
  0.0 0.8 fusion.74
  0.8 0.8 fusion.75
  1.5 0.7 constant_dynamic-update-slice_fusion.5
  2.2 0.7 constant_dynamic-update-slice_fusion.4
  3.1 0.9 fusion.18
  4.0 0.8 copy.74
  4.8 0.1 reshape_squeeze.12
  5.0 4.1 %collective-permute-start = (bf16[13056]{0:T(1024)(128)(2,1)S(1)}, bf16[13056]{0:T(1024)(128)(2,1)S(1)}, u32[]{:S(2)}, u32[]{:S(2)}) collective-permute-start(bf16[13056]{0:T(1024)(128)(2,1)S(1)} %get-tuple-element.32), channel_id=1, source_target_pairs={{0,32},{32,64},{64,96},{96,128},{128,160},{160,192},{192,224},{224... | collective-permute-start | bytes 78344 | tf_op jit(solution)/shard_map/ppermute | solution.py:24
  9.1 10.1 %collective-permute-start.1 = (bf16[13056]{0:T(1024)(128)(2,1)S(1)}, bf16[13056]{0:T(1024)(128)(2,1)S(1)}, u32[]{:S(2)}, u32[]{:S(2)}) collective-permute-start(bf16[13056]{0:T(1024)(128)(2,1)S(1)} %get-tuple-element.33), channel_id=1, source_target_pairs={{0,480},{32,0},{64,32},{96,64},{128,96},{160,128},{192,160},{224,1... | collective-permute-start | bytes 78344 | tf_op jit(solution)/shard_map/ppermute | solution.py:24
  19.3 0.7 copy.156
  20.0 0.7 copy.155
  21.0 1.0 %fusion.83 = f32[16,169]{1,0:T(8,128)S(1)} fusion(bf16[16,256]{1,0:T(8,128)(2,1)S(1)} %fusion.18, bf16[256,169]{0,1:T(8,128)(2,1)} %param.30), kind=kOutput, calls=%fused_computation.202 | convolution fusion | flops 1384448 | bytes 105536 | tf_op jit(solution)/shard_map/dot_general | solution.py:196
  22.0 0.1 reshape.488
  22.2 0.2 copy.86
  22.9 0.2 copy.101
  23.5 0.2 pad_maximum_fusion.6
  23.8 0.2 fusion.117
  24.0 0.1 fusion.77
  24.2 0.2 fusion.78
  24.5 0.6 fusion.31
  25.1 0.5 multiply_convert_fusion.1
  25.6 0.3 fusion.79
  25.9 0.1 copy-done.7
  26.0 0.3 fusion.9
  26.3 0.2 convolution_bitcast_fusion.2
  26.6 0.2 convolution_bitcast_fusion.3
  26.8 6.1 %collective-permute-start.2 = (bf16[34560]{0:T(1024)(128)(2,1)S(1)}, bf16[34560]{0:T(1024)(128)(2,1)S(1)}, u32[]{:S(2)}, u32[]{:S(2)}) collective-permute-start(bf16[34560]{0:T(1024)(128)(2,1)S(1)} %get-tuple-element.27), channel_id=1, source_target_pairs={{0,1},{1,2},{2,3},{3,4},{4,5},{5,6},{6,7},{7,8},{8,9},{9,10},{10,1... | collective-permute-start | bytes 207368 | tf_op jit(solution)/shard_map/ppermute | solution.py:24
  33.0 2.1 %collective-permute-start.3 = (bf16[34560]{0:T(1024)(128)(2,1)S(1)}, bf16[34560]{0:T(1024)(128)(2,1)S(1)}, u32[]{:S(2)}, u32[]{:S(2)}) collective-permute-start(bf16[34560]{0:T(1024)(128)(2,1)S(1)} %get-tuple-element.28), channel_id=1, source_target_pairs={{0,31},{1,0},{2,1},{3,2},{4,3},{5,4},{6,5},{7,6},{8,7},{9,8},{10,9... | collective-permute-start | bytes 207368 | tf_op jit(solution)/shard_map/ppermute | solution.py:24
  35.3 5.4 %collective-permute-done.3 = bf16[34560]{0:T(1024)(128)(2,1)S(1)} collective-permute-done((bf16[34560]{0:T(1024)(128)(2,1)S(1)}, bf16[34560]{0:T(1024)(128)(2,1)S(1)}, u32[]{:S(2)}, u32[]{:S(2)}) %collective-permute-start.3) | collective-permute-done | bytes 69152 | tf_op jit(solution)/shard_map/ppermute | solution.py:24
  40.8 0.2 pad_maximum_fusion.2
  41.0 0.1 copy.85
  41.1 0.2 reshape.485
  41.4 0.2 fusion.80
  41.5 0.2 fusion.81
  42.2 1.6 %fusion.2 = f32[1536,768]{1,0:T(8,128)S(1)} fusion(s32[1536]{0:T(1024)S(1)} %add_add_fusion, s32[1536]{0:T(1024)S(1)} %pad_add_fusion, bf16[288,256]{1,0:T(8,128)(2,1)S(1)} %get-tuple-element.23, bf16[288,256]{1,0:T(8,128)(2,1)S(1)} %get-tuple-element.22, bf16[288,256]{1,0:T(8,128)(2,1)S(1)} %get-tuple-element.21), kind=kOutput, calls=%fused_computation.7 | convolution fusion | flops 682131456 | bytes 5173248 | tf_op jit(solution)/shard_map/dot_general | solution.py:175
  43.8 0.8 multiply_convert_fusion
  44.5 0.4 fusion.82
  44.9 0.5 fusion
  45.4 0.3 convolution_bitcast_fusion.1
  45.7 0.3 convolution_bitcast_fusion
  46.2 2.4 %broadcast_multiply_fusion = bf16[169,16,2320]{2,1,0:T(8,128)(2,1)S(1)} fusion(bf16[16,2320]{1,0:T(8,128)(2,1)S(1)} %fusion.38, bf16[169,2320]{1,0:T(8,128)(2,1)S(1)} %pad_maximum_fusion), kind=kLoop, calls=%fused_computation | loop fusion | flops 6273280 | bytes 13404960 | tf_op jit(solution)/shard_map/mul | solution.py:223
  48.7 4.8 %fusion.6 = bf16[208,144,13]{0,1,2:T(8,128)(2,1)S(1)} fusion(bf16[13,208,2320]{2,1,0:T(8,128)(2,1)S(1)} %bitcast.210, s32[2320]{0:T(1024)S(1)} %constant_dynamic-update-slice_fusion.9), kind=kOutput, calls=%fused_computation.14 | convolution fusion | flops 1807428096 | bytes 13334592 | tf_op jit(solution)/shard_map/dot_general | solution.py:225
  53.5 1.8 %copy.89 = bf16[208,144,13]{1,0,2:T(8,128)(2,1)S(1)} copy(bf16[208,144,13]{0,1,2:T(8,128)(2,1)S(1)} %fusion.6) | data formatting | bytes 1557504 | tf_op jit(solution)/shard_map/convert_element_type | solution.py:228
  55.3 0.6 reshape.492
  55.9 0.5 fusion.76
  56.6 1.9 %collective-permute-start.4 = (bf16[6656]{0:T(1024)(128)(2,1)S(1)}, bf16[6656]{0:T(1024)(128)(2,1)S(1)}, u32[]{:S(2)}, u32[]{:S(2)}) collective-permute-start(bf16[6656]{0:T(1024)(128)(2,1)S(1)} %reshape.494), channel_id=1, source_target_pairs={{0,32},{32,64},{64,96},{96,128},{128,160},{160,192},{192,224},{224... | collective-permute-start | bytes 39944 | tf_op jit(solution)/shard_map/ppermute | solution.py:24
  58.5 7.0 %collective-permute-start.5 = (bf16[6656]{0:T(1024)(128)(2,1)S(1)}, bf16[6656]{0:T(1024)(128)(2,1)S(1)}, u32[]{:S(2)}, u32[]{:S(2)}) collective-permute-start(bf16[6656]{0:T(1024)(128)(2,1)S(1)} %reshape.494), channel_id=1, source_target_pairs={{0,480},{32,0},{64,32},{96,64},{128,96},{160,128},{192,160},{224,1... | collective-permute-start | bytes 39944 | tf_op jit(solution)/shard_map/ppermute | solution.py:24
  65.6 0.7 collective-permute-done.5
  66.3 0.1 pad_maximum_fusion.9
  66.5 3.0 %collective-permute-start.6 = (bf16[19968]{0:T(1024)(128)(2,1)S(1)}, bf16[19968]{0:T(1024)(128)(2,1)S(1)}, u32[]{:S(2)}, u32[]{:S(2)}) collective-permute-start(bf16[19968]{0:T(1024)(128)(2,1)S(1)} %reshape.495), channel_id=1, source_target_pairs={{0,1},{1,2},{2,3},{3,4},{4,5},{5,6},{6,7},{7,8},{8,9},{9,10},{10,1... | collective-permute-start | bytes 119816 | tf_op jit(solution)/shard_map/ppermute | solution.py:24
  69.5 1.9 %collective-permute-start.7 = (bf16[19968]{0:T(1024)(128)(2,1)S(1)}, bf16[19968]{0:T(1024)(128)(2,1)S(1)}, u32[]{:S(2)}, u32[]{:S(2)}) collective-permute-start(bf16[19968]{0:T(1024)(128)(2,1)S(1)} %reshape.495), channel_id=1, source_target_pairs={{0,31},{1,0},{2,1},{3,2},{4,3},{5,4},{6,5},{7,6},{8,7},{9,8},{10,9... | collective-permute-start | bytes 119816 | tf_op jit(solution)/shard_map/ppermute | solution.py:24
  71.5 5.4 %collective-permute-done.7 = bf16[19968]{0:T(1024)(128)(2,1)S(1)} collective-permute-done((bf16[19968]{0:T(1024)(128)(2,1)S(1)}, bf16[19968]{0:T(1024)(128)(2,1)S(1)}, u32[]{:S(2)}, u32[]{:S(2)}) %collective-permute-start.7) | collective-permute-done | bytes 39968 | tf_op jit(solution)/shard_map/ppermute | solution.py:24
  76.9 0.1 pad_maximum_fusion.3
  77.1 0.3 reshape_reshape.6
  77.5 0.5 fusion.17
  78.1 1.9 %collective-permute-start.8 = (bf16[6656]{0:T(1024)(128)(2,1)S(1)}, bf16[6656]{0:T(1024)(128)(2,1)S(1)}, u32[]{:S(2)}, u32[]{:S(2)}) collective-permute-start(bf16[6656]{0:T(1024)(128)(2,1)S(1)} %reshape.497), channel_id=1, source_target_pairs={{0,32},{32,64},{64,96},{96,128},{128,160},{160,192},{192,224},{224... | collective-permute-start | bytes 39944 | tf_op jit(solution)/shard_map/ppermute | solution.py:24
  80.1 7.0 %collective-permute-start.9 = (bf16[6656]{0:T(1024)(128)(2,1)S(1)}, bf16[6656]{0:T(1024)(128)(2,1)S(1)}, u32[]{:S(2)}, u32[]{:S(2)}) collective-permute-start(bf16[6656]{0:T(1024)(128)(2,1)S(1)} %reshape.497), channel_id=1, source_target_pairs={{0,480},{32,0},{64,32},{96,64},{128,96},{160,128},{192,160},{224,1... | collective-permute-start | bytes 39944 | tf_op jit(solution)/shard_map/ppermute | solution.py:24
  87.2 0.7 collective-permute-done.9
  88.0 3.3 %collective-permute-start.10 = (bf16[19968]{0:T(1024)(128)(2,1)S(1)}, bf16[19968]{0:T(1024)(128)(2,1)S(1)}, u32[]{:S(2)}, u32[]{:S(2)}) collective-permute-start(bf16[19968]{0:T(1024)(128)(2,1)S(1)} %reshape.498), channel_id=1, source_target_pairs={{0,1},{1,2},{2,3},{3,4},{4,5},{5,6},{6,7},{7,8},{8,9},{9,10},{10,1... | collective-permute-start | bytes 119816 | tf_op jit(solution)/shard_map/ppermute | solution.py:24
  91.4 1.9 %collective-permute-start.11 = (bf16[19968]{0:T(1024)(128)(2,1)S(1)}, bf16[19968]{0:T(1024)(128)(2,1)S(1)}, u32[]{:S(2)}, u32[]{:S(2)}) collective-permute-start(bf16[19968]{0:T(1024)(128)(2,1)S(1)} %reshape.498), channel_id=1, source_target_pairs={{0,31},{1,0},{2,1},{3,2},{4,3},{5,4},{6,5},{7,6},{8,7},{9,8},{10,9... | collective-permute-start | bytes 119816 | tf_op jit(solution)/shard_map/ppermute | solution.py:24
  93.4 5.4 %collective-permute-done.11 = bf16[19968]{0:T(1024)(128)(2,1)S(1)} collective-permute-done((bf16[19968]{0:T(1024)(128)(2,1)S(1)}, bf16[19968]{0:T(1024)(128)(2,1)S(1)}, u32[]{:S(2)}, u32[]{:S(2)}) %collective-permute-start.11) | collective-permute-done | bytes 39968 | tf_op jit(solution)/shard_map/ppermute | solution.py:24
  98.8 0.1 pad_maximum_fusion.4
  99.0 0.3 reshape_reshape.7
  99.4 1.2 %fusion.14 = f32[1,1,16,13,32]{4,2,3,1,0:T(8,128)} fusion(f32[13,16,32]{2,1,0:T(8,128)S(1)} %get-tuple-element.53, bf16[13,16,144,13]{2,1,0,3:T(8,128)(2,1)S(1)} %bitcast.213, bf16[13,144,32,1]{2,1,3,0:T(8,128)(2,1)S(1)} %bitcast.214), kind=kOutput, calls=%fused_computation.27 | convolution fusion | flops 24933376 | bytes 951808 | tf_op jit(solution)/shard_map/qak,qkv->qav/dot_general | solution.py:234
  (148 shorter events, 3.6 us)
Async XLA Ops:
  0.0 25.6 %copy-start = (bf16[256,256]{1,0:T(8,128)(2,1)S(1)}, bf16[256,256]{1,0:T(8,128)(2,1)}, u32[]{:S(2)}) copy-start(bf16[256,256]{1,0:T(8,128)(2,1)} %param.27) | copy-start | bytes 393220
  0.0 22.5 %copy-start.6 = (s32[3]{0:T(128)S(1)}, s32[3]{0:T(128)}, u32[]{:S(2)}) copy-start(s32[3]{0:T(128)} %constant.53) | copy-start | bytes 40
  0.0 22.8 %copy-start.2 = (bf16[256,169]{0,1:T(8,128)(2,1)S(1)}, bf16[256,169]{0,1:T(8,128)(2,1)}, u32[]{:S(2)}) copy-start(bf16[256,169]{0,1:T(8,128)(2,1)} %param.29) | copy-start | bytes 259588
  4.9 19.1 %copy-start.3 = (bf16[256,256]{1,0:T(8,128)(2,1)S(1)}, bf16[256,256]{1,0:T(8,128)(2,1)}, u32[]{:S(2)}) copy-start(bf16[256,256]{1,0:T(8,128)(2,1)} %param.25) | copy-start | bytes 393220
  5.0 18.2 %collective-permute-start = (bf16[13056]{0:T(1024)(128)(2,1)S(1)}, bf16[13056]{0:T(1024)(128)(2,1)S(1)}, u32[]{:S(2)}, u32[]{:S(2)}) collective-permute-start(bf16[13056]{0:T(1024)(128)(2,1)S(1)} %get-tuple-element.32), channel_id=1, source_target_pairs={{0,32},{32,64},{64,96},{96,128},{128,160},{160,192},{192,224},{224... | collective-permute-start | bytes 78344 | tf_op jit(solution)/shard_map/ppermute | solution.py:24
  9.1 14.1 %collective-permute-start.1 = (bf16[13056]{0:T(1024)(128)(2,1)S(1)}, bf16[13056]{0:T(1024)(128)(2,1)S(1)}, u32[]{:S(2)}, u32[]{:S(2)}) collective-permute-start(bf16[13056]{0:T(1024)(128)(2,1)S(1)} %get-tuple-element.33), channel_id=1, source_target_pairs={{0,480},{32,0},{64,32},{96,64},{128,96},{160,128},{192,160},{224,1... | collective-permute-start | bytes 78344 | tf_op jit(solution)/shard_map/ppermute | solution.py:24
  20.8 3.4 %copy-start.4 = (bf16[256,256]{1,0:T(8,128)(2,1)S(1)}, bf16[256,256]{1,0:T(8,128)(2,1)}, u32[]{:S(2)}) copy-start(bf16[256,256]{1,0:T(8,128)(2,1)} %param.26) | copy-start | bytes 393220
  24.0 1.1 %copy-start.8 = (bf16[16,256]{1,0:T(8,128)(2,1)S(1)}, bf16[16,256]{1,0:T(8,128)(2,1)}, u32[]{:S(2)}) copy-start(bf16[16,256]{1,0:T(8,128)(2,1)} %param.24) | copy-start | bytes 24580
  25.1 0.9 copy-start.7
  26.8 8.4 %collective-permute-start.2 = (bf16[34560]{0:T(1024)(128)(2,1)S(1)}, bf16[34560]{0:T(1024)(128)(2,1)S(1)}, u32[]{:S(2)}, u32[]{:S(2)}) collective-permute-start(bf16[34560]{0:T(1024)(128)(2,1)S(1)} %get-tuple-element.27), channel_id=1, source_target_pairs={{0,1},{1,2},{2,3},{3,4},{4,5},{5,6},{6,7},{7,8},{8,9},{9,10},{10,1... | collective-permute-start | bytes 207368 | tf_op jit(solution)/shard_map/ppermute | solution.py:24
  33.0 7.7 %collective-permute-start.3 = (bf16[34560]{0:T(1024)(128)(2,1)S(1)}, bf16[34560]{0:T(1024)(128)(2,1)S(1)}, u32[]{:S(2)}, u32[]{:S(2)}) collective-permute-start(bf16[34560]{0:T(1024)(128)(2,1)S(1)} %get-tuple-element.28), channel_id=1, source_target_pairs={{0,31},{1,0},{2,1},{3,2},{4,3},{5,4},{6,5},{7,6},{8,7},{9,8},{10,9... | collective-permute-start | bytes 207368 | tf_op jit(solution)/shard_map/ppermute | solution.py:24
  41.3 4.8 %copy-start.1 = (bf16[9,10752]{1,0:T(8,128)(2,1)}, bf16[9,10752]{1,0:T(8,128)(2,1)S(1)}, u32[]{:S(2)}) copy-start(bf16[9,10752]{1,0:T(8,128)(2,1)S(1)} %reshape.485) | copy-start | bytes 580612
  53.5 1.8 %slice-start = ((bf16[9,10752]{1,0:T(8,128)(2,1)}), bf16[9,6656]{1,0:T(8,128)(2,1)S(1)}, s32[]{:S(2)}) async-start(bf16[9,10752]{1,0:T(8,128)(2,1)} %copy-done.1), calls=%async_computation | async-start | bytes 425984 | tf_op jit(solution)/shard_map/slice | solution.py:134
  56.4 21.0 %copy-start.5 = (bf16[1,1,16,13,32]{4,2,3,1,0:T(8,128)(2,1)S(1)}, bf16[1,1,16,13,32]{4,2,3,1,0:T(8,128)(2,1)}, u32[]{:S(2)}) copy-start(bf16[1,1,16,13,32]{4,2,3,1,0:T(8,128)(2,1)} %param.19) | copy-start | bytes 39940
  56.6 9.0 %collective-permute-start.4 = (bf16[6656]{0:T(1024)(128)(2,1)S(1)}, bf16[6656]{0:T(1024)(128)(2,1)S(1)}, u32[]{:S(2)}, u32[]{:S(2)}) collective-permute-start(bf16[6656]{0:T(1024)(128)(2,1)S(1)} %reshape.494), channel_id=1, source_target_pairs={{0,32},{32,64},{64,96},{96,128},{128,160},{160,192},{192,224},{224... | collective-permute-start | bytes 39944 | tf_op jit(solution)/shard_map/ppermute | solution.py:24
  58.5 7.8 %collective-permute-start.5 = (bf16[6656]{0:T(1024)(128)(2,1)S(1)}, bf16[6656]{0:T(1024)(128)(2,1)S(1)}, u32[]{:S(2)}, u32[]{:S(2)}) collective-permute-start(bf16[6656]{0:T(1024)(128)(2,1)S(1)} %reshape.494), channel_id=1, source_target_pairs={{0,480},{32,0},{64,32},{96,64},{128,96},{160,128},{192,160},{224,1... | collective-permute-start | bytes 39944 | tf_op jit(solution)/shard_map/ppermute | solution.py:24
  66.5 5.0 %collective-permute-start.6 = (bf16[19968]{0:T(1024)(128)(2,1)S(1)}, bf16[19968]{0:T(1024)(128)(2,1)S(1)}, u32[]{:S(2)}, u32[]{:S(2)}) collective-permute-start(bf16[19968]{0:T(1024)(128)(2,1)S(1)} %reshape.495), channel_id=1, source_target_pairs={{0,1},{1,2},{2,3},{3,4},{4,5},{5,6},{6,7},{7,8},{8,9},{9,10},{10,1... | collective-permute-start | bytes 119816 | tf_op jit(solution)/shard_map/ppermute | solution.py:24
  69.5 7.4 %collective-permute-start.7 = (bf16[19968]{0:T(1024)(128)(2,1)S(1)}, bf16[19968]{0:T(1024)(128)(2,1)S(1)}, u32[]{:S(2)}, u32[]{:S(2)}) collective-permute-start(bf16[19968]{0:T(1024)(128)(2,1)S(1)} %reshape.495), channel_id=1, source_target_pairs={{0,31},{1,0},{2,1},{3,2},{4,3},{5,4},{6,5},{7,6},{8,7},{9,8},{10,9... | collective-permute-start | bytes 119816 | tf_op jit(solution)/shard_map/ppermute | solution.py:24
  78.1 9.0 %collective-permute-start.8 = (bf16[6656]{0:T(1024)(128)(2,1)S(1)}, bf16[6656]{0:T(1024)(128)(2,1)S(1)}, u32[]{:S(2)}, u32[]{:S(2)}) collective-permute-start(bf16[6656]{0:T(1024)(128)(2,1)S(1)} %reshape.497), channel_id=1, source_target_pairs={{0,32},{32,64},{64,96},{96,128},{128,160},{160,192},{192,224},{224... | collective-permute-start | bytes 39944 | tf_op jit(solution)/shard_map/ppermute | solution.py:24
  80.1 7.8 %collective-permute-start.9 = (bf16[6656]{0:T(1024)(128)(2,1)S(1)}, bf16[6656]{0:T(1024)(128)(2,1)S(1)}, u32[]{:S(2)}, u32[]{:S(2)}) collective-permute-start(bf16[6656]{0:T(1024)(128)(2,1)S(1)} %reshape.497), channel_id=1, source_target_pairs={{0,480},{32,0},{64,32},{96,64},{128,96},{160,128},{192,160},{224,1... | collective-permute-start | bytes 39944 | tf_op jit(solution)/shard_map/ppermute | solution.py:24
  88.0 5.4 %collective-permute-start.10 = (bf16[19968]{0:T(1024)(128)(2,1)S(1)}, bf16[19968]{0:T(1024)(128)(2,1)S(1)}, u32[]{:S(2)}, u32[]{:S(2)}) collective-permute-start(bf16[19968]{0:T(1024)(128)(2,1)S(1)} %reshape.498), channel_id=1, source_target_pairs={{0,1},{1,2},{2,3},{3,4},{4,5},{5,6},{6,7},{7,8},{8,9},{9,10},{10,1... | collective-permute-start | bytes 119816 | tf_op jit(solution)/shard_map/ppermute | solution.py:24
  91.4 7.4 %collective-permute-start.11 = (bf16[19968]{0:T(1024)(128)(2,1)S(1)}, bf16[19968]{0:T(1024)(128)(2,1)S(1)}, u32[]{:S(2)}, u32[]{:S(2)}) collective-permute-start(bf16[19968]{0:T(1024)(128)(2,1)S(1)} %reshape.498), channel_id=1, source_target_pairs={{0,31},{1,0},{2,1},{3,2},{4,3},{5,4},{6,5},{7,6},{8,7},{9,8},{10,9... | collective-permute-start | bytes 119816 | tf_op jit(solution)/shard_map/ppermute | solution.py:24

commit v11 on v10

--- a/solution.py
+++ b/solution.py
@@ -111,10 +111,10 @@
     vec = band_vectors.shape[4]
     orb = ORBITAL_COUNT
     slots = pair_source.shape[3]
-    kind_hot = (
-        atom_kinds[0, 0][:, None] == jnp.arange(kind_table.shape[0], dtype=jnp.int32)[None, :]
-    ).astype(f32)
-    embedded = jnp.dot(kind_hot, kind_table, precision=lax.Precision.HIGHEST)
+    kinds = atom_kinds[0, 0][:, None]
+    embedded = jnp.zeros((atom_count, feat), f32)
+    for kind in range(kind_table.shape[0]):
+        embedded = jnp.where(kinds == kind, kind_table[kind][None, :], embedded)
     atoms = (features[0, 0].astype(f32) + embedded).astype(bf16)
 
     offsets = pair_offsets[0, 0]

time: 101 us -> 103 us (1.020)
  local copies, waits for them, and re-layouts: 9.12 us -> 10.7 us
  other arithmetic: 6.88 us -> 8.34 us
    dot_general x0 -> x2, local copies, waits for them, and re-layouts: none -> 1.21 us  [on_device(): jnp.dot(atoms, w_site, preferred_element_type=f32).reshape(-1, orb, orb)]
    unnamed x9 -> x11, other arithmetic: 1.64 us -> 2.41 us
    unnamed x25 -> x26, local copies, waits for them, and re-layouts: 2.39 us -> 2.41 us
  transfers between devices with their start and end apart: 12 -> 12, of which waited for: 5 -> 5; matrix products, arithmetic and copies ran while one was open for 4% -> 5% of each run, Pallas kernels for 0% -> 0%
where the time goes in v11:
time: 103 us
  starting transfers between devices  50.4 us (49%)
  waiting for transfers between devices  17.6 us (17%)
  matrix products  14.6 us (14%)
  local copies, waits for them, and re-layouts  10.7 us (10%)
  other arithmetic  8.34 us (8%)
    ppermute x12, starting transfers between devices, shifted(): return lax.ppermute(value, axis, pairs)  50.4 us
    ppermute x12, waiting for transfers between devices, shifted(): return lax.ppermute(value, axis, pairs)  17.6 us
    dot_general x1, matrix products, on_device(): jnp.dot(spread, column_hot, preferred_element_type=f32)  4.91 us
    mul x1, other arithmetic, on_device(): blocks_t[:, None, :] * row_hot[None, :, :]  2.42 us
    unnamed x11, other arithmetic  2.41 us
    unnamed x26, local copies, waits for them, and re-layouts  2.41 us
    dot_general x3, matrix products, apply(): jnp.einsum('qak,qkv->qav', dense_parts, by_orbital, preferred_element_typ...  2.21 us
    dot_general x2, matrix products, group_blocks(): picked = jnp.dot(pick, table_parts, preferred_element_type=f32)  2.15 us
  transfers between devices with their start and end apart: 12, of which 5 were waited for; matrix products, arithmetic and copies ran while one was open for 5% of the time, Pallas kernels for 0%

profile of v11, /device:TPU:27, one launch (start us, length us, event | category | flops | bytes accessed | tf_op | source)
XLA Modules:
  0.0 102.6 jit_solution(5180664608212739131)
XLA Ops:
  0.0 0.8 fusion.81
  0.8 0.8 fusion.82
  1.5 0.7 constant_dynamic-update-slice_fusion.5
  2.2 0.7 constant_dynamic-update-slice_fusion.4
  3.1 0.8 fusion.83
  3.8 0.7 compare_bitcast_fusion.1
  4.6 0.7 convert_bitcast_fusion.1
  5.3 0.8 copy.74
  6.3 4.1 %collective-permute-start = (bf16[13056]{0:T(1024)(128)(2,1)S(1)}, bf16[13056]{0:T(1024)(128)(2,1)S(1)}, u32[]{:S(2)}, u32[]{:S(2)}) collective-permute-start(bf16[13056]{0:T(1024)(128)(2,1)S(1)} %get-tuple-element.32), channel_id=1, source_target_pairs={{0,32},{32,64},{64,96},{96,128},{128,160},{160,192},{192,224},{224... | collective-permute-start | bytes 78344 | tf_op jit(solution)/shard_map/ppermute | solution.py:24
  10.4 10.1 %collective-permute-start.1 = (bf16[13056]{0:T(1024)(128)(2,1)S(1)}, bf16[13056]{0:T(1024)(128)(2,1)S(1)}, u32[]{:S(2)}, u32[]{:S(2)}) collective-permute-start(bf16[13056]{0:T(1024)(128)(2,1)S(1)} %get-tuple-element.33), channel_id=1, source_target_pairs={{0,480},{32,0},{64,32},{96,64},{128,96},{160,128},{192,160},{224,1... | collective-permute-start | bytes 78344 | tf_op jit(solution)/shard_map/ppermute | solution.py:24
  20.6 0.7 copy.157
  21.3 0.7 copy.156
  22.3 1.0 dot_general.100
  23.3 0.9 fusion.55
  24.2 0.2 copy.86
  25.0 0.2 copy.101
  25.6 0.2 pad_maximum_fusion.6
  25.8 0.2 fusion.122
  26.1 0.1 fusion.85
  26.2 0.2 fusion.86
  26.5 0.6 fusion.30
  27.2 0.5 multiply_convert_fusion.1
  27.7 0.3 fusion.87
  27.9 0.1 copy-done.7
  28.1 0.3 fusion.9
  28.4 0.2 convolution_bitcast_fusion.2
  28.6 0.2 convolution_bitcast_fusion.3
  28.9 6.1 %collective-permute-start.2 = (bf16[34560]{0:T(1024)(128)(2,1)S(1)}, bf16[34560]{0:T(1024)(128)(2,1)S(1)}, u32[]{:S(2)}, u32[]{:S(2)}) collective-permute-start(bf16[34560]{0:T(1024)(128)(2,1)S(1)} %get-tuple-element.27), channel_id=1, source_target_pairs={{0,1},{1,2},{2,3},{3,4},{4,5},{5,6},{6,7},{7,8},{8,9},{9,10},{10,1... | collective-permute-start | bytes 207368 | tf_op jit(solution)/shard_map/ppermute | solution.py:24
  35.0 2.1 %collective-permute-start.3 = (bf16[34560]{0:T(1024)(128)(2,1)S(1)}, bf16[34560]{0:T(1024)(128)(2,1)S(1)}, u32[]{:S(2)}, u32[]{:S(2)}) collective-permute-start(bf16[34560]{0:T(1024)(128)(2,1)S(1)} %get-tuple-element.28), channel_id=1, source_target_pairs={{0,31},{1,0},{2,1},{3,2},{4,3},{5,4},{6,5},{7,6},{8,7},{9,8},{10,9... | collective-permute-start | bytes 207368 | tf_op jit(solution)/shard_map/ppermute | solution.py:24
  37.3 5.4 %collective-permute-done.3 = bf16[34560]{0:T(1024)(128)(2,1)S(1)} collective-permute-done((bf16[34560]{0:T(1024)(128)(2,1)S(1)}, bf16[34560]{0:T(1024)(128)(2,1)S(1)}, u32[]{:S(2)}, u32[]{:S(2)}) %collective-permute-start.3) | collective-permute-done | bytes 69152 | tf_op jit(solution)/shard_map/ppermute | solution.py:24
  42.8 0.2 pad_maximum_fusion.2
  43.0 0.1 copy.85
  43.1 0.2 reshape.599
  43.4 0.2 fusion.88
  43.6 0.2 fusion.89
  44.2 1.6 %fusion.2 = f32[1536,768]{1,0:T(8,128)S(1)} fusion(s32[1536]{0:T(1024)S(1)} %add_add_fusion, s32[1536]{0:T(1024)S(1)} %pad_add_fusion, bf16[288,256]{1,0:T(8,128)(2,1)S(1)} %get-tuple-element.23, bf16[288,256]{1,0:T(8,128)(2,1)S(1)} %get-tuple-element.22, bf16[288,256]{1,0:T(8,128)(2,1)S(1)} %get-tuple-element.21), kind=kOutput, calls=%fused_computation.7 | convolution fusion | flops 682131456 | bytes 5173248 | tf_op jit(solution)/shard_map/dot_general | solution.py:175
  45.8 0.8 multiply_convert_fusion
  46.6 0.4 fusion.90
  46.9 0.5 fusion
  47.5 0.3 convolution_bitcast_fusion.1
  47.8 0.3 convolution_bitcast_fusion
  48.3 2.4 %broadcast_multiply_fusion = bf16[169,16,2320]{2,1,0:T(8,128)(2,1)S(1)} fusion(bf16[16,2320]{1,0:T(8,128)(2,1)S(1)} %fusion.37, bf16[169,2320]{1,0:T(8,128)(2,1)S(1)} %pad_maximum_fusion), kind=kLoop, calls=%fused_computation | loop fusion | flops 6273280 | bytes 13404960 | tf_op jit(solution)/shard_map/mul | solution.py:223
  50.7 4.9 %fusion.6 = bf16[208,144,13]{0,1,2:T(8,128)(2,1)S(1)} fusion(bf16[13,208,2320]{2,1,0:T(8,128)(2,1)S(1)} %bitcast.218, s32[2320]{0:T(1024)S(1)} %constant_dynamic-update-slice_fusion.9), kind=kOutput, calls=%fused_computation.14 | convolution fusion | flops 1807428096 | bytes 13334592 | tf_op jit(solution)/shard_map/dot_general | solution.py:225
  55.6 1.8 %copy.89 = bf16[208,144,13]{1,0,2:T(8,128)(2,1)S(1)} copy(bf16[208,144,13]{0,1,2:T(8,128)(2,1)S(1)} %fusion.6) | data formatting | bytes 1557504 | tf_op jit(solution)/shard_map/convert_element_type | solution.py:228
  57.4 0.6 reshape.605
  58.0 0.5 fusion.84
  58.7 1.9 %collective-permute-start.4 = (bf16[6656]{0:T(1024)(128)(2,1)S(1)}, bf16[6656]{0:T(1024)(128)(2,1)S(1)}, u32[]{:S(2)}, u32[]{:S(2)}) collective-permute-start(bf16[6656]{0:T(1024)(128)(2,1)S(1)} %reshape.607), channel_id=1, source_target_pairs={{0,32},{32,64},{64,96},{96,128},{128,160},{160,192},{192,224},{224... | collective-permute-start | bytes 39944 | tf_op jit(solution)/shard_map/ppermute | solution.py:24
  60.6 7.0 %collective-permute-start.5 = (bf16[6656]{0:T(1024)(128)(2,1)S(1)}, bf16[6656]{0:T(1024)(128)(2,1)S(1)}, u32[]{:S(2)}, u32[]{:S(2)}) collective-permute-start(bf16[6656]{0:T(1024)(128)(2,1)S(1)} %reshape.607), channel_id=1, source_target_pairs={{0,480},{32,0},{64,32},{96,64},{128,96},{160,128},{192,160},{224,1... | collective-permute-start | bytes 39944 | tf_op jit(solution)/shard_map/ppermute | solution.py:24
  67.7 0.7 collective-permute-done.5
  68.6 2.9 %collective-permute-start.6 = (bf16[19968]{0:T(1024)(128)(2,1)S(1)}, bf16[19968]{0:T(1024)(128)(2,1)S(1)}, u32[]{:S(2)}, u32[]{:S(2)}) collective-permute-start(bf16[19968]{0:T(1024)(128)(2,1)S(1)} %reshape.608), channel_id=1, source_target_pairs={{0,1},{1,2},{2,3},{3,4},{4,5},{5,6},{6,7},{7,8},{8,9},{9,10},{10,1... | collective-permute-start | bytes 119816 | tf_op jit(solution)/shard_map/ppermute | solution.py:24
  71.5 1.9 %collective-permute-start.7 = (bf16[19968]{0:T(1024)(128)(2,1)S(1)}, bf16[19968]{0:T(1024)(128)(2,1)S(1)}, u32[]{:S(2)}, u32[]{:S(2)}) collective-permute-start(bf16[19968]{0:T(1024)(128)(2,1)S(1)} %reshape.608), channel_id=1, source_target_pairs={{0,31},{1,0},{2,1},{3,2},{4,3},{5,4},{6,5},{7,6},{8,7},{9,8},{10,9... | collective-permute-start | bytes 119816 | tf_op jit(solution)/shard_map/ppermute | solution.py:24
  73.6 5.4 %collective-permute-done.7 = bf16[19968]{0:T(1024)(128)(2,1)S(1)} collective-permute-done((bf16[19968]{0:T(1024)(128)(2,1)S(1)}, bf16[19968]{0:T(1024)(128)(2,1)S(1)}, u32[]{:S(2)}, u32[]{:S(2)}) %collective-permute-start.7) | collective-permute-done | bytes 39968 | tf_op jit(solution)/shard_map/ppermute | solution.py:24
  79.0 0.1 pad_maximum_fusion.3
  79.2 0.3 reshape_reshape.6
  79.5 0.5 fusion.17
  80.2 1.9 %collective-permute-start.8 = (bf16[6656]{0:T(1024)(128)(2,1)S(1)}, bf16[6656]{0:T(1024)(128)(2,1)S(1)}, u32[]{:S(2)}, u32[]{:S(2)}) collective-permute-start(bf16[6656]{0:T(1024)(128)(2,1)S(1)} %reshape.610), channel_id=1, source_target_pairs={{0,32},{32,64},{64,96},{96,128},{128,160},{160,192},{192,224},{224... | collective-permute-start | bytes 39944 | tf_op jit(solution)/shard_map/ppermute | solution.py:24
  82.1 7.0 %collective-permute-start.9 = (bf16[6656]{0:T(1024)(128)(2,1)S(1)}, bf16[6656]{0:T(1024)(128)(2,1)S(1)}, u32[]{:S(2)}, u32[]{:S(2)}) collective-permute-start(bf16[6656]{0:T(1024)(128)(2,1)S(1)} %reshape.610), channel_id=1, source_target_pairs={{0,480},{32,0},{64,32},{96,64},{128,96},{160,128},{192,160},{224,1... | collective-permute-start | bytes 39944 | tf_op jit(solution)/shard_map/ppermute | solution.py:24
  89.2 0.7 collective-permute-done.9
  90.1 3.3 %collective-permute-start.10 = (bf16[19968]{0:T(1024)(128)(2,1)S(1)}, bf16[19968]{0:T(1024)(128)(2,1)S(1)}, u32[]{:S(2)}, u32[]{:S(2)}) collective-permute-start(bf16[19968]{0:T(1024)(128)(2,1)S(1)} %reshape.611), channel_id=1, source_target_pairs={{0,1},{1,2},{2,3},{3,4},{4,5},{5,6},{6,7},{7,8},{8,9},{9,10},{10,1... | collective-permute-start | bytes 119816 | tf_op jit(solution)/shard_map/ppermute | solution.py:24
  93.4 1.9 %collective-permute-start.11 = (bf16[19968]{0:T(1024)(128)(2,1)S(1)}, bf16[19968]{0:T(1024)(128)(2,1)S(1)}, u32[]{:S(2)}, u32[]{:S(2)}) collective-permute-start(bf16[19968]{0:T(1024)(128)(2,1)S(1)} %reshape.611), channel_id=1, source_target_pairs={{0,31},{1,0},{2,1},{3,2},{4,3},{5,4},{6,5},{7,6},{8,7},{9,8},{10,9... | collective-permute-start | bytes 119816 | tf_op jit(solution)/shard_map/ppermute | solution.py:24
  95.5 5.4 %collective-permute-done.11 = bf16[19968]{0:T(1024)(128)(2,1)S(1)} collective-permute-done((bf16[19968]{0:T(1024)(128)(2,1)S(1)}, bf16[19968]{0:T(1024)(128)(2,1)S(1)}, u32[]{:S(2)}, u32[]{:S(2)}) %collective-permute-start.11) | collective-permute-done | bytes 39968 | tf_op jit(solution)/shard_map/ppermute | solution.py:24
  100.9 0.1 pad_maximum_fusion.4
  101.1 0.3 reshape_reshape.7
  101.4 1.2 %fusion.14 = f32[1,1,16,13,32]{4,2,3,1,0:T(8,128)} fusion(f32[13,16,32]{2,1,0:T(8,128)S(1)} %get-tuple-element.57, bf16[13,16,144,13]{2,1,0,3:T(8,128)(2,1)S(1)} %bitcast.221, bf16[13,144,32,1]{2,1,3,0:T(8,128)(2,1)S(1)} %bitcast.222), kind=kOutput, calls=%fused_computation.27 | convolution fusion | flops 24933376 | bytes 951808 | tf_op jit(solution)/shard_map/qak,qkv->qav/dot_general | solution.py:234
  (153 shorter events, 3.9 us)
Async XLA Ops:
  0.0 27.7 %copy-start = (bf16[256,256]{1,0:T(8,128)(2,1)S(1)}, bf16[256,256]{1,0:T(8,128)(2,1)}, u32[]{:S(2)}) copy-start(bf16[256,256]{1,0:T(8,128)(2,1)} %param.27) | copy-start | bytes 393220
  0.0 24.6 %copy-start.6 = (s32[3]{0:T(128)S(1)}, s32[3]{0:T(128)}, u32[]{:S(2)}) copy-start(s32[3]{0:T(128)} %constant.59) | copy-start | bytes 40
  0.0 24.9 %copy-start.2 = (bf16[256,169]{0,1:T(8,128)(2,1)S(1)}, bf16[256,169]{0,1:T(8,128)(2,1)}, u32[]{:S(2)}) copy-start(bf16[256,169]{0,1:T(8,128)(2,1)} %param.29) | copy-start | bytes 259588
  6.3 19.8 %copy-start.3 = (bf16[256,256]{1,0:T(8,128)(2,1)S(1)}, bf16[256,256]{1,0:T(8,128)(2,1)}, u32[]{:S(2)}) copy-start(bf16[256,256]{1,0:T(8,128)(2,1)} %param.25) | copy-start | bytes 393220
  6.3 19.0 %collective-permute-start = (bf16[13056]{0:T(1024)(128)(2,1)S(1)}, bf16[13056]{0:T(1024)(128)(2,1)S(1)}, u32[]{:S(2)}, u32[]{:S(2)}) collective-permute-start(bf16[13056]{0:T(1024)(128)(2,1)S(1)} %get-tuple-element.32), channel_id=1, source_target_pairs={{0,32},{32,64},{64,96},{96,128},{128,160},{160,192},{192,224},{224... | collective-permute-start | bytes 78344 | tf_op jit(solution)/shard_map/ppermute | solution.py:24
  10.4 14.9 %collective-permute-start.1 = (bf16[13056]{0:T(1024)(128)(2,1)S(1)}, bf16[13056]{0:T(1024)(128)(2,1)S(1)}, u32[]{:S(2)}, u32[]{:S(2)}) collective-permute-start(bf16[13056]{0:T(1024)(128)(2,1)S(1)} %get-tuple-element.33), channel_id=1, source_target_pairs={{0,480},{32,0},{64,32},{96,64},{128,96},{160,128},{192,160},{224,1... | collective-permute-start | bytes 78344 | tf_op jit(solution)/shard_map/ppermute | solution.py:24
  22.3 3.9 %copy-start.4 = (bf16[256,256]{1,0:T(8,128)(2,1)S(1)}, bf16[256,256]{1,0:T(8,128)(2,1)}, u32[]{:S(2)}) copy-start(bf16[256,256]{1,0:T(8,128)(2,1)} %param.26) | copy-start | bytes 393220
  26.1 1.1 %copy-start.8 = (bf16[16,256]{1,0:T(8,128)(2,1)S(1)}, bf16[16,256]{1,0:T(8,128)(2,1)}, u32[]{:S(2)}) copy-start(bf16[16,256]{1,0:T(8,128)(2,1)} %param.24) | copy-start | bytes 24580
  27.1 0.9 copy-start.7
  28.9 8.4 %collective-permute-start.2 = (bf16[34560]{0:T(1024)(128)(2,1)S(1)}, bf16[34560]{0:T(1024)(128)(2,1)S(1)}, u32[]{:S(2)}, u32[]{:S(2)}) collective-permute-start(bf16[34560]{0:T(1024)(128)(2,1)S(1)} %get-tuple-element.27), channel_id=1, source_target_pairs={{0,1},{1,2},{2,3},{3,4},{4,5},{5,6},{6,7},{7,8},{8,9},{9,10},{10,1... | collective-permute-start | bytes 207368 | tf_op jit(solution)/shard_map/ppermute | solution.py:24
  35.0 7.7 %collective-permute-start.3 = (bf16[34560]{0:T(1024)(128)(2,1)S(1)}, bf16[34560]{0:T(1024)(128)(2,1)S(1)}, u32[]{:S(2)}, u32[]{:S(2)}) collective-permute-start(bf16[34560]{0:T(1024)(128)(2,1)S(1)} %get-tuple-element.28), channel_id=1, source_target_pairs={{0,31},{1,0},{2,1},{3,2},{4,3},{5,4},{6,5},{7,6},{8,7},{9,8},{10,9... | collective-permute-start | bytes 207368 | tf_op jit(solution)/shard_map/ppermute | solution.py:24
  43.3 4.7 %copy-start.1 = (bf16[9,10752]{1,0:T(8,128)(2,1)}, bf16[9,10752]{1,0:T(8,128)(2,1)S(1)}, u32[]{:S(2)}) copy-start(bf16[9,10752]{1,0:T(8,128)(2,1)S(1)} %reshape.599) | copy-start | bytes 580612
  55.6 1.8 %slice-start = ((bf16[9,10752]{1,0:T(8,128)(2,1)}), bf16[9,6656]{1,0:T(8,128)(2,1)S(1)}, s32[]{:S(2)}) async-start(bf16[9,10752]{1,0:T(8,128)(2,1)} %copy-done.1), calls=%async_computation | async-start | bytes 425984 | tf_op jit(solution)/shard_map/slice | solution.py:134
  58.5 21.0 %copy-start.5 = (bf16[1,1,16,13,32]{4,2,3,1,0:T(8,128)(2,1)S(1)}, bf16[1,1,16,13,32]{4,2,3,1,0:T(8,128)(2,1)}, u32[]{:S(2)}) copy-start(bf16[1,1,16,13,32]{4,2,3,1,0:T(8,128)(2,1)} %param.19) | copy-start | bytes 39940
  58.7 9.0 %collective-permute-start.4 = (bf16[6656]{0:T(1024)(128)(2,1)S(1)}, bf16[6656]{0:T(1024)(128)(2,1)S(1)}, u32[]{:S(2)}, u32[]{:S(2)}) collective-permute-start(bf16[6656]{0:T(1024)(128)(2,1)S(1)} %reshape.607), channel_id=1, source_target_pairs={{0,32},{32,64},{64,96},{96,128},{128,160},{160,192},{192,224},{224... | collective-permute-start | bytes 39944 | tf_op jit(solution)/shard_map/ppermute | solution.py:24
  60.6 7.8 %collective-permute-start.5 = (bf16[6656]{0:T(1024)(128)(2,1)S(1)}, bf16[6656]{0:T(1024)(128)(2,1)S(1)}, u32[]{:S(2)}, u32[]{:S(2)}) collective-permute-start(bf16[6656]{0:T(1024)(128)(2,1)S(1)} %reshape.607), channel_id=1, source_target_pairs={{0,480},{32,0},{64,32},{96,64},{128,96},{160,128},{192,160},{224,1... | collective-permute-start | bytes 39944 | tf_op jit(solution)/shard_map/ppermute | solution.py:24
  68.6 5.0 %collective-permute-start.6 = (bf16[19968]{0:T(1024)(128)(2,1)S(1)}, bf16[19968]{0:T(1024)(128)(2,1)S(1)}, u32[]{:S(2)}, u32[]{:S(2)}) collective-permute-start(bf16[19968]{0:T(1024)(128)(2,1)S(1)} %reshape.608), channel_id=1, source_target_pairs={{0,1},{1,2},{2,3},{3,4},{4,5},{5,6},{6,7},{7,8},{8,9},{9,10},{10,1... | collective-permute-start | bytes 119816 | tf_op jit(solution)/shard_map/ppermute | solution.py:24
  71.5 7.4 %collective-permute-start.7 = (bf16[19968]{0:T(1024)(128)(2,1)S(1)}, bf16[19968]{0:T(1024)(128)(2,1)S(1)}, u32[]{:S(2)}, u32[]{:S(2)}) collective-permute-start(bf16[19968]{0:T(1024)(128)(2,1)S(1)} %reshape.608), channel_id=1, source_target_pairs={{0,31},{1,0},{2,1},{3,2},{4,3},{5,4},{6,5},{7,6},{8,7},{9,8},{10,9... | collective-permute-start | bytes 119816 | tf_op jit(solution)/shard_map/ppermute | solution.py:24
  80.2 9.0 %collective-permute-start.8 = (bf16[6656]{0:T(1024)(128)(2,1)S(1)}, bf16[6656]{0:T(1024)(128)(2,1)S(1)}, u32[]{:S(2)}, u32[]{:S(2)}) collective-permute-start(bf16[6656]{0:T(1024)(128)(2,1)S(1)} %reshape.610), channel_id=1, source_target_pairs={{0,32},{32,64},{64,96},{96,128},{128,160},{160,192},{192,224},{224... | collective-permute-start | bytes 39944 | tf_op jit(solution)/shard_map/ppermute | solution.py:24
  82.1 7.8 %collective-permute-start.9 = (bf16[6656]{0:T(1024)(128)(2,1)S(1)}, bf16[6656]{0:T(1024)(128)(2,1)S(1)}, u32[]{:S(2)}, u32[]{:S(2)}) collective-permute-start(bf16[6656]{0:T(1024)(128)(2,1)S(1)} %reshape.610), channel_id=1, source_target_pairs={{0,480},{32,0},{64,32},{96,64},{128,96},{160,128},{192,160},{224,1... | collective-permute-start | bytes 39944 | tf_op jit(solution)/shard_map/ppermute | solution.py:24
  90.1 5.4 %collective-permute-start.10 = (bf16[19968]{0:T(1024)(128)(2,1)S(1)}, bf16[19968]{0:T(1024)(128)(2,1)S(1)}, u32[]{:S(2)}, u32[]{:S(2)}) collective-permute-start(bf16[19968]{0:T(1024)(128)(2,1)S(1)} %reshape.611), channel_id=1, source_target_pairs={{0,1},{1,2},{2,3},{3,4},{4,5},{5,6},{6,7},{7,8},{8,9},{9,10},{10,1... | collective-permute-start | bytes 119816 | tf_op jit(solution)/shard_map/ppermute | solution.py:24
  93.4 7.4 %collective-permute-start.11 = (bf16[19968]{0:T(1024)(128)(2,1)S(1)}, bf16[19968]{0:T(1024)(128)(2,1)S(1)}, u32[]{:S(2)}, u32[]{:S(2)}) collective-permute-start(bf16[19968]{0:T(1024)(128)(2,1)S(1)} %reshape.611), channel_id=1, source_target_pairs={{0,31},{1,0},{2,1},{3,2},{4,3},{5,4},{6,5},{7,6},{8,7},{9,8},{10,9... | collective-permute-start | bytes 119816 | tf_op jit(solution)/shard_map/ppermute | solution.py:24
